TPU v7x, 32 devices: a whole 2x2x4 slice. The times are simulated.
32 devices in a mesh: narrow: 8 (over z, x), wide: 4 (over y, core).
Axes of the slice: x: 2, y: 2, z: 4, core: 2. Of those that a mesh axis runs over, the one named last changes fastest.
Arguments:
- amps: bfloat16 [16, 512, 512], P(None, 'narrow', 'wide'), may hold values from -1 to 1
- left_fit: bfloat16 [64, 512, 256], P(None, 'narrow'), may hold values from -0.375 to 0.375
- right_fit: bfloat16 [512, 512, 256], P('narrow', 'wide'), may hold values from -0.375 to 0.375
- pair_list: int32 [16, 2], P('narrow'), may hold values from 0 to 127, as said below
- occ_energy: float32 [128], replicated, may hold values from -2 to -0.5
- vir_energy: float32 [512], replicated, may hold values from 0.5 to 3
Outputs:
- update: float32 [16, 64, 512], P('narrow', None, 'wide')
Inputs may be any that keep to these rules, and one draw needn't show every extreme that they name: `pair_list`: each row (i, j) has i <= j.
All inputs are finite; a program needn't handle non-finite values.
Results may differ from a plain program's by a relative error of at most 0.0029.
Values may be sent and summed in bfloat16 or wider, within the bound.
No kernel may reach another device: no remote copies, remote signals or barrier semaphores. Data moves between devices by JAX's collectives and lax.ppermute only.
A program may use at most 128 MiB of HBM per device.

v0:
```python
import jax
import jax.numpy as jnp
from jax import lax
from jax.sharding import PartitionSpec as P

GROUPS = 2


def make_body(n_narrow, n_wide):
    span = n_narrow // GROUPS

    def body(amps, left_fit, right_fit, pair_list, occ_energy, vir_energy):
        n = lax.axis_index("narrow")
        w = lax.axis_index("wide")
        r = n % span
        g = n // span
        b_blk, d_blk, aux = right_fit.shape
        q_blk = aux // span
        rows, c_blk, _ = left_fit.shape
        pairs = amps.shape[0]
        vir_total = b_blk * n_narrow

        amps_all = lax.all_gather(amps, "narrow", axis=1, tiled=True)

        c_sub = c_blk // n_wide
        left_part = lax.dynamic_slice_in_dim(left_fit, w * c_sub, c_sub, 1)
        left_part = left_part.reshape(rows, c_sub, span, q_blk).transpose(2, 0, 1, 3)
        left_send = jnp.concatenate([left_part] * GROUPS, axis=0)
        left_recv = lax.all_to_all(left_send, "narrow", 0, 0, tiled=True)
        left_all = lax.all_gather(left_recv, "wide", axis=0, tiled=False)
        left_all = left_all.transpose(2, 1, 0, 3, 4).reshape(rows, c_blk * n_narrow, q_blk)

        right_split = right_fit.reshape(b_blk, d_blk, span, q_blk)
        chunks = []
        for shift in range(span):
            dest = (r + shift) % span
            piece = lax.dynamic_index_in_dim(right_split, dest, 2, keepdims=False)
            if shift:
                perm = [
                    (gg * span + i, gg * span + (i + shift) % span)
                    for gg in range(GROUPS)
                    for i in range(span)
                ]
                piece = lax.ppermute(piece, "narrow", perm)
            chunks.append(piece)

        inter = jnp.einsum(
            "acq,pcd->padq", left_all, amps_all, preferred_element_type=jnp.float32
        ).astype(jnp.bfloat16)

        right_group = jnp.concatenate(chunks, axis=0)
        part = lax.dot_general(
            inter.reshape(pairs * rows, d_blk * q_blk),
            right_group.reshape(span * b_blk, d_blk * q_blk),
            (((1,), (1,)), ((), ())),
            preferred_element_type=jnp.float32,
        ).reshape(pairs, rows, span, b_blk)
        flipped = jnp.concatenate(
            [part[:, :, (span - k) % span : (span - k) % span + 1] for k in range(span)] * 2, axis=2
        )
        ordered = lax.dynamic_slice_in_dim(flipped, span - r, span, 2)
        ordered = ordered.reshape(pairs, rows, span * b_blk)
        pad = jnp.zeros((pairs, rows, (GROUPS - 1) * span * b_blk), jnp.float32)
        padded = jnp.concatenate([pad, ordered, pad], axis=2)
        ladder = lax.dynamic_slice_in_dim(
            padded, (GROUPS - 1 - g) * span * b_blk, vir_total, 2
        )

        ladder = lax.psum_scatter(ladder, "wide", scatter_dimension=2, tiled=True)
        ladder = lax.psum_scatter(ladder, "narrow", scatter_dimension=0, tiled=True)

        local_cols = ladder.shape[2]
        occ_ids = jnp.arange(occ_energy.shape[0], dtype=jnp.int32)
        occ_first = jnp.sum(
            jnp.where(pair_list[:, 0:1] == occ_ids[None, :], occ_energy[None, :], 0.0), axis=1
        )
        occ_second = jnp.sum(
            jnp.where(pair_list[:, 1:2] == occ_ids[None, :], occ_energy[None, :], 0.0), axis=1
        )
        vir_cols = lax.dynamic_slice_in_dim(vir_energy, w * local_cols, local_cols, 0)
        vir_rows = vir_energy[:rows]
        denominator = (
            (occ_first + occ_second)[:, None, None] - vir_rows[None, :, None] - vir_cols[None, None, :]
        )
        return ladder / denominator

    return body


def solution(mesh):
    return jax.shard_map(
        make_body(mesh.shape["narrow"], mesh.shape["wide"]),
        mesh=mesh,
        in_specs=(
            P(None, "narrow", "wide"),
            P(None, "narrow", None),
            P("narrow", "wide", None),
            P("narrow", None),
            P(),
            P(),
        ),
        out_specs=P("narrow", None, "wide"),
        check_vma=False,
    )
```

profile of v0, /device:TPU:5, one launch (start us, length us, event | category | flops | bytes accessed | tf_op | source)
XLA Modules:
  0.0 372.5 jit_solution(8755748005040324394)
XLA Ops:
  9.0 2.0 reshape.61
  13.9 3.4 reshape.73
  17.3 30.2 %all_to_all.5 = bf16[8,2,32768]{2,1,0:T(2,128)(2,1)S(1)} all-to-all(bf16[8,2,32768]{2,1,0:T(2,128)(2,1)S(1)} %reshape.73), channel_id=1, replica_groups=mesh['narrow'=8,'wide'=4] {'narrow'}, dimensions={0} | all-to-all | bytes 2097152 | tf_op jit(solution)/shard_map/all_to_all | solution.py:29
  47.5 2.7 reshape.74
  51.1 6.4 %copy.50 = bf16[64,128,256]{1,2,0:T(8,128)(2,1)} copy(bf16[64,128,256]{2,1,0:T(8,128)(2,1)} %param.8) | data formatting | bytes 8388608 | tf_op args[2]
  57.5 5.3 %constant_dynamic-slice_fusion.1 = (bf16[64,128,1,64]{1,3,2,0:T(8,128)(2,1)S(1)}, bf16[64,128,64]{1,2,0:T(8,128)(2,1)}, bf16[64,128,64]{1,2,0:T(8,128)(2,1)}, bf16[64,128,64]{1,2,0:T(8,128)(2,1)}) fusion(bf16[64,128,4,64]{1,3,2,0:T(8,128)(2,1)} %bitcast.36, s32[]{:T(128)S(6)} %select_n.62, s32[]{:T(128)S(6)} %select_n.68, s32[]{:T(128)S(6)} %select_n.66, ...), kind=kLoop, calls=%fused_computation.24 | loop fusion | bytes 8388624 | tf_op jit(solution)/shard_map/jit(dynamic_index_in_dim)/dynamic_slice | solution.py:37
  68.3 18.6 %collective-permute-done = bf16[64,128,64]{1,2,0:T(8,128)(2,1)} collective-permute-done((bf16[64,128,64]{1,2,0:T(8,128)(2,1)}, bf16[64,128,64]{1,2,0:T(8,128)(2,1)}, u32[]{:S(2)}, u32[]{:S(2)}) %collective-permute-start) | collective-permute-done | bytes 1048608 | tf_op jit(solution)/shard_map/ppermute | solution.py:44
  86.9 2.0 copy.52
  88.9 2.5 concatenate.23
  91.4 2.0 copy.53
  93.4 2.5 concatenate.24
  95.9 15.6 %collective-permute-done.2 = bf16[64,128,64]{1,2,0:T(8,128)(2,1)} collective-permute-done((bf16[64,128,64]{1,2,0:T(8,128)(2,1)}, bf16[64,128,64]{1,2,0:T(8,128)(2,1)}, u32[]{:S(2)}, u32[]{:S(2)}) %collective-permute-start.2) | collective-permute-done | bytes 1048608 | tf_op jit(solution)/shard_map/ppermute | solution.py:44
  113.5 2.5 concatenate.25
  116.0 3.6 pad_maximum_fusion
  119.7 9.2 %copy.47 = bf16[64,8,4,16,64]{4,3,2,1,0:T(8,128)(2,1)} copy(bf16[64,8,4,16,64]{4,3,0,1,2:T(8,128)(2,1)} %bitcast.37) | data formatting | bytes 8388608 | tf_op jit(solution)/shard_map/transpose | solution.py:31
  128.9 30.3 %all-gather.4.cloned.1.call-done = bf16[16,512,128]{2,1,0:T(8,128)(2,1)} async-done(((bf16[16,64,128]{2,1,0:T(8,128)(2,1)}), bf16[16,512,128]{2,1,0:T(8,128)(2,1)}) %all-gather.4.cloned.1.call-update) | async-done | bytes 2097168 | tf_op jit(solution)/shard_map/all_gather | solution.py:23
  159.2 16.0 %convert_bitcast_fusion = bf16[16,64,128,64]{2,3,0,1:T(8,128)(2,1)} fusion(bf16[64,512,64,1]{2,1,3,0:T(8,128)(2,1)} %bitcast.35, bf16[16,512,128]{2,1,0:T(8,128)(2,1)} %all-gather.4.cloned.1.call-done), kind=kOutput, calls=%fused_computation.2 | convolution fusion | flops 8598323200 | bytes 23068672 | tf_op jit(solution)/shard_map/acq,pcd->padq/dot_general | solution.py:47
  175.2 30.3 %copy.49 = bf16[16,64,128,64]{3,2,1,0:T(8,128)(2,1)} copy(bf16[16,64,128,64]{2,3,0,1:T(8,128)(2,1)} %convert_bitcast_fusion) | data formatting | bytes 33554432 | tf_op jit(solution)/shard_map/convert_element_type | solution.py:49
  205.5 44.0 %reshape.68 = bf16[16,64,8192,1]{2,1,0,3:T(8,128)(2,1)} reshape(bf16[16,64,128,64]{3,2,1,0:T(8,128)(2,1)} %copy.49) | data formatting | bytes 33554432 | tf_op jit(solution)/shard_map/dot_general | solution.py:52
  249.5 12.2 %fusion = f32[16,64,4,64]{3,1,2,0:T(8,128)S(1)} fusion(bf16[4,64,8192,1]{2,1,0,3:T(8,128)(2,1)} %bitcast.39, bf16[16,64,8192,1]{2,1,0,3:T(8,128)(2,1)} %reshape.68), kind=kOutput, calls=%fused_computation | convolution fusion | flops 4294967296 | bytes 22020096 | tf_op jit(solution)/shard_map/dot_general | solution.py:52
  262.2 2.8 copy.55
  265.0 2.6 reshape.64
  269.6 30.1 %reduce-scatter.3.cloned.1.call-done = f32[16,64,128]{2,1,0:T(8,128)} async-done(((f32[16,64,512]{2,1,0:T(8,128)}), f32[16,64,128]{2,1,0:T(8,128)}) %reduce-scatter.3.cloned.1.call-update) | async-done | bytes 524304 | tf_op jit(solution)/shard_map/reduce_scatter | solution.py:69
  300.3 64.1 %reduce-scatter.5.cloned.1.call-done = f32[2,64,128]{2,1,0:T(8,128)} async-done(((f32[16,64,128]{2,1,0:T(8,128)}), f32[2,64,128]{2,1,0:T(8,128)}) %reduce-scatter.5.cloned.1.call-update) | async-done | bytes 65552 | tf_op jit(solution)/shard_map/reduce_scatter | solution.py:70
  (48 shorter events, 18.1 us)
Async XLA Ops:
  6.5 1.6 copy-start
  6.5 113.2 %all-gather.6.cloned.1.call-start = ((), (), s32[]{:S(2)}) async-start(), calls=%async_computation.6 | async-start | bytes 10485760 | tf_op jit(solution)/shard_map/all_gather | solution.py:30
  50.2 108.9 %all-gather.4.cloned.1.call-start = ((), (), s32[]{:S(2)}) async-start(), calls=%async_computation.3 | async-start | bytes 2359296 | tf_op jit(solution)/shard_map/all_gather | solution.py:23
  51.0 248.7 %reduce-scatter.3.cloned.1.call-start = ((), (), s32[]{:S(2)}) async-start(), calls=%async_computation.4 | async-start | bytes 2621440 | tf_op jit(solution)/shard_map/reduce_scatter | solution.py:69
  62.7 24.1 %collective-permute-start = (bf16[64,128,64]{1,2,0:T(8,128)(2,1)}, bf16[64,128,64]{1,2,0:T(8,128)(2,1)}, u32[]{:S(2)}, u32[]{:S(2)}) collective-permute-start(bf16[64,128,64]{1,2,0:T(8,128)(2,1)} %get-tuple-element.12), channel_id=1, source_target_pairs={{0,4},{4,8},{8,12},{12,0},{16,20},{20,24},{24,28},{28,16},{1,5},{5... | collective-permute-start | bytes 3145736 | tf_op jit(solution)/shard_map/ppermute | solution.py:44
  63.9 27.5 %collective-permute-start.1 = (bf16[64,128,64]{1,2,0:T(8,128)(2,1)}, bf16[64,128,64]{1,2,0:T(8,128)(2,1)}, u32[]{:S(2)}, u32[]{:S(2)}) collective-permute-start(bf16[64,128,64]{1,2,0:T(8,128)(2,1)} %get-tuple-element.11), channel_id=1, source_target_pairs={{0,8},{4,12},{8,0},{12,4},{16,24},{20,28},{24,16},{28,20},{1,9},{5... | collective-permute-start | bytes 3145736 | tf_op jit(solution)/shard_map/ppermute | solution.py:44
  63.9 47.6 %collective-permute-start.2 = (bf16[64,128,64]{1,2,0:T(8,128)(2,1)}, bf16[64,128,64]{1,2,0:T(8,128)(2,1)}, u32[]{:S(2)}, u32[]{:S(2)}) collective-permute-start(bf16[64,128,64]{1,2,0:T(8,128)(2,1)} %get-tuple-element.10), channel_id=1, source_target_pairs={{0,12},{4,0},{8,4},{12,8},{16,28},{20,16},{24,20},{28,24},{1,13},{... | collective-permute-start | bytes 3145736 | tf_op jit(solution)/shard_map/ppermute | solution.py:44
  265.0 101.0 %copy-start.1 = (bf16[64,64,256]{2,1,0:T(8,128)(2,1)S(1)}, bf16[64,64,256]{2,1,0:T(8,128)(2,1)}, u32[]{:S(2)}) copy-start(bf16[64,64,256]{2,1,0:T(8,128)(2,1)} %param.7) | copy-start | bytes 6291460
  267.6 32.1 %copy-start.4 = (f32[512]{0:T(512)S(1)}, f32[512]{0:T(512)}, u32[]{:S(2)}) copy-start(f32[512]{0:T(512)} %param.11) | copy-start | bytes 6148
  267.6 32.2 %copy-start.2 = (s32[2,2]{1,0:T(2,128)S(1)}, s32[2,2]{1,0:T(2,128)}, u32[]{:S(2)}) copy-start(s32[2,2]{1,0:T(2,128)} %param.9) | copy-start | bytes 52
  267.6 32.4 %copy-start.3 = (f32[128]{0:T(128)S(1)}, f32[128]{0:T(128)}, u32[]{:S(2)}) copy-start(f32[128]{0:T(128)} %param.10) | copy-start | bytes 1540
  267.6 32.6 %slice-start = ((f32[512]{0:T(512)}), f32[64]{0:T(128)S(1)}, s32[]{:S(2)}) async-start(f32[512]{0:T(512)} %param.11), calls=%async_computation.7 | async-start | bytes 1024 | tf_op jit(solution)/shard_map/slice | solution.py:81
  269.5 94.8 %reduce-scatter.5.cloned.1.call-start = ((), (), s32[]{:S(2)}) async-start(), calls=%async_computation.5 | async-start | bytes 589824 | tf_op jit(solution)/shard_map/reduce_scatter | solution.py:70
Sparse Core Ops, SparseCore 0:
  50.3 57.6 all-gather.5
  110.2 48.8 all-gather.3
  269.6 30.0 reduce-scatter.2
  303.3 61.0 reduce-scatter.4
where the time goes:
time: 378 us; the launch traced here: 372 us
  waiting for transfers between devices  159 us (42%)
  local copies, waits for them, and re-layouts  130 us (34%)
  blocking collectives  30.2 us (8%)
  matrix products  28.2 us (7%)
  between operations  13.5 us (4%)
  other arithmetic  8.46 us (2%)
    reduce_scatter x1, waiting for transfers between devices, body(): ladder = lax.psum_scatter(ladder, 'narrow', scatter_dimension=0, tiled=True)  64.1 us
    dot_general x1, local copies, waits for them, and re-layouts, body(): lax.dot_general(inter.reshape(pairs * rows, d_blk * q_blk), right_group.r...  44 us
    ppermute x3, waiting for transfers between devices, body(): piece = lax.ppermute(piece, 'narrow', perm)  34.2 us
    convert_element_type x1, local copies, waits for them, and re-layouts, body(): inter = jnp.einsum('acq,pcd->padq', left_all, amps_all, preferred_element...  30.3 us
    all_gather x1, waiting for transfers between devices, body(): amps_all = lax.all_gather(amps, 'narrow', axis=1, tiled=True)  30.3 us
    all_to_all x1, blocking collectives, body(): left_recv = lax.all_to_all(left_send, 'narrow', 0, 0, tiled=True)  30.2 us
    reduce_scatter x1, waiting for transfers between devices, body(): ladder = lax.psum_scatter(ladder, 'wide', scatter_dimension=2, tiled=True)  30.1 us
    dot_general x1, matrix products, body(): jnp.einsum('acq,pcd->padq', left_all, amps_all, preferred_element_type=jn...  16 us
  transfers between devices with their start and end apart: 7, of which 5 were waited for; matrix products, arithmetic and copies ran while one was open for 11% of the time, Pallas kernels for 0%

commit v1 on v0

--- a/solution.py
+++ b/solution.py
@@ -49,11 +49,8 @@
         ).astype(jnp.bfloat16)
 
         right_group = jnp.concatenate(chunks, axis=0)
-        part = lax.dot_general(
-            inter.reshape(pairs * rows, d_blk * q_blk),
-            right_group.reshape(span * b_blk, d_blk * q_blk),
-            (((1,), (1,)), ((), ())),
-            preferred_element_type=jnp.float32,
+        part = jnp.einsum(
+            "padq,bdq->pab", inter, right_group, preferred_element_type=jnp.float32
         ).reshape(pairs, rows, span, b_blk)
         flipped = jnp.concatenate(
             [part[:, :, (span - k) % span : (span - k) % span + 1] for k in range(span)] * 2, axis=2

time: 378 us -> 315 us (0.83)
  local copies, waits for them, and re-layouts: 130 us -> 68.5 us
  waiting for transfers between devices: 159 us -> 166 us
  matrix products: 28.2 us -> 23.5 us
    dot_general x1 -> x0, local copies, waits for them, and re-layouts: 44 us -> none  [body(): lax.dot_general(inter.reshape(pairs * rows, d_blk * q_blk), right_group.r...]
    all_gather x1, waiting for transfers between devices: 0.01 us -> 39.2 us  [body(): left_all = lax.all_gather(left_recv, 'wide', axis=0, tiled=False)]
    ppermute x3, waiting for transfers between devices: 34.2 us -> 0.01 us  [body(): piece = lax.ppermute(piece, 'narrow', perm)]
    convert_element_type x1 -> x0, local copies, waits for them, and re-layouts: 30.3 us -> none  [body(): inter = jnp.einsum('acq,pcd->padq', left_all, amps_all, preferred_element...]
    concatenate x1, local copies, waits for them, and re-layouts: 0.04 us -> 11.7 us  [body(): jnp.concatenate([part[:, :, (span - k) % span:(span - k) % span + 1] for...]
    reshape x0 -> x2, local copies, waits for them, and re-layouts: none -> 11 us  [the longest x1 10.1 us: body(): left_all.transpose(2, 1, 0, 3, 4).reshape(rows, c_blk * n_narrow, q_blk)]
    concatenate x4 -> x0, local copies, waits for them, and re-layouts: 9.16 us -> none  [body(): right_group = jnp.concatenate(chunks, axis=0)]
    ppermute x3 -> x0, local copies, waits for them, and re-layouts: 6.07 us -> none  [body(): piece = lax.ppermute(piece, 'narrow', perm)]
  transfers between devices with their start and end apart: 7 -> 7, of which waited for: 5 -> 4; matrix products, arithmetic and copies ran while one was open for 11% -> 11% of each run, Pallas kernels for 0% -> 0%
where the time goes in v1:
time: 315 us; the launch traced here: 309 us
  waiting for transfers between devices  166 us (53%)
  local copies, waits for them, and re-layouts  68.5 us (22%)
  blocking collectives  30.2 us (10%)
  matrix products  23.5 us (7%)
  between operations  13.4 us (4%)
  other arithmetic  4.81 us (2%)
    reduce_scatter x1, waiting for transfers between devices, body(): ladder = lax.psum_scatter(ladder, 'narrow', scatter_dimension=0, tiled=True)  64 us
    all_gather x1, waiting for transfers between devices, body(): left_all = lax.all_gather(left_recv, 'wide', axis=0, tiled=False)  39.2 us
    all_gather x1, waiting for transfers between devices, body(): amps_all = lax.all_gather(amps, 'narrow', axis=1, tiled=True)  31.8 us
    all_to_all x1, blocking collectives, body(): left_recv = lax.all_to_all(left_send, 'narrow', 0, 0, tiled=True)  30.2 us
    reduce_scatter x1, waiting for transfers between devices, body(): ladder = lax.psum_scatter(ladder, 'wide', scatter_dimension=2, tiled=True)  30.1 us
    dot_general x1, matrix products, body(): jnp.einsum('padq,bdq->pab', inter, right_group, preferred_element_type=jn...  23.5 us
    unnamed x13, local copies, waits for them, and re-layouts  14 us
    concatenate x1, local copies, waits for them, and re-layouts, body(): jnp.concatenate([part[:, :, (span - k) % span:(span - k) % span + 1] for...  11.7 us
  transfers between devices with their start and end apart: 7, of which 4 were waited for; matrix products, arithmetic and copies ran while one was open for 11% of the time, Pallas kernels for 0%

profile of v1, /device:TPU:5, one launch (start us, length us, event | category | flops | bytes accessed | tf_op | source)
XLA Modules:
  0.0 309.4 jit_solution(16666102414337268384)
XLA Ops:
  6.5 1.6 copy-done
  9.0 2.0 reshape.53
  12.2 1.7 copy.47
  13.9 3.4 %reshape.65 = bf16[8,2,32768]{2,1,0:T(2,128)(2,1)S(1)} reshape(bf16[8,64,16,64]{3,2,1,0:T(8,128)(2,1)} %copy.47) | data formatting | bytes 2097152
  17.3 30.2 %all_to_all.5 = bf16[8,2,32768]{2,1,0:T(2,128)(2,1)S(1)} all-to-all(bf16[8,2,32768]{2,1,0:T(2,128)(2,1)S(1)} %reshape.65), channel_id=1, replica_groups=mesh['narrow'=8,'wide'=4] {'narrow'}, dimensions={0} | all-to-all | bytes 2097152 | tf_op jit(solution)/shard_map/all_to_all | solution.py:29
  47.5 2.7 reshape.66
  51.1 6.4 %copy.50 = bf16[64,128,256]{1,2,0:T(8,128)(2,1)} copy(bf16[64,128,256]{2,1,0:T(8,128)(2,1)} %param.8) | data formatting | bytes 8388608 | tf_op args[2]
  57.5 3.8 %constant_dynamic-slice_fusion.4 = (bf16[64,128,1,64]{1,3,2,0:T(8,128)(2,1)S(1)}, bf16[64,128,1,64]{1,3,2,0:T(8,128)(2,1)S(1)}, bf16[64,128,1,64]{1,3,2,0:T(8,128)(2,1)S(1)}, bf16[64,128,1,64]{1,3,2,0:T(8,128)(2,1)S(1)}) fusion(bf16[64,128,4,64]{1,3,2,0:T(8,128)(2,1)} %bitcast.46, s32[]{:T(128)S(6)} %select_n.62, s32[]{:T(128)S(6)} %select_n.68, ...), kind=kLoop, calls=%fused_computation.29 | loop fusion | bytes 8388624 | tf_op jit(solution)/shard_map/jit(dynamic_index_in_dim)/dynamic_slice | solution.py:37
  63.2 1.7 copy.62
  64.8 1.7 copy.61
  66.5 1.6 collective-permute-start.2
  68.8 39.2 %all-gather.6.cloned.1.call-done = bf16[32,64,16,64]{3,2,1,0:T(8,128)(2,1)} async-done(((bf16[8,64,16,64]{3,2,1,0:T(8,128)(2,1)}), bf16[32,64,16,64]{3,2,1,0:T(8,128)(2,1)}) %all-gather.6.cloned.1.call-update) | async-done | bytes 4194320 | tf_op jit(solution)/shard_map/all_gather | solution.py:30
  108.0 9.1 %copy.48 = bf16[64,8,4,16,64]{4,3,2,1,0:T(8,128)(2,1)} copy(bf16[64,8,4,16,64]{4,3,0,1,2:T(8,128)(2,1)} %bitcast.47) | data formatting | bytes 8388608 | tf_op jit(solution)/shard_map/transpose | solution.py:31
  117.2 10.1 %copy.49 = bf16[64,512,64]{1,0,2:T(8,128)(2,1)} copy(bf16[64,512,64]{2,1,0:T(8,128)(2,1)} %bitcast.45) | data formatting | bytes 8388608 | tf_op jit(solution)/shard_map/reshape | solution.py:31
  127.3 31.8 %all-gather.4.cloned.1.call-done = bf16[16,512,128]{2,1,0:T(8,128)(2,1)} async-done(((bf16[16,64,128]{2,1,0:T(8,128)(2,1)}), bf16[16,512,128]{2,1,0:T(8,128)(2,1)}) %all-gather.4.cloned.1.call-update) | async-done | bytes 2097168 | tf_op jit(solution)/shard_map/all_gather | solution.py:23
  159.2 23.5 %fusion.17 = f32[16,64,256]{2,1,0:T(8,128)S(1)} fusion(bf16[64,128,64]{1,0,2:T(8,128)(2,1)} %collective-permute-done.2, bf16[64,128,64]{1,0,2:T(8,128)(2,1)} %collective-permute-done.1, bf16[64,128,64]{1,0,2:T(8,128)(2,1)} %collective-permute-done, bf16[64,128,64]{1,0,2:T(8,128)(2,1)S(1)} %bitcast.50, bf16[64,512,64]{1,0,2:T(8,128)(2,1)} %copy.49, ...), kind=kOutput, calls=%fused_computation.19 | convolution fusion | flops 12910067712 | bytes 11534336 | tf_op jit(solution)/shard_map/padq,bdq->pab/dot_general | solution.py:52
  183.6 2.6 fusion.27
  186.2 11.7 %concatenate.14 = f32[16,64,8,64]{3,2,1,0:T(8,128)} concatenate(f32[16,64,1,64]{3,2,1,0:T(1,128)} %get-tuple-element.16, f32[16,64,1,64]{3,2,1,0:T(1,128)} %get-tuple-element.15, f32[16,64,1,64]{3,2,1,0:T(1,128)S(1)} %get-tuple-element.14, f32[16,64,1,64]{3,2,1,0:T(1,128)S(1)} %get-tuple-element.13, f32[16,64,1,64]{3,2,1,0:T(1,128)} %get-tuple-element.16, ...), dimensions={2} | concatenate | bytes 4194304 | tf_op jit(solution)/shard_map/concatenate | solution.py:55
  197.9 4.0 %constant_dynamic-slice_fusion = f32[16,64,4,64]{3,2,1,0:T(4,128)} fusion(f32[16,64,8,64]{3,2,1,0:T(8,128)} %concatenate.14, s32[]{:T(128)S(6)} %select_n.69), kind=kLoop, calls=%fused_computation.25 | loop fusion | bytes 2097156 | tf_op jit(solution)/shard_map/dynamic_slice | solution.py:58
  201.9 2.6 reshape.57
  204.7 1.7 fusion.14
  206.5 30.1 %reduce-scatter.3.cloned.1.call-done = f32[16,64,128]{2,1,0:T(8,128)} async-done(((f32[16,64,512]{2,1,0:T(8,128)}), f32[16,64,128]{2,1,0:T(8,128)}) %reduce-scatter.3.cloned.1.call-update) | async-done | bytes 524304 | tf_op jit(solution)/shard_map/reduce_scatter | solution.py:66
  237.2 64.0 %reduce-scatter.5.cloned.1.call-done = f32[2,64,128]{2,1,0:T(8,128)} async-done(((f32[16,64,128]{2,1,0:T(8,128)}), f32[2,64,128]{2,1,0:T(8,128)}) %reduce-scatter.5.cloned.1.call-update) | async-done | bytes 65552 | tf_op jit(solution)/shard_map/reduce_scatter | solution.py:67
  301.3 1.6 subtract_divide_fusion
  (35 shorter events, 7.1 us)
Async XLA Ops:
  6.5 1.6 copy-start
  6.5 101.5 %all-gather.6.cloned.1.call-start = ((), (), s32[]{:S(2)}) async-start(), calls=%async_computation.6 | async-start | bytes 10485760 | tf_op jit(solution)/shard_map/all_gather | solution.py:30
  50.2 108.9 %all-gather.4.cloned.1.call-start = ((), (), s32[]{:S(2)}) async-start(), calls=%async_computation.3 | async-start | bytes 2359296 | tf_op jit(solution)/shard_map/all_gather | solution.py:23
  51.0 185.7 %reduce-scatter.3.cloned.1.call-start = ((), (), s32[]{:S(2)}) async-start(), calls=%async_computation.4 | async-start | bytes 2621440 | tf_op jit(solution)/shard_map/reduce_scatter | solution.py:66
  61.9 65.4 %collective-permute-start = (bf16[64,128,64]{1,0,2:T(8,128)(2,1)S(1)}, bf16[64,128,64]{1,0,2:T(8,128)(2,1)}, u32[]{:S(2)}, u32[]{:S(2)}) collective-permute-start(bf16[64,128,64]{1,0,2:T(8,128)(2,1)S(1)} %bitcast.49), channel_id=1, source_target_pairs={{0,4},{4,8},{8,12},{12,0},{16,20},{20,24},{24,28},{28,16},{1,5},{5... | collective-permute-start | bytes 3145736 | tf_op jit(solution)/shard_map/ppermute | solution.py:44
  64.8 62.5 %collective-permute-start.1 = (bf16[64,128,64]{1,0,2:T(8,128)(2,1)}, bf16[64,128,64]{1,0,2:T(8,128)(2,1)}, u32[]{:S(2)}, u32[]{:S(2)}) collective-permute-start(bf16[64,128,64]{1,0,2:T(8,128)(2,1)} %bitcast.42), channel_id=1, source_target_pairs={{0,8},{4,12},{8,0},{12,4},{16,24},{20,28},{24,16},{28,20},{1,9},{5... | collective-permute-start | bytes 3145736 | tf_op jit(solution)/shard_map/ppermute | solution.py:44
  66.5 60.8 %collective-permute-start.2 = (bf16[64,128,64]{1,0,2:T(8,128)(2,1)}, bf16[64,128,64]{1,0,2:T(8,128)(2,1)}, u32[]{:S(2)}, u32[]{:S(2)}) collective-permute-start(bf16[64,128,64]{1,0,2:T(8,128)(2,1)} %bitcast.41), channel_id=1, source_target_pairs={{0,12},{4,0},{8,4},{12,8},{16,28},{20,16},{24,20},{28,24},{1,13},{... | collective-permute-start | bytes 3145736 | tf_op jit(solution)/shard_map/ppermute | solution.py:44
  201.9 100.9 %copy-start.1 = (bf16[64,64,256]{2,1,0:T(8,128)(2,1)S(1)}, bf16[64,64,256]{2,1,0:T(8,128)(2,1)}, u32[]{:S(2)}) copy-start(bf16[64,64,256]{2,1,0:T(8,128)(2,1)} %param.7) | copy-start | bytes 6291460
  204.5 32.1 %copy-start.4 = (f32[512]{0:T(512)S(1)}, f32[512]{0:T(512)}, u32[]{:S(2)}) copy-start(f32[512]{0:T(512)} %param.11) | copy-start | bytes 6148
  204.5 32.2 %copy-start.2 = (s32[2,2]{1,0:T(2,128)S(1)}, s32[2,2]{1,0:T(2,128)}, u32[]{:S(2)}) copy-start(s32[2,2]{1,0:T(2,128)} %param.9) | copy-start | bytes 52
  204.6 32.4 %copy-start.3 = (f32[128]{0:T(128)S(1)}, f32[128]{0:T(128)}, u32[]{:S(2)}) copy-start(f32[128]{0:T(128)} %param.10) | copy-start | bytes 1540
  204.6 32.6 %slice-start = ((f32[512]{0:T(512)}), f32[64]{0:T(128)S(1)}, s32[]{:S(2)}) async-start(f32[512]{0:T(512)} %param.11), calls=%async_computation.7 | async-start | bytes 1024 | tf_op jit(solution)/shard_map/slice | solution.py:78
  206.4 94.8 %reduce-scatter.5.cloned.1.call-start = ((), (), s32[]{:S(2)}) async-start(), calls=%async_computation.5 | async-start | bytes 589824 | tf_op jit(solution)/shard_map/reduce_scatter | solution.py:67
Sparse Core Ops, SparseCore 0:
  50.3 57.6 all-gather.5
  110.2 48.8 all-gather.3
  206.6 30.0 reduce-scatter.2
  240.2 61.0 reduce-scatter.4

commit v2 on v1

--- a/solution.py
+++ b/solution.py
@@ -51,20 +51,33 @@
         right_group = jnp.concatenate(chunks, axis=0)
         part = jnp.einsum(
             "padq,bdq->pab", inter, right_group, preferred_element_type=jnp.float32
-        ).reshape(pairs, rows, span, b_blk)
+        )
+        part = lax.psum_scatter(part, "wide", scatter_dimension=0, tiled=True)
+        pairs_w = part.shape[0]
+        part = part.reshape(pairs_w, rows, span, b_blk)
         flipped = jnp.concatenate(
             [part[:, :, (span - k) % span : (span - k) % span + 1] for k in range(span)] * 2, axis=2
         )
         ordered = lax.dynamic_slice_in_dim(flipped, span - r, span, 2)
-        ordered = ordered.reshape(pairs, rows, span * b_blk)
-        pad = jnp.zeros((pairs, rows, (GROUPS - 1) * span * b_blk), jnp.float32)
-        padded = jnp.concatenate([pad, ordered, pad], axis=2)
-        ladder = lax.dynamic_slice_in_dim(
-            padded, (GROUPS - 1 - g) * span * b_blk, vir_total, 2
-        )
-
-        ladder = lax.psum_scatter(ladder, "wide", scatter_dimension=2, tiled=True)
-        ladder = lax.psum_scatter(ladder, "narrow", scatter_dimension=0, tiled=True)
+        n_per_w = n_narrow // n_wide
+        w_per_g = n_wide // GROUPS
+        cols = span * b_blk // w_per_g
+        ordered = ordered.reshape(n_per_w, pairs_w // n_per_w, rows, w_per_g, cols)
+        ladder = None
+        for t in range(span):
+            k = (t + r) % span
+            piece = lax.dynamic_index_in_dim(ordered, k // w_per_g, 0, keepdims=False)
+            piece = lax.dynamic_index_in_dim(piece, k % w_per_g, 2, keepdims=False)
+            perm = []
+            for gg in range(GROUPS):
+                for rr in range(span):
+                    for ww in range(n_wide):
+                        kk = (t + rr) % span
+                        dst_n = ww * n_per_w + kk // w_per_g
+                        dst_w = gg * w_per_g + kk % w_per_g
+                        perm.append(((gg * span + rr) * n_wide + ww, dst_n * n_wide + dst_w))
+            piece = lax.ppermute(piece, ("narrow", "wide"), perm)
+            ladder = piece if ladder is None else ladder + piece
 
         local_cols = ladder.shape[2]
         occ_ids = jnp.arange(occ_energy.shape[0], dtype=jnp.int32)

time: 315 us -> 247 us (0.78); the launches traced: 309 us -> 246 us
  waiting for transfers between devices: 166 us -> 99.8 us
  starting transfers between devices: 2.95 us -> 18.6 us
  local copies, waits for them, and re-layouts: 68.5 us -> 56.7 us
    reduce_scatter x2 -> x1, waiting for transfers between devices: 94.2 us -> 23 us  [body(): part = lax.psum_scatter(part, 'wide', scatter_dimension=0, tiled=True)]
    ppermute x0 -> x4, starting transfers between devices: none -> 15.7 us  [body(): piece = lax.ppermute(piece, ('narrow', 'wide'), perm)]
    concatenate x1, local copies, waits for them, and re-layouts: 11.7 us -> 2.83 us  [body(): jnp.concatenate([part[:, :, (span - k) % span:(span - k) % span + 1] for...]
    ppermute x0 -> x4, waiting for transfers between devices: none -> 5.91 us  [body(): piece = lax.ppermute(piece, ('narrow', 'wide'), perm)]
    unnamed x13 -> x11, local copies, waits for them, and re-layouts: 14 us -> 15.7 us
  transfers between devices with their start and end apart: 7 -> 10, of which waited for: 4 -> 5; matrix products, arithmetic and copies ran while one was open for 11% -> 15% of each run, Pallas kernels for 0% -> 0%
where the time goes in v2:
time: 247 us; the launch traced here: 246 us
  waiting for transfers between devices  99.8 us (40%)
  local copies, waits for them, and re-layouts  56.7 us (23%)
  blocking collectives  30.3 us (12%)
  matrix products  24.5 us (10%)
  starting transfers between devices  18.6 us (8%)
  between operations  13.5 us (5%)
    all_gather x1, waiting for transfers between devices, body(): left_all = lax.all_gather(left_recv, 'wide', axis=0, tiled=False)  38.3 us
    all_gather x1, waiting for transfers between devices, body(): amps_all = lax.all_gather(amps, 'narrow', axis=1, tiled=True)  31.8 us
    all_to_all x1, blocking collectives, body(): left_recv = lax.all_to_all(left_send, 'narrow', 0, 0, tiled=True)  30.3 us
    dot_general x1, matrix products, body(): jnp.einsum('padq,bdq->pab', inter, right_group, preferred_element_type=jn...  24.5 us
    reduce_scatter x1, waiting for transfers between devices, body(): part = lax.psum_scatter(part, 'wide', scatter_dimension=0, tiled=True)  23 us
    ppermute x4, starting transfers between devices, body(): piece = lax.ppermute(piece, ('narrow', 'wide'), perm)  15.7 us
    unnamed x11, local copies, waits for them, and re-layouts  15.7 us
    reshape x1, local copies, waits for them, and re-layouts, body(): left_all.transpose(2, 1, 0, 3, 4).reshape(rows, c_blk * n_narrow, q_blk)  10.2 us
  transfers between devices with their start and end apart: 10, of which 5 were waited for; matrix products, arithmetic and copies ran while one was open for 15% of the time, Pallas kernels for 0%

profile of v2, /device:TPU:5, one launch (start us, length us, event | category | flops | bytes accessed | tf_op | source)
XLA Modules:
  0.0 245.7 jit_solution(3619713711159970807)
XLA Ops:
  9.0 2.0 reshape.61
  12.2 1.7 copy.47
  13.9 3.4 %reshape.73 = bf16[8,2,32768]{2,1,0:T(2,128)(2,1)S(1)} reshape(bf16[8,64,16,64]{3,2,1,0:T(8,128)(2,1)} %copy.47) | data formatting | bytes 2097152
  17.3 30.3 %all_to_all.5 = bf16[8,2,32768]{2,1,0:T(2,128)(2,1)} all-to-all(bf16[8,2,32768]{2,1,0:T(2,128)(2,1)S(1)} %reshape.73), channel_id=1, replica_groups=mesh['narrow'=8,'wide'=4] {'narrow'}, dimensions={0} | all-to-all | bytes 2097152 | tf_op jit(solution)/shard_map/all_to_all | solution.py:29
  47.6 4.3 %reshape.74 = bf16[8,64,16,64]{3,2,1,0:T(8,128)(2,1)} reshape(bf16[8,2,32768]{2,1,0:T(2,128)(2,1)} %all_to_all.5) | data formatting | bytes 2097152
  52.8 6.4 %copy.50 = bf16[64,128,256]{1,2,0:T(8,128)(2,1)} copy(bf16[64,128,256]{2,1,0:T(8,128)(2,1)} %param.8) | data formatting | bytes 8388608 | tf_op args[2]
  59.2 3.8 %constant_dynamic-slice_fusion.8 = (bf16[64,128,1,64]{1,3,2,0:T(8,128)(2,1)S(1)}, bf16[64,128,1,64]{1,3,2,0:T(8,128)(2,1)S(1)}, bf16[64,128,1,64]{1,3,2,0:T(8,128)(2,1)S(1)}, bf16[64,128,1,64]{1,3,2,0:T(8,128)(2,1)S(1)}) fusion(bf16[64,128,4,64]{1,3,2,0:T(8,128)(2,1)} %bitcast.50, s32[]{:T(128)S(6)} %select_n.134, s32[]{:T(128)S(6)} %select_n.140, ...), kind=kLoop, calls=%fused_computation.28 | loop fusion | bytes 8388624 | tf_op jit(solution)/shard_map/jit(dynamic_index_in_dim)/dynamic_slice | solution.py:37
  63.0 1.7 copy.63
  65.8 1.7 copy.62
  67.5 1.7 copy.61
  69.2 1.6 collective-permute-start.2
  71.5 38.3 %all-gather.6.cloned.1.call-done = bf16[32,64,16,64]{3,2,1,0:T(8,128)(2,1)} async-done(((bf16[8,64,16,64]{3,2,1,0:T(8,128)(2,1)}), bf16[32,64,16,64]{3,2,1,0:T(8,128)(2,1)}) %all-gather.6.cloned.1.call-update) | async-done | bytes 4194320 | tf_op jit(solution)/shard_map/all_gather | solution.py:30
  109.8 9.1 %copy.48 = bf16[64,8,4,16,64]{4,3,2,1,0:T(8,128)(2,1)} copy(bf16[64,8,4,16,64]{4,3,0,1,2:T(8,128)(2,1)} %bitcast.51) | data formatting | bytes 8388608 | tf_op jit(solution)/shard_map/transpose | solution.py:31
  118.9 10.2 %copy.49 = bf16[64,512,64]{1,0,2:T(8,128)(2,1)} copy(bf16[64,512,64]{2,1,0:T(8,128)(2,1)} %bitcast.49) | data formatting | bytes 8388608 | tf_op jit(solution)/shard_map/reshape | solution.py:31
  129.1 31.8 %all-gather.4.cloned.1.call-done = bf16[16,512,128]{2,1,0:T(8,128)(2,1)} async-done(((bf16[16,64,128]{2,1,0:T(8,128)(2,1)}), bf16[16,512,128]{2,1,0:T(8,128)(2,1)}) %all-gather.4.cloned.1.call-update) | async-done | bytes 2097168 | tf_op jit(solution)/shard_map/all_gather | solution.py:23
  160.9 24.5 %fusion.15 = f32[16,64,256]{2,1,0:T(8,128)} fusion(bf16[64,128,64]{1,0,2:T(8,128)(2,1)} %collective-permute-done.2, bf16[64,128,64]{1,0,2:T(8,128)(2,1)} %collective-permute-done.1, bf16[64,128,64]{1,0,2:T(8,128)(2,1)} %collective-permute-done, bf16[64,128,64]{1,0,2:T(8,128)(2,1)S(1)} %bitcast.53, bf16[64,512,64]{1,0,2:T(8,128)(2,1)} %copy.49, ...), kind=kOutput, calls=%fused_computation.14 | convolution fusion | flops 12910067712 | bytes 11534336 | tf_op jit(solution)/shard_map/padq,bdq->pab/dot_general | solution.py:52
  186.1 23.0 %reduce-scatter.2.cloned.1.call-done = f32[4,64,256]{2,1,0:T(8,128)} async-done(((f32[16,64,256]{2,1,0:T(8,128)}), f32[4,64,256]{2,1,0:T(8,128)}) %reduce-scatter.2.cloned.1.call-update) | async-done | bytes 262160 | tf_op jit(solution)/shard_map/reduce_scatter | solution.py:55
  211.2 2.8 %concatenate.11 = f32[4,64,8,64]{3,2,1,0:T(8,128)S(1)} concatenate(f32[4,64,1,64]{3,2,1,0:T(1,128)} %get-tuple-element.16, f32[4,64,1,64]{3,2,1,0:T(1,128)S(1)} %get-tuple-element.15, f32[4,64,1,64]{3,2,1,0:T(1,128)S(1)} %get-tuple-element.14, f32[4,64,1,64]{3,2,1,0:T(1,128)S(1)} %get-tuple-element.13, f32[4,64,1,64]{3,2,1,0:T(1,128)} %get-tuple-element.16, ...), dimensions={2} | concatenate | bytes 1048576 | tf_op jit(solution)/shard_map/concatenate | solution.py:58
  216.7 6.8 %collective-permute-start.6 = (f32[2,64,128]{2,1,0:T(8,128)S(1)}, f32[2,64,128]{2,1,0:T(8,128)S(1)}, u32[]{:S(2)}, u32[]{:S(2)}) collective-permute-start(f32[2,64,128]{2,1,0:T(8,128)S(1)} %bitcast.57), channel_id=1, source_target_pairs={{0,5},{1,13},{2,21},{3,29},{4,0},{5,8},{6,16},{7,24},{8,1},{9,9},{... | collective-permute-start | bytes 196616 | tf_op jit(solution)/shard_map/ppermute | solution.py:79
  223.5 1.9 collective-permute-start.4
  225.4 4.7 %collective-permute-start.5 = (f32[2,64,128]{2,1,0:T(8,128)S(1)}, f32[2,64,128]{2,1,0:T(8,128)S(1)}, u32[]{:S(2)}, u32[]{:S(2)}) collective-permute-start(f32[2,64,128]{2,1,0:T(8,128)S(1)} %bitcast.55), channel_id=1, source_target_pairs={{0,4},{1,12},{2,20},{3,28},{4,5},{5,13},{6,21},{7,29},{8,0},{9,8},... | collective-permute-start | bytes 196616 | tf_op jit(solution)/shard_map/ppermute | solution.py:79
  230.2 2.2 collective-permute-start.3
  232.6 2.1 collective-permute-done.4
  234.6 3.9 %collective-permute-done.3 = f32[2,64,128]{2,1,0:T(8,128)S(1)} collective-permute-done((f32[2,64,128]{2,1,0:T(8,128)S(1)}, f32[2,64,128]{2,1,0:T(8,128)S(1)}, u32[]{:S(2)}, u32[]{:S(2)}) %collective-permute-start.3) | collective-permute-done | bytes 65568 | tf_op jit(solution)/shard_map/ppermute | solution.py:79
  (37 shorter events, 12.3 us)
Async XLA Ops:
  6.5 1.6 copy-start
  6.5 103.2 %all-gather.6.cloned.1.call-start = ((), (), s32[]{:S(2)}) async-start(), calls=%async_computation.4 | async-start | bytes 10485760 | tf_op jit(solution)/shard_map/all_gather | solution.py:30
  51.9 108.9 %all-gather.4.cloned.1.call-start = ((), (), s32[]{:S(2)}) async-start(), calls=%async_computation.2 | async-start | bytes 2359296 | tf_op jit(solution)/shard_map/all_gather | solution.py:23
  52.7 156.4 %reduce-scatter.2.cloned.1.call-start = ((), (), s32[]{:S(2)}) async-start(), calls=%async_computation.3 | async-start | bytes 1310720 | tf_op jit(solution)/shard_map/reduce_scatter | solution.py:55
  64.7 64.4 %collective-permute-start = (bf16[64,128,64]{1,0,2:T(8,128)(2,1)}, bf16[64,128,64]{1,0,2:T(8,128)(2,1)}, u32[]{:S(2)}, u32[]{:S(2)}) collective-permute-start(bf16[64,128,64]{1,0,2:T(8,128)(2,1)} %bitcast.47), channel_id=1, source_target_pairs={{0,4},{4,8},{8,12},{12,0},{16,20},{20,24},{24,28},{28,16},{1,5},{5... | collective-permute-start | bytes 3145736 | tf_op jit(solution)/shard_map/ppermute | solution.py:44
  67.5 61.6 %collective-permute-start.1 = (bf16[64,128,64]{1,0,2:T(8,128)(2,1)}, bf16[64,128,64]{1,0,2:T(8,128)(2,1)}, u32[]{:S(2)}, u32[]{:S(2)}) collective-permute-start(bf16[64,128,64]{1,0,2:T(8,128)(2,1)} %bitcast.46), channel_id=1, source_target_pairs={{0,8},{4,12},{8,0},{12,4},{16,24},{20,28},{24,16},{28,20},{1,9},{5... | collective-permute-start | bytes 3145736 | tf_op jit(solution)/shard_map/ppermute | solution.py:44
  69.2 59.9 %collective-permute-start.2 = (bf16[64,128,64]{1,0,2:T(8,128)(2,1)}, bf16[64,128,64]{1,0,2:T(8,128)(2,1)}, u32[]{:S(2)}, u32[]{:S(2)}) collective-permute-start(bf16[64,128,64]{1,0,2:T(8,128)(2,1)} %bitcast.45), channel_id=1, source_target_pairs={{0,12},{4,0},{8,4},{12,8},{16,28},{20,16},{24,20},{28,24},{1,13},{... | collective-permute-start | bytes 3145736 | tf_op jit(solution)/shard_map/ppermute | solution.py:44
  160.9 24.7 %copy-start.1 = (s32[2,2]{1,0:T(2,128)S(1)}, s32[2,2]{1,0:T(2,128)}, u32[]{:S(2)}) copy-start(s32[2,2]{1,0:T(2,128)} %param.9) | copy-start | bytes 52
  160.9 24.9 %copy-start.2 = (f32[128]{0:T(128)S(1)}, f32[128]{0:T(128)}, u32[]{:S(2)}) copy-start(f32[128]{0:T(128)} %param.10) | copy-start | bytes 1540
  185.4 47.0 %slice-start = ((f32[512]{0:T(512)}), f32[64]{0:T(128)S(1)}, s32[]{:S(2)}) async-start(f32[512]{0:T(512)} %param.11), calls=%async_computation.5 | async-start | bytes 1024 | tf_op jit(solution)/shard_map/slice | solution.py:91
  185.4 47.1 %copy-start.3 = (f32[512]{0:T(512)S(1)}, f32[512]{0:T(512)}, u32[]{:S(2)}) copy-start(f32[512]{0:T(512)} %param.11) | copy-start | bytes 6148
  216.7 15.9 %collective-permute-start.6 = (f32[2,64,128]{2,1,0:T(8,128)S(1)}, f32[2,64,128]{2,1,0:T(8,128)S(1)}, u32[]{:S(2)}, u32[]{:S(2)}) collective-permute-start(f32[2,64,128]{2,1,0:T(8,128)S(1)} %bitcast.57), channel_id=1, source_target_pairs={{0,5},{1,13},{2,21},{3,29},{4,0},{5,8},{6,16},{7,24},{8,1},{9,9},{... | collective-permute-start | bytes 196616 | tf_op jit(solution)/shard_map/ppermute | solution.py:79
  223.5 11.1 %collective-permute-start.4 = (f32[2,64,128]{2,1,0:T(8,128)S(1)}, f32[2,64,128]{2,1,0:T(8,128)S(1)}, u32[]{:S(2)}, u32[]{:S(2)}) collective-permute-start(f32[2,64,128]{2,1,0:T(8,128)S(1)} %bitcast.56), channel_id=1, source_target_pairs={{0,1},{1,9},{2,17},{3,25},{4,4},{5,12},{6,20},{7,28},{8,5},{9,13},... | collective-permute-start | bytes 196616 | tf_op jit(solution)/shard_map/ppermute | solution.py:79
  225.4 9.2 %collective-permute-start.5 = (f32[2,64,128]{2,1,0:T(8,128)S(1)}, f32[2,64,128]{2,1,0:T(8,128)S(1)}, u32[]{:S(2)}, u32[]{:S(2)}) collective-permute-start(f32[2,64,128]{2,1,0:T(8,128)S(1)} %bitcast.55), channel_id=1, source_target_pairs={{0,4},{1,12},{2,20},{3,28},{4,5},{5,13},{6,21},{7,29},{8,0},{9,8},... | collective-permute-start | bytes 196616 | tf_op jit(solution)/shard_map/ppermute | solution.py:79
  230.2 8.3 %collective-permute-start.3 = (f32[2,64,128]{2,1,0:T(8,128)S(1)}, f32[2,64,128]{2,1,0:T(8,128)S(1)}, u32[]{:S(2)}, u32[]{:S(2)}) collective-permute-start(f32[2,64,128]{2,1,0:T(8,128)S(1)} %bitcast.54), channel_id=1, source_target_pairs={{0,0},{1,8},{2,16},{3,24},{4,1},{5,9},{6,17},{7,25},{8,4},{9,12},{... | collective-permute-start | bytes 196616 | tf_op jit(solution)/shard_map/ppermute | solution.py:79
Sparse Core Ops, SparseCore 0:
  52.1 57.6 all-gather.5
  112.0 48.8 all-gather.3
  185.6 23.4 reduce-scatter.1

commit v3 on v2

--- a/solution.py
+++ b/solution.py
@@ -20,13 +20,23 @@
         pairs = amps.shape[0]
         vir_total = b_blk * n_narrow
 
-        amps_all = lax.all_gather(amps, "narrow", axis=1, tiled=True)
+        def shifted(x, shift):
+            if not shift:
+                return x
+            perm = [(i, (i + shift) % n_narrow) for i in range(n_narrow)]
+            return lax.ppermute(x, "narrow", perm)
+
+        amps_all = jnp.stack([shifted(amps, s) for s in range(n_narrow)], axis=1)
+        amps_all = amps_all.reshape(pairs, n_narrow * c_blk, amps.shape[2])
 
         c_sub = c_blk // n_wide
         left_part = lax.dynamic_slice_in_dim(left_fit, w * c_sub, c_sub, 1)
         left_part = left_part.reshape(rows, c_sub, span, q_blk).transpose(2, 0, 1, 3)
-        left_send = jnp.concatenate([left_part] * GROUPS, axis=0)
-        left_recv = lax.all_to_all(left_send, "narrow", 0, 0, tiled=True)
+        left_recv = []
+        for shift in range(n_narrow):
+            dest = ((n + shift) % n_narrow) % span
+            left_recv.append(shifted(lax.dynamic_index_in_dim(left_part, dest, 0, keepdims=False), shift))
+        left_recv = jnp.stack(left_recv, axis=0)
         left_all = lax.all_gather(left_recv, "wide", axis=0, tiled=False)
         left_all = left_all.transpose(2, 1, 0, 3, 4).reshape(rows, c_blk * n_narrow, q_blk)
 

time: 247 us -> 265 us (1.073)
  starting transfers between devices: 18.6 us -> 60.6 us
  blocking collectives: 30.3 us -> 0 us
  local copies, waits for them, and re-layouts: 56.7 us -> 68.7 us
  waiting for transfers between devices: 99.8 us -> 95.6 us
    ppermute x0 -> x14, waiting for transfers between devices: none -> 63.2 us  [shifted(): return lax.ppermute(x, 'narrow', perm)]
    ppermute x0 -> x14, starting transfers between devices: none -> 41.8 us  [shifted(): return lax.ppermute(x, 'narrow', perm)]
    all_gather x1, waiting for transfers between devices: 38.3 us -> 0.01 us  [body(): left_all = lax.all_gather(left_recv, 'wide', axis=0, tiled=False)]
    all_gather x1 -> x0, waiting for transfers between devices: 31.8 us -> none  [body(): amps_all = lax.all_gather(amps, 'narrow', axis=1, tiled=True)]
    all_to_all x1 -> x0, blocking collectives: 30.3 us -> none  [body(): left_recv = lax.all_to_all(left_send, 'narrow', 0, 0, tiled=True)]
    transpose x1 -> x0, local copies, waits for them, and re-layouts: 9.12 us -> none  [body(): left_all.transpose(2, 1, 0, 3, 4).reshape(rows, c_blk * n_narrow, q_blk)]
    all_gather x0 -> x1, local copies, waits for them, and re-layouts: none -> 9.11 us  [body(): left_all = lax.all_gather(left_recv, 'wide', axis=0, tiled=False)]
    unnamed x11 -> x32, local copies, waits for them, and re-layouts: 15.7 us -> 24 us
  transfers between devices with their start and end apart: 10 -> 23, of which waited for: 5 -> 7; matrix products, arithmetic and copies ran while one was open for 15% -> 20% of each run, Pallas kernels for 0% -> 0%
where the time goes in v3:
time: 265 us; the launch traced here: 264 us
  waiting for transfers between devices  95.6 us (36%)
  local copies, waits for them, and re-layouts  68.7 us (26%)
  starting transfers between devices  60.6 us (23%)
  matrix products  24.4 us (9%)
  between operations  13.8 us (5%)
    ppermute x14, waiting for transfers between devices, shifted(): return lax.ppermute(x, 'narrow', perm)  63.2 us
    ppermute x14, starting transfers between devices, shifted(): return lax.ppermute(x, 'narrow', perm)  41.8 us
    reduce_scatter x1, waiting for transfers between devices, body(): part = lax.psum_scatter(part, 'wide', scatter_dimension=0, tiled=True)  26.2 us
    dot_general x1, matrix products, body(): jnp.einsum('padq,bdq->pab', inter, right_group, preferred_element_type=jn...  24.4 us
    unnamed x32, local copies, waits for them, and re-layouts  24 us
    ppermute x4, starting transfers between devices, body(): piece = lax.ppermute(piece, ('narrow', 'wide'), perm)  15.4 us
    reshape x1, local copies, waits for them, and re-layouts, body(): left_all.transpose(2, 1, 0, 3, 4).reshape(rows, c_blk * n_narrow, q_blk)  10.2 us
    all_gather x1, local copies, waits for them, and re-layouts, body(): left_all = lax.all_gather(left_recv, 'wide', axis=0, tiled=False)  9.11 us
  transfers between devices with their start and end apart: 23, of which 7 were waited for; matrix products, arithmetic and copies ran while one was open for 20% of the time, Pallas kernels for 0%

profile of v3, /device:TPU:5, one launch (start us, length us, event | category | flops | bytes accessed | tf_op | source)
XLA Modules:
  0.0 264.1 jit_solution(11054348584171052671)
XLA Ops:
  11.1 4.4 %constant_dynamic-slice_fusion.9 = (bf16[64,16,1,64]{3,2,1,0:T(2,128)(2,1)S(1)}, bf16[64,16,1,64]{3,2,1,0:T(2,128)(2,1)S(1)}, bf16[64,16,1,64]{3,2,1,0:T(2,128)(...) fusion(bf16[64,16,4,64]{3,2,1,0:T(4,128)(2,1)S(1)} %reshape.80,, ...), kind=kLoop, calls=%fused_computation.50 | loop fusion | bytes 2097184 | tf_op jit(solution)/shard_map/dynamic-slice.7
  18.2 2.3 collective-permute-start.9
  21.6 2.4 collective-permute-start.11
  27.7 4.9 %collective-permute-start.13 = (bf16[64,16,64]{2,1,0:T(8,128)(2,1)S(1)}, bf16[64,16,64]{2,1,0:T(8,128)(2,1)S(1)}, u32[]{:S(2)}, u32[]{:S(2)}) collective-permute-start(bf16[64,16,64]{2,1,0:T(8,128)(2,1)S(1)} %bitcast.103), channel_id=1, source_target_pairs={{0,28},{4,0},{8,4},{12,8},{16,12},{20,16},{24,20},{28,24},{1,29},{... | collective-permute-start | bytes 393224 | tf_op jit(solution)/shard_map/ppermute | solution.py:27
  33.3 15.8 %collective-permute-done.9 = bf16[64,16,64]{2,1,0:T(8,128)(2,1)S(1)} collective-permute-done((bf16[64,16,64]{2,1,0:T(8,128)(2,1)S(1)}, bf16[64,16,64]{2,1,0:T(8,128)(2,1)S(1)}, u32[]{:S(2)}, u32[]{:S(2)}) %collective-permute-start.9) | collective-permute-done | bytes 131104 | tf_op jit(solution)/shard_map/ppermute | solution.py:27
  52.8 5.8 %collective-permute-start = (bf16[16,64,128]{2,1,0:T(8,128)(2,1)S(1)}, bf16[16,64,128]{2,1,0:T(8,128)(2,1)}, u32[]{:S(2)}, u32[]{:S(2)}) collective-permute-start(bf16[16,64,128]{2,1,0:T(8,128)(2,1)S(1)} %copy-done.1), channel_id=1, source_target_pairs={{0,4},{4,8},{8,12},{12,16},{16,20},{20,24},{24,28},{28,0},{1,5},{5... | collective-permute-start | bytes 786440 | tf_op jit(solution)/shard_map/ppermute | solution.py:27
  58.5 10.1 %collective-permute-start.1 = (bf16[16,64,128]{2,1,0:T(8,128)(2,1)S(1)}, bf16[16,64,128]{2,1,0:T(8,128)(2,1)}, u32[]{:S(2)}, u32[]{:S(2)}) collective-permute-start(bf16[16,64,128]{2,1,0:T(8,128)(2,1)S(1)} %copy-done.1), channel_id=1, source_target_pairs={{0,8},{4,12},{8,16},{12,20},{16,24},{20,28},{24,0},{28,4},{1,9},{5... | collective-permute-start | bytes 786440 | tf_op jit(solution)/shard_map/ppermute | solution.py:27
  70.2 3.1 %collective-permute-start.4 = (bf16[16,64,128]{2,1,0:T(8,128)(2,1)S(1)}, bf16[16,64,128]{2,1,0:T(8,128)(2,1)}, u32[]{:S(2)}, u32[]{:S(2)}) collective-permute-start(bf16[16,64,128]{2,1,0:T(8,128)(2,1)S(1)} %copy-done.1), channel_id=1, source_target_pairs={{0,20},{4,24},{8,28},{12,0},{16,4},{20,8},{24,12},{28,16},{1,21},{... | collective-permute-start | bytes 786440 | tf_op jit(solution)/shard_map/ppermute | solution.py:27
  74.0 6.8 %copy.33 = bf16[64,128,256]{1,2,0:T(8,128)(2,1)} copy(bf16[64,128,256]{2,1,0:T(8,128)(2,1)} %param.8) | data formatting | bytes 8388608 | tf_op args[2]
  80.8 3.2 %constant_dynamic-slice_fusion.8 = (bf16[64,128,1,64]{1,3,2,0:T(8,128)(2,1)S(1)}, bf16[64,128,1,64]{1,3,2,0:T(8,128)(2,1)S(1)}, bf16[64,128,1,64]{1,3,2,0:T(8,128)(2,1)S(1)}, bf16[64,128,1,64]{1,3,2,0:T(8,128)(2,1)S(1)}) fusion(bf16[64,128,4,64]{1,3,2,0:T(8,128)(2,1)} %bitcast.100, s32[]{:T(128)S(6)} %select_n.247, s32[]{:T(128)S(6)} %select_n.253, ...), kind=kLoop, calls=%fused_computation.49 | loop fusion | bytes 8388624 | tf_op jit(solution)/shard_map/jit(dynamic_index_in_dim)/dynamic_slice | solution.py:47
  93.4 5.5 %collective-permute-done.2 = bf16[16,64,128]{2,1,0:T(8,128)(2,1)} collective-permute-done((bf16[16,64,128]{2,1,0:T(8,128)(2,1)S(1)}, bf16[16,64,128]{2,1,0:T(8,128)(2,1)}, u32[]{:S(2)}, u32[]{:S(2)}) %collective-permute-start.2) | collective-permute-done | bytes 262176 | tf_op jit(solution)/shard_map/ppermute | solution.py:27
  98.9 3.1 %collective-permute-start.16 = (bf16[64,128,64]{1,0,2:T(8,128)(2,1)}, bf16[64,128,64]{1,0,2:T(8,128)(2,1)}, u32[]{:S(2)}, u32[]{:S(2)}) collective-permute-start(bf16[64,128,64]{1,0,2:T(8,128)(2,1)} %bitcast.88), channel_id=1, source_target_pairs={{0,12},{4,0},{8,4},{12,8},{16,28},{20,16},{24,20},{28,24},{1,13},{... | collective-permute-start | bytes 3145736 | tf_op jit(solution)/shard_map/ppermute | solution.py:54
  103.7 2.9 %collective-permute-start.5 = (bf16[16,64,128]{2,1,0:T(8,128)(2,1)S(1)}, bf16[16,64,128]{2,1,0:T(8,128)(2,1)S(1)}, u32[]{:S(2)}, u32[]{:S(2)}) collective-permute-start(bf16[16,64,128]{2,1,0:T(8,128)(2,1)S(1)} %copy-done.1), channel_id=1, source_target_pairs={{0,24},{4,28},{8,0},{12,4},{16,8},{20,12},{24,16},{28,20},{1,25},{... | collective-permute-start | bytes 786440 | tf_op jit(solution)/shard_map/ppermute | solution.py:27
  108.4 3.9 %collective-permute-start.6 = (bf16[16,64,128]{2,1,0:T(8,128)(2,1)S(1)}, bf16[16,64,128]{2,1,0:T(8,128)(2,1)S(1)}, u32[]{:S(2)}, u32[]{:S(2)}) collective-permute-start(bf16[16,64,128]{2,1,0:T(8,128)(2,1)S(1)} %copy-done.1), channel_id=1, source_target_pairs={{0,28},{4,0},{8,4},{12,8},{16,12},{20,16},{24,20},{28,24},{1,29},{... | collective-permute-start | bytes 786440 | tf_op jit(solution)/shard_map/ppermute | solution.py:27
  114.0 41.1 %collective-permute-done.5 = bf16[16,64,128]{2,1,0:T(8,128)(2,1)S(1)} collective-permute-done((bf16[16,64,128]{2,1,0:T(8,128)(2,1)S(1)}, bf16[16,64,128]{2,1,0:T(8,128)(2,1)S(1)}, u32[]{:S(2)}, u32[]{:S(2)}) %collective-permute-start.5) | collective-permute-done | bytes 262176 | tf_op jit(solution)/shard_map/ppermute | solution.py:27
  156.7 9.1 %copy.31 = bf16[4,8,64,16,64]{4,3,0,1,2:T(8,128)(2,1)} copy(bf16[4,8,64,16,64]{4,3,2,1,0:T(8,128)(2,1)} %bitcast.101) | data formatting | bytes 8388608 | tf_op jit(solution)/shard_map/all_gather | solution.py:40
  165.8 10.2 %copy.32 = bf16[64,512,64]{1,0,2:T(8,128)(2,1)} copy(bf16[64,512,64]{2,1,0:T(8,128)(2,1)} %bitcast.99) | data formatting | bytes 8388608 | tf_op jit(solution)/shard_map/reshape | solution.py:41
  176.0 24.4 %fusion.13 = f32[16,64,256]{2,1,0:T(8,128)} fusion(bf16[64,128,64]{1,0,2:T(8,128)(2,1)} %collective-permute-done.16, bf16[64,128,64]{1,0,2:T(8,128)(2,1)} %collective-permute-done.15, bf16[64,128,64]{1,0,2:T(8,128)(2,1)} %collective-permute-done.14, bf16[64,128,64]{1,0,2:T(8,128)(2,1)S(1)} %bitcast.102, bf16[16,512,128,1]{2,1,3,0:T(8,128)(2,1)} %bitcast.10, ...), kind=kOutput, calls=%fused_computation.12 | convolution fusion | flops 12910067712 | bytes 11534336 | tf_op jit(solution)/shard_map/padq,bdq->pab/dot_general | solution.py:62
  201.0 26.2 %reduce-scatter.2.cloned.1.call-done = f32[4,64,256]{2,1,0:T(8,128)} async-done(((f32[16,64,256]{2,1,0:T(8,128)}), f32[4,64,256]{2,1,0:T(8,128)}) %reduce-scatter.2.cloned.1.call-update) | async-done | bytes 262160 | tf_op jit(solution)/shard_map/reduce_scatter | solution.py:65
  229.4 2.8 %concatenate.7 = f32[4,64,8,64]{3,2,1,0:T(8,128)S(1)} concatenate(f32[4,64,1,64]{3,2,1,0:T(1,128)} %get-tuple-element.24, f32[4,64,1,64]{3,2,1,0:T(1,128)S(1)} %get-tuple-element.23, f32[4,64,1,64]{3,2,1,0:T(1,128)S(1)} %get-tuple-element.22, f32[4,64,1,64]{3,2,1,0:T(1,128)S(1)} %get-tuple-element.21, f32[4,64,1,64]{3,2,1,0:T(1,128)} %get-tuple-element.24, ...), dimensions={2} | concatenate | bytes 1048576 | tf_op jit(solution)/shard_map/concatenate | solution.py:68
  234.8 6.5 %collective-permute-start.17 = (f32[2,64,128]{2,1,0:T(8,128)S(1)}, f32[2,64,128]{2,1,0:T(8,128)S(1)}, u32[]{:S(2)}, u32[]{:S(2)}) collective-permute-start(f32[2,64,128]{2,1,0:T(8,128)S(1)} %bitcast.113), channel_id=1, source_target_pairs={{0,0},{1,8},{2,16},{3,24},{4,1},{5,9},{6,17},{7,25},{8,4},{9,12},{... | collective-permute-start | bytes 196616 | tf_op jit(solution)/shard_map/ppermute | solution.py:89
  241.3 3.0 %collective-permute-start.18 = (f32[2,64,128]{2,1,0:T(8,128)S(1)}, f32[2,64,128]{2,1,0:T(8,128)S(1)}, u32[]{:S(2)}, u32[]{:S(2)}) collective-permute-start(f32[2,64,128]{2,1,0:T(8,128)S(1)} %bitcast.112), channel_id=1, source_target_pairs={{0,1},{1,9},{2,17},{3,25},{4,4},{5,12},{6,20},{7,28},{8,5},{9,13},... | collective-permute-start | bytes 196616 | tf_op jit(solution)/shard_map/ppermute | solution.py:89
  244.4 3.6 %collective-permute-start.19 = (f32[2,64,128]{2,1,0:T(8,128)S(1)}, f32[2,64,128]{2,1,0:T(8,128)S(1)}, u32[]{:S(2)}, u32[]{:S(2)}) collective-permute-start(f32[2,64,128]{2,1,0:T(8,128)S(1)} %bitcast.111), channel_id=1, source_target_pairs={{0,4},{1,12},{2,20},{3,28},{4,5},{5,13},{6,21},{7,29},{8,0},{9,8},... | collective-permute-start | bytes 196616 | tf_op jit(solution)/shard_map/ppermute | solution.py:89
  252.4 4.1 %collective-permute-done.20 = f32[2,64,128]{2,1,0:T(8,128)S(1)} collective-permute-done((f32[2,64,128]{2,1,0:T(8,128)S(1)}, f32[2,64,128]{2,1,0:T(8,128)S(1)}, u32[]{:S(2)}, u32[]{:S(2)}) %collective-permute-start.20) | collective-permute-done | bytes 65568 | tf_op jit(solution)/shard_map/ppermute | solution.py:89
  (83 shorter events, 44.9 us)
Async XLA Ops:
  6.5 150.1 %all-gather.3.cloned.1.call-start = ((), (), s32[]{:S(2)}) async-start(), calls=%async_computation.2 | async-start | bytes 10485760 | tf_op jit(solution)/shard_map/all_gather | solution.py:40
  15.5 10.2 %collective-permute-start.7 = (bf16[64,16,64]{2,1,0:T(8,128)(2,1)S(1)}, bf16[64,16,64]{2,1,0:T(8,128)(2,1)S(1)}, u32[]{:S(2)}, u32[]{:S(2)}) collective-permute-start(bf16[64,16,64]{2,1,0:T(8,128)(2,1)S(1)} %bitcast.109), channel_id=1, source_target_pairs={{0,4},{4,8},{8,12},{12,16},{16,20},{20,24},{24,28},{28,0},{1,5},{5... | collective-permute-start | bytes 393224 | tf_op jit(solution)/shard_map/ppermute | solution.py:27
  16.8 10.9 %collective-permute-start.8 = (bf16[64,16,64]{2,1,0:T(8,128)(2,1)S(1)}, bf16[64,16,64]{2,1,0:T(8,128)(2,1)S(1)}, u32[]{:S(2)}, u32[]{:S(2)}) collective-permute-start(bf16[64,16,64]{2,1,0:T(8,128)(2,1)S(1)} %bitcast.108), channel_id=1, source_target_pairs={{0,8},{4,12},{8,16},{12,20},{16,24},{20,28},{24,0},{28,4},{1,9},{5... | collective-permute-start | bytes 393224 | tf_op jit(solution)/shard_map/ppermute | solution.py:27
  18.2 30.9 %collective-permute-start.9 = (bf16[64,16,64]{2,1,0:T(8,128)(2,1)S(1)}, bf16[64,16,64]{2,1,0:T(8,128)(2,1)S(1)}, u32[]{:S(2)}, u32[]{:S(2)}) collective-permute-start(bf16[64,16,64]{2,1,0:T(8,128)(2,1)S(1)} %bitcast.107), channel_id=1, source_target_pairs={{0,12},{4,16},{8,20},{12,24},{16,28},{20,0},{24,4},{28,8},{1,13},{... | collective-permute-start | bytes 393224 | tf_op jit(solution)/shard_map/ppermute | solution.py:27
  20.6 29.2 %collective-permute-start.10 = (bf16[64,16,64]{2,1,0:T(8,128)(2,1)S(1)}, bf16[64,16,64]{2,1,0:T(8,128)(2,1)S(1)}, u32[]{:S(2)}, u32[]{:S(2)}) collective-permute-start(bf16[64,16,64]{2,1,0:T(8,128)(2,1)S(1)} %bitcast.106), channel_id=1, source_target_pairs={{0,16},{4,20},{8,24},{12,28},{16,0},{20,4},{24,8},{28,12},{1,17},{... | collective-permute-start | bytes 393224 | tf_op jit(solution)/shard_map/ppermute | solution.py:27
  21.6 28.9 %collective-permute-start.11 = (bf16[64,16,64]{2,1,0:T(8,128)(2,1)S(1)}, bf16[64,16,64]{2,1,0:T(8,128)(2,1)S(1)}, u32[]{:S(2)}, u32[]{:S(2)}) collective-permute-start(bf16[64,16,64]{2,1,0:T(8,128)(2,1)S(1)} %bitcast.105), channel_id=1, source_target_pairs={{0,20},{4,24},{8,28},{12,0},{16,4},{20,8},{24,12},{28,16},{1,21},{... | collective-permute-start | bytes 393224 | tf_op jit(solution)/shard_map/ppermute | solution.py:27
  25.7 25.6 %collective-permute-start.12 = (bf16[64,16,64]{2,1,0:T(8,128)(2,1)S(1)}, bf16[64,16,64]{2,1,0:T(8,128)(2,1)S(1)}, u32[]{:S(2)}, u32[]{:S(2)}) collective-permute-start(bf16[64,16,64]{2,1,0:T(8,128)(2,1)S(1)} %bitcast.104), channel_id=1, source_target_pairs={{0,24},{4,28},{8,0},{12,4},{16,8},{20,12},{24,16},{28,20},{1,25},{... | collective-permute-start | bytes 393224 | tf_op jit(solution)/shard_map/ppermute | solution.py:27
  27.7 24.3 %collective-permute-start.13 = (bf16[64,16,64]{2,1,0:T(8,128)(2,1)S(1)}, bf16[64,16,64]{2,1,0:T(8,128)(2,1)S(1)}, u32[]{:S(2)}, u32[]{:S(2)}) collective-permute-start(bf16[64,16,64]{2,1,0:T(8,128)(2,1)S(1)} %bitcast.103), channel_id=1, source_target_pairs={{0,28},{4,0},{8,4},{12,8},{16,12},{20,16},{24,20},{28,24},{1,29},{... | collective-permute-start | bytes 393224 | tf_op jit(solution)/shard_map/ppermute | solution.py:27
  52.7 174.6 %reduce-scatter.2.cloned.1.call-start = ((), (), s32[]{:S(2)}) async-start(), calls=%async_computation.1 | async-start | bytes 1310720 | tf_op jit(solution)/shard_map/reduce_scatter | solution.py:65
  52.8 36.9 %collective-permute-start = (bf16[16,64,128]{2,1,0:T(8,128)(2,1)S(1)}, bf16[16,64,128]{2,1,0:T(8,128)(2,1)}, u32[]{:S(2)}, u32[]{:S(2)}) collective-permute-start(bf16[16,64,128]{2,1,0:T(8,128)(2,1)S(1)} %copy-done.1), channel_id=1, source_target_pairs={{0,4},{4,8},{8,12},{12,16},{16,20},{20,24},{24,28},{28,0},{1,5},{5... | collective-permute-start | bytes 786440 | tf_op jit(solution)/shard_map/ppermute | solution.py:27
  58.5 33.1 %collective-permute-start.1 = (bf16[16,64,128]{2,1,0:T(8,128)(2,1)S(1)}, bf16[16,64,128]{2,1,0:T(8,128)(2,1)}, u32[]{:S(2)}, u32[]{:S(2)}) collective-permute-start(bf16[16,64,128]{2,1,0:T(8,128)(2,1)S(1)} %copy-done.1), channel_id=1, source_target_pairs={{0,8},{4,12},{8,16},{12,20},{16,24},{20,28},{24,0},{28,4},{1,9},{5... | collective-permute-start | bytes 786440 | tf_op jit(solution)/shard_map/ppermute | solution.py:27
  68.6 30.2 %collective-permute-start.2 = (bf16[16,64,128]{2,1,0:T(8,128)(2,1)S(1)}, bf16[16,64,128]{2,1,0:T(8,128)(2,1)}, u32[]{:S(2)}, u32[]{:S(2)}) collective-permute-start(bf16[16,64,128]{2,1,0:T(8,128)(2,1)S(1)} %copy-done.1), channel_id=1, source_target_pairs={{0,12},{4,16},{8,20},{12,24},{16,28},{20,0},{24,4},{28,8},{1,13},{... | collective-permute-start | bytes 786440 | tf_op jit(solution)/shard_map/ppermute | solution.py:27
  68.6 35.1 %collective-permute-start.3 = (bf16[16,64,128]{2,1,0:T(8,128)(2,1)S(1)}, bf16[16,64,128]{2,1,0:T(8,128)(2,1)}, u32[]{:S(2)}, u32[]{:S(2)}) collective-permute-start(bf16[16,64,128]{2,1,0:T(8,128)(2,1)S(1)} %copy-done.1), channel_id=1, source_target_pairs={{0,16},{4,20},{8,24},{12,28},{16,0},{20,4},{24,8},{28,12},{1,17},{... | collective-permute-start | bytes 786440 | tf_op jit(solution)/shard_map/ppermute | solution.py:27
  70.2 38.2 %collective-permute-start.4 = (bf16[16,64,128]{2,1,0:T(8,128)(2,1)S(1)}, bf16[16,64,128]{2,1,0:T(8,128)(2,1)}, u32[]{:S(2)}, u32[]{:S(2)}) collective-permute-start(bf16[16,64,128]{2,1,0:T(8,128)(2,1)S(1)} %copy-done.1), channel_id=1, source_target_pairs={{0,20},{4,24},{8,28},{12,0},{16,4},{20,8},{24,12},{28,16},{1,21},{... | collective-permute-start | bytes 786440 | tf_op jit(solution)/shard_map/ppermute | solution.py:27
  89.7 86.2 %collective-permute-start.14 = (bf16[64,128,64]{1,0,2:T(8,128)(2,1)}, bf16[64,128,64]{1,0,2:T(8,128)(2,1)}, u32[]{:S(2)}, u32[]{:S(2)}) collective-permute-start(bf16[64,128,64]{1,0,2:T(8,128)(2,1)} %bitcast.90), channel_id=1, source_target_pairs={{0,4},{4,8},{8,12},{12,0},{16,20},{20,24},{24,28},{28,16},{1,5},{5... | collective-permute-start | bytes 3145736 | tf_op jit(solution)/shard_map/ppermute | solution.py:54
  91.6 84.3 %collective-permute-start.15 = (bf16[64,128,64]{1,0,2:T(8,128)(2,1)}, bf16[64,128,64]{1,0,2:T(8,128)(2,1)}, u32[]{:S(2)}, u32[]{:S(2)}) collective-permute-start(bf16[64,128,64]{1,0,2:T(8,128)(2,1)} %bitcast.89), channel_id=1, source_target_pairs={{0,8},{4,12},{8,0},{12,4},{16,24},{20,28},{24,16},{28,20},{1,9},{5... | collective-permute-start | bytes 3145736 | tf_op jit(solution)/shard_map/ppermute | solution.py:54
  98.9 77.1 %collective-permute-start.16 = (bf16[64,128,64]{1,0,2:T(8,128)(2,1)}, bf16[64,128,64]{1,0,2:T(8,128)(2,1)}, u32[]{:S(2)}, u32[]{:S(2)}) collective-permute-start(bf16[64,128,64]{1,0,2:T(8,128)(2,1)} %bitcast.88), channel_id=1, source_target_pairs={{0,12},{4,0},{8,4},{12,8},{16,28},{20,16},{24,20},{28,24},{1,13},{... | collective-permute-start | bytes 3145736 | tf_op jit(solution)/shard_map/ppermute | solution.py:54
  103.7 51.4 %collective-permute-start.5 = (bf16[16,64,128]{2,1,0:T(8,128)(2,1)S(1)}, bf16[16,64,128]{2,1,0:T(8,128)(2,1)S(1)}, u32[]{:S(2)}, u32[]{:S(2)}) collective-permute-start(bf16[16,64,128]{2,1,0:T(8,128)(2,1)S(1)} %copy-done.1), channel_id=1, source_target_pairs={{0,24},{4,28},{8,0},{12,4},{16,8},{20,12},{24,16},{28,20},{1,25},{... | collective-permute-start | bytes 786440 | tf_op jit(solution)/shard_map/ppermute | solution.py:27
  108.4 47.5 %collective-permute-start.6 = (bf16[16,64,128]{2,1,0:T(8,128)(2,1)S(1)}, bf16[16,64,128]{2,1,0:T(8,128)(2,1)S(1)}, u32[]{:S(2)}, u32[]{:S(2)}) collective-permute-start(bf16[16,64,128]{2,1,0:T(8,128)(2,1)S(1)} %copy-done.1), channel_id=1, source_target_pairs={{0,28},{4,0},{8,4},{12,8},{16,12},{20,16},{24,20},{28,24},{1,29},{... | collective-permute-start | bytes 786440 | tf_op jit(solution)/shard_map/ppermute | solution.py:27
  176.0 24.9 %copy-start.3 = (f32[128]{0:T(128)S(1)}, f32[128]{0:T(128)}, u32[]{:S(2)}) copy-start(f32[128]{0:T(128)} %param.10) | copy-start | bytes 1540
  234.8 15.6 %collective-permute-start.17 = (f32[2,64,128]{2,1,0:T(8,128)S(1)}, f32[2,64,128]{2,1,0:T(8,128)S(1)}, u32[]{:S(2)}, u32[]{:S(2)}) collective-permute-start(f32[2,64,128]{2,1,0:T(8,128)S(1)} %bitcast.113), channel_id=1, source_target_pairs={{0,0},{1,8},{2,16},{3,24},{4,1},{5,9},{6,17},{7,25},{8,4},{9,12},{... | collective-permute-start | bytes 196616 | tf_op jit(solution)/shard_map/ppermute | solution.py:89
  241.3 11.1 %collective-permute-start.18 = (f32[2,64,128]{2,1,0:T(8,128)S(1)}, f32[2,64,128]{2,1,0:T(8,128)S(1)}, u32[]{:S(2)}, u32[]{:S(2)}) collective-permute-start(f32[2,64,128]{2,1,0:T(8,128)S(1)} %bitcast.112), channel_id=1, source_target_pairs={{0,1},{1,9},{2,17},{3,25},{4,4},{5,12},{6,20},{7,28},{8,5},{9,13},... | collective-permute-start | bytes 196616 | tf_op jit(solution)/shard_map/ppermute | solution.py:89
  244.4 8.0 %collective-permute-start.19 = (f32[2,64,128]{2,1,0:T(8,128)S(1)}, f32[2,64,128]{2,1,0:T(8,128)S(1)}, u32[]{:S(2)}, u32[]{:S(2)}) collective-permute-start(f32[2,64,128]{2,1,0:T(8,128)S(1)} %bitcast.111), channel_id=1, source_target_pairs={{0,4},{1,12},{2,20},{3,28},{4,5},{5,13},{6,21},{7,29},{8,0},{9,8},... | collective-permute-start | bytes 196616 | tf_op jit(solution)/shard_map/ppermute | solution.py:89
  248.0 8.5 %collective-permute-start.20 = (f32[2,64,128]{2,1,0:T(8,128)S(1)}, f32[2,64,128]{2,1,0:T(8,128)S(1)}, u32[]{:S(2)}, u32[]{:S(2)}) collective-permute-start(f32[2,64,128]{2,1,0:T(8,128)S(1)} %bitcast.110), channel_id=1, source_target_pairs={{0,5},{1,13},{2,21},{3,29},{4,0},{5,8},{6,16},{7,24},{8,1},{9,9},{... | collective-permute-start | bytes 196616 | tf_op jit(solution)/shard_map/ppermute | solution.py:89
  (5 other events, 71.2 us)
Sparse Core Ops, SparseCore 0:
  52.8 72.2 all-gather.2
  200.6 26.6 reduce-scatter.1

commit v4 on v2

--- a/solution.py
+++ b/solution.py
@@ -20,7 +20,11 @@
         pairs = amps.shape[0]
         vir_total = b_blk * n_narrow
 
-        amps_all = lax.all_gather(amps, "narrow", axis=1, tiled=True)
+        amps_blocks = [amps]
+        for shift in range(1, n_narrow):
+            perm = [(i, (i + shift) % n_narrow) for i in range(n_narrow)]
+            amps_blocks.append(lax.ppermute(amps, "narrow", perm))
+        amps_all = jnp.stack(amps_blocks, axis=1)
 
         c_sub = c_blk // n_wide
         left_part = lax.dynamic_slice_in_dim(left_fit, w * c_sub, c_sub, 1)
@@ -44,8 +48,14 @@
                 piece = lax.ppermute(piece, "narrow", perm)
             chunks.append(piece)
 
+        left_blocks = left_all.reshape(rows, n_narrow, c_blk, q_blk)
+        left_flip = jnp.concatenate(
+            [left_blocks[:, (n_narrow - k) % n_narrow : (n_narrow - k) % n_narrow + 1] for k in range(n_narrow)] * 2,
+            axis=1,
+        )
+        left_shifted = lax.dynamic_slice_in_dim(left_flip, n_narrow - n, n_narrow, 1)
         inter = jnp.einsum(
-            "acq,pcd->padq", left_all, amps_all, preferred_element_type=jnp.float32
+            "ankq,pnkd->padq", left_shifted, amps_all, preferred_element_type=jnp.float32
         ).astype(jnp.bfloat16)
 
         right_group = jnp.concatenate(chunks, axis=0)

time: 247 us -> 269 us (1.089)
  local copies, waits for them, and re-layouts: 56.7 us -> 105 us
  waiting for transfers between devices: 99.8 us -> 53.1 us
  starting transfers between devices: 18.6 us -> 36.3 us
    unnamed x11 -> x61, local copies, waits for them, and re-layouts: 15.7 us -> 65.5 us
    all_gather x1 -> x0, waiting for transfers between devices: 31.8 us -> none  [body(): amps_all = lax.all_gather(amps, 'narrow', axis=1, tiled=True)]
    all_gather x1, waiting for transfers between devices: 38.3 us -> 8.86 us  [body(): left_all = lax.all_gather(left_recv, 'wide', axis=0, tiled=False)]
    dot_general x0 -> x1, matrix products: none -> 14.5 us  [body(): jnp.einsum('ankq,pnkd->padq', left_shifted, amps_all, preferred_element_t...]
    dot_general x1, matrix products: 24.5 us -> 12.3 us  [body(): jnp.einsum('padq,bdq->pab', inter, right_group, preferred_element_type=jn...]
    reduce_scatter x1, waiting for transfers between devices: 23 us -> 33.8 us  [body(): part = lax.psum_scatter(part, 'wide', scatter_dimension=0, tiled=True)]
    reshape x1 -> x0, local copies, waits for them, and re-layouts: 10.2 us -> none  [body(): left_all.transpose(2, 1, 0, 3, 4).reshape(rows, c_blk * n_narrow, q_blk)]
    ppermute x0 -> x7, starting transfers between devices: none -> 9.32 us  [body(): amps_blocks.append(lax.ppermute(amps, 'narrow', perm))]
  transfers between devices with their start and end apart: 10 -> 16, of which waited for: 5 -> 5; matrix products, arithmetic and copies ran while one was open for 15% -> 37% of each run, Pallas kernels for 0% -> 0%
where the time goes in v4:
time: 269 us; the launch traced here: 268 us
  local copies, waits for them, and re-layouts  105 us (39%)
  waiting for transfers between devices  53.1 us (20%)
  starting transfers between devices  36.3 us (13%)
  blocking collectives  30.2 us (11%)
  matrix products  26.7 us (10%)
  between operations  13.9 us (5%)
    unnamed x61, local copies, waits for them, and re-layouts  65.5 us
    reduce_scatter x1, waiting for transfers between devices, body(): part = lax.psum_scatter(part, 'wide', scatter_dimension=0, tiled=True)  33.8 us
    all_to_all x1, blocking collectives, body(): left_recv = lax.all_to_all(left_send, 'narrow', 0, 0, tiled=True)  30.2 us
    ppermute x4, starting transfers between devices, body(): piece = lax.ppermute(piece, ('narrow', 'wide'), perm)  15.4 us
    dot_general x1, matrix products, body(): jnp.einsum('ankq,pnkd->padq', left_shifted, amps_all, preferred_element_t...  14.5 us
    dot_general x1, matrix products, body(): jnp.einsum('padq,bdq->pab', inter, right_group, preferred_element_type=jn...  12.3 us
    ppermute x3, starting transfers between devices, body(): piece = lax.ppermute(piece, 'narrow', perm)  11.5 us
    dynamic_slice x5, local copies, waits for them, and re-layouts, body(): piece = lax.dynamic_index_in_dim(right_split, dest, 2, keepdims=False)  9.83 us
  transfers between devices with their start and end apart: 16, of which 5 were waited for; matrix products, arithmetic and copies ran while one was open for 37% of the time, Pallas kernels for 0%

profile of v4, /device:TPU:5, one launch (start us, length us, event | category | flops | bytes accessed | tf_op | source)
XLA Modules:
  0.0 267.6 jit_solution(8618134519967816250)
XLA Ops:
  13.9 3.4 %reshape.70 = bf16[8,2,32768]{2,1,0:T(2,128)(2,1)S(1)} reshape(bf16[8,64,16,64]{3,2,1,0:T(8,128)(2,1)} %copy.75) | data formatting | bytes 2097152
  17.3 30.2 %all_to_all.5 = bf16[8,2,32768]{2,1,0:T(2,128)(2,1)S(1)} all-to-all(bf16[8,2,32768]{2,1,0:T(2,128)(2,1)S(1)} %reshape.70), channel_id=1, replica_groups=mesh['narrow'=8,'wide'=4] {'narrow'}, dimensions={0} | all-to-all | bytes 2097152 | tf_op jit(solution)/shard_map/all_to_all | solution.py:33
  47.5 2.7 %reshape.71 = bf16[8,64,16,64]{3,2,1,0:T(8,128)(2,1)} reshape(bf16[8,2,32768]{2,1,0:T(2,128)(2,1)S(1)} %all_to_all.5) | data formatting | bytes 2097152
  57.8 6.8 %copy.85 = bf16[64,128,256]{1,2,0:T(8,128)(2,1)} copy(bf16[64,128,256]{2,1,0:T(8,128)(2,1)} %param.8) | data formatting | bytes 8388608 | tf_op args[2]
  64.6 3.2 %constant_dynamic-slice_fusion.8 = (bf16[64,128,1,64]{1,3,2,0:T(8,128)(2,1)S(1)}, bf16[64,128,1,64]{1,3,2,0:T(8,128)(2,1)S(1)}, bf16[64,128,1,64]{1,3,2,0:T(8,128)(2,1)S(1)}, bf16[64,128,1,64]{1,3,2,0:T(8,128)(2,1)S(1)}) fusion(bf16[64,128,4,64]{1,3,2,0:T(8,128)(2,1)} %bitcast.99, s32[]{:T(128)S(6)} %select_n.138, s32[]{:T(128)S(6)} %select_n.144, ...), kind=kLoop, calls=%fused_computation.53 | loop fusion | bytes 8388624 | tf_op jit(solution)/shard_map/jit(dynamic_index_in_dim)/dynamic_slice | solution.py:41
  79.6 4.3 %collective-permute-done.2 = bf16[16,64,128]{2,1,0:T(8,128)(2,1)S(1)} collective-permute-done((bf16[16,64,128]{2,1,0:T(8,128)(2,1)S(1)}, bf16[16,64,128]{2,1,0:T(8,128)(2,1)S(1)}, u32[]{:S(2)}, u32[]{:S(2)}) %collective-permute-start.2) | collective-permute-done | bytes 262176 | tf_op jit(solution)/shard_map/ppermute | solution.py:26
  84.7 6.7 %collective-permute-start.8 = (bf16[64,128,64]{1,0,2:T(8,128)(2,1)}, bf16[64,128,64]{1,0,2:T(8,128)(2,1)}, u32[]{:S(2)}, u32[]{:S(2)}) collective-permute-start(bf16[64,128,64]{1,0,2:T(8,128)(2,1)} %bitcast.95), channel_id=1, source_target_pairs={{0,8},{4,12},{8,0},{12,4},{16,24},{20,28},{24,16},{28,20},{1,9},{5... | collective-permute-start | bytes 3145736 | tf_op jit(solution)/shard_map/ppermute | solution.py:48
  92.2 4.7 %collective-permute-start.9 = (bf16[64,128,64]{1,0,2:T(8,128)(2,1)}, bf16[64,128,64]{1,0,2:T(8,128)(2,1)}, u32[]{:S(2)}, u32[]{:S(2)}) collective-permute-start(bf16[64,128,64]{1,0,2:T(8,128)(2,1)} %bitcast.94), channel_id=1, source_target_pairs={{0,12},{4,0},{8,4},{12,8},{16,28},{20,16},{24,20},{28,24},{1,13},{... | collective-permute-start | bytes 3145736 | tf_op jit(solution)/shard_map/ppermute | solution.py:48
  99.2 8.9 %all-gather.3.cloned.1.call-done = bf16[32,64,16,64]{3,2,1,0:T(8,128)(2,1)} async-done(((bf16[8,64,16,64]{3,2,1,0:T(8,128)(2,1)}), bf16[32,64,16,64]{3,2,1,0:T(8,128)(2,1)}) %all-gather.3.cloned.1.call-update) | async-done | bytes 4194320 | tf_op jit(solution)/shard_map/all_gather | solution.py:34
  108.1 9.1 %copy.76 = bf16[64,8,4,16,64]{4,3,2,1,0:T(8,128)(2,1)} copy(bf16[64,8,4,16,64]{4,3,0,1,2:T(8,128)(2,1)} %bitcast.100) | data formatting | bytes 8388608 | tf_op jit(solution)/shard_map/transpose | solution.py:35
  117.2 6.4 %fusion.30 = (bf16[64,1,64,64]{3,2,1,0:T(8,128)(2,1)}, bf16[64,1,64,64]{3,2,1,0:T(8,128)(2,1)S(1)}, bf16[64,1,64,64]{3,2,1,0:T(8,128)(2,1)S(1)}, bf16[64,1,64,64...) fusion(bf16[64,8,64,64]{3,2,1,0:T(8,128)(2,1)} %bitcast.98), kind=kLoop, calls=%fused_computation.64 | loop fusion | bytes 8388608 | tf_op jit(solution)/shard_map/slice | solution.py:53
  123.6 2.6 copy.93
  127.5 3.3 %copy.94 = bf16[64,1,64,64]{2,0,1,3:T(8,128)(2,1)} copy(bf16[64,1,64,64]{3,2,1,0:T(8,128)(2,1)} %get-tuple-element.15) | data formatting | bytes 1048576
  130.8 3.3 %copy.95 = bf16[64,1,64,64]{2,0,1,3:T(8,128)(2,1)} copy(bf16[64,1,64,64]{3,2,1,0:T(8,128)(2,1)} %get-tuple-element.14) | data formatting | bytes 1048576
  134.1 3.3 %copy.96 = bf16[64,1,64,64]{2,0,1,3:T(8,128)(2,1)} copy(bf16[64,1,64,64]{3,2,1,0:T(8,128)(2,1)} %get-tuple-element.13) | data formatting | bytes 1048576
  137.4 3.3 %copy.97 = bf16[64,1,64,64]{2,0,1,3:T(8,128)(2,1)} copy(bf16[64,1,64,64]{3,2,1,0:T(8,128)(2,1)} %get-tuple-element.12) | data formatting | bytes 1048576
  169.5 14.5 %fusion.43 = bf16[16,64,128,64]{2,1,3,0:T(8,128)(2,1)} fusion(bf16[64,16,64,64]{2,0,1,3:T(8,128)(2,1)} %constant_dynamic-update-slice_fusion, s32[]{:T(128)S(6)} %select_n.135, bf16[16,8,64,128]{3,2,1,0:T(8,128)(2,1)S(1)} %copy-done.10), kind=kOutput, calls=%fused_computation.1.clone.clone.clone.clone.2 | convolution fusion | flops 8598323200 | bytes 27262980 | tf_op jit(solution)/shard_map/ankq,pnkd->padq/dot_general | solution.py:57
  184.1 12.3 %fusion.18 = f32[16,64,256]{2,1,0:T(8,128)} fusion(bf16[64,128,64]{1,0,2:T(8,128)(2,1)} %collective-permute-done.9, bf16[64,128,64]{1,0,2:T(8,128)(2,1)} %collective-permute-done.8, bf16[64,128,64]{1,0,2:T(8,128)(2,1)} %collective-permute-done.7, bf16[64,128,64]{1,0,2:T(8,128)(2,1)S(1)} %bitcast.102, bf16[16,64,128,64]{2,1,3,0:T(8,128)(2,1)} %fusion.43), kind=kOutput, calls=%fused_computation.15 | convolution fusion | flops 4311744512 | bytes 22020096 | tf_op jit(solution)/shard_map/padq,bdq->pab/dot_general | solution.py:62
  196.9 33.8 %reduce-scatter.2.cloned.1.call-done = f32[4,64,256]{2,1,0:T(8,128)} async-done(((f32[16,64,256]{2,1,0:T(8,128)}), f32[4,64,256]{2,1,0:T(8,128)}) %reduce-scatter.2.cloned.1.call-update) | async-done | bytes 262160 | tf_op jit(solution)/shard_map/reduce_scatter | solution.py:65
  232.8 2.8 %concatenate.15 = f32[4,64,8,64]{3,2,1,0:T(8,128)S(1)} concatenate(f32[4,64,1,64]{3,2,1,0:T(1,128)} %get-tuple-element.24, f32[4,64,1,64]{3,2,1,0:T(1,128)S(1)} %get-tuple-element.23, f32[4,64,1,64]{3,2,1,0:T(1,128)S(1)} %get-tuple-element.22, f32[4,64,1,64]{3,2,1,0:T(1,128)S(1)} %get-tuple-element.21, f32[4,64,1,64]{3,2,1,0:T(1,128)} %get-tuple-element.24, ...), dimensions={2} | concatenate | bytes 1048576 | tf_op jit(solution)/shard_map/concatenate | solution.py:68
  238.3 6.5 %collective-permute-start.10 = (f32[2,64,128]{2,1,0:T(8,128)S(1)}, f32[2,64,128]{2,1,0:T(8,128)S(1)}, u32[]{:S(2)}, u32[]{:S(2)}) collective-permute-start(f32[2,64,128]{2,1,0:T(8,128)S(1)} %bitcast.106), channel_id=1, source_target_pairs={{0,0},{1,8},{2,16},{3,24},{4,1},{5,9},{6,17},{7,25},{8,4},{9,12},{... | collective-permute-start | bytes 196616 | tf_op jit(solution)/shard_map/ppermute | solution.py:89
  244.8 3.0 %collective-permute-start.11 = (f32[2,64,128]{2,1,0:T(8,128)S(1)}, f32[2,64,128]{2,1,0:T(8,128)S(1)}, u32[]{:S(2)}, u32[]{:S(2)}) collective-permute-start(f32[2,64,128]{2,1,0:T(8,128)S(1)} %bitcast.105), channel_id=1, source_target_pairs={{0,1},{1,9},{2,17},{3,25},{4,4},{5,12},{6,20},{7,28},{8,5},{9,13},... | collective-permute-start | bytes 196616 | tf_op jit(solution)/shard_map/ppermute | solution.py:89
  247.9 3.6 %collective-permute-start.12 = (f32[2,64,128]{2,1,0:T(8,128)S(1)}, f32[2,64,128]{2,1,0:T(8,128)S(1)}, u32[]{:S(2)}, u32[]{:S(2)}) collective-permute-start(f32[2,64,128]{2,1,0:T(8,128)S(1)} %bitcast.104), channel_id=1, source_target_pairs={{0,4},{1,12},{2,20},{3,28},{4,5},{5,13},{6,21},{7,29},{8,0},{9,8},... | collective-permute-start | bytes 196616 | tf_op jit(solution)/shard_map/ppermute | solution.py:89
  255.9 4.2 %collective-permute-done.13 = f32[2,64,128]{2,1,0:T(8,128)S(1)} collective-permute-done((f32[2,64,128]{2,1,0:T(8,128)S(1)}, f32[2,64,128]{2,1,0:T(8,128)S(1)}, u32[]{:S(2)}, u32[]{:S(2)}) %collective-permute-start.13) | collective-permute-done | bytes 65568 | tf_op jit(solution)/shard_map/ppermute | solution.py:89
  (101 shorter events, 71.0 us)
Async XLA Ops:
  6.5 101.6 %all-gather.3.cloned.1.call-start = ((), (), s32[]{:S(2)}) async-start(), calls=%async_computation.3 | async-start | bytes 10485760 | tf_op jit(solution)/shard_map/all_gather | solution.py:34
  11.0 39.3 %copy-start.9 = (bf16[16,64,128]{2,1,0:T(8,128)(2,1)S(1)}, bf16[16,64,128]{2,1,0:T(8,128)(2,1)}, u32[]{:S(2)}) copy-start(bf16[16,64,128]{2,1,0:T(8,128)(2,1)} %param.6) | copy-start | bytes 786436
  50.3 180.5 %reduce-scatter.2.cloned.1.call-start = ((), (), s32[]{:S(2)}) async-start(), calls=%async_computation.2 | async-start | bytes 1310720 | tf_op jit(solution)/shard_map/reduce_scatter | solution.py:65
  50.3 24.1 %collective-permute-start = (bf16[16,64,128]{2,1,0:T(8,128)(2,1)S(1)}, bf16[16,64,128]{2,1,0:T(8,128)(2,1)}, u32[]{:S(2)}, u32[]{:S(2)}) collective-permute-start(bf16[16,64,128]{2,1,0:T(8,128)(2,1)S(1)} %copy-done.9), channel_id=1, source_target_pairs={{0,4},{4,8},{8,12},{12,16},{16,20},{20,24},{24,28},{28,0},{1,5},{5... | collective-permute-start | bytes 786440 | tf_op jit(solution)/shard_map/ppermute | solution.py:26
  51.6 25.8 %collective-permute-start.1 = (bf16[16,64,128]{2,1,0:T(8,128)(2,1)S(1)}, bf16[16,64,128]{2,1,0:T(8,128)(2,1)S(1)}, u32[]{:S(2)}, u32[]{:S(2)}) collective-permute-start(bf16[16,64,128]{2,1,0:T(8,128)(2,1)S(1)} %copy-done.9), channel_id=1, source_target_pairs={{0,8},{4,12},{8,16},{12,20},{16,24},{20,28},{24,0},{28,4},{1,9},{5... | collective-permute-start | bytes 786440 | tf_op jit(solution)/shard_map/ppermute | solution.py:26
  51.6 32.3 %collective-permute-start.2 = (bf16[16,64,128]{2,1,0:T(8,128)(2,1)S(1)}, bf16[16,64,128]{2,1,0:T(8,128)(2,1)S(1)}, u32[]{:S(2)}, u32[]{:S(2)}) collective-permute-start(bf16[16,64,128]{2,1,0:T(8,128)(2,1)S(1)} %copy-done.9), channel_id=1, source_target_pairs={{0,12},{4,16},{8,20},{12,24},{16,28},{20,0},{24,4},{28,8},{1,13},{... | collective-permute-start | bytes 786440 | tf_op jit(solution)/shard_map/ppermute | solution.py:26
  53.4 31.3 %collective-permute-start.3 = (bf16[16,64,128]{2,1,0:T(8,128)(2,1)S(1)}, bf16[16,64,128]{2,1,0:T(8,128)(2,1)S(1)}, u32[]{:S(2)}, u32[]{:S(2)}) collective-permute-start(bf16[16,64,128]{2,1,0:T(8,128)(2,1)S(1)} %copy-done.9), channel_id=1, source_target_pairs={{0,16},{4,20},{8,24},{12,28},{16,0},{20,4},{24,8},{28,12},{1,17},{... | collective-permute-start | bytes 786440 | tf_op jit(solution)/shard_map/ppermute | solution.py:26
  55.3 36.9 %collective-permute-start.4 = (bf16[16,64,128]{2,1,0:T(8,128)(2,1)S(1)}, bf16[16,64,128]{2,1,0:T(8,128)(2,1)S(1)}, u32[]{:S(2)}, u32[]{:S(2)}) collective-permute-start(bf16[16,64,128]{2,1,0:T(8,128)(2,1)S(1)} %copy-done.9), channel_id=1, source_target_pairs={{0,20},{4,24},{8,28},{12,0},{16,4},{20,8},{24,12},{28,16},{1,21},{... | collective-permute-start | bytes 786440 | tf_op jit(solution)/shard_map/ppermute | solution.py:26
  74.4 23.2 %collective-permute-start.5 = (bf16[16,64,128]{2,1,0:T(8,128)(2,1)S(1)}, bf16[16,64,128]{2,1,0:T(8,128)(2,1)S(1)}, u32[]{:S(2)}, u32[]{:S(2)}) collective-permute-start(bf16[16,64,128]{2,1,0:T(8,128)(2,1)S(1)} %copy-done.9), channel_id=1, source_target_pairs={{0,24},{4,28},{8,0},{12,4},{16,8},{20,12},{24,16},{28,20},{1,25},{... | collective-permute-start | bytes 786440 | tf_op jit(solution)/shard_map/ppermute | solution.py:26
  77.4 21.1 %collective-permute-start.6 = (bf16[16,64,128]{2,1,0:T(8,128)(2,1)S(1)}, bf16[16,64,128]{2,1,0:T(8,128)(2,1)S(1)}, u32[]{:S(2)}, u32[]{:S(2)}) collective-permute-start(bf16[16,64,128]{2,1,0:T(8,128)(2,1)S(1)} %copy-done.9), channel_id=1, source_target_pairs={{0,28},{4,0},{8,4},{12,8},{16,12},{20,16},{24,20},{28,24},{1,29},{... | collective-permute-start | bytes 786440 | tf_op jit(solution)/shard_map/ppermute | solution.py:26
  83.9 100.1 %collective-permute-start.7 = (bf16[64,128,64]{1,0,2:T(8,128)(2,1)}, bf16[64,128,64]{1,0,2:T(8,128)(2,1)}, u32[]{:S(2)}, u32[]{:S(2)}) collective-permute-start(bf16[64,128,64]{1,0,2:T(8,128)(2,1)} %bitcast.96), channel_id=1, source_target_pairs={{0,4},{4,8},{8,12},{12,0},{16,20},{20,24},{24,28},{28,16},{1,5},{5... | collective-permute-start | bytes 3145736 | tf_op jit(solution)/shard_map/ppermute | solution.py:48
  84.7 99.3 %collective-permute-start.8 = (bf16[64,128,64]{1,0,2:T(8,128)(2,1)}, bf16[64,128,64]{1,0,2:T(8,128)(2,1)}, u32[]{:S(2)}, u32[]{:S(2)}) collective-permute-start(bf16[64,128,64]{1,0,2:T(8,128)(2,1)} %bitcast.95), channel_id=1, source_target_pairs={{0,8},{4,12},{8,0},{12,4},{16,24},{20,28},{24,16},{28,20},{1,9},{5... | collective-permute-start | bytes 3145736 | tf_op jit(solution)/shard_map/ppermute | solution.py:48
  92.2 91.8 %collective-permute-start.9 = (bf16[64,128,64]{1,0,2:T(8,128)(2,1)}, bf16[64,128,64]{1,0,2:T(8,128)(2,1)}, u32[]{:S(2)}, u32[]{:S(2)}) collective-permute-start(bf16[64,128,64]{1,0,2:T(8,128)(2,1)} %bitcast.94), channel_id=1, source_target_pairs={{0,12},{4,0},{8,4},{12,8},{16,28},{20,16},{24,20},{28,24},{1,13},{... | collective-permute-start | bytes 3145736 | tf_op jit(solution)/shard_map/ppermute | solution.py:48
  126.2 14.4 %copy-start.5 = (bf16[64,1,64,64]{2,0,1,3:T(8,128)(2,1)}, bf16[64,1,64,64]{2,0,1,3:T(8,128)(2,1)S(1)}, u32[]{:S(2)}) copy-start(bf16[64,1,64,64]{2,0,1,3:T(8,128)(2,1)S(1)} %copy.93) | copy-start | bytes 1572868
  146.5 13.6 %copy-start.6 = (bf16[64,1,64,64]{2,0,1,3:T(8,128)(2,1)S(1)}, bf16[64,1,64,64]{2,0,1,3:T(8,128)(2,1)}, u32[]{:S(2)}) copy-start(bf16[64,1,64,64]{2,0,1,3:T(8,128)(2,1)} %copy-done.5) | copy-start | bytes 1572868
  146.6 14.7 %copy-start.7 = (bf16[64,1,64,64]{2,0,1,3:T(8,128)(2,1)S(1)}, bf16[64,1,64,64]{2,0,1,3:T(8,128)(2,1)}, u32[]{:S(2)}) copy-start(bf16[64,1,64,64]{2,0,1,3:T(8,128)(2,1)} %copy.94) | copy-start | bytes 1572868
  169.5 14.5 %copy-start.8 = (bf16[64,128,1,64]{1,0,3,2:T(8,128)(2,1)S(1)}, bf16[64,128,1,64]{1,0,3,2:T(8,128)(2,1)}, u32[]{:S(2)}) copy-start(bf16[64,128,1,64]{1,0,3,2:T(8,128)(2,1)} %copy.108) | copy-start | bytes 3145732
  184.0 69.8 %slice-start = ((f32[512]{0:T(512)}), f32[64]{0:T(128)S(1)}, s32[]{:S(2)}) async-start(f32[512]{0:T(512)} %param.11), calls=%async_computation.4 | async-start | bytes 1024 | tf_op jit(solution)/shard_map/slice | solution.py:101
  184.0 69.8 %copy-start.13 = (f32[512]{0:T(512)S(1)}, f32[512]{0:T(512)}, u32[]{:S(2)}) copy-start(f32[512]{0:T(512)} %param.11) | copy-start | bytes 6148
  184.0 76.7 %copy-start.1 = (bf16[64,64,256]{2,1,0:T(8,128)(2,1)S(1)}, bf16[64,64,256]{2,1,0:T(8,128)(2,1)}, u32[]{:S(2)}) copy-start(bf16[64,64,256]{2,1,0:T(8,128)(2,1)} %param.7) | copy-start | bytes 6291460
  238.3 15.6 %collective-permute-start.10 = (f32[2,64,128]{2,1,0:T(8,128)S(1)}, f32[2,64,128]{2,1,0:T(8,128)S(1)}, u32[]{:S(2)}, u32[]{:S(2)}) collective-permute-start(f32[2,64,128]{2,1,0:T(8,128)S(1)} %bitcast.106), channel_id=1, source_target_pairs={{0,0},{1,8},{2,16},{3,24},{4,1},{5,9},{6,17},{7,25},{8,4},{9,12},{... | collective-permute-start | bytes 196616 | tf_op jit(solution)/shard_map/ppermute | solution.py:89
  244.8 11.1 %collective-permute-start.11 = (f32[2,64,128]{2,1,0:T(8,128)S(1)}, f32[2,64,128]{2,1,0:T(8,128)S(1)}, u32[]{:S(2)}, u32[]{:S(2)}) collective-permute-start(f32[2,64,128]{2,1,0:T(8,128)S(1)} %bitcast.105), channel_id=1, source_target_pairs={{0,1},{1,9},{2,17},{3,25},{4,4},{5,12},{6,20},{7,28},{8,5},{9,13},... | collective-permute-start | bytes 196616 | tf_op jit(solution)/shard_map/ppermute | solution.py:89
  247.9 8.0 %collective-permute-start.12 = (f32[2,64,128]{2,1,0:T(8,128)S(1)}, f32[2,64,128]{2,1,0:T(8,128)S(1)}, u32[]{:S(2)}, u32[]{:S(2)}) collective-permute-start(f32[2,64,128]{2,1,0:T(8,128)S(1)} %bitcast.104), channel_id=1, source_target_pairs={{0,4},{1,12},{2,20},{3,28},{4,5},{5,13},{6,21},{7,29},{8,0},{9,8},... | collective-permute-start | bytes 196616 | tf_op jit(solution)/shard_map/ppermute | solution.py:89
  251.5 8.5 %collective-permute-start.13 = (f32[2,64,128]{2,1,0:T(8,128)S(1)}, f32[2,64,128]{2,1,0:T(8,128)S(1)}, u32[]{:S(2)}, u32[]{:S(2)}) collective-permute-start(f32[2,64,128]{2,1,0:T(8,128)S(1)} %bitcast.103), channel_id=1, source_target_pairs={{0,5},{1,13},{2,21},{3,29},{4,0},{5,8},{6,16},{7,24},{8,1},{9,9},{... | collective-permute-start | bytes 196616 | tf_op jit(solution)/shard_map/ppermute | solution.py:89
  (7 other events, 72.4 us)
Sparse Core Ops, SparseCore 0:
  50.4 57.6 all-gather.2
  196.5 34.2 reduce-scatter.1

commit v5 on v2

--- a/solution.py
+++ b/solution.py
@@ -20,7 +20,14 @@
         pairs = amps.shape[0]
         vir_total = b_blk * n_narrow
 
-        amps_all = lax.all_gather(amps, "narrow", axis=1, tiled=True)
+        amps_blocks = [amps]
+        for shift in range(1, n_narrow):
+            perm = [(i, (i + shift) % n_narrow) for i in range(n_narrow)]
+            amps_blocks.append(lax.ppermute(amps, "narrow", perm))
+        amps_rev = [amps_blocks[(n_narrow - j) % n_narrow] for j in range(n_narrow)]
+        amps_all = lax.dynamic_slice_in_dim(
+            jnp.concatenate(amps_rev * 2, axis=1), (n_narrow - n) * c_blk, n_narrow * c_blk, 1
+        )
 
         c_sub = c_blk // n_wide
         left_part = lax.dynamic_slice_in_dim(left_fit, w * c_sub, c_sub, 1)

time: 247 us -> 241 us (0.976)
  waiting for transfers between devices: 99.8 us -> 43.5 us
  local copies, waits for them, and re-layouts: 56.7 us -> 83.1 us
  starting transfers between devices: 18.6 us -> 41.8 us
    all_gather x1, waiting for transfers between devices: 38.3 us -> 0.01 us  [body(): left_all = lax.all_gather(left_recv, 'wide', axis=0, tiled=False)]
    all_gather x1 -> x0, waiting for transfers between devices: 31.8 us -> none  [body(): amps_all = lax.all_gather(amps, 'narrow', axis=1, tiled=True)]
    ppermute x0 -> x7, starting transfers between devices: none -> 22 us  [body(): amps_blocks.append(lax.ppermute(amps, 'narrow', perm))]
    unnamed x11 -> x32, local copies, waits for them, and re-layouts: 15.7 us -> 37.1 us
    ppermute x3, waiting for transfers between devices: 0.01 us -> 11.2 us  [body(): piece = lax.ppermute(piece, 'narrow', perm)]
    dynamic_slice x5, local copies, waits for them, and re-layouts: 9.47 us -> 13.6 us  [body(): piece = lax.dynamic_index_in_dim(right_split, dest, 2, keepdims=False)]
  transfers between devices with their start and end apart: 10 -> 16, of which waited for: 5 -> 6; matrix products, arithmetic and copies ran while one was open for 15% -> 26% of each run, Pallas kernels for 0% -> 0%
where the time goes in v5:
time: 241 us; the launch traced here: 239 us
  local copies, waits for them, and re-layouts  83.1 us (34%)
  waiting for transfers between devices  43.5 us (18%)
  starting transfers between devices  41.8 us (17%)
  blocking collectives  30.5 us (13%)
  matrix products  24.5 us (10%)
  between operations  13.7 us (6%)
    unnamed x32, local copies, waits for them, and re-layouts  37.1 us
    all_to_all x1, blocking collectives, body(): left_recv = lax.all_to_all(left_send, 'narrow', 0, 0, tiled=True)  30.5 us
    dot_general x1, matrix products, body(): jnp.einsum('padq,bdq->pab', inter, right_group, preferred_element_type=jn...  24.5 us
    reduce_scatter x1, waiting for transfers between devices, body(): part = lax.psum_scatter(part, 'wide', scatter_dimension=0, tiled=True)  24.2 us
    ppermute x7, starting transfers between devices, body(): amps_blocks.append(lax.ppermute(amps, 'narrow', perm))  22 us
    ppermute x4, starting transfers between devices, body(): piece = lax.ppermute(piece, ('narrow', 'wide'), perm)  15.7 us
    dynamic_slice x5, local copies, waits for them, and re-layouts, body(): piece = lax.dynamic_index_in_dim(right_split, dest, 2, keepdims=False)  13.6 us
    ppermute x3, waiting for transfers between devices, body(): piece = lax.ppermute(piece, 'narrow', perm)  11.2 us
  transfers between devices with their start and end apart: 16, of which 6 were waited for; matrix products, arithmetic and copies ran while one was open for 26% of the time, Pallas kernels for 0%

profile of v5, /device:TPU:5, one launch (start us, length us, event | category | flops | bytes accessed | tf_op | source)
XLA Modules:
  0.0 239.4 jit_solution(9081037101214975195)
XLA Ops:
  9.0 2.0 reshape.61
  13.9 3.4 %reshape.73 = bf16[8,2,32768]{2,1,0:T(2,128)(2,1)S(1)} reshape(bf16[8,64,16,64]{3,2,1,0:T(8,128)(2,1)} %copy.47) | data formatting | bytes 2097152
  17.3 30.5 %all_to_all.5 = bf16[8,2,32768]{2,1,0:T(2,128)(2,1)} all-to-all(bf16[8,2,32768]{2,1,0:T(2,128)(2,1)S(1)} %reshape.73), channel_id=1, replica_groups=mesh['narrow'=8,'wide'=4] {'narrow'}, dimensions={0} | all-to-all | bytes 2097152 | tf_op jit(solution)/shard_map/all_to_all | solution.py:36
  47.8 4.3 %reshape.74 = bf16[8,64,16,64]{3,2,1,0:T(8,128)(2,1)} reshape(bf16[8,2,32768]{2,1,0:T(2,128)(2,1)} %all_to_all.5) | data formatting | bytes 2097152
  53.2 2.8 %collective-permute-start.2 = (bf16[16,64,128]{2,1,0:T(8,128)(2,1)S(1)}, bf16[16,64,128]{2,1,0:T(8,128)(2,1)}, u32[]{:S(2)}, u32[]{:S(2)}) collective-permute-start(bf16[16,64,128]{2,1,0:T(8,128)(2,1)S(1)} %copy-done.3), channel_id=1, source_target_pairs={{0,20},{4,24},{8,28},{12,0},{16,4},{20,8},{24,12},{28,16},{1,21},{... | collective-permute-start | bytes 786440 | tf_op jit(solution)/shard_map/ppermute | solution.py:26
  56.0 2.8 %collective-permute-start.1 = (bf16[16,64,128]{2,1,0:T(8,128)(2,1)S(1)}, bf16[16,64,128]{2,1,0:T(8,128)(2,1)}, u32[]{:S(2)}, u32[]{:S(2)}) collective-permute-start(bf16[16,64,128]{2,1,0:T(8,128)(2,1)S(1)} %copy-done.3), channel_id=1, source_target_pairs={{0,24},{4,28},{8,0},{12,4},{16,8},{20,12},{24,16},{28,20},{1,25},{... | collective-permute-start | bytes 786440 | tf_op jit(solution)/shard_map/ppermute | solution.py:26
  58.9 6.8 %copy.50 = bf16[64,128,256]{1,2,0:T(8,128)(2,1)} copy(bf16[64,128,256]{2,1,0:T(8,128)(2,1)} %param.8) | data formatting | bytes 8388608 | tf_op args[2]
  65.7 4.4 %constant_dynamic-slice_fusion.8 = (bf16[64,128,1,64]{1,3,2,0:T(8,128)(2,1)}, bf16[64,128,1,64]{1,3,2,0:T(8,128)(2,1)}, bf16[64,128,1,64]{1,3,2,0:T(8,128)(2,1)}, bf16[64,128,1,64]{1,3,2,0:T(8,128)(2,1)S(1)}) fusion(bf16[64,128,4,64]{1,3,2,0:T(8,128)(2,1)} %bitcast.50, s32[]{:T(128)S(6)} %select_n.138, s32[]{:T(128)S(6)} %select_n.144, s32[]{:T(128)S(6)} %select_n.142, ...), kind=kLoop, calls=%fused_computation.45 | loop fusion | bytes 8388624 | tf_op jit(solution)/shard_map/jit(dynamic_index_in_dim)/dynamic_slice | solution.py:44
  70.8 3.0 %copy.64 = bf16[64,128,1,64]{1,0,3,2:T(8,128)(2,1)} copy(bf16[64,128,1,64]{1,3,2,0:T(8,128)(2,1)} %get-tuple-element.9) | data formatting | bytes 2097152 | tf_op jit(solution)/shard_map/jit(dynamic_index_in_dim)/dynamic_slice | solution.py:44
  73.7 2.9 %copy.61 = bf16[64,128,1,64]{1,0,3,2:T(8,128)(2,1)} copy(bf16[64,128,1,64]{1,3,2,0:T(8,128)(2,1)} %get-tuple-element.10) | data formatting | bytes 2097152 | tf_op jit(solution)/shard_map/jit(dynamic_index_in_dim)/dynamic_slice | solution.py:44
  80.0 15.3 %collective-permute-start.3 = (bf16[16,64,128]{2,1,0:T(8,128)(2,1)S(1)}, bf16[16,64,128]{2,1,0:T(8,128)(2,1)S(1)}, u32[]{:S(2)}, u32[]{:S(2)}) collective-permute-start(bf16[16,64,128]{2,1,0:T(8,128)(2,1)S(1)} %copy-done.3), channel_id=1, source_target_pairs={{0,16},{4,20},{8,24},{12,28},{16,0},{20,4},{24,8},{28,12},{1,17},{... | collective-permute-start | bytes 786440 | tf_op jit(solution)/shard_map/ppermute | solution.py:26
  103.6 2.8 %collective-permute-start.9 = (bf16[64,128,64]{1,0,2:T(8,128)(2,1)}, bf16[64,128,64]{1,0,2:T(8,128)(2,1)}, u32[]{:S(2)}, u32[]{:S(2)}) collective-permute-start(bf16[64,128,64]{1,0,2:T(8,128)(2,1)} %bitcast.54), channel_id=1, source_target_pairs={{0,12},{4,0},{8,4},{12,8},{16,28},{20,16},{24,20},{28,24},{1,13},{... | collective-permute-start | bytes 3145736 | tf_op jit(solution)/shard_map/ppermute | solution.py:51
  122.7 9.1 %copy.48 = bf16[64,8,4,16,64]{4,3,2,1,0:T(8,128)(2,1)} copy(bf16[64,8,4,16,64]{4,3,0,1,2:T(8,128)(2,1)} %bitcast.51) | data formatting | bytes 8388608 | tf_op jit(solution)/shard_map/transpose | solution.py:38
  131.8 10.1 %copy.49 = bf16[64,512,64]{1,0,2:T(8,128)(2,1)} copy(bf16[64,512,64]{2,1,0:T(8,128)(2,1)} %bitcast.49) | data formatting | bytes 8388608 | tf_op jit(solution)/shard_map/reshape | solution.py:38
  141.9 11.2 %collective-permute-done.9 = bf16[64,128,64]{1,0,2:T(8,128)(2,1)} collective-permute-done((bf16[64,128,64]{1,0,2:T(8,128)(2,1)}, bf16[64,128,64]{1,0,2:T(8,128)(2,1)}, u32[]{:S(2)}, u32[]{:S(2)}) %collective-permute-start.9) | collective-permute-done | bytes 1048608 | tf_op jit(solution)/shard_map/ppermute | solution.py:51
  153.2 24.5 %fusion.17 = f32[16,64,256]{2,1,0:T(8,128)} fusion(bf16[64,128,64]{1,0,2:T(8,128)(2,1)} %collective-permute-done.9, bf16[64,128,64]{1,0,2:T(8,128)(2,1)} %collective-permute-done.8, bf16[64,128,64]{1,0,2:T(8,128)(2,1)} %collective-permute-done.7, bf16[64,128,64]{1,0,2:T(8,128)(2,1)S(1)} %bitcast.53, bf16[64,512,64]{1,0,2:T(8,128)(2,1)} %copy.49, ...), kind=kOutput, calls=%fused_computation.15 | convolution fusion | flops 12910067712 | bytes 11534340 | tf_op jit(solution)/shard_map/padq,bdq->pab/dot_general | solution.py:59
  178.3 24.2 %reduce-scatter.2.cloned.1.call-done = f32[4,64,256]{2,1,0:T(8,128)} async-done(((f32[16,64,256]{2,1,0:T(8,128)}), f32[4,64,256]{2,1,0:T(8,128)}) %reduce-scatter.2.cloned.1.call-update) | async-done | bytes 262160 | tf_op jit(solution)/shard_map/reduce_scatter | solution.py:62
  204.6 2.8 %concatenate.15 = f32[4,64,8,64]{3,2,1,0:T(8,128)S(1)} concatenate(f32[4,64,1,64]{3,2,1,0:T(1,128)} %get-tuple-element.16, f32[4,64,1,64]{3,2,1,0:T(1,128)S(1)} %get-tuple-element.15, f32[4,64,1,64]{3,2,1,0:T(1,128)S(1)} %get-tuple-element.14, f32[4,64,1,64]{3,2,1,0:T(1,128)S(1)} %get-tuple-element.13, f32[4,64,1,64]{3,2,1,0:T(1,128)} %get-tuple-element.16, ...), dimensions={2} | concatenate | bytes 1048576 | tf_op jit(solution)/shard_map/concatenate | solution.py:65
  210.1 6.9 %collective-permute-start.13 = (f32[2,64,128]{2,1,0:T(8,128)S(1)}, f32[2,64,128]{2,1,0:T(8,128)S(1)}, u32[]{:S(2)}, u32[]{:S(2)}) collective-permute-start(f32[2,64,128]{2,1,0:T(8,128)S(1)} %bitcast.60), channel_id=1, source_target_pairs={{0,5},{1,13},{2,21},{3,29},{4,0},{5,8},{6,16},{7,24},{8,1},{9,9},{... | collective-permute-start | bytes 196616 | tf_op jit(solution)/shard_map/ppermute | solution.py:86
  216.9 1.9 collective-permute-start.11
  218.9 4.7 %collective-permute-start.12 = (f32[2,64,128]{2,1,0:T(8,128)S(1)}, f32[2,64,128]{2,1,0:T(8,128)S(1)}, u32[]{:S(2)}, u32[]{:S(2)}) collective-permute-start(f32[2,64,128]{2,1,0:T(8,128)S(1)} %bitcast.58), channel_id=1, source_target_pairs={{0,4},{1,12},{2,20},{3,28},{4,5},{5,13},{6,21},{7,29},{8,0},{9,8},... | collective-permute-start | bytes 196616 | tf_op jit(solution)/shard_map/ppermute | solution.py:86
  223.6 2.2 collective-permute-start.10
  226.0 2.1 collective-permute-done.11
  228.0 3.8 %collective-permute-done.10 = f32[2,64,128]{2,1,0:T(8,128)S(1)} collective-permute-done((f32[2,64,128]{2,1,0:T(8,128)S(1)}, f32[2,64,128]{2,1,0:T(8,128)S(1)}, u32[]{:S(2)}, u32[]{:S(2)}) %collective-permute-start.10) | collective-permute-done | bytes 65568 | tf_op jit(solution)/shard_map/ppermute | solution.py:86
  (70 shorter events, 41.2 us)
Async XLA Ops:
  6.5 1.6 copy-start
  6.5 116.1 %all-gather.3.cloned.1.call-start = ((), (), s32[]{:S(2)}) async-start(), calls=%async_computation.3 | async-start | bytes 10485760 | tf_op jit(solution)/shard_map/all_gather | solution.py:37
  17.3 34.9 %copy-start.3 = (bf16[16,64,128]{2,1,0:T(8,128)(2,1)S(1)}, bf16[16,64,128]{2,1,0:T(8,128)(2,1)}, u32[]{:S(2)}) copy-start(bf16[16,64,128]{2,1,0:T(8,128)(2,1)} %param.6) | copy-start | bytes 786436
  52.1 150.3 %reduce-scatter.2.cloned.1.call-start = ((), (), s32[]{:S(2)}) async-start(), calls=%async_computation.2 | async-start | bytes 1310720 | tf_op jit(solution)/shard_map/reduce_scatter | solution.py:62
  52.2 55.9 %collective-permute-start.5 = (bf16[16,64,128]{2,1,0:T(8,128)(2,1)S(1)}, bf16[16,64,128]{2,1,0:T(8,128)(2,1)}, u32[]{:S(2)}, u32[]{:S(2)}) collective-permute-start(bf16[16,64,128]{2,1,0:T(8,128)(2,1)S(1)} %copy-done.3), channel_id=1, source_target_pairs={{0,8},{4,12},{8,16},{12,20},{16,24},{20,28},{24,0},{28,4},{1,9},{5... | collective-permute-start | bytes 786440 | tf_op jit(solution)/shard_map/ppermute | solution.py:26
  52.7 50.8 %collective-permute-start.4 = (bf16[16,64,128]{2,1,0:T(8,128)(2,1)S(1)}, bf16[16,64,128]{2,1,0:T(8,128)(2,1)}, u32[]{:S(2)}, u32[]{:S(2)}) collective-permute-start(bf16[16,64,128]{2,1,0:T(8,128)(2,1)S(1)} %copy-done.3), channel_id=1, source_target_pairs={{0,12},{4,16},{8,20},{12,24},{16,28},{20,0},{24,4},{28,8},{1,13},{... | collective-permute-start | bytes 786440 | tf_op jit(solution)/shard_map/ppermute | solution.py:26
  53.2 45.6 %collective-permute-start.2 = (bf16[16,64,128]{2,1,0:T(8,128)(2,1)S(1)}, bf16[16,64,128]{2,1,0:T(8,128)(2,1)}, u32[]{:S(2)}, u32[]{:S(2)}) collective-permute-start(bf16[16,64,128]{2,1,0:T(8,128)(2,1)S(1)} %copy-done.3), channel_id=1, source_target_pairs={{0,20},{4,24},{8,28},{12,0},{16,4},{20,8},{24,12},{28,16},{1,21},{... | collective-permute-start | bytes 786440 | tf_op jit(solution)/shard_map/ppermute | solution.py:26
  56.0 41.1 %collective-permute-start.1 = (bf16[16,64,128]{2,1,0:T(8,128)(2,1)S(1)}, bf16[16,64,128]{2,1,0:T(8,128)(2,1)}, u32[]{:S(2)}, u32[]{:S(2)}) collective-permute-start(bf16[16,64,128]{2,1,0:T(8,128)(2,1)S(1)} %copy-done.3), channel_id=1, source_target_pairs={{0,24},{4,28},{8,0},{12,4},{16,8},{20,12},{24,16},{28,20},{1,25},{... | collective-permute-start | bytes 786440 | tf_op jit(solution)/shard_map/ppermute | solution.py:26
  58.8 21.3 %collective-permute-start = (bf16[16,64,128]{2,1,0:T(8,128)(2,1)S(1)}, bf16[16,64,128]{2,1,0:T(8,128)(2,1)}, u32[]{:S(2)}, u32[]{:S(2)}) collective-permute-start(bf16[16,64,128]{2,1,0:T(8,128)(2,1)S(1)} %copy-done.3), channel_id=1, source_target_pairs={{0,28},{4,0},{8,4},{12,8},{16,12},{20,16},{24,20},{28,24},{1,29},{... | collective-permute-start | bytes 786440 | tf_op jit(solution)/shard_map/ppermute | solution.py:26
  70.8 5.9 %copy-start.1 = (bf16[64,128,1,64]{1,3,2,0:T(8,128)(2,1)S(1)}, bf16[64,128,1,64]{1,3,2,0:T(8,128)(2,1)}, u32[]{:S(2)}) copy-start(bf16[64,128,1,64]{1,3,2,0:T(8,128)(2,1)} %get-tuple-element.11) | copy-start | bytes 3145732
  80.0 21.5 %collective-permute-start.3 = (bf16[16,64,128]{2,1,0:T(8,128)(2,1)S(1)}, bf16[16,64,128]{2,1,0:T(8,128)(2,1)S(1)}, u32[]{:S(2)}, u32[]{:S(2)}) collective-permute-start(bf16[16,64,128]{2,1,0:T(8,128)(2,1)S(1)} %copy-done.3), channel_id=1, source_target_pairs={{0,16},{4,20},{8,24},{12,28},{16,0},{20,4},{24,8},{28,12},{1,17},{... | collective-permute-start | bytes 786440 | tf_op jit(solution)/shard_map/ppermute | solution.py:26
  97.1 13.9 %collective-permute-start.6 = (bf16[16,64,128]{2,1,0:T(8,128)(2,1)S(1)}, bf16[16,64,128]{2,1,0:T(8,128)(2,1)S(1)}, u32[]{:S(2)}, u32[]{:S(2)}) collective-permute-start(bf16[16,64,128]{2,1,0:T(8,128)(2,1)S(1)} %copy-done.3), channel_id=1, source_target_pairs={{0,4},{4,8},{8,12},{12,16},{16,20},{20,24},{24,28},{28,0},{1,5},{5... | collective-permute-start | bytes 786440 | tf_op jit(solution)/shard_map/ppermute | solution.py:26
  98.8 43.1 %collective-permute-start.7 = (bf16[64,128,64]{1,0,2:T(8,128)(2,1)}, bf16[64,128,64]{1,0,2:T(8,128)(2,1)}, u32[]{:S(2)}, u32[]{:S(2)}) collective-permute-start(bf16[64,128,64]{1,0,2:T(8,128)(2,1)} %bitcast.56), channel_id=1, source_target_pairs={{0,4},{4,8},{8,12},{12,0},{16,20},{20,24},{24,28},{28,16},{1,5},{5... | collective-permute-start | bytes 3145736 | tf_op jit(solution)/shard_map/ppermute | solution.py:51
  101.6 40.4 %collective-permute-start.8 = (bf16[64,128,64]{1,0,2:T(8,128)(2,1)}, bf16[64,128,64]{1,0,2:T(8,128)(2,1)}, u32[]{:S(2)}, u32[]{:S(2)}) collective-permute-start(bf16[64,128,64]{1,0,2:T(8,128)(2,1)} %bitcast.55), channel_id=1, source_target_pairs={{0,8},{4,12},{8,0},{12,4},{16,24},{20,28},{24,16},{28,20},{1,9},{5... | collective-permute-start | bytes 3145736 | tf_op jit(solution)/shard_map/ppermute | solution.py:51
  103.6 49.6 %collective-permute-start.9 = (bf16[64,128,64]{1,0,2:T(8,128)(2,1)}, bf16[64,128,64]{1,0,2:T(8,128)(2,1)}, u32[]{:S(2)}, u32[]{:S(2)}) collective-permute-start(bf16[64,128,64]{1,0,2:T(8,128)(2,1)} %bitcast.54), channel_id=1, source_target_pairs={{0,12},{4,0},{8,4},{12,8},{16,28},{20,16},{24,20},{28,24},{1,13},{... | collective-permute-start | bytes 3145736 | tf_op jit(solution)/shard_map/ppermute | solution.py:51
  131.8 21.4 %copy-start.2 = (bf16[64,128,1,64]{1,0,3,2:T(8,128)(2,1)S(1)}, bf16[64,128,1,64]{1,0,3,2:T(8,128)(2,1)}, u32[]{:S(2)}) copy-start(bf16[64,128,1,64]{1,0,3,2:T(8,128)(2,1)} %copy.64) | copy-start | bytes 3145732
  153.2 24.7 %copy-start.4 = (s32[2,2]{1,0:T(2,128)S(1)}, s32[2,2]{1,0:T(2,128)}, u32[]{:S(2)}) copy-start(s32[2,2]{1,0:T(2,128)} %param.9) | copy-start | bytes 52
  153.2 24.9 %copy-start.5 = (f32[128]{0:T(128)S(1)}, f32[128]{0:T(128)}, u32[]{:S(2)}) copy-start(f32[128]{0:T(128)} %param.10) | copy-start | bytes 1540
  177.6 48.2 %slice-start = ((f32[512]{0:T(512)}), f32[64]{0:T(128)S(1)}, s32[]{:S(2)}) async-start(f32[512]{0:T(512)} %param.11), calls=%async_computation.4 | async-start | bytes 1024 | tf_op jit(solution)/shard_map/slice | solution.py:98
  177.6 48.3 %copy-start.6 = (f32[512]{0:T(512)S(1)}, f32[512]{0:T(512)}, u32[]{:S(2)}) copy-start(f32[512]{0:T(512)} %param.11) | copy-start | bytes 6148
  210.1 15.9 %collective-permute-start.13 = (f32[2,64,128]{2,1,0:T(8,128)S(1)}, f32[2,64,128]{2,1,0:T(8,128)S(1)}, u32[]{:S(2)}, u32[]{:S(2)}) collective-permute-start(f32[2,64,128]{2,1,0:T(8,128)S(1)} %bitcast.60), channel_id=1, source_target_pairs={{0,5},{1,13},{2,21},{3,29},{4,0},{5,8},{6,16},{7,24},{8,1},{9,9},{... | collective-permute-start | bytes 196616 | tf_op jit(solution)/shard_map/ppermute | solution.py:86
  216.9 11.1 %collective-permute-start.11 = (f32[2,64,128]{2,1,0:T(8,128)S(1)}, f32[2,64,128]{2,1,0:T(8,128)S(1)}, u32[]{:S(2)}, u32[]{:S(2)}) collective-permute-start(f32[2,64,128]{2,1,0:T(8,128)S(1)} %bitcast.59), channel_id=1, source_target_pairs={{0,1},{1,9},{2,17},{3,25},{4,4},{5,12},{6,20},{7,28},{8,5},{9,13},... | collective-permute-start | bytes 196616 | tf_op jit(solution)/shard_map/ppermute | solution.py:86
  218.9 9.2 %collective-permute-start.12 = (f32[2,64,128]{2,1,0:T(8,128)S(1)}, f32[2,64,128]{2,1,0:T(8,128)S(1)}, u32[]{:S(2)}, u32[]{:S(2)}) collective-permute-start(f32[2,64,128]{2,1,0:T(8,128)S(1)} %bitcast.58), channel_id=1, source_target_pairs={{0,4},{1,12},{2,20},{3,28},{4,5},{5,13},{6,21},{7,29},{8,0},{9,8},... | collective-permute-start | bytes 196616 | tf_op jit(solution)/shard_map/ppermute | solution.py:86
  223.6 8.3 %collective-permute-start.10 = (f32[2,64,128]{2,1,0:T(8,128)S(1)}, f32[2,64,128]{2,1,0:T(8,128)S(1)}, u32[]{:S(2)}, u32[]{:S(2)}) collective-permute-start(f32[2,64,128]{2,1,0:T(8,128)S(1)} %bitcast.57), channel_id=1, source_target_pairs={{0,0},{1,8},{2,16},{3,24},{4,1},{5,9},{6,17},{7,25},{8,4},{9,12},{... | collective-permute-start | bytes 196616 | tf_op jit(solution)/shard_map/ppermute | solution.py:86
Sparse Core Ops, SparseCore 0:
  52.3 57.6 all-gather.2
  177.8 24.6 reduce-scatter.1

commit v6 on v2

--- a/solution.py
+++ b/solution.py
@@ -25,8 +25,18 @@
         c_sub = c_blk // n_wide
         left_part = lax.dynamic_slice_in_dim(left_fit, w * c_sub, c_sub, 1)
         left_part = left_part.reshape(rows, c_sub, span, q_blk).transpose(2, 0, 1, 3)
-        left_send = jnp.concatenate([left_part] * GROUPS, axis=0)
-        left_recv = lax.all_to_all(left_send, "narrow", 0, 0, tiled=True)
+        left_blocks = []
+        for shift in range(n_narrow):
+            dest = ((n + shift) % n_narrow) % span
+            piece = lax.dynamic_index_in_dim(left_part, dest, 0, keepdims=True)
+            if shift:
+                perm = [(i, (i + shift) % n_narrow) for i in range(n_narrow)]
+                piece = lax.ppermute(piece, "narrow", perm)
+            left_blocks.append(piece)
+        left_rev = [left_blocks[(n_narrow - j) % n_narrow] for j in range(n_narrow)]
+        left_recv = lax.dynamic_slice_in_dim(
+            jnp.concatenate(left_rev * 2, axis=0), n_narrow - n, n_narrow, 0
+        )
         left_all = lax.all_gather(left_recv, "wide", axis=0, tiled=False)
         left_all = left_all.transpose(2, 1, 0, 3, 4).reshape(rows, c_blk * n_narrow, q_blk)
 

time: 247 us -> 276 us (1.12)
  blocking collectives: 30.3 us -> 0 us
  waiting for transfers between devices: 99.8 us -> 128 us
  local copies, waits for them, and re-layouts: 56.7 us -> 81.4 us
  starting transfers between devices: 18.6 us -> 27.1 us
    all_to_all x1 -> x0, blocking collectives: 30.3 us -> none  [body(): left_recv = lax.all_to_all(left_send, 'narrow', 0, 0, tiled=True)]
    ppermute x3 -> x10, waiting for transfers between devices: 0.01 us -> 29.3 us  [body(): piece = lax.ppermute(piece, 'narrow', perm)]
    unnamed x11 -> x37, local copies, waits for them, and re-layouts: 15.7 us -> 32.7 us
    transpose x1 -> x0, local copies, waits for them, and re-layouts: 9.12 us -> none  [body(): left_all.transpose(2, 1, 0, 3, 4).reshape(rows, c_blk * n_narrow, q_blk)]
    all_gather x0 -> x1, local copies, waits for them, and re-layouts: none -> 9.1 us  [body(): left_all = lax.all_gather(left_recv, 'wide', axis=0, tiled=False)]
    ppermute x3 -> x10, starting transfers between devices: 2.78 us -> 11.5 us  [body(): piece = lax.ppermute(piece, 'narrow', perm)]
    another operation x0 -> x1, local copies, waits for them, and re-layouts: none -> 5.35 us
    dynamic_slice x0 -> x1, local copies, waits for them, and re-layouts: none -> 3.27 us  [body(): lax.dynamic_slice_in_dim(jnp.concatenate(left_rev * 2, axis=0), n_narrow...]
  transfers between devices with their start and end apart: 10 -> 17, of which waited for: 5 -> 8; matrix products, arithmetic and copies ran while one was open for 15% -> 18% of each run, Pallas kernels for 0% -> 0%
where the time goes in v6:
time: 276 us; the launch traced here: 275 us
  waiting for transfers between devices  128 us (46%)
  local copies, waits for them, and re-layouts  81.4 us (29%)
  starting transfers between devices  27.1 us (10%)
  matrix products  24.5 us (9%)
  between operations  13.5 us (5%)
    all_gather x1, waiting for transfers between devices, body(): left_all = lax.all_gather(left_recv, 'wide', axis=0, tiled=False)  36.7 us
    unnamed x37, local copies, waits for them, and re-layouts  32.7 us
    all_gather x1, waiting for transfers between devices, body(): amps_all = lax.all_gather(amps, 'narrow', axis=1, tiled=True)  31.9 us
    ppermute x10, waiting for transfers between devices, body(): piece = lax.ppermute(piece, 'narrow', perm)  29.3 us
    dot_general x1, matrix products, body(): jnp.einsum('padq,bdq->pab', inter, right_group, preferred_element_type=jn...  24.5 us
    reduce_scatter x1, waiting for transfers between devices, body(): part = lax.psum_scatter(part, 'wide', scatter_dimension=0, tiled=True)  23 us
    ppermute x4, starting transfers between devices, body(): piece = lax.ppermute(piece, ('narrow', 'wide'), perm)  15.5 us
    ppermute x10, starting transfers between devices, body(): piece = lax.ppermute(piece, 'narrow', perm)  11.5 us
  transfers between devices with their start and end apart: 17, of which 8 were waited for; matrix products, arithmetic and copies ran while one was open for 18% of the time, Pallas kernels for 0%

profile of v6, /device:TPU:5, one launch (start us, length us, event | category | flops | bytes accessed | tf_op | source)
XLA Modules:
  0.0 275.2 jit_solution(6967259460889001470)
XLA Ops:
  9.0 2.0 reshape.69
  11.1 5.4 %constant_dynamic-slice_fusion.10 = (bf16[64,16,1,64]{3,2,1,0:T(2,128)(2,1)}, bf16[64,16,1,64]{3,2,1,0:T(2,128)(2,1)}, bf16[64,16,1,64]{3,2,1,0:T(2,128)(2,1)S(1...) fusion(bf16[64,16,4,64]{3,2,1,0:T(4,128)(2,1)S(1)} %reshape.69,, ...), kind=kLoop, calls=%fused_computation.52 | loop fusion | bytes 2097184 | tf_op jit(solution)/shard_map/dynamic-slice.7
  17.2 4.2 %collective-permute-start = (bf16[1,64,16,64]{3,2,1,0:T(8,128)(2,1)}, bf16[1,64,16,64]{3,2,1,0:T(8,128)(2,1)S(1)}, u32[]{:S(2)}, u32[]{:S(2)}) collective-permute-start(bf16[1,64,16,64]{3,2,1,0:T(8,128)(2,1)} %bitcast.71), channel_id=1, source_target_pairs={{0,28},{4,0},{8,4},{12,8},{16,12},{20,16},{24,20},{28,24},{1,29},{... | collective-permute-start | bytes 393224 | tf_op jit(solution)/shard_map/ppermute | solution.py:34
  23.8 2.4 collective-permute-start.3
  27.8 1.8 copy.66
  35.1 3.0 %collective-permute-done.2 = bf16[1,64,16,64]{3,2,1,0:T(8,128)(2,1)} collective-permute-done((bf16[1,64,16,64]{3,2,1,0:T(8,128)(2,1)}, bf16[1,64,16,64]{3,2,1,0:T(8,128)(2,1)}, u32[]{:S(2)}, u32[]{:S(2)}) %collective-permute-start.2) | collective-permute-done | bytes 131104 | tf_op jit(solution)/shard_map/ppermute | solution.py:34
  39.7 26.2 %collective-permute-done.3 = bf16[1,64,16,64]{3,2,1,0:T(8,128)(2,1)} collective-permute-done((bf16[1,64,16,64]{3,2,1,0:T(8,128)(2,1)}, bf16[1,64,16,64]{3,2,1,0:T(8,128)(2,1)}, u32[]{:S(2)}, u32[]{:S(2)}) %collective-permute-start.3) | collective-permute-done | bytes 131104 | tf_op jit(solution)/shard_map/ppermute | solution.py:34
  80.2 3.3 %constant_dynamic-slice_fusion.9 = bf16[8,64,16,64]{3,2,1,0:T(8,128)(2,1)} fusion(bf16[16,64,16,64]{3,2,1,0:T(8,128)(2,1)} %constant_dynamic-update-slice_fusion, s32[]{:T(128)S(6)} %select_n.248), kind=kLoop, calls=%fused_computation.51 | loop fusion | bytes 2097156 | tf_op jit(solution)/shard_map/dynamic_slice | solution.py:37
  84.4 6.5 %copy.33 = bf16[64,128,256]{1,2,0:T(8,128)(2,1)} copy(bf16[64,128,256]{2,1,0:T(8,128)(2,1)} %param.8) | data formatting | bytes 8388608 | tf_op args[2]
  90.9 3.7 %constant_dynamic-slice_fusion.8 = (bf16[64,128,1,64]{1,3,2,0:T(8,128)(2,1)S(1)}, bf16[64,128,1,64]{1,3,2,0:T(8,128)(2,1)S(1)}, bf16[64,128,1,64]{1,3,2,0:T(8,128)(2,1)S(1)}, bf16[64,128,1,64]{1,3,2,0:T(8,128)(2,1)S(1)}) fusion(bf16[64,128,4,64]{1,3,2,0:T(8,128)(2,1)} %bitcast.73, s32[]{:T(128)S(6)} %select_n.251, s32[]{:T(128)S(6)} %select_n.257, ...), kind=kLoop, calls=%fused_computation.50 | loop fusion | bytes 8388624 | tf_op jit(solution)/shard_map/jit(dynamic_index_in_dim)/dynamic_slice | solution.py:47
  99.6 2.4 collective-permute-start.9
  102.7 36.7 %all-gather.6.cloned.1.call-done = bf16[32,64,16,64]{3,2,1,0:T(8,128)(2,1)} async-done(((bf16[8,64,16,64]{3,2,1,0:T(8,128)(2,1)}), bf16[32,64,16,64]{3,2,1,0:T(8,128)(2,1)}) %all-gather.6.cloned.1.call-update) | async-done | bytes 4194320 | tf_op jit(solution)/shard_map/all_gather | solution.py:40
  139.3 9.1 %copy.31 = bf16[4,8,64,16,64]{4,3,0,1,2:T(8,128)(2,1)} copy(bf16[4,8,64,16,64]{4,3,2,1,0:T(8,128)(2,1)} %bitcast.74) | data formatting | bytes 8388608 | tf_op jit(solution)/shard_map/all_gather | solution.py:40
  148.4 10.1 %copy.32 = bf16[64,512,64]{1,0,2:T(8,128)(2,1)} copy(bf16[64,512,64]{2,1,0:T(8,128)(2,1)} %bitcast.72) | data formatting | bytes 8388608 | tf_op jit(solution)/shard_map/reshape | solution.py:41
  158.6 31.9 %all-gather.4.cloned.1.call-done = bf16[16,512,128]{2,1,0:T(8,128)(2,1)} async-done(((bf16[16,64,128]{2,1,0:T(8,128)(2,1)}), bf16[16,512,128]{2,1,0:T(8,128)(2,1)}) %all-gather.4.cloned.1.call-update) | async-done | bytes 2097168 | tf_op jit(solution)/shard_map/all_gather | solution.py:23
  190.5 24.5 %fusion.15 = f32[16,64,256]{2,1,0:T(8,128)} fusion(bf16[64,128,64]{1,0,2:T(8,128)(2,1)} %collective-permute-done.9, bf16[64,128,64]{1,0,2:T(8,128)(2,1)} %collective-permute-done.8, bf16[64,128,64]{1,0,2:T(8,128)(2,1)} %collective-permute-done.7, bf16[64,128,64]{1,0,2:T(8,128)(2,1)S(1)} %bitcast.75, bf16[64,512,64]{1,0,2:T(8,128)(2,1)} %copy.32, ...), kind=kOutput, calls=%fused_computation.13 | convolution fusion | flops 12910067712 | bytes 11534336 | tf_op jit(solution)/shard_map/padq,bdq->pab/dot_general | solution.py:62
  215.6 23.0 %reduce-scatter.2.cloned.1.call-done = f32[4,64,256]{2,1,0:T(8,128)} async-done(((f32[16,64,256]{2,1,0:T(8,128)}), f32[4,64,256]{2,1,0:T(8,128)}) %reduce-scatter.2.cloned.1.call-update) | async-done | bytes 262160 | tf_op jit(solution)/shard_map/reduce_scatter | solution.py:65
  240.8 2.8 %concatenate.11 = f32[4,64,8,64]{3,2,1,0:T(8,128)S(1)} concatenate(f32[4,64,1,64]{3,2,1,0:T(1,128)} %get-tuple-element.24, f32[4,64,1,64]{3,2,1,0:T(1,128)S(1)} %get-tuple-element.23, f32[4,64,1,64]{3,2,1,0:T(1,128)S(1)} %get-tuple-element.22, f32[4,64,1,64]{3,2,1,0:T(1,128)S(1)} %get-tuple-element.21, f32[4,64,1,64]{3,2,1,0:T(1,128)} %get-tuple-element.24, ...), dimensions={2} | concatenate | bytes 1048576 | tf_op jit(solution)/shard_map/concatenate | solution.py:68
  246.3 6.5 %collective-permute-start.10 = (f32[2,64,128]{2,1,0:T(8,128)S(1)}, f32[2,64,128]{2,1,0:T(8,128)S(1)}, u32[]{:S(2)}, u32[]{:S(2)}) collective-permute-start(f32[2,64,128]{2,1,0:T(8,128)S(1)} %bitcast.81), channel_id=1, source_target_pairs={{0,0},{1,8},{2,16},{3,24},{4,1},{5,9},{6,17},{7,25},{8,4},{9,12},{... | collective-permute-start | bytes 196616 | tf_op jit(solution)/shard_map/ppermute | solution.py:89
  252.8 3.0 %collective-permute-start.11 = (f32[2,64,128]{2,1,0:T(8,128)S(1)}, f32[2,64,128]{2,1,0:T(8,128)S(1)}, u32[]{:S(2)}, u32[]{:S(2)}) collective-permute-start(f32[2,64,128]{2,1,0:T(8,128)S(1)} %bitcast.80), channel_id=1, source_target_pairs={{0,1},{1,9},{2,17},{3,25},{4,4},{5,12},{6,20},{7,28},{8,5},{9,13},... | collective-permute-start | bytes 196616 | tf_op jit(solution)/shard_map/ppermute | solution.py:89
  255.8 3.6 %collective-permute-start.12 = (f32[2,64,128]{2,1,0:T(8,128)S(1)}, f32[2,64,128]{2,1,0:T(8,128)S(1)}, u32[]{:S(2)}, u32[]{:S(2)}) collective-permute-start(f32[2,64,128]{2,1,0:T(8,128)S(1)} %bitcast.79), channel_id=1, source_target_pairs={{0,4},{1,12},{2,20},{3,28},{4,5},{5,13},{6,21},{7,29},{8,0},{9,8},... | collective-permute-start | bytes 196616 | tf_op jit(solution)/shard_map/ppermute | solution.py:89
  259.4 2.3 collective-permute-start.13
  261.9 1.9 collective-permute-done.11
  263.8 4.1 %collective-permute-done.13 = f32[2,64,128]{2,1,0:T(8,128)S(1)} collective-permute-done((f32[2,64,128]{2,1,0:T(8,128)S(1)}, f32[2,64,128]{2,1,0:T(8,128)S(1)}, u32[]{:S(2)}, u32[]{:S(2)}) %collective-permute-start.13) | collective-permute-done | bytes 65568 | tf_op jit(solution)/shard_map/ppermute | solution.py:89
  (77 shorter events, 41.1 us)
Async XLA Ops:
  6.5 132.8 %all-gather.6.cloned.1.call-start = ((), (), s32[]{:S(2)}) async-start(), calls=%async_computation.3 | async-start | bytes 10485760 | tf_op jit(solution)/shard_map/all_gather | solution.py:40
  16.4 10.6 %copy-start.1 = (bf16[64,16,1,64]{3,2,1,0:T(2,128)(2,1)}, bf16[64,16,1,64]{3,2,1,0:T(2,128)(2,1)S(1)}, u32[]{:S(2)}) copy-start(bf16[64,16,1,64]{3,2,1,0:T(2,128)(2,1)S(1)} %get-tuple-element.20) | copy-start | bytes 393220
  16.4 13.2 %copy-start.3 = (bf16[64,16,1,64]{3,2,1,0:T(2,128)(2,1)S(1)}, bf16[64,16,1,64]{3,2,1,0:T(2,128)(2,1)}, u32[]{:S(2)}) copy-start(bf16[64,16,1,64]{3,2,1,0:T(2,128)(2,1)} %get-tuple-element.13) | copy-start | bytes 393220
  17.2 13.2 %collective-permute-start = (bf16[1,64,16,64]{3,2,1,0:T(8,128)(2,1)}, bf16[1,64,16,64]{3,2,1,0:T(8,128)(2,1)S(1)}, u32[]{:S(2)}, u32[]{:S(2)}) collective-permute-start(bf16[1,64,16,64]{3,2,1,0:T(8,128)(2,1)} %bitcast.71), channel_id=1, source_target_pairs={{0,28},{4,0},{8,4},{12,8},{16,12},{20,16},{24,20},{28,24},{1,29},{... | collective-permute-start | bytes 393224 | tf_op jit(solution)/shard_map/ppermute | solution.py:34
  22.2 10.2 %collective-permute-start.1 = (bf16[1,64,16,64]{3,2,1,0:T(8,128)(2,1)}, bf16[1,64,16,64]{3,2,1,0:T(8,128)(2,1)}, u32[]{:S(2)}, u32[]{:S(2)}) collective-permute-start(bf16[1,64,16,64]{3,2,1,0:T(8,128)(2,1)} %bitcast.70), channel_id=1, source_target_pairs={{0,24},{4,28},{8,0},{12,4},{16,8},{20,12},{24,16},{28,20},{1,25},{... | collective-permute-start | bytes 393224 | tf_op jit(solution)/shard_map/ppermute | solution.py:34
  23.1 15.0 %collective-permute-start.2 = (bf16[1,64,16,64]{3,2,1,0:T(8,128)(2,1)}, bf16[1,64,16,64]{3,2,1,0:T(8,128)(2,1)}, u32[]{:S(2)}, u32[]{:S(2)}) collective-permute-start(bf16[1,64,16,64]{3,2,1,0:T(8,128)(2,1)} %bitcast.69), channel_id=1, source_target_pairs={{0,20},{4,24},{8,28},{12,0},{16,4},{20,8},{24,12},{28,16},{1,21},{... | collective-permute-start | bytes 393224 | tf_op jit(solution)/shard_map/ppermute | solution.py:34
  23.8 42.1 %collective-permute-start.3 = (bf16[1,64,16,64]{3,2,1,0:T(8,128)(2,1)}, bf16[1,64,16,64]{3,2,1,0:T(8,128)(2,1)}, u32[]{:S(2)}, u32[]{:S(2)}) collective-permute-start(bf16[1,64,16,64]{3,2,1,0:T(8,128)(2,1)} %bitcast.68), channel_id=1, source_target_pairs={{0,16},{4,20},{8,24},{12,28},{16,0},{20,4},{24,8},{28,12},{1,17},{... | collective-permute-start | bytes 393224 | tf_op jit(solution)/shard_map/ppermute | solution.py:34
  27.0 40.6 %collective-permute-start.4 = (bf16[1,64,16,64]{3,2,1,0:T(8,128)(2,1)}, bf16[1,64,16,64]{3,2,1,0:T(8,128)(2,1)}, u32[]{:S(2)}, u32[]{:S(2)}) collective-permute-start(bf16[1,64,16,64]{3,2,1,0:T(8,128)(2,1)} %bitcast.67), channel_id=1, source_target_pairs={{0,12},{4,16},{8,20},{12,24},{16,28},{20,0},{24,4},{28,8},{1,13},{... | collective-permute-start | bytes 393224 | tf_op jit(solution)/shard_map/ppermute | solution.py:34
  27.8 42.9 %copy-start.2 = (bf16[64,16,1,64]{3,2,1,0:T(2,128)(2,1)S(1)}, bf16[64,16,1,64]{3,2,1,0:T(2,128)(2,1)}, u32[]{:S(2)}) copy-start(bf16[64,16,1,64]{3,2,1,0:T(2,128)(2,1)} %copy-done.1) | copy-start | bytes 393220
  30.3 38.9 %collective-permute-start.5 = (bf16[1,64,16,64]{3,2,1,0:T(8,128)(2,1)}, bf16[1,64,16,64]{3,2,1,0:T(8,128)(2,1)S(1)}, u32[]{:S(2)}, u32[]{:S(2)}) collective-permute-start(bf16[1,64,16,64]{3,2,1,0:T(8,128)(2,1)} %bitcast.77), channel_id=1, source_target_pairs={{0,8},{4,12},{8,16},{12,20},{16,24},{20,28},{24,0},{28,4},{1,9},{5... | collective-permute-start | bytes 393224 | tf_op jit(solution)/shard_map/ppermute | solution.py:34
  32.4 37.6 %collective-permute-start.6 = (bf16[1,64,16,64]{3,2,1,0:T(8,128)(2,1)}, bf16[1,64,16,64]{3,2,1,0:T(8,128)(2,1)S(1)}, u32[]{:S(2)}, u32[]{:S(2)}) collective-permute-start(bf16[1,64,16,64]{3,2,1,0:T(8,128)(2,1)} %bitcast.76), channel_id=1, source_target_pairs={{0,4},{4,8},{8,12},{12,16},{16,20},{20,24},{24,28},{28,0},{1,5},{5... | collective-permute-start | bytes 393224 | tf_op jit(solution)/shard_map/ppermute | solution.py:34
  83.5 106.9 %all-gather.4.cloned.1.call-start = ((), (), s32[]{:S(2)}) async-start(), calls=%async_computation.1 | async-start | bytes 2359296 | tf_op jit(solution)/shard_map/all_gather | solution.py:23
  84.3 154.4 %reduce-scatter.2.cloned.1.call-start = ((), (), s32[]{:S(2)}) async-start(), calls=%async_computation.2 | async-start | bytes 1310720 | tf_op jit(solution)/shard_map/reduce_scatter | solution.py:65
  96.2 62.3 %collective-permute-start.7 = (bf16[64,128,64]{1,0,2:T(8,128)(2,1)}, bf16[64,128,64]{1,0,2:T(8,128)(2,1)}, u32[]{:S(2)}, u32[]{:S(2)}) collective-permute-start(bf16[64,128,64]{1,0,2:T(8,128)(2,1)} %bitcast.63), channel_id=1, source_target_pairs={{0,4},{4,8},{8,12},{12,0},{16,20},{20,24},{24,28},{28,16},{1,5},{5... | collective-permute-start | bytes 3145736 | tf_op jit(solution)/shard_map/ppermute | solution.py:54
  97.9 60.7 %collective-permute-start.8 = (bf16[64,128,64]{1,0,2:T(8,128)(2,1)}, bf16[64,128,64]{1,0,2:T(8,128)(2,1)}, u32[]{:S(2)}, u32[]{:S(2)}) collective-permute-start(bf16[64,128,64]{1,0,2:T(8,128)(2,1)} %bitcast.62), channel_id=1, source_target_pairs={{0,8},{4,12},{8,0},{12,4},{16,24},{20,28},{24,16},{28,20},{1,9},{5... | collective-permute-start | bytes 3145736 | tf_op jit(solution)/shard_map/ppermute | solution.py:54
  99.6 59.0 %collective-permute-start.9 = (bf16[64,128,64]{1,0,2:T(8,128)(2,1)}, bf16[64,128,64]{1,0,2:T(8,128)(2,1)}, u32[]{:S(2)}, u32[]{:S(2)}) collective-permute-start(bf16[64,128,64]{1,0,2:T(8,128)(2,1)} %bitcast.61), channel_id=1, source_target_pairs={{0,12},{4,0},{8,4},{12,8},{16,28},{20,16},{24,20},{28,24},{1,13},{... | collective-permute-start | bytes 3145736 | tf_op jit(solution)/shard_map/ppermute | solution.py:54
  190.5 24.8 %copy-start.4 = (s32[2,2]{1,0:T(2,128)S(1)}, s32[2,2]{1,0:T(2,128)}, u32[]{:S(2)}) copy-start(s32[2,2]{1,0:T(2,128)} %param.9) | copy-start | bytes 52
  190.5 25.0 %copy-start.5 = (f32[128]{0:T(128)S(1)}, f32[128]{0:T(128)}, u32[]{:S(2)}) copy-start(f32[128]{0:T(128)} %param.10) | copy-start | bytes 1540
  215.0 46.7 %slice-start = ((f32[512]{0:T(512)}), f32[64]{0:T(128)S(1)}, s32[]{:S(2)}) async-start(f32[512]{0:T(512)} %param.11), calls=%async_computation.4 | async-start | bytes 1024 | tf_op jit(solution)/shard_map/slice | solution.py:101
  215.0 46.8 %copy-start.6 = (f32[512]{0:T(512)S(1)}, f32[512]{0:T(512)}, u32[]{:S(2)}) copy-start(f32[512]{0:T(512)} %param.11) | copy-start | bytes 6148
  246.3 15.6 %collective-permute-start.10 = (f32[2,64,128]{2,1,0:T(8,128)S(1)}, f32[2,64,128]{2,1,0:T(8,128)S(1)}, u32[]{:S(2)}, u32[]{:S(2)}) collective-permute-start(f32[2,64,128]{2,1,0:T(8,128)S(1)} %bitcast.81), channel_id=1, source_target_pairs={{0,0},{1,8},{2,16},{3,24},{4,1},{5,9},{6,17},{7,25},{8,4},{9,12},{... | collective-permute-start | bytes 196616 | tf_op jit(solution)/shard_map/ppermute | solution.py:89
  252.8 11.1 %collective-permute-start.11 = (f32[2,64,128]{2,1,0:T(8,128)S(1)}, f32[2,64,128]{2,1,0:T(8,128)S(1)}, u32[]{:S(2)}, u32[]{:S(2)}) collective-permute-start(f32[2,64,128]{2,1,0:T(8,128)S(1)} %bitcast.80), channel_id=1, source_target_pairs={{0,1},{1,9},{2,17},{3,25},{4,4},{5,12},{6,20},{7,28},{8,5},{9,13},... | collective-permute-start | bytes 196616 | tf_op jit(solution)/shard_map/ppermute | solution.py:89
  255.8 8.0 %collective-permute-start.12 = (f32[2,64,128]{2,1,0:T(8,128)S(1)}, f32[2,64,128]{2,1,0:T(8,128)S(1)}, u32[]{:S(2)}, u32[]{:S(2)}) collective-permute-start(f32[2,64,128]{2,1,0:T(8,128)S(1)} %bitcast.79), channel_id=1, source_target_pairs={{0,4},{1,12},{2,20},{3,28},{4,5},{5,13},{6,21},{7,29},{8,0},{9,8},... | collective-permute-start | bytes 196616 | tf_op jit(solution)/shard_map/ppermute | solution.py:89
  259.4 8.5 %collective-permute-start.13 = (f32[2,64,128]{2,1,0:T(8,128)S(1)}, f32[2,64,128]{2,1,0:T(8,128)S(1)}, u32[]{:S(2)}, u32[]{:S(2)}) collective-permute-start(f32[2,64,128]{2,1,0:T(8,128)S(1)} %bitcast.78), channel_id=1, source_target_pairs={{0,5},{1,13},{2,21},{3,29},{4,0},{5,8},{6,16},{7,24},{8,1},{9,9},{... | collective-permute-start | bytes 196616 | tf_op jit(solution)/shard_map/ppermute | solution.py:89
  (1 other events, 1.6 us)
Sparse Core Ops, SparseCore 0:
  83.6 55.6 all-gather.5
  141.5 48.8 all-gather.3
  215.2 23.4 reduce-scatter.1

commit v7 on v5

--- a/solution.py
+++ b/solution.py
@@ -24,18 +24,19 @@
         for shift in range(1, n_narrow):
             perm = [(i, (i + shift) % n_narrow) for i in range(n_narrow)]
             amps_blocks.append(lax.ppermute(amps, "narrow", perm))
-        amps_rev = [amps_blocks[(n_narrow - j) % n_narrow] for j in range(n_narrow)]
-        amps_all = lax.dynamic_slice_in_dim(
-            jnp.concatenate(amps_rev * 2, axis=1), (n_narrow - n) * c_blk, n_narrow * c_blk, 1
-        )
+        amps_all = jnp.stack(amps_blocks, axis=1)
 
         c_sub = c_blk // n_wide
         left_part = lax.dynamic_slice_in_dim(left_fit, w * c_sub, c_sub, 1)
         left_part = left_part.reshape(rows, c_sub, span, q_blk).transpose(2, 0, 1, 3)
         left_send = jnp.concatenate([left_part] * GROUPS, axis=0)
         left_recv = lax.all_to_all(left_send, "narrow", 0, 0, tiled=True)
+        left_rev = [left_recv[(n_narrow - j) % n_narrow][None] for j in range(n_narrow)]
+        left_recv = lax.dynamic_slice_in_dim(
+            jnp.concatenate(left_rev * 2, axis=0), n_narrow - n, n_narrow, 0
+        )
         left_all = lax.all_gather(left_recv, "wide", axis=0, tiled=False)
-        left_all = left_all.transpose(2, 1, 0, 3, 4).reshape(rows, c_blk * n_narrow, q_blk)
+        amps_all = amps_all.reshape(pairs, n_narrow, n_wide, c_sub, amps.shape[2])
 
         right_split = right_fit.reshape(b_blk, d_blk, span, q_blk)
         chunks = []
@@ -52,7 +53,7 @@
             chunks.append(piece)
 
         inter = jnp.einsum(
-            "acq,pcd->padq", left_all, amps_all, preferred_element_type=jnp.float32
+            "wkaiq,pkwid->padq", left_all, amps_all, preferred_element_type=jnp.float32
         ).astype(jnp.bfloat16)
 
         right_group = jnp.concatenate(chunks, axis=0)

time: 241 us -> 228 us (0.946)
  waiting for transfers between devices: 43.5 us -> 76.2 us
  blocking collectives: 30.5 us -> 0 us
  local copies, waits for them, and re-layouts: 83.1 us -> 65.5 us
  matrix products: 24.5 us -> 28.4 us
    all_to_all x1 -> x0, blocking collectives: 30.5 us -> none  [body(): left_recv = lax.all_to_all(left_send, 'narrow', 0, 0, tiled=True)]
    all_to_all x0 -> x1, waiting for transfers between devices: none -> 24.6 us  [body(): left_recv = lax.all_to_all(left_send, 'narrow', 0, 0, tiled=True)]
    all_gather x0 -> x1, local copies, waits for them, and re-layouts: none -> 16.4 us  [body(): left_all = lax.all_gather(left_recv, 'wide', axis=0, tiled=False)]
    dot_general x0 -> x1, matrix products: none -> 16.2 us  [body(): jnp.einsum('wkaiq,pkwid->padq', left_all, amps_all, preferred_element_typ...]
    ppermute x7, starting transfers between devices: 22 us -> 9.68 us  [body(): amps_blocks.append(lax.ppermute(amps, 'narrow', perm))]
    dot_general x1, matrix products: 24.5 us -> 12.2 us  [body(): jnp.einsum('padq,bdq->pab', inter, right_group, preferred_element_type=jn...]
    unnamed x32 -> x39, local copies, waits for them, and re-layouts: 37.1 us -> 25.5 us
    ppermute x3, waiting for transfers between devices: 11.2 us -> 0.01 us  [body(): piece = lax.ppermute(piece, 'narrow', perm)]
  transfers between devices with their start and end apart: 16 -> 17, of which waited for: 6 -> 6; matrix products, arithmetic and copies ran while one was open for 26% -> 26% of each run, Pallas kernels for 0% -> 0%
where the time goes in v7:
time: 228 us; the launch traced here: 226 us
  waiting for transfers between devices  76.2 us (33%)
  local copies, waits for them, and re-layouts  65.5 us (29%)
  starting transfers between devices  40 us (18%)
  matrix products  28.4 us (12%)
  between operations  13.9 us (6%)
    reduce_scatter x1, waiting for transfers between devices, body(): part = lax.psum_scatter(part, 'wide', scatter_dimension=0, tiled=True)  32.6 us
    unnamed x39, local copies, waits for them, and re-layouts  25.5 us
    all_to_all x1, waiting for transfers between devices, body(): left_recv = lax.all_to_all(left_send, 'narrow', 0, 0, tiled=True)  24.6 us
    all_gather x1, local copies, waits for them, and re-layouts, body(): left_all = lax.all_gather(left_recv, 'wide', axis=0, tiled=False)  16.4 us
    dot_general x1, matrix products, body(): jnp.einsum('wkaiq,pkwid->padq', left_all, amps_all, preferred_element_typ...  16.2 us
    ppermute x4, starting transfers between devices, body(): piece = lax.ppermute(piece, ('narrow', 'wide'), perm)  15.4 us
    dot_general x1, matrix products, body(): jnp.einsum('padq,bdq->pab', inter, right_group, preferred_element_type=jn...  12.2 us
    ppermute x7, starting transfers between devices, body(): amps_blocks.append(lax.ppermute(amps, 'narrow', perm))  9.68 us
  transfers between devices with their start and end apart: 17, of which 6 were waited for; matrix products, arithmetic and copies ran while one was open for 26% of the time, Pallas kernels for 0%

profile of v7, /device:TPU:5, one launch (start us, length us, event | category | flops | bytes accessed | tf_op | source)
XLA Modules:
  0.0 226.3 jit_solution(7488015168493718970)
XLA Ops:
  9.0 2.0 reshape.75
  13.9 4.3 %reshape.87 = bf16[8,2,32768]{2,1,0:T(2,128)(2,1)} reshape(bf16[8,64,16,64]{3,2,1,0:T(8,128)(2,1)} %copy.38) | data formatting | bytes 2097152
  18.2 5.5 %all-to-all-start = ((bf16[8,2,32768]{2,1,0:T(2,128)(2,1)}), bf16[8,2,32768]{2,1,0:T(2,128)(2,1)S(1)}, u32[]{:S(2)}, u32[]{:S(2)}) async-start(bf16[8,2,32768]{2,1,0:T(2,128)(2,1)} %reshape.87), calls=%async_computation | async-start | bytes 2097152 | tf_op jit(solution)/shard_map/all_to_all | solution.py:33
  23.8 24.6 %all-to-all-done = bf16[8,2,32768]{2,1,0:T(2,128)(2,1)S(1)} async-done(((bf16[8,2,32768]{2,1,0:T(2,128)(2,1)}), bf16[8,2,32768]{2,1,0:T(2,128)(2,1)S(1)}, u32[]{:S(2)}, u32[]{:S(2)}) %all-to-all-start) | async-done | bytes 1048608 | tf_op jit(solution)/shard_map/all_to_all | solution.py:33
  52.3 1.9 collective-permute-start
  54.2 2.1 collective-permute-start.2
  57.5 2.4 %collective-permute-start.4 = (bf16[16,64,128]{2,1,0:T(8,128)(2,1)S(1)}, bf16[16,64,128]{2,1,0:T(8,128)(2,1)}, u32[]{:S(2)}, u32[]{:S(2)}) collective-permute-start(bf16[16,64,128]{2,1,0:T(8,128)(2,1)S(1)} %copy-done.2), channel_id=1, source_target_pairs={{0,20},{4,24},{8,28},{12,0},{16,4},{20,8},{24,12},{28,16},{1,21},{... | collective-permute-start | bytes 786440 | tf_op jit(solution)/shard_map/ppermute | solution.py:26
  59.8 6.8 %copy.40 = bf16[64,128,256]{1,2,0:T(8,128)(2,1)} copy(bf16[64,128,256]{2,1,0:T(8,128)(2,1)} %param.8) | data formatting | bytes 8388608 | tf_op args[2]
  66.6 3.2 %constant_dynamic-slice_fusion.8 = (bf16[64,128,1,64]{1,3,2,0:T(8,128)(2,1)S(1)}, bf16[64,128,1,64]{1,3,2,0:T(8,128)(2,1)S(1)}, bf16[64,128,1,64]{1,3,2,0:T(8,128)(2,1)S(1)}, bf16[64,128,1,64]{1,3,2,0:T(8,128)(2,1)S(1)}) fusion(bf16[64,128,4,64]{1,3,2,0:T(8,128)(2,1)} %bitcast.55, s32[]{:T(128)S(6)} %select_n.138, s32[]{:T(128)S(6)} %select_n.144, ...), kind=kLoop, calls=%fused_computation.51 | loop fusion | bytes 8388624 | tf_op jit(solution)/shard_map/jit(dynamic_index_in_dim)/dynamic_slice | solution.py:45
  81.7 4.2 %collective-permute-done.2 = bf16[16,64,128]{2,1,0:T(8,128)(2,1)} collective-permute-done((bf16[16,64,128]{2,1,0:T(8,128)(2,1)S(1)}, bf16[16,64,128]{2,1,0:T(8,128)(2,1)}, u32[]{:S(2)}, u32[]{:S(2)}) %collective-permute-start.2) | collective-permute-done | bytes 262176 | tf_op jit(solution)/shard_map/ppermute | solution.py:26
  87.6 5.3 %collective-permute-start.8 = (bf16[64,128,64]{1,0,2:T(8,128)(2,1)}, bf16[64,128,64]{1,0,2:T(8,128)(2,1)}, u32[]{:S(2)}, u32[]{:S(2)}) collective-permute-start(bf16[64,128,64]{1,0,2:T(8,128)(2,1)} %bitcast.52), channel_id=1, source_target_pairs={{0,8},{4,12},{8,0},{12,4},{16,24},{20,28},{24,16},{28,20},{1,9},{5... | collective-permute-start | bytes 3145736 | tf_op jit(solution)/shard_map/ppermute | solution.py:52
  94.6 3.9 %collective-permute-start.9 = (bf16[64,128,64]{1,0,2:T(8,128)(2,1)}, bf16[64,128,64]{1,0,2:T(8,128)(2,1)}, u32[]{:S(2)}, u32[]{:S(2)}) collective-permute-start(bf16[64,128,64]{1,0,2:T(8,128)(2,1)} %bitcast.51), channel_id=1, source_target_pairs={{0,12},{4,0},{8,4},{12,8},{16,28},{20,16},{24,20},{28,24},{1,13},{... | collective-permute-start | bytes 3145736 | tf_op jit(solution)/shard_map/ppermute | solution.py:52
  101.6 8.7 %all-gather.3.cloned.1.call-done = bf16[32,64,16,64]{3,2,1,0:T(8,128)(2,1)} async-done(((bf16[8,64,16,64]{3,2,1,0:T(8,128)(2,1)}), bf16[32,64,16,64]{3,2,1,0:T(8,128)(2,1)}) %all-gather.3.cloned.1.call-update) | async-done | bytes 4194320 | tf_op jit(solution)/shard_map/all_gather | solution.py:38
  110.4 16.4 %copy.47 = bf16[4,8,64,16,64,1]{2,3,0,5,4,1:T(8,128)(2,1)} copy(bf16[4,8,64,16,64,1]{4,3,2,1,0,5:T(8,128)(2,1)} %bitcast.56) | data formatting | bytes 8388608 | tf_op jit(solution)/shard_map/all_gather | solution.py:38
  126.8 16.2 %fusion.9 = bf16[16,128,64,64,1,1]{1,2,5,0,3,4:T(8,128)(2,1)} fusion(bf16[4,8,64,16,64,1]{2,3,0,5,4,1:T(8,128)(2,1)} %copy.47, bf16[16,8,4,16,128]{4,3,2,0,1:T(8,128)(2,1)} %constant_dynamic-update-slice_fusion), kind=kOutput, calls=%fused_computation.11 | convolution fusion | flops 8589934592 | bytes 23068672 | tf_op jit(solution)/shard_map/wkaiq,pkwid->padq/dot_general | solution.py:55
  144.0 12.2 %fusion.11 = f32[16,64,256]{2,1,0:T(8,128)} fusion(bf16[64,128,64]{1,0,2:T(8,128)(2,1)} %collective-permute-done.9, bf16[64,128,64]{1,0,2:T(8,128)(2,1)} %collective-permute-done.8, bf16[64,128,64]{1,0,2:T(8,128)(2,1)} %copy-done.6, bf16[64,128,64]{1,0,2:T(8,128)(2,1)S(1)} %bitcast.58, bf16[16,128,64,64,1,1]{1,2,5,0,3,4:T(8,128)(2,1)} %fusion.9), kind=kOutput, calls=%fused_computation.13 | convolution fusion | flops 4311744512 | bytes 22020096 | tf_op jit(solution)/shard_map/padq,bdq->pab/dot_general | solution.py:60
  156.8 32.6 %reduce-scatter.2.cloned.1.call-done = f32[4,64,256]{2,1,0:T(8,128)} async-done(((f32[16,64,256]{2,1,0:T(8,128)}), f32[4,64,256]{2,1,0:T(8,128)}) %reduce-scatter.2.cloned.1.call-update) | async-done | bytes 262160 | tf_op jit(solution)/shard_map/reduce_scatter | solution.py:63
  191.5 2.8 %concatenate.16 = f32[4,64,8,64]{3,2,1,0:T(8,128)S(1)} concatenate(f32[4,64,1,64]{3,2,1,0:T(1,128)} %get-tuple-element.16, f32[4,64,1,64]{3,2,1,0:T(1,128)S(1)} %get-tuple-element.15, f32[4,64,1,64]{3,2,1,0:T(1,128)S(1)} %get-tuple-element.14, f32[4,64,1,64]{3,2,1,0:T(1,128)S(1)} %get-tuple-element.13, f32[4,64,1,64]{3,2,1,0:T(1,128)} %get-tuple-element.16, ...), dimensions={2} | concatenate | bytes 1048576 | tf_op jit(solution)/shard_map/concatenate | solution.py:66
  197.0 6.5 %collective-permute-start.10 = (f32[2,64,128]{2,1,0:T(8,128)S(1)}, f32[2,64,128]{2,1,0:T(8,128)S(1)}, u32[]{:S(2)}, u32[]{:S(2)}) collective-permute-start(f32[2,64,128]{2,1,0:T(8,128)S(1)} %bitcast.65), channel_id=1, source_target_pairs={{0,0},{1,8},{2,16},{3,24},{4,1},{5,9},{6,17},{7,25},{8,4},{9,12},{... | collective-permute-start | bytes 196616 | tf_op jit(solution)/shard_map/ppermute | solution.py:87
  203.5 3.0 %collective-permute-start.11 = (f32[2,64,128]{2,1,0:T(8,128)S(1)}, f32[2,64,128]{2,1,0:T(8,128)S(1)}, u32[]{:S(2)}, u32[]{:S(2)}) collective-permute-start(f32[2,64,128]{2,1,0:T(8,128)S(1)} %bitcast.64), channel_id=1, source_target_pairs={{0,1},{1,9},{2,17},{3,25},{4,4},{5,12},{6,20},{7,28},{8,5},{9,13},... | collective-permute-start | bytes 196616 | tf_op jit(solution)/shard_map/ppermute | solution.py:87
  206.5 3.6 %collective-permute-start.12 = (f32[2,64,128]{2,1,0:T(8,128)S(1)}, f32[2,64,128]{2,1,0:T(8,128)S(1)}, u32[]{:S(2)}, u32[]{:S(2)}) collective-permute-start(f32[2,64,128]{2,1,0:T(8,128)S(1)} %bitcast.63), channel_id=1, source_target_pairs={{0,4},{1,12},{2,20},{3,28},{4,5},{5,13},{6,21},{7,29},{8,0},{9,8},... | collective-permute-start | bytes 196616 | tf_op jit(solution)/shard_map/ppermute | solution.py:87
  210.2 2.3 %collective-permute-start.13 = (f32[2,64,128]{2,1,0:T(8,128)S(1)}, f32[2,64,128]{2,1,0:T(8,128)S(1)}, u32[]{:S(2)}, u32[]{:S(2)}) collective-permute-start(f32[2,64,128]{2,1,0:T(8,128)S(1)} %bitcast.62), channel_id=1, source_target_pairs={{0,5},{1,13},{2,21},{3,29},{4,0},{5,8},{6,16},{7,24},{8,1},{9,9},{... | collective-permute-start | bytes 196616 | tf_op jit(solution)/shard_map/ppermute | solution.py:87
  212.6 1.9 collective-permute-done.11
  214.6 4.1 %collective-permute-done.13 = f32[2,64,128]{2,1,0:T(8,128)S(1)} collective-permute-done((f32[2,64,128]{2,1,0:T(8,128)S(1)}, f32[2,64,128]{2,1,0:T(8,128)S(1)}, u32[]{:S(2)}, u32[]{:S(2)}) %collective-permute-start.13) | collective-permute-done | bytes 65568 | tf_op jit(solution)/shard_map/ppermute | solution.py:87
  (80 shorter events, 35.7 us)
Async XLA Ops:
  6.5 1.6 copy-start
  18.2 30.1 %all-to-all-start = ((bf16[8,2,32768]{2,1,0:T(2,128)(2,1)}), bf16[8,2,32768]{2,1,0:T(2,128)(2,1)S(1)}, u32[]{:S(2)}, u32[]{:S(2)}) async-start(bf16[8,2,32768]{2,1,0:T(2,128)(2,1)} %reshape.87), calls=%async_computation | async-start | bytes 2097152 | tf_op jit(solution)/shard_map/all_to_all | solution.py:33
  23.8 86.6 %all-gather.3.cloned.1.call-start = ((), (), s32[]{:S(2)}) async-start(), calls=%async_computation.3 | async-start | bytes 10485760 | tf_op jit(solution)/shard_map/all_gather | solution.py:38
  50.3 2.0 copy-start.2
  52.2 137.2 %reduce-scatter.2.cloned.1.call-start = ((), (), s32[]{:S(2)}) async-start(), calls=%async_computation.2 | async-start | bytes 1310720 | tf_op jit(solution)/shard_map/reduce_scatter | solution.py:63
  52.3 23.9 %collective-permute-start = (bf16[16,64,128]{2,1,0:T(8,128)(2,1)S(1)}, bf16[16,64,128]{2,1,0:T(8,128)(2,1)}, u32[]{:S(2)}, u32[]{:S(2)}) collective-permute-start(bf16[16,64,128]{2,1,0:T(8,128)(2,1)S(1)} %copy-done.2), channel_id=1, source_target_pairs={{0,4},{4,8},{8,12},{12,16},{16,20},{20,24},{24,28},{28,0},{1,5},{5... | collective-permute-start | bytes 786440 | tf_op jit(solution)/shard_map/ppermute | solution.py:26
  54.1 25.0 %collective-permute-start.1 = (bf16[16,64,128]{2,1,0:T(8,128)(2,1)S(1)}, bf16[16,64,128]{2,1,0:T(8,128)(2,1)}, u32[]{:S(2)}, u32[]{:S(2)}) collective-permute-start(bf16[16,64,128]{2,1,0:T(8,128)(2,1)S(1)} %copy-done.2), channel_id=1, source_target_pairs={{0,8},{4,12},{8,16},{12,20},{16,24},{20,28},{24,0},{28,4},{1,9},{5... | collective-permute-start | bytes 786440 | tf_op jit(solution)/shard_map/ppermute | solution.py:26
  54.2 31.8 %collective-permute-start.2 = (bf16[16,64,128]{2,1,0:T(8,128)(2,1)S(1)}, bf16[16,64,128]{2,1,0:T(8,128)(2,1)}, u32[]{:S(2)}, u32[]{:S(2)}) collective-permute-start(bf16[16,64,128]{2,1,0:T(8,128)(2,1)S(1)} %copy-done.2), channel_id=1, source_target_pairs={{0,12},{4,16},{8,20},{12,24},{16,28},{20,0},{24,4},{28,8},{1,13},{... | collective-permute-start | bytes 786440 | tf_op jit(solution)/shard_map/ppermute | solution.py:26
  56.3 31.3 %collective-permute-start.3 = (bf16[16,64,128]{2,1,0:T(8,128)(2,1)S(1)}, bf16[16,64,128]{2,1,0:T(8,128)(2,1)}, u32[]{:S(2)}, u32[]{:S(2)}) collective-permute-start(bf16[16,64,128]{2,1,0:T(8,128)(2,1)S(1)} %copy-done.2), channel_id=1, source_target_pairs={{0,16},{4,20},{8,24},{12,28},{16,0},{20,4},{24,8},{28,12},{1,17},{... | collective-permute-start | bytes 786440 | tf_op jit(solution)/shard_map/ppermute | solution.py:26
  57.5 37.1 %collective-permute-start.4 = (bf16[16,64,128]{2,1,0:T(8,128)(2,1)S(1)}, bf16[16,64,128]{2,1,0:T(8,128)(2,1)}, u32[]{:S(2)}, u32[]{:S(2)}) collective-permute-start(bf16[16,64,128]{2,1,0:T(8,128)(2,1)S(1)} %copy-done.2), channel_id=1, source_target_pairs={{0,20},{4,24},{8,28},{12,0},{16,4},{20,8},{24,12},{28,16},{1,21},{... | collective-permute-start | bytes 786440 | tf_op jit(solution)/shard_map/ppermute | solution.py:26
  76.2 24.0 %collective-permute-start.5 = (bf16[16,64,128]{2,1,0:T(8,128)(2,1)S(1)}, bf16[16,64,128]{2,1,0:T(8,128)(2,1)S(1)}, u32[]{:S(2)}, u32[]{:S(2)}) collective-permute-start(bf16[16,64,128]{2,1,0:T(8,128)(2,1)S(1)} %copy-done.2), channel_id=1, source_target_pairs={{0,24},{4,28},{8,0},{12,4},{16,8},{20,12},{24,16},{28,20},{1,25},{... | collective-permute-start | bytes 786440 | tf_op jit(solution)/shard_map/ppermute | solution.py:26
  79.2 21.8 %collective-permute-start.6 = (bf16[16,64,128]{2,1,0:T(8,128)(2,1)S(1)}, bf16[16,64,128]{2,1,0:T(8,128)(2,1)S(1)}, u32[]{:S(2)}, u32[]{:S(2)}) collective-permute-start(bf16[16,64,128]{2,1,0:T(8,128)(2,1)S(1)} %copy-done.2), channel_id=1, source_target_pairs={{0,28},{4,0},{8,4},{12,8},{16,12},{20,16},{24,20},{28,24},{1,29},{... | collective-permute-start | bytes 786440 | tf_op jit(solution)/shard_map/ppermute | solution.py:26
  85.9 57.0 %collective-permute-start.7 = (bf16[64,128,64]{1,0,2:T(8,128)(2,1)}, bf16[64,128,64]{1,0,2:T(8,128)(2,1)S(1)}, u32[]{:S(2)}, u32[]{:S(2)}) collective-permute-start(bf16[64,128,64]{1,0,2:T(8,128)(2,1)} %bitcast.53), channel_id=1, source_target_pairs={{0,4},{4,8},{8,12},{12,0},{16,20},{20,24},{24,28},{28,16},{1,5},{5... | collective-permute-start | bytes 3145736 | tf_op jit(solution)/shard_map/ppermute | solution.py:52
  87.6 55.3 %collective-permute-start.8 = (bf16[64,128,64]{1,0,2:T(8,128)(2,1)}, bf16[64,128,64]{1,0,2:T(8,128)(2,1)}, u32[]{:S(2)}, u32[]{:S(2)}) collective-permute-start(bf16[64,128,64]{1,0,2:T(8,128)(2,1)} %bitcast.52), channel_id=1, source_target_pairs={{0,8},{4,12},{8,0},{12,4},{16,24},{20,28},{24,16},{28,20},{1,9},{5... | collective-permute-start | bytes 3145736 | tf_op jit(solution)/shard_map/ppermute | solution.py:52
  94.6 48.3 %collective-permute-start.9 = (bf16[64,128,64]{1,0,2:T(8,128)(2,1)}, bf16[64,128,64]{1,0,2:T(8,128)(2,1)}, u32[]{:S(2)}, u32[]{:S(2)}) collective-permute-start(bf16[64,128,64]{1,0,2:T(8,128)(2,1)} %bitcast.51), channel_id=1, source_target_pairs={{0,12},{4,0},{8,4},{12,8},{16,28},{20,16},{24,20},{28,24},{1,13},{... | collective-permute-start | bytes 3145736 | tf_op jit(solution)/shard_map/ppermute | solution.py:52
  144.0 12.5 %copy-start.3 = (s32[2,2]{1,0:T(2,128)S(1)}, s32[2,2]{1,0:T(2,128)}, u32[]{:S(2)}) copy-start(s32[2,2]{1,0:T(2,128)} %param.9) | copy-start | bytes 52
  144.0 12.7 %copy-start.4 = (f32[128]{0:T(128)S(1)}, f32[128]{0:T(128)}, u32[]{:S(2)}) copy-start(f32[128]{0:T(128)} %param.10) | copy-start | bytes 1540
  144.0 75.5 %copy-start.1 = (bf16[64,64,256]{2,1,0:T(8,128)(2,1)S(1)}, bf16[64,64,256]{2,1,0:T(8,128)(2,1)}, u32[]{:S(2)}) copy-start(bf16[64,64,256]{2,1,0:T(8,128)(2,1)} %param.7) | copy-start | bytes 6291460
  156.2 56.2 %slice-start = ((f32[512]{0:T(512)}), f32[64]{0:T(128)S(1)}, s32[]{:S(2)}) async-start(f32[512]{0:T(512)} %param.11), calls=%async_computation.4 | async-start | bytes 1024 | tf_op jit(solution)/shard_map/slice | solution.py:99
  156.2 56.3 %copy-start.5 = (f32[512]{0:T(512)S(1)}, f32[512]{0:T(512)}, u32[]{:S(2)}) copy-start(f32[512]{0:T(512)} %param.11) | copy-start | bytes 6148
  197.0 15.6 %collective-permute-start.10 = (f32[2,64,128]{2,1,0:T(8,128)S(1)}, f32[2,64,128]{2,1,0:T(8,128)S(1)}, u32[]{:S(2)}, u32[]{:S(2)}) collective-permute-start(f32[2,64,128]{2,1,0:T(8,128)S(1)} %bitcast.65), channel_id=1, source_target_pairs={{0,0},{1,8},{2,16},{3,24},{4,1},{5,9},{6,17},{7,25},{8,4},{9,12},{... | collective-permute-start | bytes 196616 | tf_op jit(solution)/shard_map/ppermute | solution.py:87
  203.5 11.1 %collective-permute-start.11 = (f32[2,64,128]{2,1,0:T(8,128)S(1)}, f32[2,64,128]{2,1,0:T(8,128)S(1)}, u32[]{:S(2)}, u32[]{:S(2)}) collective-permute-start(f32[2,64,128]{2,1,0:T(8,128)S(1)} %bitcast.64), channel_id=1, source_target_pairs={{0,1},{1,9},{2,17},{3,25},{4,4},{5,12},{6,20},{7,28},{8,5},{9,13},... | collective-permute-start | bytes 196616 | tf_op jit(solution)/shard_map/ppermute | solution.py:87
  206.5 8.0 %collective-permute-start.12 = (f32[2,64,128]{2,1,0:T(8,128)S(1)}, f32[2,64,128]{2,1,0:T(8,128)S(1)}, u32[]{:S(2)}, u32[]{:S(2)}) collective-permute-start(f32[2,64,128]{2,1,0:T(8,128)S(1)} %bitcast.63), channel_id=1, source_target_pairs={{0,4},{1,12},{2,20},{3,28},{4,5},{5,13},{6,21},{7,29},{8,0},{9,8},... | collective-permute-start | bytes 196616 | tf_op jit(solution)/shard_map/ppermute | solution.py:87
  210.2 8.5 %collective-permute-start.13 = (f32[2,64,128]{2,1,0:T(8,128)S(1)}, f32[2,64,128]{2,1,0:T(8,128)S(1)}, u32[]{:S(2)}, u32[]{:S(2)}) collective-permute-start(f32[2,64,128]{2,1,0:T(8,128)S(1)} %bitcast.62), channel_id=1, source_target_pairs={{0,5},{1,13},{2,21},{3,29},{4,0},{5,8},{6,16},{7,24},{8,1},{9,9},{... | collective-permute-start | bytes 196616 | tf_op jit(solution)/shard_map/ppermute | solution.py:87
  (1 other events, 1.0 us)
Sparse Core Ops, SparseCore 0:
  52.4 57.9 all-gather.2
  156.4 33.0 reduce-scatter.1

commit v8 on v7

--- a/solution.py
+++ b/solution.py
@@ -28,7 +28,7 @@
 
         c_sub = c_blk // n_wide
         left_part = lax.dynamic_slice_in_dim(left_fit, w * c_sub, c_sub, 1)
-        left_part = left_part.reshape(rows, c_sub, span, q_blk).transpose(2, 0, 1, 3)
+        left_part = left_part.reshape(rows, c_sub, span, q_blk).transpose(2, 3, 1, 0)
         left_send = jnp.concatenate([left_part] * GROUPS, axis=0)
         left_recv = lax.all_to_all(left_send, "narrow", 0, 0, tiled=True)
         left_rev = [left_recv[(n_narrow - j) % n_narrow][None] for j in range(n_narrow)]
@@ -53,7 +53,7 @@
             chunks.append(piece)
 
         inter = jnp.einsum(
-            "wkaiq,pkwid->padq", left_all, amps_all, preferred_element_type=jnp.float32
+            "wkqia,pkwid->padq", left_all, amps_all, preferred_element_type=jnp.float32
         ).astype(jnp.bfloat16)
 
         right_group = jnp.concatenate(chunks, axis=0)

time: 228 us -> 219 us (0.961)
  local copies, waits for them, and re-layouts: 65.5 us -> 48.6 us
  waiting for transfers between devices: 76.2 us -> 85.3 us
    all_gather x1 -> x0, local copies, waits for them, and re-layouts: 16.4 us -> none  [body(): left_all = lax.all_gather(left_recv, 'wide', axis=0, tiled=False)]
    ppermute x3, waiting for transfers between devices: 0.01 us -> 13.7 us  [body(): piece = lax.ppermute(piece, 'narrow', perm)]
    reduce_scatter x1, waiting for transfers between devices: 32.6 us -> 27.9 us  [body(): part = lax.psum_scatter(part, 'wide', scatter_dimension=0, tiled=True)]
    dynamic_slice x1 -> x2, local copies, waits for them, and re-layouts: 1.71 us -> 4.75 us  [body(): lax.dynamic_slice_in_dim(jnp.concatenate(left_rev * 2, axis=0), n_narrow...]
  transfers between devices with their start and end apart: 17 -> 17, of which waited for: 6 -> 7; matrix products, arithmetic and copies ran while one was open for 26% -> 20% of each run, Pallas kernels for 0% -> 0%
where the time goes in v8:
time: 219 us
  waiting for transfers between devices  85.3 us (39%)
  local copies, waits for them, and re-layouts  48.6 us (22%)
  starting transfers between devices  40 us (18%)
  matrix products  28.4 us (13%)
  between operations  13.9 us (6%)
  other arithmetic  2.23 us (1%)
    reduce_scatter x1, waiting for transfers between devices, body(): part = lax.psum_scatter(part, 'wide', scatter_dimension=0, tiled=True)  27.9 us
    all_to_all x1, waiting for transfers between devices, body(): left_recv = lax.all_to_all(left_send, 'narrow', 0, 0, tiled=True)  24.6 us
    unnamed x39, local copies, waits for them, and re-layouts  24.4 us
    dot_general x1, matrix products, body(): jnp.einsum('wkqia,pkwid->padq', left_all, amps_all, preferred_element_typ...  16.2 us
    ppermute x4, starting transfers between devices, body(): piece = lax.ppermute(piece, ('narrow', 'wide'), perm)  15.5 us
    ppermute x3, waiting for transfers between devices, body(): piece = lax.ppermute(piece, 'narrow', perm)  13.7 us
    dot_general x1, matrix products, body(): jnp.einsum('padq,bdq->pab', inter, right_group, preferred_element_type=jn...  12.2 us
    ppermute x7, starting transfers between devices, body(): amps_blocks.append(lax.ppermute(amps, 'narrow', perm))  9.65 us
  transfers between devices with their start and end apart: 17, of which 7 were waited for; matrix products, arithmetic and copies ran while one was open for 20% of the time, Pallas kernels for 0%

profile of v8, /device:TPU:5, one launch (start us, length us, event | category | flops | bytes accessed | tf_op | source)
XLA Modules:
  0.0 218.5 jit_solution(3518379699950791101)
XLA Ops:
  11.5 4.3 %reshape.87 = bf16[8,2,32768]{2,1,0:T(2,128)(2,1)} reshape(bf16[8,64,16,64]{3,2,1,0:T(8,128)(2,1)} %bitcast.75) | data formatting | bytes 2097152
  15.8 5.5 %all-to-all-start = ((bf16[8,2,32768]{2,1,0:T(2,128)(2,1)}), bf16[8,2,32768]{2,1,0:T(2,128)(2,1)S(1)}, u32[]{:S(2)}, u32[]{:S(2)}) async-start(bf16[8,2,32768]{2,1,0:T(2,128)(2,1)} %reshape.87), calls=%async_computation | async-start | bytes 2097152 | tf_op jit(solution)/shard_map/all_to_all | solution.py:33
  21.4 24.6 %all-to-all-done = bf16[8,2,32768]{2,1,0:T(2,128)(2,1)S(1)} async-done(((bf16[8,2,32768]{2,1,0:T(2,128)(2,1)}), bf16[8,2,32768]{2,1,0:T(2,128)(2,1)S(1)}, u32[]{:S(2)}, u32[]{:S(2)}) %all-to-all-start) | async-done | bytes 1048608 | tf_op jit(solution)/shard_map/all_to_all | solution.py:33
  48.4 4.4 %copy.48 = bf16[8,64,16,64]{3,2,1,0:T(8,128)(2,1)} copy(bf16[8,64,16,64]{1,2,3,0:T(8,128)(2,1)S(1)} %constant_dynamic-slice_fusion.9) | data formatting | bytes 2097152 | tf_op jit(solution)/shard_map/dynamic_slice | solution.py:35
  52.9 1.9 collective-permute-start
  54.8 2.1 collective-permute-start.2
  58.1 2.4 %collective-permute-start.4 = (bf16[16,64,128]{2,1,0:T(8,128)(2,1)S(1)}, bf16[16,64,128]{2,1,0:T(8,128)(2,1)}, u32[]{:S(2)}, u32[]{:S(2)}) collective-permute-start(bf16[16,64,128]{2,1,0:T(8,128)(2,1)S(1)} %copy-done.2), channel_id=1, source_target_pairs={{0,20},{4,24},{8,28},{12,0},{16,4},{20,8},{24,12},{28,16},{1,21},{... | collective-permute-start | bytes 786440 | tf_op jit(solution)/shard_map/ppermute | solution.py:26
  60.5 6.7 %copy.50 = bf16[64,128,256]{1,2,0:T(8,128)(2,1)} copy(bf16[64,128,256]{2,1,0:T(8,128)(2,1)} %param.8) | data formatting | bytes 8388608 | tf_op args[2]
  67.1 3.2 %constant_dynamic-slice_fusion.8 = (bf16[64,128,1,64]{1,3,2,0:T(8,128)(2,1)S(1)}, bf16[64,128,1,64]{1,3,2,0:T(8,128)(2,1)S(1)}, bf16[64,128,1,64]{1,3,2,0:T(8,128)(2,1)S(1)}, bf16[64,128,1,64]{1,3,2,0:T(8,128)(2,1)S(1)}) fusion(bf16[64,128,4,64]{1,3,2,0:T(8,128)(2,1)} %bitcast.74, s32[]{:T(128)S(6)} %select_n.138, s32[]{:T(128)S(6)} %select_n.144, ...), kind=kLoop, calls=%fused_computation.52 | loop fusion | bytes 8388624 | tf_op jit(solution)/shard_map/jit(dynamic_index_in_dim)/dynamic_slice | solution.py:45
  82.2 4.3 %collective-permute-done.2 = bf16[16,64,128]{2,1,0:T(8,128)(2,1)} collective-permute-done((bf16[16,64,128]{2,1,0:T(8,128)(2,1)S(1)}, bf16[16,64,128]{2,1,0:T(8,128)(2,1)}, u32[]{:S(2)}, u32[]{:S(2)}) %collective-permute-start.2) | collective-permute-done | bytes 262176 | tf_op jit(solution)/shard_map/ppermute | solution.py:26
  88.2 5.3 %collective-permute-start.8 = (bf16[64,128,64]{1,0,2:T(8,128)(2,1)}, bf16[64,128,64]{1,0,2:T(8,128)(2,1)}, u32[]{:S(2)}, u32[]{:S(2)}) collective-permute-start(bf16[64,128,64]{1,0,2:T(8,128)(2,1)} %bitcast.54), channel_id=1, source_target_pairs={{0,8},{4,12},{8,0},{12,4},{16,24},{20,28},{24,16},{28,20},{1,9},{5... | collective-permute-start | bytes 3145736 | tf_op jit(solution)/shard_map/ppermute | solution.py:52
  95.2 3.9 %collective-permute-start.9 = (bf16[64,128,64]{1,0,2:T(8,128)(2,1)}, bf16[64,128,64]{1,0,2:T(8,128)(2,1)}, u32[]{:S(2)}, u32[]{:S(2)}) collective-permute-start(bf16[64,128,64]{1,0,2:T(8,128)(2,1)} %bitcast.53), channel_id=1, source_target_pairs={{0,12},{4,0},{8,4},{12,8},{16,28},{20,16},{24,20},{28,24},{1,13},{... | collective-permute-start | bytes 3145736 | tf_op jit(solution)/shard_map/ppermute | solution.py:52
  102.2 8.7 %all-gather.3.cloned.1.call-done = bf16[32,64,16,64]{3,2,1,0:T(8,128)(2,1)} async-done(((bf16[8,64,16,64]{3,2,1,0:T(8,128)(2,1)}), bf16[32,64,16,64]{3,2,1,0:T(8,128)(2,1)}) %all-gather.3.cloned.1.call-update) | async-done | bytes 4194320 | tf_op jit(solution)/shard_map/all_gather | solution.py:38
  111.0 16.2 %fusion.3 = bf16[16,128,64,64,1,1]{1,3,5,0,2,4:T(8,128)(2,1)} fusion(bf16[4,8,64,16,64,1]{4,3,2,1,0,5:T(8,128)(2,1)} %bitcast.85, bf16[16,8,4,16,128]{4,3,2,0,1:T(8,128)(2,1)} %constant_dynamic-update-slice_fusion), kind=kOutput, calls=%fused_computation.3 | convolution fusion | flops 8589934592 | bytes 23068672 | tf_op jit(solution)/shard_map/wkqia,pkwid->padq/dot_general | solution.py:55
  127.2 13.7 %collective-permute-done.9 = bf16[64,128,64]{1,0,2:T(8,128)(2,1)} collective-permute-done((bf16[64,128,64]{1,0,2:T(8,128)(2,1)}, bf16[64,128,64]{1,0,2:T(8,128)(2,1)}, u32[]{:S(2)}, u32[]{:S(2)}) %collective-permute-start.9) | collective-permute-done | bytes 1048608 | tf_op jit(solution)/shard_map/ppermute | solution.py:52
  140.9 12.2 %fusion.12 = f32[16,64,256]{2,1,0:T(8,128)} fusion(bf16[64,128,64]{1,0,2:T(8,128)(2,1)} %collective-permute-done.9, bf16[64,128,64]{1,0,2:T(8,128)(2,1)} %collective-permute-done.8, bf16[64,128,64]{1,0,2:T(8,128)(2,1)} %copy-done.6, bf16[64,128,64]{1,0,2:T(8,128)(2,1)S(1)} %bitcast.77, bf16[16,128,64,64,1,1]{1,3,5,0,2,4:T(8,128)(2,1)} %fusion.3), kind=kOutput, calls=%fused_computation.14 | convolution fusion | flops 4311744512 | bytes 22020096 | tf_op jit(solution)/shard_map/padq,bdq->pab/dot_general | solution.py:60
  153.7 27.9 %reduce-scatter.2.cloned.1.call-done = f32[4,64,256]{2,1,0:T(8,128)} async-done(((f32[16,64,256]{2,1,0:T(8,128)}), f32[4,64,256]{2,1,0:T(8,128)}) %reduce-scatter.2.cloned.1.call-update) | async-done | bytes 262160 | tf_op jit(solution)/shard_map/reduce_scatter | solution.py:63
  183.7 2.8 %concatenate.16 = f32[4,64,8,64]{3,2,1,0:T(8,128)S(1)} concatenate(f32[4,64,1,64]{3,2,1,0:T(1,128)} %get-tuple-element.16, f32[4,64,1,64]{3,2,1,0:T(1,128)S(1)} %get-tuple-element.15, f32[4,64,1,64]{3,2,1,0:T(1,128)S(1)} %get-tuple-element.14, f32[4,64,1,64]{3,2,1,0:T(1,128)S(1)} %get-tuple-element.13, f32[4,64,1,64]{3,2,1,0:T(1,128)} %get-tuple-element.16, ...), dimensions={2} | concatenate | bytes 1048576 | tf_op jit(solution)/shard_map/concatenate | solution.py:66
  189.2 6.5 %collective-permute-start.10 = (f32[2,64,128]{2,1,0:T(8,128)S(1)}, f32[2,64,128]{2,1,0:T(8,128)S(1)}, u32[]{:S(2)}, u32[]{:S(2)}) collective-permute-start(f32[2,64,128]{2,1,0:T(8,128)S(1)} %bitcast.84), channel_id=1, source_target_pairs={{0,0},{1,8},{2,16},{3,24},{4,1},{5,9},{6,17},{7,25},{8,4},{9,12},{... | collective-permute-start | bytes 196616 | tf_op jit(solution)/shard_map/ppermute | solution.py:87
  195.7 3.1 %collective-permute-start.11 = (f32[2,64,128]{2,1,0:T(8,128)S(1)}, f32[2,64,128]{2,1,0:T(8,128)S(1)}, u32[]{:S(2)}, u32[]{:S(2)}) collective-permute-start(f32[2,64,128]{2,1,0:T(8,128)S(1)} %bitcast.83), channel_id=1, source_target_pairs={{0,1},{1,9},{2,17},{3,25},{4,4},{5,12},{6,20},{7,28},{8,5},{9,13},... | collective-permute-start | bytes 196616 | tf_op jit(solution)/shard_map/ppermute | solution.py:87
  198.8 3.6 %collective-permute-start.12 = (f32[2,64,128]{2,1,0:T(8,128)S(1)}, f32[2,64,128]{2,1,0:T(8,128)S(1)}, u32[]{:S(2)}, u32[]{:S(2)}) collective-permute-start(f32[2,64,128]{2,1,0:T(8,128)S(1)} %bitcast.82), channel_id=1, source_target_pairs={{0,4},{1,12},{2,20},{3,28},{4,5},{5,13},{6,21},{7,29},{8,0},{9,8},... | collective-permute-start | bytes 196616 | tf_op jit(solution)/shard_map/ppermute | solution.py:87
  202.4 2.3 %collective-permute-start.13 = (f32[2,64,128]{2,1,0:T(8,128)S(1)}, f32[2,64,128]{2,1,0:T(8,128)S(1)}, u32[]{:S(2)}, u32[]{:S(2)}) collective-permute-start(f32[2,64,128]{2,1,0:T(8,128)S(1)} %bitcast.81), channel_id=1, source_target_pairs={{0,5},{1,13},{2,21},{3,29},{4,0},{5,8},{6,16},{7,24},{8,1},{9,9},{... | collective-permute-start | bytes 196616 | tf_op jit(solution)/shard_map/ppermute | solution.py:87
  204.8 2.0 collective-permute-done.11
  206.8 4.2 %collective-permute-done.13 = f32[2,64,128]{2,1,0:T(8,128)S(1)} collective-permute-done((f32[2,64,128]{2,1,0:T(8,128)S(1)}, f32[2,64,128]{2,1,0:T(8,128)S(1)}, u32[]{:S(2)}, u32[]{:S(2)}) %collective-permute-start.13) | collective-permute-done | bytes 65568 | tf_op jit(solution)/shard_map/ppermute | solution.py:87
  (80 shorter events, 33.0 us)
Async XLA Ops:
  15.8 30.1 %all-to-all-start = ((bf16[8,2,32768]{2,1,0:T(2,128)(2,1)}), bf16[8,2,32768]{2,1,0:T(2,128)(2,1)S(1)}, u32[]{:S(2)}, u32[]{:S(2)}) async-start(bf16[8,2,32768]{2,1,0:T(2,128)(2,1)} %reshape.87), calls=%async_computation | async-start | bytes 2097152 | tf_op jit(solution)/shard_map/all_to_all | solution.py:33
  21.3 89.7 %all-gather.3.cloned.1.call-start = ((), (), s32[]{:S(2)}) async-start(), calls=%async_computation.3 | async-start | bytes 10485760 | tf_op jit(solution)/shard_map/all_gather | solution.py:38
  48.4 4.5 %copy-start.2 = (bf16[16,64,128]{2,1,0:T(8,128)(2,1)S(1)}, bf16[16,64,128]{2,1,0:T(8,128)(2,1)}, u32[]{:S(2)}) copy-start(bf16[16,64,128]{2,1,0:T(8,128)(2,1)} %param.6) | copy-start | bytes 786436
  52.8 128.8 %reduce-scatter.2.cloned.1.call-start = ((), (), s32[]{:S(2)}) async-start(), calls=%async_computation.2 | async-start | bytes 1310720 | tf_op jit(solution)/shard_map/reduce_scatter | solution.py:63
  52.9 23.8 %collective-permute-start = (bf16[16,64,128]{2,1,0:T(8,128)(2,1)S(1)}, bf16[16,64,128]{2,1,0:T(8,128)(2,1)}, u32[]{:S(2)}, u32[]{:S(2)}) collective-permute-start(bf16[16,64,128]{2,1,0:T(8,128)(2,1)S(1)} %copy-done.2), channel_id=1, source_target_pairs={{0,4},{4,8},{8,12},{12,16},{16,20},{20,24},{24,28},{28,0},{1,5},{5... | collective-permute-start | bytes 786440 | tf_op jit(solution)/shard_map/ppermute | solution.py:26
  54.8 25.0 %collective-permute-start.1 = (bf16[16,64,128]{2,1,0:T(8,128)(2,1)S(1)}, bf16[16,64,128]{2,1,0:T(8,128)(2,1)}, u32[]{:S(2)}, u32[]{:S(2)}) collective-permute-start(bf16[16,64,128]{2,1,0:T(8,128)(2,1)S(1)} %copy-done.2), channel_id=1, source_target_pairs={{0,8},{4,12},{8,16},{12,20},{16,24},{20,28},{24,0},{28,4},{1,9},{5... | collective-permute-start | bytes 786440 | tf_op jit(solution)/shard_map/ppermute | solution.py:26
  54.8 31.8 %collective-permute-start.2 = (bf16[16,64,128]{2,1,0:T(8,128)(2,1)S(1)}, bf16[16,64,128]{2,1,0:T(8,128)(2,1)}, u32[]{:S(2)}, u32[]{:S(2)}) collective-permute-start(bf16[16,64,128]{2,1,0:T(8,128)(2,1)S(1)} %copy-done.2), channel_id=1, source_target_pairs={{0,12},{4,16},{8,20},{12,24},{16,28},{20,0},{24,4},{28,8},{1,13},{... | collective-permute-start | bytes 786440 | tf_op jit(solution)/shard_map/ppermute | solution.py:26
  56.9 31.3 %collective-permute-start.3 = (bf16[16,64,128]{2,1,0:T(8,128)(2,1)S(1)}, bf16[16,64,128]{2,1,0:T(8,128)(2,1)}, u32[]{:S(2)}, u32[]{:S(2)}) collective-permute-start(bf16[16,64,128]{2,1,0:T(8,128)(2,1)S(1)} %copy-done.2), channel_id=1, source_target_pairs={{0,16},{4,20},{8,24},{12,28},{16,0},{20,4},{24,8},{28,12},{1,17},{... | collective-permute-start | bytes 786440 | tf_op jit(solution)/shard_map/ppermute | solution.py:26
  58.1 37.1 %collective-permute-start.4 = (bf16[16,64,128]{2,1,0:T(8,128)(2,1)S(1)}, bf16[16,64,128]{2,1,0:T(8,128)(2,1)}, u32[]{:S(2)}, u32[]{:S(2)}) collective-permute-start(bf16[16,64,128]{2,1,0:T(8,128)(2,1)S(1)} %copy-done.2), channel_id=1, source_target_pairs={{0,20},{4,24},{8,28},{12,0},{16,4},{20,8},{24,12},{28,16},{1,21},{... | collective-permute-start | bytes 786440 | tf_op jit(solution)/shard_map/ppermute | solution.py:26
  76.7 24.1 %collective-permute-start.5 = (bf16[16,64,128]{2,1,0:T(8,128)(2,1)S(1)}, bf16[16,64,128]{2,1,0:T(8,128)(2,1)S(1)}, u32[]{:S(2)}, u32[]{:S(2)}) collective-permute-start(bf16[16,64,128]{2,1,0:T(8,128)(2,1)S(1)} %copy-done.2), channel_id=1, source_target_pairs={{0,24},{4,28},{8,0},{12,4},{16,8},{20,12},{24,16},{28,20},{1,25},{... | collective-permute-start | bytes 786440 | tf_op jit(solution)/shard_map/ppermute | solution.py:26
  79.7 21.8 %collective-permute-start.6 = (bf16[16,64,128]{2,1,0:T(8,128)(2,1)S(1)}, bf16[16,64,128]{2,1,0:T(8,128)(2,1)S(1)}, u32[]{:S(2)}, u32[]{:S(2)}) collective-permute-start(bf16[16,64,128]{2,1,0:T(8,128)(2,1)S(1)} %copy-done.2), channel_id=1, source_target_pairs={{0,28},{4,0},{8,4},{12,8},{16,12},{20,16},{24,20},{28,24},{1,29},{... | collective-permute-start | bytes 786440 | tf_op jit(solution)/shard_map/ppermute | solution.py:26
  86.5 40.6 %collective-permute-start.7 = (bf16[64,128,64]{1,0,2:T(8,128)(2,1)}, bf16[64,128,64]{1,0,2:T(8,128)(2,1)S(1)}, u32[]{:S(2)}, u32[]{:S(2)}) collective-permute-start(bf16[64,128,64]{1,0,2:T(8,128)(2,1)} %bitcast.55), channel_id=1, source_target_pairs={{0,4},{4,8},{8,12},{12,0},{16,20},{20,24},{24,28},{28,16},{1,5},{5... | collective-permute-start | bytes 3145736 | tf_op jit(solution)/shard_map/ppermute | solution.py:52
  88.2 38.9 %collective-permute-start.8 = (bf16[64,128,64]{1,0,2:T(8,128)(2,1)}, bf16[64,128,64]{1,0,2:T(8,128)(2,1)}, u32[]{:S(2)}, u32[]{:S(2)}) collective-permute-start(bf16[64,128,64]{1,0,2:T(8,128)(2,1)} %bitcast.54), channel_id=1, source_target_pairs={{0,8},{4,12},{8,0},{12,4},{16,24},{20,28},{24,16},{28,20},{1,9},{5... | collective-permute-start | bytes 3145736 | tf_op jit(solution)/shard_map/ppermute | solution.py:52
  95.2 45.6 %collective-permute-start.9 = (bf16[64,128,64]{1,0,2:T(8,128)(2,1)}, bf16[64,128,64]{1,0,2:T(8,128)(2,1)}, u32[]{:S(2)}, u32[]{:S(2)}) collective-permute-start(bf16[64,128,64]{1,0,2:T(8,128)(2,1)} %bitcast.53), channel_id=1, source_target_pairs={{0,12},{4,0},{8,4},{12,8},{16,28},{20,16},{24,20},{28,24},{1,13},{... | collective-permute-start | bytes 3145736 | tf_op jit(solution)/shard_map/ppermute | solution.py:52
  127.1 13.7 %copy-start.6 = (bf16[64,128,64]{1,0,2:T(8,128)(2,1)}, bf16[64,128,64]{1,0,2:T(8,128)(2,1)S(1)}, u32[]{:S(2)}) copy-start(bf16[64,128,64]{1,0,2:T(8,128)(2,1)S(1)} %collective-permute-done.7) | copy-start | bytes 3145732
  140.8 12.5 %copy-start.3 = (s32[2,2]{1,0:T(2,128)S(1)}, s32[2,2]{1,0:T(2,128)}, u32[]{:S(2)}) copy-start(s32[2,2]{1,0:T(2,128)} %param.9) | copy-start | bytes 52
  140.8 12.7 %copy-start.4 = (f32[128]{0:T(128)S(1)}, f32[128]{0:T(128)}, u32[]{:S(2)}) copy-start(f32[128]{0:T(128)} %param.10) | copy-start | bytes 1540
  140.8 70.8 %copy-start.1 = (bf16[64,64,256]{2,1,0:T(8,128)(2,1)S(1)}, bf16[64,64,256]{2,1,0:T(8,128)(2,1)}, u32[]{:S(2)}) copy-start(bf16[64,64,256]{2,1,0:T(8,128)(2,1)} %param.7) | copy-start | bytes 6291460
  153.1 51.6 %slice-start = ((f32[512]{0:T(512)}), f32[64]{0:T(128)S(1)}, s32[]{:S(2)}) async-start(f32[512]{0:T(512)} %param.11), calls=%async_computation.4 | async-start | bytes 1024 | tf_op jit(solution)/shard_map/slice | solution.py:99
  153.1 51.7 %copy-start.5 = (f32[512]{0:T(512)S(1)}, f32[512]{0:T(512)}, u32[]{:S(2)}) copy-start(f32[512]{0:T(512)} %param.11) | copy-start | bytes 6148
  189.2 15.6 %collective-permute-start.10 = (f32[2,64,128]{2,1,0:T(8,128)S(1)}, f32[2,64,128]{2,1,0:T(8,128)S(1)}, u32[]{:S(2)}, u32[]{:S(2)}) collective-permute-start(f32[2,64,128]{2,1,0:T(8,128)S(1)} %bitcast.84), channel_id=1, source_target_pairs={{0,0},{1,8},{2,16},{3,24},{4,1},{5,9},{6,17},{7,25},{8,4},{9,12},{... | collective-permute-start | bytes 196616 | tf_op jit(solution)/shard_map/ppermute | solution.py:87
  195.7 11.1 %collective-permute-start.11 = (f32[2,64,128]{2,1,0:T(8,128)S(1)}, f32[2,64,128]{2,1,0:T(8,128)S(1)}, u32[]{:S(2)}, u32[]{:S(2)}) collective-permute-start(f32[2,64,128]{2,1,0:T(8,128)S(1)} %bitcast.83), channel_id=1, source_target_pairs={{0,1},{1,9},{2,17},{3,25},{4,4},{5,12},{6,20},{7,28},{8,5},{9,13},... | collective-permute-start | bytes 196616 | tf_op jit(solution)/shard_map/ppermute | solution.py:87
  198.8 8.0 %collective-permute-start.12 = (f32[2,64,128]{2,1,0:T(8,128)S(1)}, f32[2,64,128]{2,1,0:T(8,128)S(1)}, u32[]{:S(2)}, u32[]{:S(2)}) collective-permute-start(f32[2,64,128]{2,1,0:T(8,128)S(1)} %bitcast.82), channel_id=1, source_target_pairs={{0,4},{1,12},{2,20},{3,28},{4,5},{5,13},{6,21},{7,29},{8,0},{9,8},... | collective-permute-start | bytes 196616 | tf_op jit(solution)/shard_map/ppermute | solution.py:87
  202.4 8.5 %collective-permute-start.13 = (f32[2,64,128]{2,1,0:T(8,128)S(1)}, f32[2,64,128]{2,1,0:T(8,128)S(1)}, u32[]{:S(2)}, u32[]{:S(2)}) collective-permute-start(f32[2,64,128]{2,1,0:T(8,128)S(1)} %bitcast.81), channel_id=1, source_target_pairs={{0,5},{1,13},{2,21},{3,29},{4,0},{5,8},{6,16},{7,24},{8,1},{9,9},{... | collective-permute-start | bytes 196616 | tf_op jit(solution)/shard_map/ppermute | solution.py:87
  (1 other events, 1.6 us)
Sparse Core Ops, SparseCore 0:
  53.0 57.9 all-gather.2
  153.3 28.3 reduce-scatter.1

commit v9 on v8

--- a/solution.py
+++ b/solution.py
@@ -60,8 +60,14 @@
         part = jnp.einsum(
             "padq,bdq->pab", inter, right_group, preferred_element_type=jnp.float32
         )
-        part = lax.psum_scatter(part, "wide", scatter_dimension=0, tiled=True)
-        pairs_w = part.shape[0]
+        pairs_w = pairs // n_wide
+        part = part.reshape(n_wide, pairs_w, rows, span * b_blk)
+        summed = lax.dynamic_index_in_dim(part, w, 0, keepdims=False)
+        for shift in range(1, n_wide):
+            perm = [(i, (i + shift) % n_wide) for i in range(n_wide)]
+            piece = lax.dynamic_index_in_dim(part, (w + shift) % n_wide, 0, keepdims=False)
+            summed = summed + lax.ppermute(piece, "wide", perm)
+        part = summed
         part = part.reshape(pairs_w, rows, span, b_blk)
         flipped = jnp.concatenate(
             [part[:, :, (span - k) % span : (span - k) % span + 1] for k in range(span)] * 2, axis=2

time: 219 us -> 210 us (0.959)
  waiting for transfers between devices: 85.3 us -> 71.7 us
    reduce_scatter x1 -> x0, waiting for transfers between devices: 27.9 us -> none  [body(): part = lax.psum_scatter(part, 'wide', scatter_dimension=0, tiled=True)]
    ppermute x0 -> x3, waiting for transfers between devices: none -> 10.1 us  [body(): summed = summed + lax.ppermute(piece, 'wide', perm)]
    ppermute x3, waiting for transfers between devices: 13.7 us -> 20.4 us  [body(): piece = lax.ppermute(piece, 'narrow', perm)]
    ppermute x0 -> x3, starting transfers between devices: none -> 3.05 us  [body(): summed = summed + lax.ppermute(piece, 'wide', perm)]
  transfers between devices with their start and end apart: 17 -> 19, of which waited for: 7 -> 9; matrix products, arithmetic and copies ran while one was open for 20% -> 21% of each run, Pallas kernels for 0% -> 0%
where the time goes in v9:
time: 210 us; the launch traced here: 208 us
  waiting for transfers between devices  71.7 us (34%)
  local copies, waits for them, and re-layouts  50.1 us (24%)
  starting transfers between devices  41.3 us (20%)
  matrix products  27.3 us (13%)
  between operations  13.7 us (7%)
  other arithmetic  3.49 us (2%)
    all_to_all x1, waiting for transfers between devices, body(): left_recv = lax.all_to_all(left_send, 'narrow', 0, 0, tiled=True)  24.6 us
    unnamed x39, local copies, waits for them, and re-layouts  24.4 us
    ppermute x3, waiting for transfers between devices, body(): piece = lax.ppermute(piece, 'narrow', perm)  20.4 us
    dot_general x1, matrix products, body(): jnp.einsum('wkqia,pkwid->padq', left_all, amps_all, preferred_element_typ...  16.1 us
    ppermute x4, starting transfers between devices, body(): piece = lax.ppermute(piece, ('narrow', 'wide'), perm)  13.5 us
    dot_general x1, matrix products, body(): jnp.einsum('padq,bdq->pab', inter, right_group, preferred_element_type=jn...  11.1 us
    dynamic_slice x5, local copies, waits for them, and re-layouts, body(): piece = lax.dynamic_index_in_dim(right_split, dest, 2, keepdims=False)  10.4 us
    ppermute x3, waiting for transfers between devices, body(): summed = summed + lax.ppermute(piece, 'wide', perm)  10.1 us
  transfers between devices with their start and end apart: 19, of which 9 were waited for; matrix products, arithmetic and copies ran while one was open for 21% of the time, Pallas kernels for 0%

profile of v9, /device:TPU:5, one launch (start us, length us, event | category | flops | bytes accessed | tf_op | source)
XLA Modules:
  0.0 207.6 jit_solution(11532685280041711486)
XLA Ops:
  11.5 4.3 %reshape.91 = bf16[8,2,32768]{2,1,0:T(2,128)(2,1)} reshape(bf16[8,64,16,64]{3,2,1,0:T(8,128)(2,1)} %bitcast.82) | data formatting | bytes 2097152
  15.8 5.5 %all-to-all-start = ((bf16[8,2,32768]{2,1,0:T(2,128)(2,1)}), bf16[8,2,32768]{2,1,0:T(2,128)(2,1)S(1)}, u32[]{:S(2)}, u32[]{:S(2)}) async-start(bf16[8,2,32768]{2,1,0:T(2,128)(2,1)} %reshape.91), calls=%async_computation | async-start | bytes 2097152 | tf_op jit(solution)/shard_map/all_to_all | solution.py:33
  21.4 24.6 %all-to-all-done = bf16[8,2,32768]{2,1,0:T(2,128)(2,1)S(1)} async-done(((bf16[8,2,32768]{2,1,0:T(2,128)(2,1)}), bf16[8,2,32768]{2,1,0:T(2,128)(2,1)S(1)}, u32[]{:S(2)}, u32[]{:S(2)}) %all-to-all-start) | async-done | bytes 1048608 | tf_op jit(solution)/shard_map/all_to_all | solution.py:33
  48.4 4.4 %copy.48 = bf16[8,64,16,64]{3,2,1,0:T(8,128)(2,1)} copy(bf16[8,64,16,64]{1,2,3,0:T(8,128)(2,1)S(1)} %constant_dynamic-slice_fusion.9) | data formatting | bytes 2097152 | tf_op jit(solution)/shard_map/dynamic_slice | solution.py:35
  54.7 2.1 %collective-permute-start.2 = (bf16[16,64,128]{2,1,0:T(8,128)(2,1)S(1)}, bf16[16,64,128]{2,1,0:T(8,128)(2,1)}, u32[]{:S(2)}, u32[]{:S(2)}) collective-permute-start(bf16[16,64,128]{2,1,0:T(8,128)(2,1)S(1)} %copy-done.3), channel_id=1, source_target_pairs={{0,12},{4,16},{8,20},{12,24},{16,28},{20,0},{24,4},{28,8},{1,13},{... | collective-permute-start | bytes 786440 | tf_op jit(solution)/shard_map/ppermute | solution.py:26
  58.0 2.4 %collective-permute-start.4 = (bf16[16,64,128]{2,1,0:T(8,128)(2,1)S(1)}, bf16[16,64,128]{2,1,0:T(8,128)(2,1)}, u32[]{:S(2)}, u32[]{:S(2)}) collective-permute-start(bf16[16,64,128]{2,1,0:T(8,128)(2,1)S(1)} %copy-done.3), channel_id=1, source_target_pairs={{0,20},{4,24},{8,28},{12,0},{16,4},{20,8},{24,12},{28,16},{1,21},{... | collective-permute-start | bytes 786440 | tf_op jit(solution)/shard_map/ppermute | solution.py:26
  60.4 6.7 %copy.50 = bf16[64,128,256]{1,2,0:T(8,128)(2,1)} copy(bf16[64,128,256]{2,1,0:T(8,128)(2,1)} %param.8) | data formatting | bytes 8388608 | tf_op args[2]
  67.1 4.5 %constant_dynamic-slice_fusion.8 = (bf16[64,128,1,64]{1,3,2,0:T(8,128)(2,1)S(1)}, bf16[64,128,1,64]{1,3,2,0:T(8,128)(2,1)}, bf16[64,128,1,64]{1,3,2,0:T(8,128)(2,1)S(1)}, bf16[64,128,1,64]{1,3,2,0:T(8,128)(2,1)S(1)}) fusion(bf16[64,128,4,64]{1,3,2,0:T(8,128)(2,1)} %bitcast.81, s32[]{:T(128)S(6)} %select_n.163, s32[]{:T(128)S(6)} %select_n.169, ...), kind=kLoop, calls=%fused_computation.57 | loop fusion | bytes 8388624 | tf_op jit(solution)/shard_map/jit(dynamic_index_in_dim)/dynamic_slice | solution.py:45
  72.3 2.9 %copy.74 = bf16[64,128,1,64]{1,0,3,2:T(8,128)(2,1)} copy(bf16[64,128,1,64]{1,3,2,0:T(8,128)(2,1)} %get-tuple-element.10) | data formatting | bytes 2097152 | tf_op jit(solution)/shard_map/jit(dynamic_index_in_dim)/dynamic_slice | solution.py:45
  83.7 2.8 %collective-permute-done.2 = bf16[16,64,128]{2,1,0:T(8,128)(2,1)} collective-permute-done((bf16[16,64,128]{2,1,0:T(8,128)(2,1)S(1)}, bf16[16,64,128]{2,1,0:T(8,128)(2,1)}, u32[]{:S(2)}, u32[]{:S(2)}) %collective-permute-start.2) | collective-permute-done | bytes 262176 | tf_op jit(solution)/shard_map/ppermute | solution.py:26
  86.5 5.3 %collective-permute-start.9 = (bf16[64,128,64]{1,0,2:T(8,128)(2,1)}, bf16[64,128,64]{1,0,2:T(8,128)(2,1)}, u32[]{:S(2)}, u32[]{:S(2)}) collective-permute-start(bf16[64,128,64]{1,0,2:T(8,128)(2,1)} %bitcast.89), channel_id=1, source_target_pairs={{0,12},{4,0},{8,4},{12,8},{16,28},{20,16},{24,20},{28,24},{1,13},{... | collective-permute-start | bytes 3145736 | tf_op jit(solution)/shard_map/ppermute | solution.py:52
  95.2 4.2 %collective-permute-start.7 = (bf16[64,128,64]{1,0,2:T(8,128)(2,1)S(1)}, bf16[64,128,64]{1,0,2:T(8,128)(2,1)}, u32[]{:S(2)}, u32[]{:S(2)}) collective-permute-start(bf16[64,128,64]{1,0,2:T(8,128)(2,1)S(1)} %bitcast.87), channel_id=1, source_target_pairs={{0,4},{4,8},{8,12},{12,0},{16,20},{20,24},{24,28},{28,16},{1,5},{5... | collective-permute-start | bytes 3145736 | tf_op jit(solution)/shard_map/ppermute | solution.py:52
  102.5 8.5 %all-gather.3.cloned.1.call-done = bf16[32,64,16,64]{3,2,1,0:T(8,128)(2,1)} async-done(((bf16[8,64,16,64]{3,2,1,0:T(8,128)(2,1)}), bf16[32,64,16,64]{3,2,1,0:T(8,128)(2,1)}) %all-gather.3.cloned.1.call-update) | async-done | bytes 4194320 | tf_op jit(solution)/shard_map/all_gather | solution.py:38
  111.0 16.1 %fusion.3 = bf16[16,128,64,64,1,1]{1,3,5,0,2,4:T(8,128)(2,1)} fusion(bf16[4,8,64,16,64,1]{4,3,2,1,0,5:T(8,128)(2,1)} %bitcast.97, bf16[16,8,4,16,128]{4,3,2,0,1:T(8,128)(2,1)} %constant_dynamic-update-slice_fusion), kind=kOutput, calls=%fused_computation.3 | convolution fusion | flops 8589934592 | bytes 23068672 | tf_op jit(solution)/shard_map/wkqia,pkwid->padq/dot_general | solution.py:55
  127.1 20.4 %collective-permute-done.8 = bf16[64,128,64]{1,0,2:T(8,128)(2,1)} collective-permute-done((bf16[64,128,64]{1,0,2:T(8,128)(2,1)}, bf16[64,128,64]{1,0,2:T(8,128)(2,1)}, u32[]{:S(2)}, u32[]{:S(2)}) %collective-permute-start.8) | collective-permute-done | bytes 1048608 | tf_op jit(solution)/shard_map/ppermute | solution.py:52
  147.5 11.1 %fusion.1 = f32[16,64,256,1]{2,1,3,0:T(8,128)S(1)} fusion(bf16[16,128,64,64,1,1]{1,3,5,0,2,4:T(8,128)(2,1)} %fusion.3, bf16[64,128,64]{1,0,2:T(8,128)(2,1)} %collective-permute-done.9, bf16[64,128,64]{1,0,2:T(8,128)(2,1)} %collective-permute-done.8, bf16[64,128,64]{1,0,2:T(8,128)(2,1)} %collective-permute-done.7, bf16[64,128,64]{1,0,2:T(8,128)(2,1)S(1)} %bitcast.86), kind=kOutput, calls=%fused_computation.2 | convolution fusion | flops 4311744512 | bytes 22020096 | tf_op jit(solution)/shard_map/padq,bdq->pab/dot_general | solution.py:60
  163.0 4.7 %collective-permute-done.12 = f32[4,64,256]{2,1,0:T(8,128)} collective-permute-done((f32[4,64,256]{2,1,0:T(8,128)}, f32[4,64,256]{2,1,0:T(8,128)}, u32[]{:S(2)}, u32[]{:S(2)}) %collective-permute-start.12) | collective-permute-done | bytes 262176 | tf_op jit(solution)/shard_map/ppermute | solution.py:69
  169.5 3.6 %collective-permute-done.10 = f32[4,64,256]{2,1,0:T(8,128)} collective-permute-done((f32[4,64,256]{2,1,0:T(8,128)S(1)}, f32[4,64,256]{2,1,0:T(8,128)}, u32[]{:S(2)}, u32[]{:S(2)}) %collective-permute-start.10) | collective-permute-done | bytes 262176 | tf_op jit(solution)/shard_map/ppermute | solution.py:69
  175.5 2.8 %concatenate.16 = f32[4,64,8,64]{3,2,1,0:T(8,128)S(1)} concatenate(f32[4,64,1,64]{3,2,1,0:T(1,128)} %get-tuple-element.19, f32[4,64,1,64]{3,2,1,0:T(1,128)S(1)} %get-tuple-element.18, f32[4,64,1,64]{3,2,1,0:T(1,128)S(1)} %get-tuple-element.17, f32[4,64,1,64]{3,2,1,0:T(1,128)S(1)} %get-tuple-element.16, f32[4,64,1,64]{3,2,1,0:T(1,128)} %get-tuple-element.19, ...), dimensions={2} | concatenate | bytes 1048576 | tf_op jit(solution)/shard_map/concatenate | solution.py:72
  181.0 2.9 %collective-permute-start.16 = (f32[2,64,128]{2,1,0:T(8,128)S(1)}, f32[2,64,128]{2,1,0:T(8,128)S(1)}, u32[]{:S(2)}, u32[]{:S(2)}) collective-permute-start(f32[2,64,128]{2,1,0:T(8,128)S(1)} %bitcast.96), channel_id=1, source_target_pairs={{0,5},{1,13},{2,21},{3,29},{4,0},{5,8},{6,16},{7,24},{8,1},{9,9},{... | collective-permute-start | bytes 196616 | tf_op jit(solution)/shard_map/ppermute | solution.py:93
  183.9 6.7 %collective-permute-start.15 = (f32[2,64,128]{2,1,0:T(8,128)S(1)}, f32[2,64,128]{2,1,0:T(8,128)S(1)}, u32[]{:S(2)}, u32[]{:S(2)}) collective-permute-start(f32[2,64,128]{2,1,0:T(8,128)S(1)} %bitcast.95), channel_id=1, source_target_pairs={{0,4},{1,12},{2,20},{3,28},{4,5},{5,13},{6,21},{7,29},{8,0},{9,8},... | collective-permute-start | bytes 196616 | tf_op jit(solution)/shard_map/ppermute | solution.py:93
  190.6 1.9 collective-permute-start.13
  192.5 1.9 collective-permute-start.14
  194.6 5.0 %collective-permute-done.13 = f32[2,64,128]{2,1,0:T(8,128)S(1)} collective-permute-done((f32[2,64,128]{2,1,0:T(8,128)S(1)}, f32[2,64,128]{2,1,0:T(8,128)S(1)}, u32[]{:S(2)}, u32[]{:S(2)}) %collective-permute-start.13) | collective-permute-done | bytes 65568 | tf_op jit(solution)/shard_map/ppermute | solution.py:93
  (85 shorter events, 38.4 us)
Async XLA Ops:
  15.8 30.1 %all-to-all-start = ((bf16[8,2,32768]{2,1,0:T(2,128)(2,1)}), bf16[8,2,32768]{2,1,0:T(2,128)(2,1)S(1)}, u32[]{:S(2)}, u32[]{:S(2)}) async-start(bf16[8,2,32768]{2,1,0:T(2,128)(2,1)} %reshape.91), calls=%async_computation | async-start | bytes 2097152 | tf_op jit(solution)/shard_map/all_to_all | solution.py:33
  21.3 89.7 %all-gather.3.cloned.1.call-start = ((), (), s32[]{:S(2)}) async-start(), calls=%async_computation.1 | async-start | bytes 10485760 | tf_op jit(solution)/shard_map/all_gather | solution.py:38
  52.9 25.4 %collective-permute-start = (bf16[16,64,128]{2,1,0:T(8,128)(2,1)S(1)}, bf16[16,64,128]{2,1,0:T(8,128)(2,1)}, u32[]{:S(2)}, u32[]{:S(2)}) collective-permute-start(bf16[16,64,128]{2,1,0:T(8,128)(2,1)S(1)} %copy-done.3), channel_id=1, source_target_pairs={{0,4},{4,8},{8,12},{12,16},{16,20},{20,24},{24,28},{28,0},{1,5},{5... | collective-permute-start | bytes 786440 | tf_op jit(solution)/shard_map/ppermute | solution.py:26
  54.7 26.5 %collective-permute-start.1 = (bf16[16,64,128]{2,1,0:T(8,128)(2,1)S(1)}, bf16[16,64,128]{2,1,0:T(8,128)(2,1)}, u32[]{:S(2)}, u32[]{:S(2)}) collective-permute-start(bf16[16,64,128]{2,1,0:T(8,128)(2,1)S(1)} %copy-done.3), channel_id=1, source_target_pairs={{0,8},{4,12},{8,16},{12,20},{16,24},{20,28},{24,0},{28,4},{1,9},{5... | collective-permute-start | bytes 786440 | tf_op jit(solution)/shard_map/ppermute | solution.py:26
  54.7 31.8 %collective-permute-start.2 = (bf16[16,64,128]{2,1,0:T(8,128)(2,1)S(1)}, bf16[16,64,128]{2,1,0:T(8,128)(2,1)}, u32[]{:S(2)}, u32[]{:S(2)}) collective-permute-start(bf16[16,64,128]{2,1,0:T(8,128)(2,1)S(1)} %copy-done.3), channel_id=1, source_target_pairs={{0,12},{4,16},{8,20},{12,24},{16,28},{20,0},{24,4},{28,8},{1,13},{... | collective-permute-start | bytes 786440 | tf_op jit(solution)/shard_map/ppermute | solution.py:26
  56.9 36.6 %collective-permute-start.3 = (bf16[16,64,128]{2,1,0:T(8,128)(2,1)S(1)}, bf16[16,64,128]{2,1,0:T(8,128)(2,1)}, u32[]{:S(2)}, u32[]{:S(2)}) collective-permute-start(bf16[16,64,128]{2,1,0:T(8,128)(2,1)S(1)} %copy-done.3), channel_id=1, source_target_pairs={{0,16},{4,20},{8,24},{12,28},{16,0},{20,4},{24,8},{28,12},{1,17},{... | collective-permute-start | bytes 786440 | tf_op jit(solution)/shard_map/ppermute | solution.py:26
  58.0 37.1 %collective-permute-start.4 = (bf16[16,64,128]{2,1,0:T(8,128)(2,1)S(1)}, bf16[16,64,128]{2,1,0:T(8,128)(2,1)}, u32[]{:S(2)}, u32[]{:S(2)}) collective-permute-start(bf16[16,64,128]{2,1,0:T(8,128)(2,1)S(1)} %copy-done.3), channel_id=1, source_target_pairs={{0,20},{4,24},{8,28},{12,0},{16,4},{20,8},{24,12},{28,16},{1,21},{... | collective-permute-start | bytes 786440 | tf_op jit(solution)/shard_map/ppermute | solution.py:26
  78.2 22.8 %collective-permute-start.5 = (bf16[16,64,128]{2,1,0:T(8,128)(2,1)S(1)}, bf16[16,64,128]{2,1,0:T(8,128)(2,1)S(1)}, u32[]{:S(2)}, u32[]{:S(2)}) collective-permute-start(bf16[16,64,128]{2,1,0:T(8,128)(2,1)S(1)} %copy-done.3), channel_id=1, source_target_pairs={{0,24},{4,28},{8,0},{12,4},{16,8},{20,12},{24,16},{28,20},{1,25},{... | collective-permute-start | bytes 786440 | tf_op jit(solution)/shard_map/ppermute | solution.py:26
  81.2 20.5 %collective-permute-start.6 = (bf16[16,64,128]{2,1,0:T(8,128)(2,1)S(1)}, bf16[16,64,128]{2,1,0:T(8,128)(2,1)S(1)}, u32[]{:S(2)}, u32[]{:S(2)}) collective-permute-start(bf16[16,64,128]{2,1,0:T(8,128)(2,1)S(1)} %copy-done.3), channel_id=1, source_target_pairs={{0,28},{4,0},{8,4},{12,8},{16,12},{20,16},{24,20},{28,24},{1,29},{... | collective-permute-start | bytes 786440 | tf_op jit(solution)/shard_map/ppermute | solution.py:26
  86.5 40.6 %collective-permute-start.9 = (bf16[64,128,64]{1,0,2:T(8,128)(2,1)}, bf16[64,128,64]{1,0,2:T(8,128)(2,1)}, u32[]{:S(2)}, u32[]{:S(2)}) collective-permute-start(bf16[64,128,64]{1,0,2:T(8,128)(2,1)} %bitcast.89), channel_id=1, source_target_pairs={{0,12},{4,0},{8,4},{12,8},{16,28},{20,16},{24,20},{28,24},{1,13},{... | collective-permute-start | bytes 3145736 | tf_op jit(solution)/shard_map/ppermute | solution.py:52
  93.5 54.0 %collective-permute-start.8 = (bf16[64,128,64]{1,0,2:T(8,128)(2,1)}, bf16[64,128,64]{1,0,2:T(8,128)(2,1)}, u32[]{:S(2)}, u32[]{:S(2)}) collective-permute-start(bf16[64,128,64]{1,0,2:T(8,128)(2,1)} %bitcast.88), channel_id=1, source_target_pairs={{0,8},{4,12},{8,0},{12,4},{16,24},{20,28},{24,16},{28,20},{1,9},{5... | collective-permute-start | bytes 3145736 | tf_op jit(solution)/shard_map/ppermute | solution.py:52
  95.2 52.4 %collective-permute-start.7 = (bf16[64,128,64]{1,0,2:T(8,128)(2,1)S(1)}, bf16[64,128,64]{1,0,2:T(8,128)(2,1)}, u32[]{:S(2)}, u32[]{:S(2)}) collective-permute-start(bf16[64,128,64]{1,0,2:T(8,128)(2,1)S(1)} %bitcast.87), channel_id=1, source_target_pairs={{0,4},{4,8},{8,12},{12,0},{16,20},{20,24},{24,28},{28,16},{1,5},{5... | collective-permute-start | bytes 3145736 | tf_op jit(solution)/shard_map/ppermute | solution.py:52
  147.5 15.1 %copy-start.4 = (s32[2,2]{1,0:T(2,128)S(1)}, s32[2,2]{1,0:T(2,128)}, u32[]{:S(2)}) copy-start(s32[2,2]{1,0:T(2,128)} %param.9) | copy-start | bytes 52
  147.5 15.3 %copy-start.5 = (f32[128]{0:T(128)S(1)}, f32[128]{0:T(128)}, u32[]{:S(2)}) copy-start(f32[128]{0:T(128)} %param.10) | copy-start | bytes 1540
  158.7 42.0 %copy-start.1 = (bf16[64,64,256]{2,1,0:T(8,128)(2,1)S(1)}, bf16[64,64,256]{2,1,0:T(8,128)(2,1)}, u32[]{:S(2)}) copy-start(bf16[64,64,256]{2,1,0:T(8,128)(2,1)} %param.7) | copy-start | bytes 6291460
  159.5 34.9 %slice-start = ((f32[512]{0:T(512)}), f32[64]{0:T(128)S(1)}, s32[]{:S(2)}) async-start(f32[512]{0:T(512)} %param.11), calls=%async_computation.2 | async-start | bytes 1024 | tf_op jit(solution)/shard_map/slice | solution.py:105
  159.5 35.0 %copy-start.6 = (f32[512]{0:T(512)S(1)}, f32[512]{0:T(512)}, u32[]{:S(2)}) copy-start(f32[512]{0:T(512)} %param.11) | copy-start | bytes 6148
  159.6 8.2 %collective-permute-start.12 = (f32[4,64,256]{2,1,0:T(8,128)}, f32[4,64,256]{2,1,0:T(8,128)}, u32[]{:S(2)}, u32[]{:S(2)}) collective-permute-start(f32[4,64,256]{2,1,0:T(8,128)} %get-tuple-element.14), channel_id=1, source_target_pairs={{0,3},{1,0},{2,1},{3,2},{4,7},{5,4},{6,5},{7,6},{8,11},{9,8},{10,9... | collective-permute-start | bytes 786440 | tf_op jit(solution)/shard_map/ppermute | solution.py:69
  160.9 8.6 %collective-permute-start.11 = (f32[4,64,256]{2,1,0:T(8,128)}, f32[4,64,256]{2,1,0:T(8,128)}, u32[]{:S(2)}, u32[]{:S(2)}) collective-permute-start(f32[4,64,256]{2,1,0:T(8,128)} %get-tuple-element.15), channel_id=1, source_target_pairs={{0,2},{1,3},{2,0},{3,1},{4,6},{5,7},{6,4},{7,5},{8,10},{9,11},{10,... | collective-permute-start | bytes 786440 | tf_op jit(solution)/shard_map/ppermute | solution.py:69
  161.1 11.9 %collective-permute-start.10 = (f32[4,64,256]{2,1,0:T(8,128)S(1)}, f32[4,64,256]{2,1,0:T(8,128)}, u32[]{:S(2)}, u32[]{:S(2)}) collective-permute-start(f32[4,64,256]{2,1,0:T(8,128)S(1)} %get-tuple-element.13), channel_id=1, source_target_pairs={{0,1},{1,2},{2,3},{3,0},{4,5},{5,6},{6,7},{7,4},{8,9},{9,10},{10,1... | collective-permute-start | bytes 786440 | tf_op jit(solution)/shard_map/ppermute | solution.py:69
  181.0 13.7 %collective-permute-start.16 = (f32[2,64,128]{2,1,0:T(8,128)S(1)}, f32[2,64,128]{2,1,0:T(8,128)S(1)}, u32[]{:S(2)}, u32[]{:S(2)}) collective-permute-start(f32[2,64,128]{2,1,0:T(8,128)S(1)} %bitcast.96), channel_id=1, source_target_pairs={{0,5},{1,13},{2,21},{3,29},{4,0},{5,8},{6,16},{7,24},{8,1},{9,9},{... | collective-permute-start | bytes 196616 | tf_op jit(solution)/shard_map/ppermute | solution.py:93
  183.9 10.8 %collective-permute-start.15 = (f32[2,64,128]{2,1,0:T(8,128)S(1)}, f32[2,64,128]{2,1,0:T(8,128)S(1)}, u32[]{:S(2)}, u32[]{:S(2)}) collective-permute-start(f32[2,64,128]{2,1,0:T(8,128)S(1)} %bitcast.95), channel_id=1, source_target_pairs={{0,4},{1,12},{2,20},{3,28},{4,5},{5,13},{6,21},{7,29},{8,0},{9,8},... | collective-permute-start | bytes 196616 | tf_op jit(solution)/shard_map/ppermute | solution.py:93
  190.6 9.1 %collective-permute-start.13 = (f32[2,64,128]{2,1,0:T(8,128)S(1)}, f32[2,64,128]{2,1,0:T(8,128)S(1)}, u32[]{:S(2)}, u32[]{:S(2)}) collective-permute-start(f32[2,64,128]{2,1,0:T(8,128)S(1)} %bitcast.94), channel_id=1, source_target_pairs={{0,0},{1,8},{2,16},{3,24},{4,1},{5,9},{6,17},{7,25},{8,4},{9,12},{... | collective-permute-start | bytes 196616 | tf_op jit(solution)/shard_map/ppermute | solution.py:93
  192.5 7.5 %collective-permute-start.14 = (f32[2,64,128]{2,1,0:T(8,128)S(1)}, f32[2,64,128]{2,1,0:T(8,128)S(1)}, u32[]{:S(2)}, u32[]{:S(2)}) collective-permute-start(f32[2,64,128]{2,1,0:T(8,128)S(1)} %bitcast.93), channel_id=1, source_target_pairs={{0,1},{1,9},{2,17},{3,25},{4,4},{5,12},{6,20},{7,28},{8,5},{9,13},... | collective-permute-start | bytes 196616 | tf_op jit(solution)/shard_map/ppermute | solution.py:93
  (3 other events, 16.9 us)
Sparse Core Ops, SparseCore 0:
  53.0 57.9 all-gather.2

commit v10 on v9

--- a/solution.py
+++ b/solution.py
@@ -20,37 +20,47 @@
         pairs = amps.shape[0]
         vir_total = b_blk * n_narrow
 
-        amps_blocks = [amps]
-        for shift in range(1, n_narrow):
-            perm = [(i, (i + shift) % n_narrow) for i in range(n_narrow)]
-            amps_blocks.append(lax.ppermute(amps, "narrow", perm))
+        right_split = right_fit.reshape(b_blk, d_blk, span, q_blk)
+        amps_size = amps.size
+
+        def perm_of(shift, step):
+            return [
+                (gg * span + i, ((gg + step) % GROUPS) * span + (i + shift) % span)
+                for gg in range(GROUPS)
+                for i in range(span)
+            ]
+
+        amps_blocks = []
+        chunks = []
+        for step in range(GROUPS):
+            for shift in range(span):
+                if step == 0 and shift == 0:
+                    amps_blocks.append(amps)
+                    chunks.append(lax.dynamic_index_in_dim(right_split, r, 2, keepdims=False))
+                elif step == 0:
+                    piece = lax.dynamic_index_in_dim(right_split, (r + shift) % span, 2, keepdims=False)
+                    both = jnp.concatenate([amps.reshape(-1), piece.reshape(-1)])
+                    both = lax.ppermute(both, "narrow", perm_of(shift, 0))
+                    amps_blocks.append(both[:amps_size].reshape(amps.shape))
+                    chunks.append(both[amps_size:].reshape(piece.shape))
+                else:
+                    amps_blocks.append(lax.ppermute(amps, "narrow", perm_of(shift, step)))
         amps_all = jnp.stack(amps_blocks, axis=1)
+
+        def rotate_back(x, by, size, axis):
+            rev = [lax.slice_in_dim(x, (size - j) % size, (size - j) % size + 1, axis=axis) for j in range(size)]
+            return lax.dynamic_slice_in_dim(jnp.concatenate(rev * 2, axis=axis), size - by, size, axis)
 
         c_sub = c_blk // n_wide
         left_part = lax.dynamic_slice_in_dim(left_fit, w * c_sub, c_sub, 1)
         left_part = left_part.reshape(rows, c_sub, span, q_blk).transpose(2, 3, 1, 0)
         left_send = jnp.concatenate([left_part] * GROUPS, axis=0)
         left_recv = lax.all_to_all(left_send, "narrow", 0, 0, tiled=True)
-        left_rev = [left_recv[(n_narrow - j) % n_narrow][None] for j in range(n_narrow)]
-        left_recv = lax.dynamic_slice_in_dim(
-            jnp.concatenate(left_rev * 2, axis=0), n_narrow - n, n_narrow, 0
-        )
+        left_recv = left_recv.reshape((GROUPS, span) + left_recv.shape[1:])
+        left_recv = rotate_back(rotate_back(left_recv, r, span, 1), g, GROUPS, 0)
+        left_recv = left_recv.reshape((n_narrow,) + left_recv.shape[2:])
         left_all = lax.all_gather(left_recv, "wide", axis=0, tiled=False)
         amps_all = amps_all.reshape(pairs, n_narrow, n_wide, c_sub, amps.shape[2])
-
-        right_split = right_fit.reshape(b_blk, d_blk, span, q_blk)
-        chunks = []
-        for shift in range(span):
-            dest = (r + shift) % span
-            piece = lax.dynamic_index_in_dim(right_split, dest, 2, keepdims=False)
-            if shift:
-                perm = [
-                    (gg * span + i, gg * span + (i + shift) % span)
-                    for gg in range(GROUPS)
-                    for i in range(span)
-                ]
-                piece = lax.ppermute(piece, "narrow", perm)
-            chunks.append(piece)
 
         inter = jnp.einsum(
             "wkqia,pkwid->padq", left_all, amps_all, preferred_element_type=jnp.float32

time: 210 us -> 240 us (1.14)
  local copies, waits for them, and re-layouts: 50.1 us -> 74.8 us
  other arithmetic: 3.49 us -> 8.57 us
  waiting for transfers between devices: 71.7 us -> 74.7 us
    ppermute x10 -> x7, waiting for transfers between devices: 23.2 us -> 55.1 us  [the longest x3 46.4 us: body(): both = lax.ppermute(both, 'narrow', perm_of(shift, 0))]
    all_to_all x1, waiting for transfers between devices: 24.6 us -> 3.18 us  [body(): left_recv = lax.all_to_all(left_send, 'narrow', 0, 0, tiled=True)]
    slice x0 -> x14, local copies, waits for them, and re-layouts: none -> 11.3 us  [the longest x11 10.3 us: body(): chunks.append(both[amps_size:].reshape(piece.shape))]
    all_gather x1, waiting for transfers between devices: 8.48 us -> 0.01 us  [body(): left_all = lax.all_gather(left_recv, 'wide', axis=0, tiled=False)]
    ppermute x10 -> x7, starting transfers between devices: 19.2 us -> 13 us  [the longest x4 10 us: body(): amps_blocks.append(lax.ppermute(amps, 'narrow', perm_of(shift, step)))]
    reshape x0 -> x3, local copies, waits for them, and re-layouts: none -> 5.32 us  [body(): both = jnp.concatenate([amps.reshape(-1), piece.reshape(-1)])]
    concatenate x0 -> x2, other arithmetic: none -> 5.32 us  [the longest x1 2.98 us: body(): both = jnp.concatenate([amps.reshape(-1), piece.reshape(-1)])]
    ppermute x4, starting transfers between devices: 13.5 us -> 17.7 us  [body(): piece = lax.ppermute(piece, ('narrow', 'wide'), perm)]
  transfers between devices with their start and end apart: 19 -> 16, of which waited for: 9 -> 10; matrix products, arithmetic and copies ran while one was open for 21% -> 20% of each run, Pallas kernels for 0% -> 0%
where the time goes in v10:
time: 240 us; the launch traced here: 239 us
  local copies, waits for them, and re-layouts  74.8 us (31%)
  waiting for transfers between devices  74.7 us (31%)
  starting transfers between devices  39.6 us (16%)
  matrix products  27.8 us (12%)
  between operations  13.8 us (6%)
  other arithmetic  8.57 us (4%)
    ppermute x3, waiting for transfers between devices, body(): both = lax.ppermute(both, 'narrow', perm_of(shift, 0))  46.4 us
    unnamed x39, local copies, waits for them, and re-layouts  25.4 us
    ppermute x4, starting transfers between devices, body(): piece = lax.ppermute(piece, ('narrow', 'wide'), perm)  17.7 us
    dot_general x1, matrix products, body(): jnp.einsum('wkqia,pkwid->padq', left_all, amps_all, preferred_element_typ...  16.3 us
    dot_general x1, matrix products, body(): jnp.einsum('padq,bdq->pab', inter, right_group, preferred_element_type=jn...  11.5 us
    ppermute x3, waiting for transfers between devices, body(): summed = summed + lax.ppermute(piece, 'wide', perm)  11.3 us
    slice x11, local copies, waits for them, and re-layouts, body(): chunks.append(both[amps_size:].reshape(piece.shape))  10.3 us
    ppermute x4, starting transfers between devices, body(): amps_blocks.append(lax.ppermute(amps, 'narrow', perm_of(shift, step)))  10 us
  transfers between devices with their start and end apart: 16, of which 10 were waited for; matrix products, arithmetic and copies ran while one was open for 20% of the time, Pallas kernels for 0%

profile of v10, /device:TPU:5, one launch (start us, length us, event | category | flops | bytes accessed | tf_op | source)
XLA Modules:
  0.0 239.2 jit_solution(16112076313452175335)
XLA Ops:
  13.9 4.4 %reshape.166 = bf16[8,2,32768]{2,1,0:T(2,128)(2,1)} reshape(bf16[8,64,16,64]{3,2,1,0:T(8,128)(2,1)} %bitcast.83) | data formatting | bytes 2097152
  18.3 5.5 %all-to-all-start = ((bf16[8,2,32768]{2,1,0:T(2,128)(2,1)}), bf16[8,2,32768]{2,1,0:T(2,128)(2,1)}, u32[]{:S(2)}, u32[]{:S(2)}) async-start(bf16[8,2,32768]{2,1,0:T(2,128)(2,1)} %reshape.166), calls=%async_computation | async-start | bytes 2097152 | tf_op jit(solution)/shard_map/all_to_all | solution.py:58
  23.9 6.4 %copy.39 = bf16[64,128,256]{1,2,0:T(8,128)(2,1)} copy(bf16[64,128,256]{2,1,0:T(8,128)(2,1)} %param.8) | data formatting | bytes 8388608 | tf_op args[2]
  30.3 4.6 %constant_dynamic-slice_fusion.5 = (bf16[64,128,1,64]{1,3,2,0:T(8,128)(2,1)}, bf16[64,128,1,64]{1,3,2,0:T(8,128)(2,1)S(1)}, bf16[64,128,1,64]{1,3,2,0:T(8,128)(2,1)}, bf16[64,128,1,64]{1,3,2,0:T(8,128)(2,1)}) fusion(bf16[64,128,4,64]{1,3,2,0:T(8,128)(2,1)} %bitcast.81, s32[]{:T(128)S(6)} %select_n.172, s32[]{:T(128)S(6)} %select_n.167, s32[]{:T(128)S(6)} %select_n.165, ...), kind=kLoop, calls=%fused_computation.49 | loop fusion | bytes 8388624 | tf_op jit(solution)/shard_map/jit(dynamic_index_in_dim)/dynamic_slice | solution.py:39
  45.3 3.2 %all-to-all-done = bf16[8,2,32768]{2,1,0:T(2,128)(2,1)} async-done(((bf16[8,2,32768]{2,1,0:T(2,128)(2,1)}), bf16[8,2,32768]{2,1,0:T(2,128)(2,1)}, u32[]{:S(2)}, u32[]{:S(2)}) %all-to-all-start) | async-done | bytes 1048608 | tf_op jit(solution)/shard_map/all_to_all | solution.py:58
  48.5 3.1 %reshape.167 = bf16[8,64,16,64]{3,2,1,0:T(8,128)(2,1)S(1)} reshape(bf16[8,2,32768]{2,1,0:T(2,128)(2,1)} %all-to-all-done) | data formatting | bytes 2097152
  54.9 5.3 %copy.44 = bf16[2,4,64,16,64]{4,3,2,1,0:T(8,128)(2,1)} copy(bf16[2,4,64,16,64]{2,3,4,1,0:T(8,128)(2,1)} %fusion.11) | data formatting | bytes 2097152 | tf_op jit(solution)/shard_map/dynamic_slice | solution.py:52
  61.8 3.0 %pad_maximum_fusion.1 = (bf16[655360]{0:T(1024)(128)(2,1)}, bf16[655360]{0:T(1024)(128)(2,1)}, bf16[655360]{0:T(1024)(128)(2,1)}) fusion(bf16[131072]{0:T(1024)(128)(2,1)} %bitcast.1, bf16[524288]{0:T(1024)(128)(2,1)S(1)} %reshape.153, bf16[524288]{0:T(1024)(128)(2,1)S(1)} %copy-done.2, bf16[524288]{0:T(1024)(128)(2,1)S(1)} %copy-done.3), kind=kLoop, calls=%fused_computation.17 | loop fusion | flops 6553600 | bytes 7340032 | tf_op jit(solution)/shard_map/concatenate | solution.py:42
  70.1 3.0 %copy.66 = bf16[64,128,1,64]{1,0,3,2:T(8,128)(2,1)} copy(bf16[64,128,1,64]{1,3,2,0:T(8,128)(2,1)} %get-tuple-element.9) | data formatting | bytes 2097152 | tf_op jit(solution)/shard_map/jit(dynamic_index_in_dim)/dynamic_slice | solution.py:39
  74.9 24.8 %collective-permute-done = bf16[655360]{0:T(1024)(128)(2,1)S(1)} collective-permute-done((bf16[655360]{0:T(1024)(128)(2,1)}, bf16[655360]{0:T(1024)(128)(2,1)S(1)}, u32[]{:S(2)}, u32[]{:S(2)}) %collective-permute-start) | collective-permute-done | bytes 1310752 | tf_op jit(solution)/shard_map/ppermute | solution.py:43
  99.7 4.5 %collective-permute-start.6 = (bf16[16,64,128]{2,1,0:T(8,128)(2,1)}, bf16[16,64,128]{2,1,0:T(8,128)(2,1)}, u32[]{:S(2)}, u32[]{:S(2)}) collective-permute-start(bf16[16,64,128]{2,1,0:T(8,128)(2,1)} %param.6), channel_id=1, source_target_pairs={{0,28},{4,16},{8,20},{12,24},{16,12},{20,0},{24,4},{28,8},{1,29},{... | collective-permute-start | bytes 786440 | tf_op jit(solution)/shard_map/ppermute | solution.py:47
  106.6 3.1 %collective-permute-start.5 = (bf16[16,64,128]{2,1,0:T(8,128)(2,1)}, bf16[16,64,128]{2,1,0:T(8,128)(2,1)}, u32[]{:S(2)}, u32[]{:S(2)}) collective-permute-start(bf16[16,64,128]{2,1,0:T(8,128)(2,1)} %param.6), channel_id=1, source_target_pairs={{0,24},{4,28},{8,16},{12,20},{16,8},{20,12},{24,0},{28,4},{1,25},{... | collective-permute-start | bytes 786440 | tf_op jit(solution)/shard_map/ppermute | solution.py:47
  110.5 19.8 %collective-permute-done.2 = bf16[655360]{0:T(1024)(128)(2,1)} collective-permute-done((bf16[655360]{0:T(1024)(128)(2,1)}, bf16[655360]{0:T(1024)(128)(2,1)}, u32[]{:S(2)}, u32[]{:S(2)}) %collective-permute-start.2) | collective-permute-done | bytes 1310752 | tf_op jit(solution)/shard_map/ppermute | solution.py:43
  132.1 6.3 %collective-permute-done.3 = bf16[16,64,128]{2,1,0:T(8,128)(2,1)S(1)} collective-permute-done((bf16[16,64,128]{2,1,0:T(8,128)(2,1)}, bf16[16,64,128]{2,1,0:T(8,128)(2,1)S(1)}, u32[]{:S(2)}, u32[]{:S(2)}) %collective-permute-start.3) | collective-permute-done | bytes 262176 | tf_op jit(solution)/shard_map/ppermute | solution.py:47
  157.0 16.3 %fusion.3 = bf16[16,128,64,64,1,1]{1,3,5,2,0,4:T(8,128)(2,1)} fusion(bf16[16,8,4,16,128]{4,3,2,0,1:T(8,128)(2,1)} %constant_dynamic-update-slice_fusion, bf16[4,8,64,16,64]{4,3,2,1,0:T(8,128)(2,1)} %all-gather.2.cloned.1.call-done), kind=kOutput, calls=%fused_computation.3 | convolution fusion | flops 8589934592 | bytes 23068672 | tf_op jit(solution)/shard_map/wkqia,pkwid->padq/dot_general | solution.py:65
  173.3 11.5 %fusion.1 = f32[16,64,256,1]{2,1,0,3:T(8,128)} fusion(bf16[16,128,64,64,1,1]{1,3,5,2,0,4:T(8,128)(2,1)} %fusion.3, bf16[64,128,64]{1,0,2:T(8,128)(2,1)S(1)} %copy-done.6, bf16[64,128,64]{1,0,2:T(8,128)(2,1)S(1)} %copy-done.7, bf16[64,128,64]{1,0,2:T(8,128)(2,1)S(1)} %copy.47, bf16[64,128,64]{1,0,2:T(8,128)(2,1)} %bitcast.87), kind=kOutput, calls=%fused_computation.2 | convolution fusion | flops 4311744512 | bytes 22020096 | tf_op jit(solution)/shard_map/padq,bdq->pab/dot_general | solution.py:70
  192.3 4.3 %collective-permute-done.9 = f32[4,64,256]{2,1,0:T(8,128)S(1)} collective-permute-done((f32[4,64,256]{2,1,0:T(8,128)S(1)}, f32[4,64,256]{2,1,0:T(8,128)S(1)}, u32[]{:S(2)}, u32[]{:S(2)}) %collective-permute-start.9) | collective-permute-done | bytes 262176 | tf_op jit(solution)/shard_map/ppermute | solution.py:79
  196.6 4.4 %collective-permute-done.8 = f32[4,64,256]{2,1,0:T(8,128)S(1)} collective-permute-done((f32[4,64,256]{2,1,0:T(8,128)S(1)}, f32[4,64,256]{2,1,0:T(8,128)S(1)}, u32[]{:S(2)}, u32[]{:S(2)}) %collective-permute-start.8) | collective-permute-done | bytes 262176 | tf_op jit(solution)/shard_map/ppermute | solution.py:79
  203.2 2.9 %concatenate.33 = f32[4,64,8,64]{3,2,1,0:T(8,128)S(1)} concatenate(f32[4,64,1,64]{3,2,1,0:T(1,128)} %get-tuple-element.19, f32[4,64,1,64]{3,2,1,0:T(1,128)S(1)} %get-tuple-element.18, f32[4,64,1,64]{3,2,1,0:T(1,128)S(1)} %get-tuple-element.17, f32[4,64,1,64]{3,2,1,0:T(1,128)S(1)} %get-tuple-element.16, f32[4,64,1,64]{3,2,1,0:T(1,128)} %get-tuple-element.19, ...), dimensions={2} | concatenate | bytes 1048576 | tf_op jit(solution)/shard_map/concatenate | solution.py:82
  208.7 6.2 %collective-permute-start.13 = (f32[2,64,128]{2,1,0:T(8,128)S(1)}, f32[2,64,128]{2,1,0:T(8,128)S(1)}, u32[]{:S(2)}, u32[]{:S(2)}) collective-permute-start(f32[2,64,128]{2,1,0:T(8,128)S(1)} %bitcast.95), channel_id=1, source_target_pairs={{0,5},{1,13},{2,21},{3,29},{4,0},{5,8},{6,16},{7,24},{8,1},{9,9},{... | collective-permute-start | bytes 196616 | tf_op jit(solution)/shard_map/ppermute | solution.py:103
  215.0 2.6 %collective-permute-start.11 = (f32[2,64,128]{2,1,0:T(8,128)S(1)}, f32[2,64,128]{2,1,0:T(8,128)S(1)}, u32[]{:S(2)}, u32[]{:S(2)}) collective-permute-start(f32[2,64,128]{2,1,0:T(8,128)S(1)} %bitcast.94), channel_id=1, source_target_pairs={{0,1},{1,9},{2,17},{3,25},{4,4},{5,12},{6,20},{7,28},{8,5},{9,13},... | collective-permute-start | bytes 196616 | tf_op jit(solution)/shard_map/ppermute | solution.py:103
  217.6 5.1 %collective-permute-start.12 = (f32[2,64,128]{2,1,0:T(8,128)S(1)}, f32[2,64,128]{2,1,0:T(8,128)S(1)}, u32[]{:S(2)}, u32[]{:S(2)}) collective-permute-start(f32[2,64,128]{2,1,0:T(8,128)S(1)} %bitcast.93), channel_id=1, source_target_pairs={{0,4},{1,12},{2,20},{3,28},{4,5},{5,13},{6,21},{7,29},{8,0},{9,8},... | collective-permute-start | bytes 196616 | tf_op jit(solution)/shard_map/ppermute | solution.py:103
  222.7 3.7 %collective-permute-start.10 = (f32[2,64,128]{2,1,0:T(8,128)S(1)}, f32[2,64,128]{2,1,0:T(8,128)S(1)}, u32[]{:S(2)}, u32[]{:S(2)}) collective-permute-start(f32[2,64,128]{2,1,0:T(8,128)S(1)} %bitcast.92), channel_id=1, source_target_pairs={{0,0},{1,8},{2,16},{3,24},{4,1},{5,9},{6,17},{7,25},{8,4},{9,12},{... | collective-permute-start | bytes 196616 | tf_op jit(solution)/shard_map/ppermute | solution.py:103
  226.6 5.1 %collective-permute-done.10 = f32[2,64,128]{2,1,0:T(8,128)S(1)} collective-permute-done((f32[2,64,128]{2,1,0:T(8,128)S(1)}, f32[2,64,128]{2,1,0:T(8,128)S(1)}, u32[]{:S(2)}, u32[]{:S(2)}) %collective-permute-start.10) | collective-permute-done | bytes 65568 | tf_op jit(solution)/shard_map/ppermute | solution.py:103
  (98 shorter events, 66.3 us)
Async XLA Ops:
  18.3 30.2 %all-to-all-start = ((bf16[8,2,32768]{2,1,0:T(2,128)(2,1)}), bf16[8,2,32768]{2,1,0:T(2,128)(2,1)}, u32[]{:S(2)}, u32[]{:S(2)}) async-start(bf16[8,2,32768]{2,1,0:T(2,128)(2,1)} %reshape.166), calls=%async_computation | async-start | bytes 2097152 | tf_op jit(solution)/shard_map/all_to_all | solution.py:58
  23.8 133.1 %all-gather.2.cloned.1.call-start = ((), (), s32[]{:S(2)}) async-start(), calls=%async_computation.1 | async-start | bytes 10485760 | tf_op jit(solution)/shard_map/all_gather | solution.py:62
  64.7 35.0 %collective-permute-start = (bf16[655360]{0:T(1024)(128)(2,1)}, bf16[655360]{0:T(1024)(128)(2,1)S(1)}, u32[]{:S(2)}, u32[]{:S(2)}) collective-permute-start(bf16[655360]{0:T(1024)(128)(2,1)} %get-tuple-element.26), channel_id=1, source_target_pairs={{0,4},{4,8},{8,12},{12,0},{16,20},{20,24},{24,28},{28,16},{1,5},{5... | collective-permute-start | bytes 3932168 | tf_op jit(solution)/shard_map/ppermute | solution.py:43
  66.5 40.1 %collective-permute-start.1 = (bf16[655360]{0:T(1024)(128)(2,1)}, bf16[655360]{0:T(1024)(128)(2,1)S(1)}, u32[]{:S(2)}, u32[]{:S(2)}) collective-permute-start(bf16[655360]{0:T(1024)(128)(2,1)} %get-tuple-element.25), channel_id=1, source_target_pairs={{0,8},{4,12},{8,0},{12,4},{16,24},{20,28},{24,16},{28,20},{1,9},{5... | collective-permute-start | bytes 3932168 | tf_op jit(solution)/shard_map/ppermute | solution.py:43
  66.5 63.8 %collective-permute-start.2 = (bf16[655360]{0:T(1024)(128)(2,1)}, bf16[655360]{0:T(1024)(128)(2,1)}, u32[]{:S(2)}, u32[]{:S(2)}) collective-permute-start(bf16[655360]{0:T(1024)(128)(2,1)} %get-tuple-element.24), channel_id=1, source_target_pairs={{0,12},{4,0},{8,4},{12,8},{16,28},{20,16},{24,20},{28,24},{1,13},{... | collective-permute-start | bytes 3932168 | tf_op jit(solution)/shard_map/ppermute | solution.py:43
  67.7 81.7 %collective-permute-start.4 = (bf16[16,64,128]{2,1,0:T(8,128)(2,1)}, bf16[16,64,128]{2,1,0:T(8,128)(2,1)}, u32[]{:S(2)}, u32[]{:S(2)}) collective-permute-start(bf16[16,64,128]{2,1,0:T(8,128)(2,1)} %param.6), channel_id=1, source_target_pairs={{0,20},{4,24},{8,28},{12,16},{16,4},{20,8},{24,12},{28,0},{1,21},{... | collective-permute-start | bytes 786440 | tf_op jit(solution)/shard_map/ppermute | solution.py:47
  70.1 68.2 %collective-permute-start.3 = (bf16[16,64,128]{2,1,0:T(8,128)(2,1)}, bf16[16,64,128]{2,1,0:T(8,128)(2,1)S(1)}, u32[]{:S(2)}, u32[]{:S(2)}) collective-permute-start(bf16[16,64,128]{2,1,0:T(8,128)(2,1)} %param.6), channel_id=1, source_target_pairs={{0,16},{4,20},{8,24},{12,28},{16,0},{20,4},{24,8},{28,12},{1,17},{... | collective-permute-start | bytes 786440 | tf_op jit(solution)/shard_map/ppermute | solution.py:47
  99.7 38.6 %copy-start.5 = (bf16[655360]{0:T(1024)(128)(2,1)}, bf16[655360]{0:T(1024)(128)(2,1)S(1)}, u32[]{:S(2)}) copy-start(bf16[655360]{0:T(1024)(128)(2,1)S(1)} %collective-permute-done) | copy-start | bytes 3932164
  99.7 55.5 %collective-permute-start.6 = (bf16[16,64,128]{2,1,0:T(8,128)(2,1)}, bf16[16,64,128]{2,1,0:T(8,128)(2,1)}, u32[]{:S(2)}, u32[]{:S(2)}) collective-permute-start(bf16[16,64,128]{2,1,0:T(8,128)(2,1)} %param.6), channel_id=1, source_target_pairs={{0,28},{4,16},{8,20},{12,24},{16,12},{20,0},{24,4},{28,8},{1,29},{... | collective-permute-start | bytes 786440 | tf_op jit(solution)/shard_map/ppermute | solution.py:47
  106.6 32.5 %copy-start.4 = (bf16[655360]{0:T(1024)(128)(2,1)}, bf16[655360]{0:T(1024)(128)(2,1)S(1)}, u32[]{:S(2)}) copy-start(bf16[655360]{0:T(1024)(128)(2,1)S(1)} %collective-permute-done.1) | copy-start | bytes 3932164
  106.6 46.9 %collective-permute-start.5 = (bf16[16,64,128]{2,1,0:T(8,128)(2,1)}, bf16[16,64,128]{2,1,0:T(8,128)(2,1)}, u32[]{:S(2)}, u32[]{:S(2)}) collective-permute-start(bf16[16,64,128]{2,1,0:T(8,128)(2,1)} %param.6), channel_id=1, source_target_pairs={{0,24},{4,28},{8,16},{12,20},{16,8},{20,12},{24,0},{28,4},{1,25},{... | collective-permute-start | bytes 786440 | tf_op jit(solution)/shard_map/ppermute | solution.py:47
  156.9 16.3 %copy-start.6 = (bf16[64,128,64]{1,0,2:T(8,128)(2,1)S(1)}, bf16[64,128,64]{1,0,2:T(8,128)(2,1)}, u32[]{:S(2)}) copy-start(bf16[64,128,64]{1,0,2:T(8,128)(2,1)} %copy.49) | copy-start | bytes 3145732
  157.0 16.3 %copy-start.7 = (bf16[64,128,64]{1,0,2:T(8,128)(2,1)S(1)}, bf16[64,128,64]{1,0,2:T(8,128)(2,1)}, u32[]{:S(2)}) copy-start(bf16[64,128,64]{1,0,2:T(8,128)(2,1)} %copy.48) | copy-start | bytes 3145732
  173.3 16.2 %copy-start.9 = (f32[128]{0:T(128)S(1)}, f32[128]{0:T(128)}, u32[]{:S(2)}) copy-start(f32[128]{0:T(128)} %param.10) | copy-start | bytes 1540
  185.9 6.3 %collective-permute-start.7 = (f32[4,64,256]{2,1,0:T(8,128)S(1)}, f32[4,64,256]{2,1,0:T(8,128)S(1)}, u32[]{:S(2)}, u32[]{:S(2)}) collective-permute-start(f32[4,64,256]{2,1,0:T(8,128)S(1)} %get-tuple-element.13), channel_id=1, source_target_pairs={{0,1},{1,2},{2,3},{3,0},{4,5},{5,6},{6,7},{7,4},{8,9},{9,10},{10,1... | collective-permute-start | bytes 786440 | tf_op jit(solution)/shard_map/ppermute | solution.py:79
  188.0 8.6 %collective-permute-start.9 = (f32[4,64,256]{2,1,0:T(8,128)S(1)}, f32[4,64,256]{2,1,0:T(8,128)S(1)}, u32[]{:S(2)}, u32[]{:S(2)}) collective-permute-start(f32[4,64,256]{2,1,0:T(8,128)S(1)} %get-tuple-element.14), channel_id=1, source_target_pairs={{0,3},{1,0},{2,1},{3,2},{4,7},{5,4},{6,5},{7,6},{8,11},{9,8},{10,9... | collective-permute-start | bytes 786440 | tf_op jit(solution)/shard_map/ppermute | solution.py:79
  188.2 12.8 %collective-permute-start.8 = (f32[4,64,256]{2,1,0:T(8,128)S(1)}, f32[4,64,256]{2,1,0:T(8,128)S(1)}, u32[]{:S(2)}, u32[]{:S(2)}) collective-permute-start(f32[4,64,256]{2,1,0:T(8,128)S(1)} %get-tuple-element.15), channel_id=1, source_target_pairs={{0,2},{1,3},{2,0},{3,1},{4,6},{5,7},{6,4},{7,5},{8,10},{9,11},{10,... | collective-permute-start | bytes 786440 | tf_op jit(solution)/shard_map/ppermute | solution.py:79
  203.1 29.3 %copy-start.1 = (bf16[64,64,256]{2,1,0:T(8,128)(2,1)S(1)}, bf16[64,64,256]{2,1,0:T(8,128)(2,1)}, u32[]{:S(2)}) copy-start(bf16[64,64,256]{2,1,0:T(8,128)(2,1)} %param.7) | copy-start | bytes 6291460
  203.2 23.3 %slice-start.2 = ((f32[512]{0:T(512)}), f32[64]{0:T(128)S(1)}, s32[]{:S(2)}) async-start(f32[512]{0:T(512)} %param.11), calls=%async_computation.4 | async-start | bytes 1024 | tf_op jit(solution)/shard_map/slice | solution.py:115
  203.2 23.4 %copy-start.10 = (f32[512]{0:T(512)S(1)}, f32[512]{0:T(512)}, u32[]{:S(2)}) copy-start(f32[512]{0:T(512)} %param.11) | copy-start | bytes 6148
  208.7 17.9 %collective-permute-start.13 = (f32[2,64,128]{2,1,0:T(8,128)S(1)}, f32[2,64,128]{2,1,0:T(8,128)S(1)}, u32[]{:S(2)}, u32[]{:S(2)}) collective-permute-start(f32[2,64,128]{2,1,0:T(8,128)S(1)} %bitcast.95), channel_id=1, source_target_pairs={{0,5},{1,13},{2,21},{3,29},{4,0},{5,8},{6,16},{7,24},{8,1},{9,9},{... | collective-permute-start | bytes 196616 | tf_op jit(solution)/shard_map/ppermute | solution.py:103
  215.0 11.6 %collective-permute-start.11 = (f32[2,64,128]{2,1,0:T(8,128)S(1)}, f32[2,64,128]{2,1,0:T(8,128)S(1)}, u32[]{:S(2)}, u32[]{:S(2)}) collective-permute-start(f32[2,64,128]{2,1,0:T(8,128)S(1)} %bitcast.94), channel_id=1, source_target_pairs={{0,1},{1,9},{2,17},{3,25},{4,4},{5,12},{6,20},{7,28},{8,5},{9,13},... | collective-permute-start | bytes 196616 | tf_op jit(solution)/shard_map/ppermute | solution.py:103
  217.6 9.0 %collective-permute-start.12 = (f32[2,64,128]{2,1,0:T(8,128)S(1)}, f32[2,64,128]{2,1,0:T(8,128)S(1)}, u32[]{:S(2)}, u32[]{:S(2)}) collective-permute-start(f32[2,64,128]{2,1,0:T(8,128)S(1)} %bitcast.93), channel_id=1, source_target_pairs={{0,4},{1,12},{2,20},{3,28},{4,5},{5,13},{6,21},{7,29},{8,0},{9,8},... | collective-permute-start | bytes 196616 | tf_op jit(solution)/shard_map/ppermute | solution.py:103
  222.7 9.0 %collective-permute-start.10 = (f32[2,64,128]{2,1,0:T(8,128)S(1)}, f32[2,64,128]{2,1,0:T(8,128)S(1)}, u32[]{:S(2)}, u32[]{:S(2)}) collective-permute-start(f32[2,64,128]{2,1,0:T(8,128)S(1)} %bitcast.92), channel_id=1, source_target_pairs={{0,0},{1,8},{2,16},{3,24},{4,1},{5,9},{6,17},{7,25},{8,4},{9,12},{... | collective-permute-start | bytes 196616 | tf_op jit(solution)/shard_map/ppermute | solution.py:103
  (6 other events, 25.2 us)
Sparse Core Ops, SparseCore 0:
  60.4 57.9 all-gather.1

commit v11 on v9

--- a/solution.py
+++ b/solution.py
@@ -20,23 +20,18 @@
         pairs = amps.shape[0]
         vir_total = b_blk * n_narrow
 
-        amps_blocks = [amps]
-        for shift in range(1, n_narrow):
-            perm = [(i, (i + shift) % n_narrow) for i in range(n_narrow)]
-            amps_blocks.append(lax.ppermute(amps, "narrow", perm))
-        amps_all = jnp.stack(amps_blocks, axis=1)
-
         c_sub = c_blk // n_wide
         left_part = lax.dynamic_slice_in_dim(left_fit, w * c_sub, c_sub, 1)
         left_part = left_part.reshape(rows, c_sub, span, q_blk).transpose(2, 3, 1, 0)
-        left_send = jnp.concatenate([left_part] * GROUPS, axis=0)
-        left_recv = lax.all_to_all(left_send, "narrow", 0, 0, tiled=True)
-        left_rev = [left_recv[(n_narrow - j) % n_narrow][None] for j in range(n_narrow)]
-        left_recv = lax.dynamic_slice_in_dim(
-            jnp.concatenate(left_rev * 2, axis=0), n_narrow - n, n_narrow, 0
+        left_piece = left_part[0].size
+        left_send = jnp.concatenate([left_part.reshape(span, left_piece)] * GROUPS, axis=0)
+        amps_send = jnp.broadcast_to(amps.reshape(1, -1), (n_narrow, amps.size))
+        both = lax.all_to_all(
+            jnp.concatenate([left_send, amps_send], axis=1), "narrow", 0, 0, tiled=True
         )
+        left_recv = both[:, :left_piece].reshape((n_narrow,) + left_part.shape[1:])
+        amps_all = both[:, left_piece:].reshape(n_narrow, pairs, n_wide, c_sub, amps.shape[2])
         left_all = lax.all_gather(left_recv, "wide", axis=0, tiled=False)
-        amps_all = amps_all.reshape(pairs, n_narrow, n_wide, c_sub, amps.shape[2])
 
         right_split = right_fit.reshape(b_blk, d_blk, span, q_blk)
         chunks = []
@@ -53,7 +48,7 @@
             chunks.append(piece)
 
         inter = jnp.einsum(
-            "wkqia,pkwid->padq", left_all, amps_all, preferred_element_type=jnp.float32
+            "wkqia,kpwid->padq", left_all, amps_all, preferred_element_type=jnp.float32
         ).astype(jnp.bfloat16)
 
         right_group = jnp.concatenate(chunks, axis=0)

time: 210 us -> 263 us (1.25)
  blocking collectives: 0 us -> 75.5 us
  starting transfers between devices: 41.3 us -> 20.9 us
  waiting for transfers between devices: 71.7 us -> 51.8 us
  other arithmetic: 3.49 us -> 12 us
  local copies, waits for them, and re-layouts: 50.1 us -> 58.2 us
    all_to_all x0 -> x1, blocking collectives: none -> 75.5 us  [body(): lax.all_to_all(jnp.concatenate([left_send, amps_send], axis=1), 'narrow',...]
    all_gather x1, waiting for transfers between devices: 8.48 us -> 37.2 us  [body(): left_all = lax.all_gather(left_recv, 'wide', axis=0, tiled=False)]
    all_to_all x1 -> x0, waiting for transfers between devices: 24.6 us -> none  [body(): left_recv = lax.all_to_all(left_send, 'narrow', 0, 0, tiled=True)]
    ppermute x3, waiting for transfers between devices: 20.4 us -> 0.01 us  [body(): piece = lax.ppermute(piece, 'narrow', perm)]
    unnamed x39 -> x24, local copies, waits for them, and re-layouts: 24.4 us -> 34.2 us
    all_to_all x0 -> x2, other arithmetic: none -> 9.74 us  [body(): lax.all_to_all(jnp.concatenate([left_send, amps_send], axis=1), 'narrow',...]
    ppermute x7 -> x0, starting transfers between devices: 9.66 us -> none  [body(): amps_blocks.append(lax.ppermute(amps, 'narrow', perm))]
    ppermute x3, starting transfers between devices: 9.55 us -> 2.4 us  [body(): piece = lax.ppermute(piece, 'narrow', perm)]
  transfers between devices with their start and end apart: 19 -> 11, of which waited for: 9 -> 5; matrix products, arithmetic and copies ran while one was open for 21% -> 14% of each run, Pallas kernels for 0% -> 0%
where the time goes in v11:
time: 263 us; the launch traced here: 259 us
  blocking collectives  75.5 us (29%)
  local copies, waits for them, and re-layouts  58.2 us (22%)
  waiting for transfers between devices  51.8 us (20%)
  matrix products  27.4 us (10%)
  starting transfers between devices  20.9 us (8%)
  between operations  13.7 us (5%)
  other arithmetic  12 us (5%)
    all_to_all x1, blocking collectives, body(): lax.all_to_all(jnp.concatenate([left_send, amps_send], axis=1), 'narrow',...  75.5 us
    all_gather x1, waiting for transfers between devices, body(): left_all = lax.all_gather(left_recv, 'wide', axis=0, tiled=False)  37.2 us
    unnamed x24, local copies, waits for them, and re-layouts  34.2 us
    dot_general x1, matrix products, body(): jnp.einsum('wkqia,kpwid->padq', left_all, amps_all, preferred_element_typ...  16.2 us
    ppermute x4, starting transfers between devices, body(): piece = lax.ppermute(piece, ('narrow', 'wide'), perm)  15 us
    dot_general x1, matrix products, body(): jnp.einsum('padq,bdq->pab', inter, right_group, preferred_element_type=jn...  11.1 us
    all_to_all x2, other arithmetic, body(): lax.all_to_all(jnp.concatenate([left_send, amps_send], axis=1), 'narrow',...  9.74 us
    ppermute x3, waiting for transfers between devices, body(): summed = summed + lax.ppermute(piece, 'wide', perm)  9.41 us
  transfers between devices with their start and end apart: 11, of which 5 were waited for; matrix products, arithmetic and copies ran while one was open for 14% of the time, Pallas kernels for 0%

profile of v11, /device:TPU:5, one launch (start us, length us, event | category | flops | bytes accessed | tf_op | source)
XLA Modules:
  0.0 259.5 jit_solution(11586436388293654202)
XLA Ops:
  10.9 4.5 %maximum_bitcast_fusion.2 = bf16[8,1,196608]{2,0,1:T(8,128)(2,1)} fusion(bf16[4,65536]{1,0:T(4,128)(2,1)S(1)} %reshape.72, bf16[196608]{0:T(1024)(128)(2,1)S(1)} %pad.6.clone), kind=kLoop, calls=%fused_computation.12 | loop fusion | flops 9437184 | bytes 4063232 | tf_op jit(solution)/shard_map/all_to_all | solution.py:29
  15.9 5.2 %reduce.4 = bf16[8,196608]{1,0:T(8,128)(2,1)} reduce(bf16[8,1,196608]{2,0,1:T(8,128)(2,1)} %maximum_bitcast_fusion.2, bf16[]{:T(256)} %broadcast.44), dimensions={1}, to_apply=%copy.48.reduce_sub_computation | reduce | bytes 6291458 | tf_op jit(solution)/shard_map/all_to_all | solution.py:29
  21.2 6.4 %reshape.87 = bf16[8,2,98304]{2,1,0:T(2,128)(2,1)} reshape(bf16[8,196608]{1,0:T(8,128)(2,1)} %reduce.4) | data formatting | bytes 6291456
  27.6 75.5 %all_to_all.12 = bf16[8,2,98304]{2,1,0:T(2,128)(2,1)} all-to-all(bf16[8,2,98304]{2,1,0:T(2,128)(2,1)} %reshape.87), channel_id=1, replica_groups=mesh['narrow'=8,'wide'=4] {'narrow'}, dimensions={0} | all-to-all | bytes 6291456 | tf_op jit(solution)/shard_map/all_to_all | solution.py:29
  103.1 7.8 %reshape.88 = bf16[8,1,196608]{2,1,0:T(2,128)(2,1)} reshape(bf16[8,2,98304]{2,1,0:T(2,128)(2,1)} %all_to_all.12) | data formatting | bytes 6291456
  110.8 6.8 %copy.72 = bf16[8,1,196608]{2,0,1:T(8,128)(2,1)S(1)} copy(bf16[8,1,196608]{2,1,0:T(2,128)(2,1)} %reshape.88) | data formatting | bytes 6291456
  119.4 3.6 %all_gather_reshape.3 = bf16[1,8,64,16,64]{4,3,2,1,0:T(8,128)(2,1)} reshape(bf16[8,65536]{1,0:T(8,128)(2,1)S(1)} %slice.37) | data formatting | bytes 2097152 | tf_op jit(solution)/shard_map/all_gather;reshape | solution.py:34
  123.1 6.4 %copy.50 = bf16[64,128,256]{1,2,0:T(8,128)(2,1)} copy(bf16[64,128,256]{2,1,0:T(8,128)(2,1)} %param.8) | data formatting | bytes 8388608 | tf_op args[2]
  129.5 3.7 %constant_dynamic-slice_fusion.8 = (bf16[64,128,1,64]{1,3,2,0:T(8,128)(2,1)S(1)}, bf16[64,128,1,64]{1,3,2,0:T(8,128)(2,1)S(1)}, bf16[64,128,1,64]{1,3,2,0:T(8,128)(2,1)S(1)}, bf16[64,128,1,64]{1,3,2,0:T(8,128)(2,1)S(1)}) fusion(bf16[64,128,4,64]{1,3,2,0:T(8,128)(2,1)} %bitcast.68, s32[]{:T(128)S(6)} %select_n.159, s32[]{:T(128)S(6)} %select_n.165, ...), kind=kLoop, calls=%fused_computation.35 | loop fusion | bytes 8388624 | tf_op jit(solution)/shard_map/jit(dynamic_index_in_dim)/dynamic_slice | solution.py:40
  135.6 2.3 collective-permute-start.1
  141.3 1.8 slice_bitcast_fusion
  144.8 37.2 %all-gather.2.cloned.1.call-done = bf16[4,8,64,16,64]{4,3,0,2,1:T(8,128)(2,1)} async-done(((bf16[1,8,64,16,64]{4,3,0,2,1:T(8,128)(2,1)}), bf16[4,8,64,16,64]{4,3,0,2,1:T(8,128)(2,1)}) %all-gather.2.cloned.1.call-update) | async-done | bytes 4194320 | tf_op jit(solution)/shard_map/all_gather | solution.py:34
  182.0 16.2 %fusion.3 = bf16[16,128,64,64,1,1]{1,3,5,2,0,4:T(8,128)(2,1)} fusion(bf16[4,8,64,16,64]{4,3,0,2,1:T(8,128)(2,1)} %all-gather.2.cloned.1.call-done, bf16[8,16,4,16,128,1]{4,3,2,1,0,5:T(8,128)(2,1)} %bitcast.73), kind=kOutput, calls=%fused_computation.3 | convolution fusion | flops 8589934592 | bytes 23068672 | tf_op jit(solution)/shard_map/wkqia,kpwid->padq/dot_general | solution.py:50
  198.3 11.1 %fusion.1 = f32[16,64,256,1]{2,1,0,3:T(8,128)S(1)} fusion(bf16[16,128,64,64,1,1]{1,3,5,2,0,4:T(8,128)(2,1)} %fusion.3, bf16[64,128,64]{1,0,2:T(8,128)(2,1)} %collective-permute-done.2, bf16[64,128,64]{1,0,2:T(8,128)(2,1)} %collective-permute-done.1, bf16[64,128,64]{1,0,2:T(8,128)(2,1)} %collective-permute-done, bf16[64,128,64]{1,0,2:T(8,128)(2,1)S(1)} %bitcast.77), kind=kOutput, calls=%fused_computation.2 | convolution fusion | flops 4311744512 | bytes 22020096 | tf_op jit(solution)/shard_map/padq,bdq->pab/dot_general | solution.py:55
  212.0 1.8 collective-permute-start.3
  214.2 5.3 %collective-permute-done.5 = f32[4,64,256]{2,1,0:T(8,128)} collective-permute-done((f32[4,64,256]{2,1,0:T(8,128)}, f32[4,64,256]{2,1,0:T(8,128)}, u32[]{:S(2)}, u32[]{:S(2)}) %collective-permute-start.5) | collective-permute-done | bytes 262176 | tf_op jit(solution)/shard_map/ppermute | solution.py:64
  219.5 4.1 %collective-permute-done.3 = f32[4,64,256]{2,1,0:T(8,128)} collective-permute-done((f32[4,64,256]{2,1,0:T(8,128)S(1)}, f32[4,64,256]{2,1,0:T(8,128)}, u32[]{:S(2)}, u32[]{:S(2)}) %collective-permute-start.3) | collective-permute-done | bytes 262176 | tf_op jit(solution)/shard_map/ppermute | solution.py:64
  226.0 2.8 %concatenate.15 = f32[4,64,8,64]{3,2,1,0:T(8,128)S(1)} concatenate(f32[4,64,1,64]{3,2,1,0:T(1,128)} %get-tuple-element.19, f32[4,64,1,64]{3,2,1,0:T(1,128)S(1)} %get-tuple-element.18, f32[4,64,1,64]{3,2,1,0:T(1,128)S(1)} %get-tuple-element.17, f32[4,64,1,64]{3,2,1,0:T(1,128)S(1)} %get-tuple-element.16, f32[4,64,1,64]{3,2,1,0:T(1,128)} %get-tuple-element.19, ...), dimensions={2} | concatenate | bytes 1048576 | tf_op jit(solution)/shard_map/concatenate | solution.py:67
  231.5 5.9 %collective-permute-start.9 = (f32[2,64,128]{2,1,0:T(8,128)S(1)}, f32[2,64,128]{2,1,0:T(8,128)S(1)}, u32[]{:S(2)}, u32[]{:S(2)}) collective-permute-start(f32[2,64,128]{2,1,0:T(8,128)S(1)} %bitcast.82), channel_id=1, source_target_pairs={{0,5},{1,13},{2,21},{3,29},{4,0},{5,8},{6,16},{7,24},{8,1},{9,9},{... | collective-permute-start | bytes 196616 | tf_op jit(solution)/shard_map/ppermute | solution.py:88
  237.3 3.2 %collective-permute-start.8 = (f32[2,64,128]{2,1,0:T(8,128)S(1)}, f32[2,64,128]{2,1,0:T(8,128)S(1)}, u32[]{:S(2)}, u32[]{:S(2)}) collective-permute-start(f32[2,64,128]{2,1,0:T(8,128)S(1)} %bitcast.81), channel_id=1, source_target_pairs={{0,4},{1,12},{2,20},{3,28},{4,5},{5,13},{6,21},{7,29},{8,0},{9,8},... | collective-permute-start | bytes 196616 | tf_op jit(solution)/shard_map/ppermute | solution.py:88
  240.5 2.6 collective-permute-start.6
  243.1 3.4 %collective-permute-start.7 = (f32[2,64,128]{2,1,0:T(8,128)S(1)}, f32[2,64,128]{2,1,0:T(8,128)S(1)}, u32[]{:S(2)}, u32[]{:S(2)}) collective-permute-start(f32[2,64,128]{2,1,0:T(8,128)S(1)} %bitcast.79), channel_id=1, source_target_pairs={{0,1},{1,9},{2,17},{3,25},{4,4},{5,12},{6,20},{7,28},{8,5},{9,13},... | collective-permute-start | bytes 196616 | tf_op jit(solution)/shard_map/ppermute | solution.py:88
  246.7 2.6 collective-permute-done.6
  249.3 2.6 %collective-permute-done.7 = f32[2,64,128]{2,1,0:T(8,128)S(1)} collective-permute-done((f32[2,64,128]{2,1,0:T(8,128)S(1)}, f32[2,64,128]{2,1,0:T(8,128)S(1)}, u32[]{:S(2)}, u32[]{:S(2)}) %collective-permute-start.7) | collective-permute-done | bytes 65568 | tf_op jit(solution)/shard_map/ppermute | solution.py:88
  (57 shorter events, 22.9 us)
Async XLA Ops:
  6.5 1.6 copy-start
  6.5 4.3 %copy-start.5 = (bf16[16,64,128]{2,1,0:T(8,128)(2,1)S(1)}, bf16[16,64,128]{2,1,0:T(8,128)(2,1)}, u32[]{:S(2)}) copy-start(bf16[16,64,128]{2,1,0:T(8,128)(2,1)} %param.6) | copy-start | bytes 786436
  6.5 175.4 %all-gather.2.cloned.1.call-start = ((), (), s32[]{:S(2)}) async-start(), calls=%async_computation.1 | async-start | bytes 10485760 | tf_op jit(solution)/shard_map/all_gather | solution.py:34
  117.6 1.7 copy-start.2
  133.9 64.3 %collective-permute-start.2 = (bf16[64,128,64]{1,0,2:T(8,128)(2,1)S(1)}, bf16[64,128,64]{1,0,2:T(8,128)(2,1)}, u32[]{:S(2)}, u32[]{:S(2)}) collective-permute-start(bf16[64,128,64]{1,0,2:T(8,128)(2,1)S(1)} %bitcast.76), channel_id=1, source_target_pairs={{0,12},{4,0},{8,4},{12,8},{16,28},{20,16},{24,20},{28,24},{1,13},{... | collective-permute-start | bytes 3145736 | tf_op jit(solution)/shard_map/ppermute | solution.py:47
  135.6 62.6 %collective-permute-start.1 = (bf16[64,128,64]{1,0,2:T(8,128)(2,1)}, bf16[64,128,64]{1,0,2:T(8,128)(2,1)}, u32[]{:S(2)}, u32[]{:S(2)}) collective-permute-start(bf16[64,128,64]{1,0,2:T(8,128)(2,1)} %bitcast.65), channel_id=1, source_target_pairs={{0,8},{4,12},{8,0},{12,4},{16,24},{20,28},{24,16},{28,20},{1,9},{5... | collective-permute-start | bytes 3145736 | tf_op jit(solution)/shard_map/ppermute | solution.py:47
  139.6 58.6 %collective-permute-start = (bf16[64,128,64]{1,0,2:T(8,128)(2,1)}, bf16[64,128,64]{1,0,2:T(8,128)(2,1)}, u32[]{:S(2)}, u32[]{:S(2)}) collective-permute-start(bf16[64,128,64]{1,0,2:T(8,128)(2,1)} %bitcast.66), channel_id=1, source_target_pairs={{0,4},{4,8},{8,12},{12,0},{16,20},{20,24},{24,28},{28,16},{1,5},{5... | collective-permute-start | bytes 3145736 | tf_op jit(solution)/shard_map/ppermute | solution.py:47
  182.0 16.3 %copy-start.4 = (bf16[64,128,1,64]{1,0,3,2:T(8,128)(2,1)S(1)}, bf16[64,128,1,64]{1,0,3,2:T(8,128)(2,1)}, u32[]{:S(2)}) copy-start(bf16[64,128,1,64]{1,0,3,2:T(8,128)(2,1)} %copy.76) | copy-start | bytes 3145732
  198.3 15.5 %copy-start.6 = (s32[2,2]{1,0:T(2,128)S(1)}, s32[2,2]{1,0:T(2,128)}, u32[]{:S(2)}) copy-start(s32[2,2]{1,0:T(2,128)} %param.9) | copy-start | bytes 52
  198.3 15.7 %copy-start.7 = (f32[128]{0:T(128)S(1)}, f32[128]{0:T(128)}, u32[]{:S(2)}) copy-start(f32[128]{0:T(128)} %param.10) | copy-start | bytes 1540
  209.4 10.1 %copy-start.3 = (f32[16,64,256,1]{2,1,0,3:T(8,128)}, f32[16,64,256,1]{2,1,0,3:T(8,128)S(1)}, u32[]{:S(2)}) copy-start(f32[16,64,256,1]{2,1,0,3:T(8,128)S(1)} %fusion.1) | copy-start | bytes 3145732
  209.4 43.2 %copy-start.1 = (bf16[64,64,256]{2,1,0:T(8,128)(2,1)S(1)}, bf16[64,64,256]{2,1,0:T(8,128)(2,1)}, u32[]{:S(2)}) copy-start(bf16[64,64,256]{2,1,0:T(8,128)(2,1)} %param.7) | copy-start | bytes 6291460
  210.3 36.2 %slice-start = ((f32[512]{0:T(512)}), f32[64]{0:T(128)S(1)}, s32[]{:S(2)}) async-start(f32[512]{0:T(512)} %param.11), calls=%async_computation.2 | async-start | bytes 1024 | tf_op jit(solution)/shard_map/slice | solution.py:100
  210.3 36.3 %copy-start.8 = (f32[512]{0:T(512)S(1)}, f32[512]{0:T(512)}, u32[]{:S(2)}) copy-start(f32[512]{0:T(512)} %param.11) | copy-start | bytes 6148
  210.3 9.2 %collective-permute-start.5 = (f32[4,64,256]{2,1,0:T(8,128)}, f32[4,64,256]{2,1,0:T(8,128)}, u32[]{:S(2)}, u32[]{:S(2)}) collective-permute-start(f32[4,64,256]{2,1,0:T(8,128)} %get-tuple-element.14), channel_id=1, source_target_pairs={{0,3},{1,0},{2,1},{3,2},{4,7},{5,4},{6,5},{7,6},{8,11},{9,8},{10,9... | collective-permute-start | bytes 786440 | tf_op jit(solution)/shard_map/ppermute | solution.py:64
  210.5 9.0 %collective-permute-start.4 = (f32[4,64,256]{2,1,0:T(8,128)}, f32[4,64,256]{2,1,0:T(8,128)}, u32[]{:S(2)}, u32[]{:S(2)}) collective-permute-start(f32[4,64,256]{2,1,0:T(8,128)} %get-tuple-element.15), channel_id=1, source_target_pairs={{0,2},{1,3},{2,0},{3,1},{4,6},{5,7},{6,4},{7,5},{8,10},{9,11},{10,... | collective-permute-start | bytes 786440 | tf_op jit(solution)/shard_map/ppermute | solution.py:64
  212.0 11.6 %collective-permute-start.3 = (f32[4,64,256]{2,1,0:T(8,128)S(1)}, f32[4,64,256]{2,1,0:T(8,128)}, u32[]{:S(2)}, u32[]{:S(2)}) collective-permute-start(f32[4,64,256]{2,1,0:T(8,128)S(1)} %get-tuple-element.13), channel_id=1, source_target_pairs={{0,1},{1,2},{2,3},{3,0},{4,5},{5,6},{6,7},{7,4},{8,9},{9,10},{10,1... | collective-permute-start | bytes 786440 | tf_op jit(solution)/shard_map/ppermute | solution.py:64
  231.5 15.2 %collective-permute-start.9 = (f32[2,64,128]{2,1,0:T(8,128)S(1)}, f32[2,64,128]{2,1,0:T(8,128)S(1)}, u32[]{:S(2)}, u32[]{:S(2)}) collective-permute-start(f32[2,64,128]{2,1,0:T(8,128)S(1)} %bitcast.82), channel_id=1, source_target_pairs={{0,5},{1,13},{2,21},{3,29},{4,0},{5,8},{6,16},{7,24},{8,1},{9,9},{... | collective-permute-start | bytes 196616 | tf_op jit(solution)/shard_map/ppermute | solution.py:88
  237.3 9.3 %collective-permute-start.8 = (f32[2,64,128]{2,1,0:T(8,128)S(1)}, f32[2,64,128]{2,1,0:T(8,128)S(1)}, u32[]{:S(2)}, u32[]{:S(2)}) collective-permute-start(f32[2,64,128]{2,1,0:T(8,128)S(1)} %bitcast.81), channel_id=1, source_target_pairs={{0,4},{1,12},{2,20},{3,28},{4,5},{5,13},{6,21},{7,29},{8,0},{9,8},... | collective-permute-start | bytes 196616 | tf_op jit(solution)/shard_map/ppermute | solution.py:88
  240.5 8.7 %collective-permute-start.6 = (f32[2,64,128]{2,1,0:T(8,128)S(1)}, f32[2,64,128]{2,1,0:T(8,128)S(1)}, u32[]{:S(2)}, u32[]{:S(2)}) collective-permute-start(f32[2,64,128]{2,1,0:T(8,128)S(1)} %bitcast.80), channel_id=1, source_target_pairs={{0,0},{1,8},{2,16},{3,24},{4,1},{5,9},{6,17},{7,25},{8,4},{9,12},{... | collective-permute-start | bytes 196616 | tf_op jit(solution)/shard_map/ppermute | solution.py:88
  243.1 8.8 %collective-permute-start.7 = (f32[2,64,128]{2,1,0:T(8,128)S(1)}, f32[2,64,128]{2,1,0:T(8,128)S(1)}, u32[]{:S(2)}, u32[]{:S(2)}) collective-permute-start(f32[2,64,128]{2,1,0:T(8,128)S(1)} %bitcast.79), channel_id=1, source_target_pairs={{0,1},{1,9},{2,17},{3,25},{4,4},{5,12},{6,20},{7,28},{8,5},{9,13},... | collective-permute-start | bytes 196616 | tf_op jit(solution)/shard_map/ppermute | solution.py:88
Sparse Core Ops, SparseCore 0:
  123.2 58.7 all-gather.1

commit v12 on v9

--- a/solution.py
+++ b/solution.py
@@ -20,23 +20,26 @@
         pairs = amps.shape[0]
         vir_total = b_blk * n_narrow
 
-        amps_blocks = [amps]
-        for shift in range(1, n_narrow):
-            perm = [(i, (i + shift) % n_narrow) for i in range(n_narrow)]
-            amps_blocks.append(lax.ppermute(amps, "narrow", perm))
-        amps_all = jnp.stack(amps_blocks, axis=1)
+        amps_all = lax.all_gather(amps, "narrow", axis=1, tiled=True)
 
         c_sub = c_blk // n_wide
         left_part = lax.dynamic_slice_in_dim(left_fit, w * c_sub, c_sub, 1)
         left_part = left_part.reshape(rows, c_sub, span, q_blk).transpose(2, 3, 1, 0)
         left_send = jnp.concatenate([left_part] * GROUPS, axis=0)
         left_recv = lax.all_to_all(left_send, "narrow", 0, 0, tiled=True)
-        left_rev = [left_recv[(n_narrow - j) % n_narrow][None] for j in range(n_narrow)]
-        left_recv = lax.dynamic_slice_in_dim(
-            jnp.concatenate(left_rev * 2, axis=0), n_narrow - n, n_narrow, 0
+        left_slots = [left_recv]
+        for shift in range(1, n_wide):
+            perm = [(i, (i + shift) % n_wide) for i in range(n_wide)]
+            left_slots.append(lax.ppermute(left_recv, "wide", perm))
+        left_all = jnp.stack(left_slots, axis=0)
+        amps_all = amps_all.reshape(pairs, n_narrow, n_wide, c_sub, amps.shape[2])
+        amps_rev = [
+            lax.slice_in_dim(amps_all, (n_wide - j) % n_wide, (n_wide - j) % n_wide + 1, axis=2)
+            for j in range(n_wide)
+        ]
+        amps_all = lax.dynamic_slice_in_dim(
+            jnp.concatenate(amps_rev * 2, axis=2), n_wide - w, n_wide, 2
         )
-        left_all = lax.all_gather(left_recv, "wide", axis=0, tiled=False)
-        amps_all = amps_all.reshape(pairs, n_narrow, n_wide, c_sub, amps.shape[2])
 
         right_split = right_fit.reshape(b_blk, d_blk, span, q_blk)
         chunks = []

time: 210 us -> 238 us (1.13)
  waiting for transfers between devices: 71.7 us -> 117 us
  starting transfers between devices: 41.3 us -> 28.2 us
  matrix products: 27.3 us -> 24.4 us
    ppermute x7 -> x3, waiting for transfers between devices: 2.8 us -> 48 us  [body(): left_slots.append(lax.ppermute(left_recv, 'wide', perm))]
    all_gather x1, waiting for transfers between devices: 8.48 us -> 37 us  [body(): amps_all = lax.all_gather(amps, 'narrow', axis=1, tiled=True)]
    ppermute x3, waiting for transfers between devices: 20.4 us -> 0.01 us  [body(): piece = lax.ppermute(piece, 'narrow', perm)]
    dot_general x1 -> x0, matrix products: 16.1 us -> none  [body(): jnp.einsum('wkqia,pkwid->padq', left_all, amps_all, preferred_element_typ...]
    dot_general x1, matrix products: 11.1 us -> 24.4 us  [body(): jnp.einsum('padq,bdq->pab', inter, right_group, preferred_element_type=jn...]
    all_to_all x1, waiting for transfers between devices: 24.6 us -> 14.4 us  [body(): left_recv = lax.all_to_all(left_send, 'narrow', 0, 0, tiled=True)]
    ppermute x7 -> x3, starting transfers between devices: 9.66 us -> 2.75 us  [body(): left_slots.append(lax.ppermute(left_recv, 'wide', perm))]
    ppermute x3, starting transfers between devices: 9.55 us -> 3.82 us  [body(): piece = lax.ppermute(piece, 'narrow', perm)]
  transfers between devices with their start and end apart: 19 -> 15, of which waited for: 9 -> 10; matrix products, arithmetic and copies ran while one was open for 21% -> 18% of each run, Pallas kernels for 0% -> 0%
where the time goes in v12:
time: 238 us; the launch traced here: 237 us
  waiting for transfers between devices  117 us (49%)
  local copies, waits for them, and re-layouts  50.8 us (21%)
  starting transfers between devices  28.2 us (12%)
  matrix products  24.4 us (10%)
  between operations  13.6 us (6%)
  other arithmetic  3.49 us (1%)
    ppermute x3, waiting for transfers between devices, body(): left_slots.append(lax.ppermute(left_recv, 'wide', perm))  48 us
    all_gather x1, waiting for transfers between devices, body(): amps_all = lax.all_gather(amps, 'narrow', axis=1, tiled=True)  37 us
    dot_general x1, matrix products, body(): jnp.einsum('padq,bdq->pab', inter, right_group, preferred_element_type=jn...  24.4 us
    unnamed x26, local copies, waits for them, and re-layouts  20.8 us
    ppermute x4, starting transfers between devices, body(): piece = lax.ppermute(piece, ('narrow', 'wide'), perm)  15 us
    all_to_all x1, waiting for transfers between devices, body(): left_recv = lax.all_to_all(left_send, 'narrow', 0, 0, tiled=True)  14.4 us
    dynamic_slice x5, local copies, waits for them, and re-layouts, body(): piece = lax.dynamic_index_in_dim(right_split, dest, 2, keepdims=False)  12 us
    ppermute x3, waiting for transfers between devices, body(): summed = summed + lax.ppermute(piece, 'wide', perm)  11.3 us
  transfers between devices with their start and end apart: 15, of which 10 were waited for; matrix products, arithmetic and copies ran while one was open for 18% of the time, Pallas kernels for 0%

profile of v12, /device:TPU:5, one launch (start us, length us, event | category | flops | bytes accessed | tf_op | source)
XLA Modules:
  0.0 237.0 jit_solution(10217274804497664668)
XLA Ops:
  9.0 2.0 reshape.65
  12.2 1.7 copy.57
  13.9 4.3 %reshape.77 = bf16[8,2,32768]{2,1,0:T(2,128)(2,1)} reshape(bf16[8,64,16,64]{3,2,1,0:T(8,128)(2,1)} %bitcast.78) | data formatting | bytes 2097152
  18.3 5.5 %all-to-all-start = ((bf16[8,2,32768]{2,1,0:T(2,128)(2,1)}), bf16[8,2,32768]{2,1,0:T(2,128)(2,1)S(1)}, u32[]{:S(2)}, u32[]{:S(2)}) async-start(bf16[8,2,32768]{2,1,0:T(2,128)(2,1)} %reshape.77), calls=%async_computation | async-start | bytes 2097152 | tf_op jit(solution)/shard_map/all_to_all | solution.py:29
  23.8 6.4 %copy.40 = bf16[64,128,256]{1,2,0:T(8,128)(2,1)} copy(bf16[64,128,256]{2,1,0:T(8,128)(2,1)} %param.8) | data formatting | bytes 8388608 | tf_op args[2]
  30.1 4.2 %constant_dynamic-slice_fusion.8 = (bf16[64,128,1,64]{1,3,2,0:T(8,128)(2,1)}, bf16[64,128,1,64]{1,3,2,0:T(8,128)(2,1)S(1)}, bf16[64,128,1,64]{1,3,2,0:T(8,128)(2,1)S(1)}, bf16[64,128,1,64]{1,3,2,0:T(8,128)(2,1)S(1)}) fusion(bf16[64,128,4,64]{1,3,2,0:T(8,128)(2,1)} %bitcast.69, s32[]{:T(128)S(6)} %select_n.163, s32[]{:T(128)S(6)} %select_n.169, ...), kind=kLoop, calls=%fused_computation.48 | loop fusion | bytes 8388624 | tf_op jit(solution)/shard_map/jit(dynamic_index_in_dim)/dynamic_slice | solution.py:48
  34.3 1.7 copy.55
  37.5 1.7 copy.54
  43.1 2.9 %copy.56 = bf16[64,128,1,64]{1,0,3,2:T(8,128)(2,1)} copy(bf16[64,128,1,64]{1,3,2,0:T(8,128)(2,1)} %get-tuple-element.9) | data formatting | bytes 2097152 | tf_op jit(solution)/shard_map/jit(dynamic_index_in_dim)/dynamic_slice | solution.py:48
  46.0 14.4 %all-to-all-done = bf16[8,2,32768]{2,1,0:T(2,128)(2,1)S(1)} async-done(((bf16[8,2,32768]{2,1,0:T(2,128)(2,1)}), bf16[8,2,32768]{2,1,0:T(2,128)(2,1)S(1)}, u32[]{:S(2)}, u32[]{:S(2)}) %all-to-all-start) | async-done | bytes 1048608 | tf_op jit(solution)/shard_map/all_to_all | solution.py:29
  60.4 2.7 %reshape.78 = bf16[8,64,16,64]{3,2,1,0:T(8,128)(2,1)} reshape(bf16[8,2,32768]{2,1,0:T(2,128)(2,1)S(1)} %all-to-all-done) | data formatting | bytes 2097152
  63.1 5.4 %copy.36 = bf16[8,64,16,64]{3,2,0,1:T(8,128)(2,1)} copy(bf16[8,64,16,64]{1,2,3,0:T(8,128)(2,1)} %bitcast.79) | data formatting | bytes 2097152 | tf_op jit(solution)/shard_map/all_to_all | solution.py:29
  70.6 37.0 %all-gather.2.cloned.1.call-done = bf16[16,512,128]{2,1,0:T(8,128)(2,1)} async-done(((bf16[16,64,128]{2,1,0:T(8,128)(2,1)}), bf16[16,512,128]{2,1,0:T(8,128)(2,1)}) %all-gather.2.cloned.1.call-update) | async-done | bytes 2097168 | tf_op jit(solution)/shard_map/all_gather | solution.py:23
  114.7 46.6 %collective-permute-done.1 = bf16[8,64,16,64]{3,2,0,1:T(8,128)(2,1)} collective-permute-done((bf16[8,64,16,64]{3,2,0,1:T(8,128)(2,1)}, bf16[8,64,16,64]{3,2,0,1:T(8,128)(2,1)}, u32[]{:S(2)}, u32[]{:S(2)}) %collective-permute-start.1) | collective-permute-done | bytes 1048608 | tf_op jit(solution)/shard_map/ppermute | solution.py:33
  163.0 24.4 %fusion.1 = f32[16,64,256,1]{2,1,3,0:T(8,128)S(1)} fusion(bf16[1,8,64,16,64]{4,3,0,1,2:T(8,128)(2,1)} %bitcast.89, bf16[1,8,64,16,64]{4,3,0,1,2:T(8,128)(2,1)} %bitcast.6, bf16[1,8,64,16,64]{4,3,0,1,2:T(8,128)(2,1)} %bitcast.5, bf16[1,8,64,16,64]{4,3,0,1,2:T(8,128)(2,1)} %bitcast.81, bf16[64,128,64]{1,0,2:T(8,128)(2,1)} %collective-permute-done.5, ...), kind=kOutput, calls=%fused_computation.2 | convolution fusion | flops 12926844928 | bytes 15728644 | tf_op jit(solution)/shard_map/padq,bdq->pab/dot_general | solution.py:63
  189.9 3.7 %collective-permute-done.6 = f32[4,64,256]{2,1,0:T(8,128)} collective-permute-done((f32[4,64,256]{2,1,0:T(8,128)}, f32[4,64,256]{2,1,0:T(8,128)}, u32[]{:S(2)}, u32[]{:S(2)}) %collective-permute-start.6) | collective-permute-done | bytes 262176 | tf_op jit(solution)/shard_map/ppermute | solution.py:72
  193.6 5.6 %collective-permute-done.7 = f32[4,64,256]{2,1,0:T(8,128)} collective-permute-done((f32[4,64,256]{2,1,0:T(8,128)}, f32[4,64,256]{2,1,0:T(8,128)}, u32[]{:S(2)}, u32[]{:S(2)}) %collective-permute-start.7) | collective-permute-done | bytes 262176 | tf_op jit(solution)/shard_map/ppermute | solution.py:72
  199.2 2.0 collective-permute-done.8
  203.6 2.8 %concatenate.15 = f32[4,64,8,64]{3,2,1,0:T(8,128)S(1)} concatenate(f32[4,64,1,64]{3,2,1,0:T(1,128)} %get-tuple-element.19, f32[4,64,1,64]{3,2,1,0:T(1,128)S(1)} %get-tuple-element.18, f32[4,64,1,64]{3,2,1,0:T(1,128)S(1)} %get-tuple-element.17, f32[4,64,1,64]{3,2,1,0:T(1,128)S(1)} %get-tuple-element.16, f32[4,64,1,64]{3,2,1,0:T(1,128)} %get-tuple-element.19, ...), dimensions={2} | concatenate | bytes 1048576 | tf_op jit(solution)/shard_map/concatenate | solution.py:75
  209.1 4.1 %collective-permute-start.10 = (f32[2,64,128]{2,1,0:T(8,128)S(1)}, f32[2,64,128]{2,1,0:T(8,128)S(1)}, u32[]{:S(2)}, u32[]{:S(2)}) collective-permute-start(f32[2,64,128]{2,1,0:T(8,128)S(1)} %bitcast.88), channel_id=1, source_target_pairs={{0,1},{1,9},{2,17},{3,25},{4,4},{5,12},{6,20},{7,28},{8,5},{9,13},... | collective-permute-start | bytes 196616 | tf_op jit(solution)/shard_map/ppermute | solution.py:96
  213.3 2.6 %collective-permute-start.11 = (f32[2,64,128]{2,1,0:T(8,128)S(1)}, f32[2,64,128]{2,1,0:T(8,128)S(1)}, u32[]{:S(2)}, u32[]{:S(2)}) collective-permute-start(f32[2,64,128]{2,1,0:T(8,128)S(1)} %bitcast.87), channel_id=1, source_target_pairs={{0,4},{1,12},{2,20},{3,28},{4,5},{5,13},{6,21},{7,29},{8,0},{9,8},... | collective-permute-start | bytes 196616 | tf_op jit(solution)/shard_map/ppermute | solution.py:96
  215.9 5.1 %collective-permute-start.12 = (f32[2,64,128]{2,1,0:T(8,128)S(1)}, f32[2,64,128]{2,1,0:T(8,128)S(1)}, u32[]{:S(2)}, u32[]{:S(2)}) collective-permute-start(f32[2,64,128]{2,1,0:T(8,128)S(1)} %bitcast.86), channel_id=1, source_target_pairs={{0,5},{1,13},{2,21},{3,29},{4,0},{5,8},{6,16},{7,24},{8,1},{9,9},{... | collective-permute-start | bytes 196616 | tf_op jit(solution)/shard_map/ppermute | solution.py:96
  221.0 3.1 %collective-permute-start.9 = (f32[2,64,128]{2,1,0:T(8,128)S(1)}, f32[2,64,128]{2,1,0:T(8,128)S(1)}, u32[]{:S(2)}, u32[]{:S(2)}) collective-permute-start(f32[2,64,128]{2,1,0:T(8,128)S(1)} %bitcast.85), channel_id=1, source_target_pairs={{0,0},{1,8},{2,16},{3,24},{4,1},{5,9},{6,17},{7,25},{8,4},{9,12},{... | collective-permute-start | bytes 196616 | tf_op jit(solution)/shard_map/ppermute | solution.py:96
  224.8 4.6 %collective-permute-done.9 = f32[2,64,128]{2,1,0:T(8,128)S(1)} collective-permute-done((f32[2,64,128]{2,1,0:T(8,128)S(1)}, f32[2,64,128]{2,1,0:T(8,128)S(1)}, u32[]{:S(2)}, u32[]{:S(2)}) %collective-permute-start.9) | collective-permute-done | bytes 65568 | tf_op jit(solution)/shard_map/ppermute | solution.py:96
  (61 shorter events, 28.8 us)
Async XLA Ops:
  6.5 1.6 copy-start
  6.5 101.1 %all-gather.2.cloned.1.call-start = ((), (), s32[]{:S(2)}) async-start(), calls=%async_computation.1 | async-start | bytes 2359296 | tf_op jit(solution)/shard_map/all_gather | solution.py:23
  18.3 42.2 %all-to-all-start = ((bf16[8,2,32768]{2,1,0:T(2,128)(2,1)}), bf16[8,2,32768]{2,1,0:T(2,128)(2,1)S(1)}, u32[]{:S(2)}, u32[]{:S(2)}) async-start(bf16[8,2,32768]{2,1,0:T(2,128)(2,1)} %reshape.77), calls=%async_computation | async-start | bytes 2097152 | tf_op jit(solution)/shard_map/all_to_all | solution.py:29
  36.0 75.3 %collective-permute-start.3 = (bf16[64,128,64]{1,0,2:T(8,128)(2,1)}, bf16[64,128,64]{1,0,2:T(8,128)(2,1)}, u32[]{:S(2)}, u32[]{:S(2)}) collective-permute-start(bf16[64,128,64]{1,0,2:T(8,128)(2,1)} %bitcast.66), channel_id=1, source_target_pairs={{0,4},{4,8},{8,12},{12,0},{16,20},{20,24},{24,28},{28,16},{1,5},{5... | collective-permute-start | bytes 3145736 | tf_op jit(solution)/shard_map/ppermute | solution.py:55
  39.1 74.5 %collective-permute-start.4 = (bf16[64,128,64]{1,0,2:T(8,128)(2,1)}, bf16[64,128,64]{1,0,2:T(8,128)(2,1)}, u32[]{:S(2)}, u32[]{:S(2)}) collective-permute-start(bf16[64,128,64]{1,0,2:T(8,128)(2,1)} %bitcast.65), channel_id=1, source_target_pairs={{0,8},{4,12},{8,0},{12,4},{16,24},{20,28},{24,16},{28,20},{1,9},{5... | collective-permute-start | bytes 3145736 | tf_op jit(solution)/shard_map/ppermute | solution.py:55
  42.0 71.7 %collective-permute-start.5 = (bf16[64,128,64]{1,0,2:T(8,128)(2,1)}, bf16[64,128,64]{1,0,2:T(8,128)(2,1)}, u32[]{:S(2)}, u32[]{:S(2)}) collective-permute-start(bf16[64,128,64]{1,0,2:T(8,128)(2,1)} %bitcast.64), channel_id=1, source_target_pairs={{0,12},{4,0},{8,4},{12,8},{16,28},{20,16},{24,20},{28,24},{1,13},{... | collective-permute-start | bytes 3145736 | tf_op jit(solution)/shard_map/ppermute | solution.py:55
  68.6 46.1 %collective-permute-start = (bf16[8,64,16,64]{3,2,0,1:T(8,128)(2,1)}, bf16[8,64,16,64]{3,2,0,1:T(8,128)(2,1)}, u32[]{:S(2)}, u32[]{:S(2)}) collective-permute-start(bf16[8,64,16,64]{3,2,0,1:T(8,128)(2,1)} %copy.36), channel_id=1, source_target_pairs={{0,1},{1,2},{2,3},{3,0},{4,5},{5,6},{6,7},{7,4},{8,9},{9,10},{10,1... | collective-permute-start | bytes 3145736 | tf_op jit(solution)/shard_map/ppermute | solution.py:33
  69.4 91.8 %collective-permute-start.1 = (bf16[8,64,16,64]{3,2,0,1:T(8,128)(2,1)}, bf16[8,64,16,64]{3,2,0,1:T(8,128)(2,1)}, u32[]{:S(2)}, u32[]{:S(2)}) collective-permute-start(bf16[8,64,16,64]{3,2,0,1:T(8,128)(2,1)} %copy.36), channel_id=1, source_target_pairs={{0,2},{1,3},{2,0},{3,1},{4,6},{5,7},{6,4},{7,5},{8,10},{9,11},{10,... | collective-permute-start | bytes 3145736 | tf_op jit(solution)/shard_map/ppermute | solution.py:33
  107.6 5.5 %copy-start.1 = (bf16[16,512,128]{2,1,0:T(8,128)(2,1)S(1)}, bf16[16,512,128]{2,1,0:T(8,128)(2,1)}, u32[]{:S(2)}) copy-start(bf16[16,512,128]{2,1,0:T(8,128)(2,1)} %all-gather.2.cloned.1.call-done) | copy-start | bytes 6291460
  111.3 50.4 %collective-permute-start.2 = (bf16[8,64,16,64]{3,2,0,1:T(8,128)(2,1)}, bf16[8,64,16,64]{3,2,0,1:T(8,128)(2,1)S(1)}, u32[]{:S(2)}, u32[]{:S(2)}) collective-permute-start(bf16[8,64,16,64]{3,2,0,1:T(8,128)(2,1)} %copy.36), channel_id=1, source_target_pairs={{0,3},{1,0},{2,1},{3,2},{4,7},{5,4},{6,5},{7,6},{8,11},{9,8},{10,9... | collective-permute-start | bytes 3145736 | tf_op jit(solution)/shard_map/ppermute | solution.py:33
  113.7 48.0 %copy-start.3 = (bf16[16,8,8,16,128]{4,3,2,1,0:T(8,128)(2,1)}, bf16[16,8,8,16,128]{4,3,2,1,0:T(8,128)(2,1)S(1)}, u32[]{:S(2)}) copy-start(bf16[16,8,8,16,128]{4,3,2,1,0:T(8,128)(2,1)S(1)} %slice_dynamic-update-slice_fusion.1) | copy-start | bytes 12582916
  161.7 1.3 copy-start.7
  163.0 26.5 %copy-start.4 = (s32[2,2]{1,0:T(2,128)S(1)}, s32[2,2]{1,0:T(2,128)}, u32[]{:S(2)}) copy-start(s32[2,2]{1,0:T(2,128)} %param.9) | copy-start | bytes 52
  163.0 26.7 %copy-start.5 = (f32[128]{0:T(128)S(1)}, f32[128]{0:T(128)}, u32[]{:S(2)}) copy-start(f32[128]{0:T(128)} %param.10) | copy-start | bytes 1540
  187.4 11.8 %copy-start.2 = (f32[16,64,256,1]{2,1,3,0:T(8,128)}, f32[16,64,256,1]{2,1,3,0:T(8,128)S(1)}, u32[]{:S(2)}) copy-start(f32[16,64,256,1]{2,1,3,0:T(8,128)S(1)} %fusion.1) | copy-start | bytes 3145732
  188.4 35.7 %slice-start = ((f32[512]{0:T(512)}), f32[64]{0:T(128)S(1)}, s32[]{:S(2)}) async-start(f32[512]{0:T(512)} %param.11), calls=%async_computation.2 | async-start | bytes 1024 | tf_op jit(solution)/shard_map/slice | solution.py:108
  188.4 35.8 %copy-start.6 = (f32[512]{0:T(512)S(1)}, f32[512]{0:T(512)}, u32[]{:S(2)}) copy-start(f32[512]{0:T(512)} %param.11) | copy-start | bytes 6148
  188.4 5.2 %collective-permute-start.6 = (f32[4,64,256]{2,1,0:T(8,128)}, f32[4,64,256]{2,1,0:T(8,128)}, u32[]{:S(2)}, u32[]{:S(2)}) collective-permute-start(f32[4,64,256]{2,1,0:T(8,128)} %get-tuple-element.13), channel_id=1, source_target_pairs={{0,1},{1,2},{2,3},{3,0},{4,5},{5,6},{6,7},{7,4},{8,9},{9,10},{10,1... | collective-permute-start | bytes 786440 | tf_op jit(solution)/shard_map/ppermute | solution.py:72
  188.4 10.8 %collective-permute-start.7 = (f32[4,64,256]{2,1,0:T(8,128)}, f32[4,64,256]{2,1,0:T(8,128)}, u32[]{:S(2)}, u32[]{:S(2)}) collective-permute-start(f32[4,64,256]{2,1,0:T(8,128)} %get-tuple-element.15), channel_id=1, source_target_pairs={{0,2},{1,3},{2,0},{3,1},{4,6},{5,7},{6,4},{7,5},{8,10},{9,11},{10,... | collective-permute-start | bytes 786440 | tf_op jit(solution)/shard_map/ppermute | solution.py:72
  188.8 12.4 %collective-permute-start.8 = (f32[4,64,256]{2,1,0:T(8,128)S(1)}, f32[4,64,256]{2,1,0:T(8,128)}, u32[]{:S(2)}, u32[]{:S(2)}) collective-permute-start(f32[4,64,256]{2,1,0:T(8,128)S(1)} %get-tuple-element.14), channel_id=1, source_target_pairs={{0,3},{1,0},{2,1},{3,2},{4,7},{5,4},{6,5},{7,6},{8,11},{9,8},{10,9... | collective-permute-start | bytes 786440 | tf_op jit(solution)/shard_map/ppermute | solution.py:72
  209.1 15.2 %collective-permute-start.10 = (f32[2,64,128]{2,1,0:T(8,128)S(1)}, f32[2,64,128]{2,1,0:T(8,128)S(1)}, u32[]{:S(2)}, u32[]{:S(2)}) collective-permute-start(f32[2,64,128]{2,1,0:T(8,128)S(1)} %bitcast.88), channel_id=1, source_target_pairs={{0,1},{1,9},{2,17},{3,25},{4,4},{5,12},{6,20},{7,28},{8,5},{9,13},... | collective-permute-start | bytes 196616 | tf_op jit(solution)/shard_map/ppermute | solution.py:96
  213.3 11.0 %collective-permute-start.11 = (f32[2,64,128]{2,1,0:T(8,128)S(1)}, f32[2,64,128]{2,1,0:T(8,128)S(1)}, u32[]{:S(2)}, u32[]{:S(2)}) collective-permute-start(f32[2,64,128]{2,1,0:T(8,128)S(1)} %bitcast.87), channel_id=1, source_target_pairs={{0,4},{1,12},{2,20},{3,28},{4,5},{5,13},{6,21},{7,29},{8,0},{9,8},... | collective-permute-start | bytes 196616 | tf_op jit(solution)/shard_map/ppermute | solution.py:96
  215.9 9.0 %collective-permute-start.12 = (f32[2,64,128]{2,1,0:T(8,128)S(1)}, f32[2,64,128]{2,1,0:T(8,128)S(1)}, u32[]{:S(2)}, u32[]{:S(2)}) collective-permute-start(f32[2,64,128]{2,1,0:T(8,128)S(1)} %bitcast.86), channel_id=1, source_target_pairs={{0,5},{1,13},{2,21},{3,29},{4,0},{5,8},{6,16},{7,24},{8,1},{9,9},{... | collective-permute-start | bytes 196616 | tf_op jit(solution)/shard_map/ppermute | solution.py:96
  221.0 8.4 %collective-permute-start.9 = (f32[2,64,128]{2,1,0:T(8,128)S(1)}, f32[2,64,128]{2,1,0:T(8,128)S(1)}, u32[]{:S(2)}, u32[]{:S(2)}) collective-permute-start(f32[2,64,128]{2,1,0:T(8,128)S(1)} %bitcast.85), channel_id=1, source_target_pairs={{0,0},{1,8},{2,16},{3,24},{4,1},{5,9},{6,17},{7,25},{8,4},{9,12},{... | collective-permute-start | bytes 196616 | tf_op jit(solution)/shard_map/ppermute | solution.py:96
Sparse Core Ops, SparseCore 0:
  9.5 98.0 all-gather.1

commit v13 on v9

--- a/solution.py
+++ b/solution.py
@@ -20,17 +20,18 @@
         pairs = amps.shape[0]
         vir_total = b_blk * n_narrow
 
+        c_sub = c_blk // n_wide
+        left_part = lax.dynamic_slice_in_dim(left_fit, w * c_sub, c_sub, 1)
+        left_part = left_part.reshape(rows, c_sub, span, q_blk).transpose(2, 3, 1, 0)
+        left_send = jnp.concatenate([left_part] * GROUPS, axis=0)
+        left_recv = lax.all_to_all(left_send, "narrow", 0, 0, tiled=True)
+        amps, left_recv = lax.optimization_barrier((amps, left_recv))
         amps_blocks = [amps]
         for shift in range(1, n_narrow):
             perm = [(i, (i + shift) % n_narrow) for i in range(n_narrow)]
             amps_blocks.append(lax.ppermute(amps, "narrow", perm))
         amps_all = jnp.stack(amps_blocks, axis=1)
 
-        c_sub = c_blk // n_wide
-        left_part = lax.dynamic_slice_in_dim(left_fit, w * c_sub, c_sub, 1)
-        left_part = left_part.reshape(rows, c_sub, span, q_blk).transpose(2, 3, 1, 0)
-        left_send = jnp.concatenate([left_part] * GROUPS, axis=0)
-        left_recv = lax.all_to_all(left_send, "narrow", 0, 0, tiled=True)
         left_rev = [left_recv[(n_narrow - j) % n_narrow][None] for j in range(n_narrow)]
         left_recv = lax.dynamic_slice_in_dim(
             jnp.concatenate(left_rev * 2, axis=0), n_narrow - n, n_narrow, 0

time: 210 us -> 241 us (1.15)
  starting transfers between devices: 41.3 us -> 65.4 us
  waiting for transfers between devices: 71.7 us -> 83.2 us
  local copies, waits for them, and re-layouts: 50.1 us -> 45.1 us
    ppermute x7, waiting for transfers between devices: 2.8 us -> 40.4 us  [body(): amps_blocks.append(lax.ppermute(amps, 'narrow', perm))]
    ppermute x3, starting transfers between devices: 3.05 us -> 22.9 us  [body(): summed = summed + lax.ppermute(piece, 'wide', perm)]
    ppermute x3, waiting for transfers between devices: 20.4 us -> 2.92 us  [body(): piece = lax.ppermute(piece, 'narrow', perm)]
    ppermute x7, starting transfers between devices: 9.66 us -> 22 us  [body(): amps_blocks.append(lax.ppermute(amps, 'narrow', perm))]
    all_gather x1, waiting for transfers between devices: 8.48 us -> 0.01 us  [body(): left_all = lax.all_gather(left_recv, 'wide', axis=0, tiled=False)]
    ppermute x3, starting transfers between devices: 9.55 us -> 2.48 us  [body(): piece = lax.ppermute(piece, 'narrow', perm)]
    unnamed x39, local copies, waits for them, and re-layouts: 24.4 us -> 21.3 us
  transfers between devices with their start and end apart: 19 -> 19, of which waited for: 9 -> 10; matrix products, arithmetic and copies ran while one was open for 21% -> 16% of each run, Pallas kernels for 0% -> 0%
where the time goes in v13:
time: 241 us; the launch traced here: 238 us
  waiting for transfers between devices  83.2 us (35%)
  starting transfers between devices  65.4 us (27%)
  local copies, waits for them, and re-layouts  45.1 us (19%)
  matrix products  27.2 us (11%)
  between operations  13.8 us (6%)
  other arithmetic  3.49 us (1%)
    ppermute x7, waiting for transfers between devices, body(): amps_blocks.append(lax.ppermute(amps, 'narrow', perm))  40.4 us
    all_to_all x1, waiting for transfers between devices, body(): left_recv = lax.all_to_all(left_send, 'narrow', 0, 0, tiled=True)  24.6 us
    ppermute x3, starting transfers between devices, body(): summed = summed + lax.ppermute(piece, 'wide', perm)  22.9 us
    ppermute x7, starting transfers between devices, body(): amps_blocks.append(lax.ppermute(amps, 'narrow', perm))  22 us
    unnamed x39, local copies, waits for them, and re-layouts  21.3 us
    dot_general x1, matrix products, body(): jnp.einsum('wkqia,pkwid->padq', left_all, amps_all, preferred_element_typ...  16.1 us
    ppermute x4, starting transfers between devices, body(): piece = lax.ppermute(piece, ('narrow', 'wide'), perm)  12.5 us
    dot_general x1, matrix products, body(): jnp.einsum('padq,bdq->pab', inter, right_group, preferred_element_type=jn...  11.1 us
  transfers between devices with their start and end apart: 19, of which 10 were waited for; matrix products, arithmetic and copies ran while one was open for 16% of the time, Pallas kernels for 0%

profile of v13, /device:TPU:5, one launch (start us, length us, event | category | flops | bytes accessed | tf_op | source)
XLA Modules:
  0.0 238.3 jit_solution(4142716600556169213)
XLA Ops:
  11.5 4.3 %reshape.91 = bf16[8,2,32768]{2,1,0:T(2,128)(2,1)} reshape(bf16[8,64,16,64]{3,2,1,0:T(8,128)(2,1)} %bitcast.82) | data formatting | bytes 2097152
  15.8 5.5 %all-to-all-start = ((bf16[8,2,32768]{2,1,0:T(2,128)(2,1)}), bf16[8,2,32768]{2,1,0:T(2,128)(2,1)S(1)}, u32[]{:S(2)}, u32[]{:S(2)}) async-start(bf16[8,2,32768]{2,1,0:T(2,128)(2,1)} %reshape.91), calls=%async_computation | async-start | bytes 2097152 | tf_op jit(solution)/shard_map/all_to_all | solution.py:27
  21.4 24.6 %all-to-all-done = bf16[8,2,32768]{2,1,0:T(2,128)(2,1)S(1)} async-done(((bf16[8,2,32768]{2,1,0:T(2,128)(2,1)}), bf16[8,2,32768]{2,1,0:T(2,128)(2,1)S(1)}, u32[]{:S(2)}, u32[]{:S(2)}) %all-to-all-start) | async-done | bytes 1048608 | tf_op jit(solution)/shard_map/all_to_all | solution.py:27
  48.4 4.4 %copy.48 = bf16[8,64,16,64]{3,2,1,0:T(8,128)(2,1)} copy(bf16[8,64,16,64]{1,2,3,0:T(8,128)(2,1)S(1)} %constant_dynamic-slice_fusion.9) | data formatting | bytes 2097152 | tf_op jit(solution)/shard_map/dynamic_slice | solution.py:36
  52.9 6.4 %copy.50 = bf16[64,128,256]{1,2,0:T(8,128)(2,1)} copy(bf16[64,128,256]{2,1,0:T(8,128)(2,1)} %param.8) | data formatting | bytes 8388608 | tf_op args[2]
  61.1 3.8 %constant_dynamic-slice_fusion.8 = (bf16[64,128,1,64]{1,3,2,0:T(8,128)(2,1)S(1)}, bf16[64,128,1,64]{1,3,2,0:T(8,128)(2,1)S(1)}, bf16[64,128,1,64]{1,3,2,0:T(8,128)(2,1)S(1)}, bf16[64,128,1,64]{1,3,2,0:T(8,128)(2,1)S(1)}) fusion(bf16[64,128,4,64]{1,3,2,0:T(8,128)(2,1)} %bitcast.81, s32[]{:T(128)S(6)} %select_n.163, s32[]{:T(128)S(6)} %select_n.169, ...), kind=kLoop, calls=%fused_computation.57 | loop fusion | bytes 8388624 | tf_op jit(solution)/shard_map/jit(dynamic_index_in_dim)/dynamic_slice | solution.py:46
  73.2 2.5 %collective-permute-start.3 = (bf16[16,64,128]{2,1,0:T(8,128)(2,1)S(1)}, bf16[16,64,128]{2,1,0:T(8,128)(2,1)S(1)}, u32[]{:S(2)}, u32[]{:S(2)}) collective-permute-start(bf16[16,64,128]{2,1,0:T(8,128)(2,1)S(1)} %copy-done.3), channel_id=1, source_target_pairs={{0,16},{4,20},{8,24},{12,28},{16,0},{20,4},{24,8},{28,12},{1,17},{... | collective-permute-start | bytes 786440 | tf_op jit(solution)/shard_map/ppermute | solution.py:32
  77.4 2.3 collective-permute-start.4
  81.3 35.9 %collective-permute-done.2 = bf16[16,64,128]{2,1,0:T(8,128)(2,1)S(1)} collective-permute-done((bf16[16,64,128]{2,1,0:T(8,128)(2,1)S(1)}, bf16[16,64,128]{2,1,0:T(8,128)(2,1)S(1)}, u32[]{:S(2)}, u32[]{:S(2)}) %collective-permute-start.2) | collective-permute-done | bytes 262176 | tf_op jit(solution)/shard_map/ppermute | solution.py:32
  117.2 6.5 %collective-permute-start.5 = (bf16[16,64,128]{2,1,0:T(8,128)(2,1)S(1)}, bf16[16,64,128]{2,1,0:T(8,128)(2,1)S(1)}, u32[]{:S(2)}, u32[]{:S(2)}) collective-permute-start(bf16[16,64,128]{2,1,0:T(8,128)(2,1)S(1)} %copy-done.3), channel_id=1, source_target_pairs={{0,24},{4,28},{8,0},{12,4},{16,8},{20,12},{24,16},{28,20},{1,25},{... | collective-permute-start | bytes 786440 | tf_op jit(solution)/shard_map/ppermute | solution.py:32
  124.4 8.4 %collective-permute-start.6 = (bf16[16,64,128]{2,1,0:T(8,128)(2,1)S(1)}, bf16[16,64,128]{2,1,0:T(8,128)(2,1)S(1)}, u32[]{:S(2)}, u32[]{:S(2)}) collective-permute-start(bf16[16,64,128]{2,1,0:T(8,128)(2,1)S(1)} %copy-done.3), channel_id=1, source_target_pairs={{0,28},{4,0},{8,4},{12,8},{16,12},{20,16},{24,20},{28,24},{1,29},{... | collective-permute-start | bytes 786440 | tf_op jit(solution)/shard_map/ppermute | solution.py:32
  134.5 4.0 %collective-permute-done.5 = bf16[16,64,128]{2,1,0:T(8,128)(2,1)S(1)} collective-permute-done((bf16[16,64,128]{2,1,0:T(8,128)(2,1)S(1)}, bf16[16,64,128]{2,1,0:T(8,128)(2,1)S(1)}, u32[]{:S(2)}, u32[]{:S(2)}) %collective-permute-start.5) | collective-permute-done | bytes 262176 | tf_op jit(solution)/shard_map/ppermute | solution.py:32
  140.4 16.1 %fusion.3 = bf16[16,128,64,64,1,1]{1,3,5,0,2,4:T(8,128)(2,1)} fusion(bf16[4,8,64,16,64,1]{4,3,2,1,0,5:T(8,128)(2,1)} %bitcast.99, bf16[16,8,4,16,128]{4,3,2,0,1:T(8,128)(2,1)} %constant_dynamic-update-slice_fusion), kind=kOutput, calls=%fused_computation.3 | convolution fusion | flops 8589934592 | bytes 23068672 | tf_op jit(solution)/shard_map/wkqia,pkwid->padq/dot_general | solution.py:56
  156.6 2.9 %collective-permute-done.7 = bf16[64,128,64]{1,0,2:T(8,128)(2,1)} collective-permute-done((bf16[64,128,64]{1,0,2:T(8,128)(2,1)}, bf16[64,128,64]{1,0,2:T(8,128)(2,1)}, u32[]{:S(2)}, u32[]{:S(2)}) %collective-permute-start.7) | collective-permute-done | bytes 1048608 | tf_op jit(solution)/shard_map/ppermute | solution.py:53
  159.5 11.1 %fusion.1 = f32[16,64,256,1]{2,1,3,0:T(8,128)S(1)} fusion(bf16[16,128,64,64,1,1]{1,3,5,0,2,4:T(8,128)(2,1)} %fusion.3, bf16[64,128,64]{1,0,2:T(8,128)(2,1)} %collective-permute-done.9, bf16[64,128,64]{1,0,2:T(8,128)(2,1)} %collective-permute-done.8, bf16[64,128,64]{1,0,2:T(8,128)(2,1)} %collective-permute-done.7, bf16[64,128,64]{1,0,2:T(8,128)(2,1)S(1)} %bitcast.87), kind=kOutput, calls=%fused_computation.2 | convolution fusion | flops 4311744512 | bytes 22020096 | tf_op jit(solution)/shard_map/padq,bdq->pab/dot_general | solution.py:61
  171.5 21.2 %collective-permute-start.12 = (f32[4,64,256]{2,1,0:T(8,128)}, f32[4,64,256]{2,1,0:T(8,128)}, u32[]{:S(2)}, u32[]{:S(2)}) collective-permute-start(f32[4,64,256]{2,1,0:T(8,128)} %get-tuple-element.18), channel_id=1, source_target_pairs={{0,3},{1,0},{2,1},{3,2},{4,7},{5,4},{6,5},{7,6},{8,11},{9,8},{10,9... | collective-permute-start | bytes 786440 | tf_op jit(solution)/shard_map/ppermute | solution.py:70
  194.8 4.1 %collective-permute-done.12 = f32[4,64,256]{2,1,0:T(8,128)} collective-permute-done((f32[4,64,256]{2,1,0:T(8,128)}, f32[4,64,256]{2,1,0:T(8,128)}, u32[]{:S(2)}, u32[]{:S(2)}) %collective-permute-start.12) | collective-permute-done | bytes 262176 | tf_op jit(solution)/shard_map/ppermute | solution.py:70
  198.9 2.5 %collective-permute-done.11 = f32[4,64,256]{2,1,0:T(8,128)} collective-permute-done((f32[4,64,256]{2,1,0:T(8,128)}, f32[4,64,256]{2,1,0:T(8,128)}, u32[]{:S(2)}, u32[]{:S(2)}) %collective-permute-start.11) | collective-permute-done | bytes 262176 | tf_op jit(solution)/shard_map/ppermute | solution.py:70
  201.4 3.5 %collective-permute-done.10 = f32[4,64,256]{2,1,0:T(8,128)} collective-permute-done((f32[4,64,256]{2,1,0:T(8,128)S(1)}, f32[4,64,256]{2,1,0:T(8,128)}, u32[]{:S(2)}, u32[]{:S(2)}) %collective-permute-start.10) | collective-permute-done | bytes 262176 | tf_op jit(solution)/shard_map/ppermute | solution.py:70
  207.3 2.8 %concatenate.16 = f32[4,64,8,64]{3,2,1,0:T(8,128)S(1)} concatenate(f32[4,64,1,64]{3,2,1,0:T(1,128)} %get-tuple-element.23, f32[4,64,1,64]{3,2,1,0:T(1,128)S(1)} %get-tuple-element.22, f32[4,64,1,64]{3,2,1,0:T(1,128)S(1)} %get-tuple-element.21, f32[4,64,1,64]{3,2,1,0:T(1,128)S(1)} %get-tuple-element.20, f32[4,64,1,64]{3,2,1,0:T(1,128)} %get-tuple-element.23, ...), dimensions={2} | concatenate | bytes 1048576 | tf_op jit(solution)/shard_map/concatenate | solution.py:73
  214.7 4.8 %collective-permute-start.15 = (f32[2,64,128]{2,1,0:T(8,128)S(1)}, f32[2,64,128]{2,1,0:T(8,128)S(1)}, u32[]{:S(2)}, u32[]{:S(2)}) collective-permute-start(f32[2,64,128]{2,1,0:T(8,128)S(1)} %bitcast.97), channel_id=1, source_target_pairs={{0,4},{1,12},{2,20},{3,28},{4,5},{5,13},{6,21},{7,29},{8,0},{9,8},... | collective-permute-start | bytes 196616 | tf_op jit(solution)/shard_map/ppermute | solution.py:94
  219.5 2.9 %collective-permute-start.13 = (f32[2,64,128]{2,1,0:T(8,128)S(1)}, f32[2,64,128]{2,1,0:T(8,128)S(1)}, u32[]{:S(2)}, u32[]{:S(2)}) collective-permute-start(f32[2,64,128]{2,1,0:T(8,128)S(1)} %bitcast.96), channel_id=1, source_target_pairs={{0,0},{1,8},{2,16},{3,24},{4,1},{5,9},{6,17},{7,25},{8,4},{9,12},{... | collective-permute-start | bytes 196616 | tf_op jit(solution)/shard_map/ppermute | solution.py:94
  222.4 2.9 %collective-permute-start.14 = (f32[2,64,128]{2,1,0:T(8,128)S(1)}, f32[2,64,128]{2,1,0:T(8,128)S(1)}, u32[]{:S(2)}, u32[]{:S(2)}) collective-permute-start(f32[2,64,128]{2,1,0:T(8,128)S(1)} %bitcast.95), channel_id=1, source_target_pairs={{0,1},{1,9},{2,17},{3,25},{4,4},{5,12},{6,20},{7,28},{8,5},{9,13},... | collective-permute-start | bytes 196616 | tf_op jit(solution)/shard_map/ppermute | solution.py:94
  225.5 3.5 %collective-permute-done.13 = f32[2,64,128]{2,1,0:T(8,128)S(1)} collective-permute-done((f32[2,64,128]{2,1,0:T(8,128)S(1)}, f32[2,64,128]{2,1,0:T(8,128)S(1)}, u32[]{:S(2)}, u32[]{:S(2)}) %collective-permute-start.13) | collective-permute-done | bytes 65568 | tf_op jit(solution)/shard_map/ppermute | solution.py:94
  (85 shorter events, 37.6 us)
Async XLA Ops:
  15.8 30.1 %all-to-all-start = ((bf16[8,2,32768]{2,1,0:T(2,128)(2,1)}), bf16[8,2,32768]{2,1,0:T(2,128)(2,1)S(1)}, u32[]{:S(2)}, u32[]{:S(2)}) async-start(bf16[8,2,32768]{2,1,0:T(2,128)(2,1)} %reshape.91), calls=%async_computation | async-start | bytes 2097152 | tf_op jit(solution)/shard_map/all_to_all | solution.py:27
  21.3 119.1 %all-gather.3.cloned.1.call-start = ((), (), s32[]{:S(2)}) async-start(), calls=%async_computation.1 | async-start | bytes 10485760 | tf_op jit(solution)/shard_map/all_gather | solution.py:39
  59.3 13.8 %collective-permute-start = (bf16[16,64,128]{2,1,0:T(8,128)(2,1)S(1)}, bf16[16,64,128]{2,1,0:T(8,128)(2,1)}, u32[]{:S(2)}, u32[]{:S(2)}) collective-permute-start(bf16[16,64,128]{2,1,0:T(8,128)(2,1)S(1)} %copy-done.3), channel_id=1, source_target_pairs={{0,4},{4,8},{8,12},{12,16},{16,20},{20,24},{24,28},{28,0},{1,5},{5... | collective-permute-start | bytes 786440 | tf_op jit(solution)/shard_map/ppermute | solution.py:32
  61.1 16.2 %collective-permute-start.1 = (bf16[16,64,128]{2,1,0:T(8,128)(2,1)S(1)}, bf16[16,64,128]{2,1,0:T(8,128)(2,1)}, u32[]{:S(2)}, u32[]{:S(2)}) collective-permute-start(bf16[16,64,128]{2,1,0:T(8,128)(2,1)S(1)} %copy-done.3), channel_id=1, source_target_pairs={{0,8},{4,12},{8,16},{12,20},{16,24},{20,28},{24,0},{28,4},{1,9},{5... | collective-permute-start | bytes 786440 | tf_op jit(solution)/shard_map/ppermute | solution.py:32
  65.6 91.0 %collective-permute-start.9 = (bf16[64,128,64]{1,0,2:T(8,128)(2,1)S(1)}, bf16[64,128,64]{1,0,2:T(8,128)(2,1)}, u32[]{:S(2)}, u32[]{:S(2)}) collective-permute-start(bf16[64,128,64]{1,0,2:T(8,128)(2,1)S(1)} %bitcast.86), channel_id=1, source_target_pairs={{0,12},{4,0},{8,4},{12,8},{16,28},{20,16},{24,20},{28,24},{1,13},{... | collective-permute-start | bytes 3145736 | tf_op jit(solution)/shard_map/ppermute | solution.py:53
  69.5 87.1 %collective-permute-start.8 = (bf16[64,128,64]{1,0,2:T(8,128)(2,1)}, bf16[64,128,64]{1,0,2:T(8,128)(2,1)}, u32[]{:S(2)}, u32[]{:S(2)}) collective-permute-start(bf16[64,128,64]{1,0,2:T(8,128)(2,1)} %bitcast.61), channel_id=1, source_target_pairs={{0,8},{4,12},{8,0},{12,4},{16,24},{20,28},{24,16},{28,20},{1,9},{5... | collective-permute-start | bytes 3145736 | tf_op jit(solution)/shard_map/ppermute | solution.py:53
  71.9 45.4 %collective-permute-start.2 = (bf16[16,64,128]{2,1,0:T(8,128)(2,1)S(1)}, bf16[16,64,128]{2,1,0:T(8,128)(2,1)S(1)}, u32[]{:S(2)}, u32[]{:S(2)}) collective-permute-start(bf16[16,64,128]{2,1,0:T(8,128)(2,1)S(1)} %copy-done.3), channel_id=1, source_target_pairs={{0,12},{4,16},{8,20},{12,24},{16,28},{20,0},{24,4},{28,8},{1,13},{... | collective-permute-start | bytes 786440 | tf_op jit(solution)/shard_map/ppermute | solution.py:32
  73.2 51.3 %collective-permute-start.3 = (bf16[16,64,128]{2,1,0:T(8,128)(2,1)S(1)}, bf16[16,64,128]{2,1,0:T(8,128)(2,1)S(1)}, u32[]{:S(2)}, u32[]{:S(2)}) collective-permute-start(bf16[16,64,128]{2,1,0:T(8,128)(2,1)S(1)} %copy-done.3), channel_id=1, source_target_pairs={{0,16},{4,20},{8,24},{12,28},{16,0},{20,4},{24,8},{28,12},{1,17},{... | collective-permute-start | bytes 786440 | tf_op jit(solution)/shard_map/ppermute | solution.py:32
  77.4 56.2 %collective-permute-start.4 = (bf16[16,64,128]{2,1,0:T(8,128)(2,1)S(1)}, bf16[16,64,128]{2,1,0:T(8,128)(2,1)S(1)}, u32[]{:S(2)}, u32[]{:S(2)}) collective-permute-start(bf16[16,64,128]{2,1,0:T(8,128)(2,1)S(1)} %copy-done.3), channel_id=1, source_target_pairs={{0,20},{4,24},{8,28},{12,0},{16,4},{20,8},{24,12},{28,16},{1,21},{... | collective-permute-start | bytes 786440 | tf_op jit(solution)/shard_map/ppermute | solution.py:32
  117.2 21.3 %collective-permute-start.5 = (bf16[16,64,128]{2,1,0:T(8,128)(2,1)S(1)}, bf16[16,64,128]{2,1,0:T(8,128)(2,1)S(1)}, u32[]{:S(2)}, u32[]{:S(2)}) collective-permute-start(bf16[16,64,128]{2,1,0:T(8,128)(2,1)S(1)} %copy-done.3), channel_id=1, source_target_pairs={{0,24},{4,28},{8,0},{12,4},{16,8},{20,12},{24,16},{28,20},{1,25},{... | collective-permute-start | bytes 786440 | tf_op jit(solution)/shard_map/ppermute | solution.py:32
  124.4 15.3 %collective-permute-start.6 = (bf16[16,64,128]{2,1,0:T(8,128)(2,1)S(1)}, bf16[16,64,128]{2,1,0:T(8,128)(2,1)S(1)}, u32[]{:S(2)}, u32[]{:S(2)}) collective-permute-start(bf16[16,64,128]{2,1,0:T(8,128)(2,1)S(1)} %copy-done.3), channel_id=1, source_target_pairs={{0,28},{4,0},{8,4},{12,8},{16,12},{20,16},{24,20},{28,24},{1,29},{... | collective-permute-start | bytes 786440 | tf_op jit(solution)/shard_map/ppermute | solution.py:32
  133.5 25.9 %collective-permute-start.7 = (bf16[64,128,64]{1,0,2:T(8,128)(2,1)}, bf16[64,128,64]{1,0,2:T(8,128)(2,1)}, u32[]{:S(2)}, u32[]{:S(2)}) collective-permute-start(bf16[64,128,64]{1,0,2:T(8,128)(2,1)} %bitcast.88), channel_id=1, source_target_pairs={{0,4},{4,8},{8,12},{12,0},{16,20},{20,24},{24,28},{28,16},{1,5},{5... | collective-permute-start | bytes 3145736 | tf_op jit(solution)/shard_map/ppermute | solution.py:53
  159.5 34.9 %copy-start.4 = (s32[2,2]{1,0:T(2,128)S(1)}, s32[2,2]{1,0:T(2,128)}, u32[]{:S(2)}) copy-start(s32[2,2]{1,0:T(2,128)} %param.9) | copy-start | bytes 52
  159.5 35.1 %copy-start.5 = (f32[128]{0:T(128)S(1)}, f32[128]{0:T(128)}, u32[]{:S(2)}) copy-start(f32[128]{0:T(128)} %param.10) | copy-start | bytes 1540
  170.6 60.8 %copy-start.1 = (bf16[64,64,256]{2,1,0:T(8,128)(2,1)S(1)}, bf16[64,64,256]{2,1,0:T(8,128)(2,1)}, u32[]{:S(2)}) copy-start(bf16[64,64,256]{2,1,0:T(8,128)(2,1)} %param.7) | copy-start | bytes 6291460
  171.5 53.8 %slice-start = ((f32[512]{0:T(512)}), f32[64]{0:T(128)S(1)}, s32[]{:S(2)}) async-start(f32[512]{0:T(512)} %param.11), calls=%async_computation.2 | async-start | bytes 1024 | tf_op jit(solution)/shard_map/slice | solution.py:106
  171.5 53.9 %copy-start.6 = (f32[512]{0:T(512)S(1)}, f32[512]{0:T(512)}, u32[]{:S(2)}) copy-start(f32[512]{0:T(512)} %param.11) | copy-start | bytes 6148
  171.5 27.4 %collective-permute-start.12 = (f32[4,64,256]{2,1,0:T(8,128)}, f32[4,64,256]{2,1,0:T(8,128)}, u32[]{:S(2)}, u32[]{:S(2)}) collective-permute-start(f32[4,64,256]{2,1,0:T(8,128)} %get-tuple-element.18), channel_id=1, source_target_pairs={{0,3},{1,0},{2,1},{3,2},{4,7},{5,4},{6,5},{7,6},{8,11},{9,8},{10,9... | collective-permute-start | bytes 786440 | tf_op jit(solution)/shard_map/ppermute | solution.py:70
  192.7 8.6 %collective-permute-start.11 = (f32[4,64,256]{2,1,0:T(8,128)}, f32[4,64,256]{2,1,0:T(8,128)}, u32[]{:S(2)}, u32[]{:S(2)}) collective-permute-start(f32[4,64,256]{2,1,0:T(8,128)} %get-tuple-element.19), channel_id=1, source_target_pairs={{0,2},{1,3},{2,0},{3,1},{4,6},{5,7},{6,4},{7,5},{8,10},{9,11},{10,... | collective-permute-start | bytes 786440 | tf_op jit(solution)/shard_map/ppermute | solution.py:70
  192.9 11.9 %collective-permute-start.10 = (f32[4,64,256]{2,1,0:T(8,128)S(1)}, f32[4,64,256]{2,1,0:T(8,128)}, u32[]{:S(2)}, u32[]{:S(2)}) collective-permute-start(f32[4,64,256]{2,1,0:T(8,128)S(1)} %get-tuple-element.17), channel_id=1, source_target_pairs={{0,1},{1,2},{2,3},{3,0},{4,5},{5,6},{6,7},{7,4},{8,9},{9,10},{10,1... | collective-permute-start | bytes 786440 | tf_op jit(solution)/shard_map/ppermute | solution.py:70
  212.8 12.7 %collective-permute-start.16 = (f32[2,64,128]{2,1,0:T(8,128)S(1)}, f32[2,64,128]{2,1,0:T(8,128)S(1)}, u32[]{:S(2)}, u32[]{:S(2)}) collective-permute-start(f32[2,64,128]{2,1,0:T(8,128)S(1)} %bitcast.98), channel_id=1, source_target_pairs={{0,5},{1,13},{2,21},{3,29},{4,0},{5,8},{6,16},{7,24},{8,1},{9,9},{... | collective-permute-start | bytes 196616 | tf_op jit(solution)/shard_map/ppermute | solution.py:94
  214.7 10.8 %collective-permute-start.15 = (f32[2,64,128]{2,1,0:T(8,128)S(1)}, f32[2,64,128]{2,1,0:T(8,128)S(1)}, u32[]{:S(2)}, u32[]{:S(2)}) collective-permute-start(f32[2,64,128]{2,1,0:T(8,128)S(1)} %bitcast.97), channel_id=1, source_target_pairs={{0,4},{1,12},{2,20},{3,28},{4,5},{5,13},{6,21},{7,29},{8,0},{9,8},... | collective-permute-start | bytes 196616 | tf_op jit(solution)/shard_map/ppermute | solution.py:94
  219.5 9.5 %collective-permute-start.13 = (f32[2,64,128]{2,1,0:T(8,128)S(1)}, f32[2,64,128]{2,1,0:T(8,128)S(1)}, u32[]{:S(2)}, u32[]{:S(2)}) collective-permute-start(f32[2,64,128]{2,1,0:T(8,128)S(1)} %bitcast.96), channel_id=1, source_target_pairs={{0,0},{1,8},{2,16},{3,24},{4,1},{5,9},{6,17},{7,25},{8,4},{9,12},{... | collective-permute-start | bytes 196616 | tf_op jit(solution)/shard_map/ppermute | solution.py:94
  222.4 8.3 %collective-permute-start.14 = (f32[2,64,128]{2,1,0:T(8,128)S(1)}, f32[2,64,128]{2,1,0:T(8,128)S(1)}, u32[]{:S(2)}, u32[]{:S(2)}) collective-permute-start(f32[2,64,128]{2,1,0:T(8,128)S(1)} %bitcast.95), channel_id=1, source_target_pairs={{0,1},{1,9},{2,17},{3,25},{4,4},{5,12},{6,20},{7,28},{8,5},{9,13},... | collective-permute-start | bytes 196616 | tf_op jit(solution)/shard_map/ppermute | solution.py:94
  (3 other events, 38.8 us)
Sparse Core Ops, SparseCore 0:
  53.0 57.9 all-gather.2

commit v14 on v11

--- a/solution.py
+++ b/solution.py
@@ -20,18 +20,34 @@
         pairs = amps.shape[0]
         vir_total = b_blk * n_narrow
 
+        def perm_of(shift, step):
+            return [
+                (gg * span + i, ((gg + step) % GROUPS) * span + (i + shift) % span)
+                for gg in range(GROUPS)
+                for i in range(span)
+            ]
+
+        own_set = [amps] + [lax.ppermute(amps, "narrow", perm_of(0, step)) for step in range(1, GROUPS)]
+        group_set = jnp.stack(own_set, axis=0)
+        shifted_sets = [group_set] + [
+            lax.ppermute(group_set, "narrow", perm_of(shift, 0)) for shift in range(1, span)
+        ]
+        amps_all = jnp.stack(shifted_sets, axis=1)
+
+        def rotate_back(x, by, size, axis):
+            rev = [lax.slice_in_dim(x, (size - j) % size, (size - j) % size + 1, axis=axis) for j in range(size)]
+            return lax.dynamic_slice_in_dim(jnp.concatenate(rev * 2, axis=axis), size - by, size, axis)
+
         c_sub = c_blk // n_wide
         left_part = lax.dynamic_slice_in_dim(left_fit, w * c_sub, c_sub, 1)
         left_part = left_part.reshape(rows, c_sub, span, q_blk).transpose(2, 3, 1, 0)
-        left_piece = left_part[0].size
-        left_send = jnp.concatenate([left_part.reshape(span, left_piece)] * GROUPS, axis=0)
-        amps_send = jnp.broadcast_to(amps.reshape(1, -1), (n_narrow, amps.size))
-        both = lax.all_to_all(
-            jnp.concatenate([left_send, amps_send], axis=1), "narrow", 0, 0, tiled=True
-        )
-        left_recv = both[:, :left_piece].reshape((n_narrow,) + left_part.shape[1:])
-        amps_all = both[:, left_piece:].reshape(n_narrow, pairs, n_wide, c_sub, amps.shape[2])
+        left_send = jnp.concatenate([left_part] * GROUPS, axis=0)
+        left_recv = lax.all_to_all(left_send, "narrow", 0, 0, tiled=True)
+        left_recv = left_recv.reshape((GROUPS, span) + left_recv.shape[1:])
+        left_recv = rotate_back(rotate_back(left_recv, r, span, 1), g, GROUPS, 0)
+        left_recv = left_recv.reshape((n_narrow,) + left_recv.shape[2:])
         left_all = lax.all_gather(left_recv, "wide", axis=0, tiled=False)
+        amps_all = amps_all.reshape(n_narrow, pairs, n_wide, c_sub, amps.shape[2])
 
         right_split = right_fit.reshape(b_blk, d_blk, span, q_blk)
         chunks = []

time: 263 us -> 207 us (0.79)
  blocking collectives: 75.5 us -> 0 us
  waiting for transfers between devices: 51.8 us -> 86.6 us
  local copies, waits for them, and re-layouts: 58.2 us -> 42.1 us
  starting transfers between devices: 20.9 us -> 27.7 us
  other arithmetic: 12 us -> 7.53 us
    all_to_all x1 -> x0, blocking collectives: 75.5 us -> none  [body(): lax.all_to_all(jnp.concatenate([left_send, amps_send], axis=1), 'narrow',...]
    all_to_all x0 -> x1, waiting for transfers between devices: none -> 24.5 us  [body(): left_recv = lax.all_to_all(left_send, 'narrow', 0, 0, tiled=True)]
    all_gather x1, waiting for transfers between devices: 37.2 us -> 15.9 us  [body(): left_all = lax.all_gather(left_recv, 'wide', axis=0, tiled=False)]
    unnamed x24, local copies, waits for them, and re-layouts: 34.2 us -> 14.2 us
    ppermute x0 -> x4, waiting for transfers between devices: none -> 18.7 us  [the longest x1 14.6 us: body(): lax.ppermute(amps, 'narrow', perm_of(0, step))]
    ppermute x3, waiting for transfers between devices: 0.01 us -> 11.7 us  [body(): piece = lax.ppermute(piece, 'narrow', perm)]
    all_to_all x2 -> x0, other arithmetic: 9.74 us -> none  [body(): lax.all_to_all(jnp.concatenate([left_send, amps_send], axis=1), 'narrow',...]
    dynamic_slice x0 -> x2, local copies, waits for them, and re-layouts: none -> 5.71 us  [rotate_back(): lax.dynamic_slice_in_dim(jnp.concatenate(rev * 2, axis=axis), size - by,...]
  transfers between devices with their start and end apart: 11 -> 16, of which waited for: 5 -> 10; matrix products, arithmetic and copies ran while one was open for 14% -> 17% of each run, Pallas kernels for 0% -> 0%
where the time goes in v14:
time: 207 us; the launch traced here: 205 us
  waiting for transfers between devices  86.6 us (42%)
  local copies, waits for them, and re-layouts  42.1 us (20%)
  starting transfers between devices  27.7 us (13%)
  matrix products  27.2 us (13%)
  between operations  13.7 us (7%)
  other arithmetic  7.53 us (4%)
    all_to_all x1, waiting for transfers between devices, body(): left_recv = lax.all_to_all(left_send, 'narrow', 0, 0, tiled=True)  24.5 us
    all_gather x1, waiting for transfers between devices, body(): left_all = lax.all_gather(left_recv, 'wide', axis=0, tiled=False)  15.9 us
    dot_general x1, matrix products, body(): jnp.einsum('wkqia,kpwid->padq', left_all, amps_all, preferred_element_typ...  15.8 us
    ppermute x1, waiting for transfers between devices, body(): lax.ppermute(amps, 'narrow', perm_of(0, step))  14.6 us
    unnamed x24, local copies, waits for them, and re-layouts  14.2 us
    ppermute x4, starting transfers between devices, body(): piece = lax.ppermute(piece, ('narrow', 'wide'), perm)  13.4 us
    ppermute x3, waiting for transfers between devices, body(): piece = lax.ppermute(piece, 'narrow', perm)  11.7 us
    dot_general x1, matrix products, body(): jnp.einsum('padq,bdq->pab', inter, right_group, preferred_element_type=jn...  11.4 us
  transfers between devices with their start and end apart: 16, of which 10 were waited for; matrix products, arithmetic and copies ran while one was open for 17% of the time, Pallas kernels for 0%

profile of v14, /device:TPU:5, one launch (start us, length us, event | category | flops | bytes accessed | tf_op | source)
XLA Modules:
  0.0 204.7 jit_solution(2698379274252519986)
XLA Ops:
  9.0 2.0 reshape.68
  13.9 4.3 %reshape.81 = bf16[8,2,32768]{2,1,0:T(2,128)(2,1)} reshape(bf16[8,64,16,64]{3,2,1,0:T(8,128)(2,1)} %bitcast.85) | data formatting | bytes 2097152
  18.2 5.5 %all-to-all-start = ((bf16[8,2,32768]{2,1,0:T(2,128)(2,1)}), bf16[8,2,32768]{2,1,0:T(2,128)(2,1)S(1)}, u32[]{:S(2)}, u32[]{:S(2)}) async-start(bf16[8,2,32768]{2,1,0:T(2,128)(2,1)} %reshape.81), calls=%async_computation | async-start | bytes 2097152 | tf_op jit(solution)/shard_map/all_to_all | solution.py:45
  23.8 24.5 %all-to-all-done = bf16[8,2,32768]{2,1,0:T(2,128)(2,1)S(1)} async-done(((bf16[8,2,32768]{2,1,0:T(2,128)(2,1)}), bf16[8,2,32768]{2,1,0:T(2,128)(2,1)S(1)}, u32[]{:S(2)}, u32[]{:S(2)}) %all-to-all-start) | async-done | bytes 1048608 | tf_op jit(solution)/shard_map/all_to_all | solution.py:45
  50.8 2.4 %fusion.11 = bf16[2,4,64,16,64]{2,3,4,1,0:T(8,128)(2,1)} fusion(s32[]{:T(128)S(6)} %select_n.167, bf16[2,4,64,16,64]{2,3,4,1,0:T(8,128)(2,1)S(1)} %constant_dynamic-slice_fusion.9), kind=kLoop, calls=%fused_computation.14 | loop fusion | flops 524288 | bytes 2097156 | tf_op jit(solution)/shard_map/concatenate | solution.py:39
  53.1 5.3 %copy.46 = bf16[2,4,64,16,64]{4,3,2,1,0:T(8,128)(2,1)} copy(bf16[2,4,64,16,64]{2,3,4,1,0:T(8,128)(2,1)} %fusion.11) | data formatting | bytes 2097152 | tf_op jit(solution)/shard_map/dynamic_slice | solution.py:39
  58.6 14.6 %collective-permute-done = bf16[16,64,128]{2,1,0:T(8,128)(2,1)S(1)} collective-permute-done((bf16[16,64,128]{2,1,0:T(8,128)(2,1)S(1)}, bf16[16,64,128]{2,1,0:T(8,128)(2,1)S(1)}, u32[]{:S(2)}, u32[]{:S(2)}) %collective-permute-start) | collective-permute-done | bytes 262176 | tf_op jit(solution)/shard_map/ppermute | solution.py:30
  73.3 2.9 %collective-permute-start.2 = (bf16[2,16,64,128]{3,2,1,0:T(8,128)(2,1)S(1)}, bf16[2,16,64,128]{3,2,1,0:T(8,128)(2,1)}, u32[]{:S(2)}, u32[]{:S(2)}) collective-permute-start(bf16[2,16,64,128]{3,2,1,0:T(8,128)(2,1)S(1)} %get-tuple-element.21), channel_id=1, source_target_pairs={{0,8},{4,12},{8,0},{12,4},{16,24},{20,28},{24,16},{28,20},{1,9},{5... | collective-permute-start | bytes 1572872 | tf_op jit(solution)/shard_map/ppermute | solution.py:33
  76.2 6.3 %copy.48 = bf16[64,128,256]{1,2,0:T(8,128)(2,1)} copy(bf16[64,128,256]{2,1,0:T(8,128)(2,1)} %param.8) | data formatting | bytes 8388608 | tf_op args[2]
  82.5 3.2 %constant_dynamic-slice_fusion.8 = (bf16[64,128,1,64]{1,3,2,0:T(8,128)(2,1)S(1)}, bf16[64,128,1,64]{1,3,2,0:T(8,128)(2,1)S(1)}, bf16[64,128,1,64]{1,3,2,0:T(8,128)(2,1)S(1)}, bf16[64,128,1,64]{1,3,2,0:T(8,128)(2,1)S(1)}) fusion(bf16[64,128,4,64]{1,3,2,0:T(8,128)(2,1)} %bitcast.83, s32[]{:T(128)S(6)} %select_n.169, s32[]{:T(128)S(6)} %select_n.175, ...), kind=kLoop, calls=%fused_computation.45 | loop fusion | bytes 8388624 | tf_op jit(solution)/shard_map/jit(dynamic_index_in_dim)/dynamic_slice | solution.py:56
  87.4 2.4 %collective-permute-start.6 = (bf16[64,128,64]{1,0,2:T(8,128)(2,1)}, bf16[64,128,64]{1,0,2:T(8,128)(2,1)}, u32[]{:S(2)}, u32[]{:S(2)}) collective-permute-start(bf16[64,128,64]{1,0,2:T(8,128)(2,1)} %bitcast.70), channel_id=1, source_target_pairs={{0,12},{4,0},{8,4},{12,8},{16,28},{20,16},{24,20},{28,24},{1,13},{... | collective-permute-start | bytes 3145736 | tf_op jit(solution)/shard_map/ppermute | solution.py:63
  95.1 4.0 %collective-permute-done.2 = bf16[2,16,64,128]{3,2,1,0:T(8,128)(2,1)} collective-permute-done((bf16[2,16,64,128]{3,2,1,0:T(8,128)(2,1)S(1)}, bf16[2,16,64,128]{3,2,1,0:T(8,128)(2,1)}, u32[]{:S(2)}, u32[]{:S(2)}) %collective-permute-start.2) | collective-permute-done | bytes 524320 | tf_op jit(solution)/shard_map/ppermute | solution.py:33
  100.7 15.9 %all-gather.2.cloned.1.call-done = bf16[4,8,64,16,64]{4,3,2,1,0:T(8,128)(2,1)} async-done(((bf16[1,8,64,16,64]{4,3,2,1,0:T(8,128)(2,1)}), bf16[4,8,64,16,64]{4,3,2,1,0:T(8,128)(2,1)}) %all-gather.2.cloned.1.call-update) | async-done | bytes 4194320 | tf_op jit(solution)/shard_map/all_gather | solution.py:49
  116.6 15.8 %fusion.3 = bf16[16,128,64,64,1,1]{1,3,5,2,0,4:T(8,128)(2,1)} fusion(bf16[8,16,4,16,128,1]{4,3,2,5,1,0:T(8,128)(2,1)S(1)} %bitcast.87, bf16[4,8,64,16,64]{4,3,2,1,0:T(8,128)(2,1)} %all-gather.2.cloned.1.call-done), kind=kOutput, calls=%fused_computation.3 | convolution fusion | flops 8589934592 | bytes 23068672 | tf_op jit(solution)/shard_map/wkqia,kpwid->padq/dot_general | solution.py:66
  132.4 11.7 %collective-permute-done.5 = bf16[64,128,64]{1,0,2:T(8,128)(2,1)} collective-permute-done((bf16[64,128,64]{1,0,2:T(8,128)(2,1)}, bf16[64,128,64]{1,0,2:T(8,128)(2,1)}, u32[]{:S(2)}, u32[]{:S(2)}) %collective-permute-start.5) | collective-permute-done | bytes 1048608 | tf_op jit(solution)/shard_map/ppermute | solution.py:63
  144.1 11.4 %fusion.1 = f32[16,64,256,1]{2,1,0,3:T(8,128)S(1)} fusion(bf16[16,128,64,64,1,1]{1,3,5,2,0,4:T(8,128)(2,1)} %fusion.3, bf16[64,128,64]{1,0,2:T(8,128)(2,1)} %collective-permute-done.6, bf16[64,128,64]{1,0,2:T(8,128)(2,1)} %collective-permute-done.5, bf16[64,128,64]{1,0,2:T(8,128)(2,1)} %collective-permute-done.4, bf16[64,128,64]{1,0,2:T(8,128)(2,1)} %bitcast.90), kind=kOutput, calls=%fused_computation.2 | convolution fusion | flops 4311744512 | bytes 22020096 | tf_op jit(solution)/shard_map/padq,bdq->pab/dot_general | solution.py:71
  159.9 4.7 %collective-permute-done.9 = f32[4,64,256]{2,1,0:T(8,128)} collective-permute-done((f32[4,64,256]{2,1,0:T(8,128)}, f32[4,64,256]{2,1,0:T(8,128)}, u32[]{:S(2)}, u32[]{:S(2)}) %collective-permute-start.9) | collective-permute-done | bytes 262176 | tf_op jit(solution)/shard_map/ppermute | solution.py:80
  166.4 3.6 %collective-permute-done.7 = f32[4,64,256]{2,1,0:T(8,128)} collective-permute-done((f32[4,64,256]{2,1,0:T(8,128)S(1)}, f32[4,64,256]{2,1,0:T(8,128)}, u32[]{:S(2)}, u32[]{:S(2)}) %collective-permute-start.7) | collective-permute-done | bytes 262176 | tf_op jit(solution)/shard_map/ppermute | solution.py:80
  172.4 2.8 %concatenate.20 = f32[4,64,8,64]{3,2,1,0:T(8,128)S(1)} concatenate(f32[4,64,1,64]{3,2,1,0:T(1,128)} %get-tuple-element.19, f32[4,64,1,64]{3,2,1,0:T(1,128)S(1)} %get-tuple-element.18, f32[4,64,1,64]{3,2,1,0:T(1,128)S(1)} %get-tuple-element.17, f32[4,64,1,64]{3,2,1,0:T(1,128)S(1)} %get-tuple-element.16, f32[4,64,1,64]{3,2,1,0:T(1,128)} %get-tuple-element.19, ...), dimensions={2} | concatenate | bytes 1048576 | tf_op jit(solution)/shard_map/concatenate | solution.py:83
  177.9 4.7 %collective-permute-start.13 = (f32[2,64,128]{2,1,0:T(8,128)S(1)}, f32[2,64,128]{2,1,0:T(8,128)S(1)}, u32[]{:S(2)}, u32[]{:S(2)}) collective-permute-start(f32[2,64,128]{2,1,0:T(8,128)S(1)} %bitcast.97), channel_id=1, source_target_pairs={{0,5},{1,13},{2,21},{3,29},{4,0},{5,8},{6,16},{7,24},{8,1},{9,9},{... | collective-permute-start | bytes 196616 | tf_op jit(solution)/shard_map/ppermute | solution.py:104
  182.6 4.9 %collective-permute-start.12 = (f32[2,64,128]{2,1,0:T(8,128)S(1)}, f32[2,64,128]{2,1,0:T(8,128)S(1)}, u32[]{:S(2)}, u32[]{:S(2)}) collective-permute-start(f32[2,64,128]{2,1,0:T(8,128)S(1)} %bitcast.96), channel_id=1, source_target_pairs={{0,4},{1,12},{2,20},{3,28},{4,5},{5,13},{6,21},{7,29},{8,0},{9,8},... | collective-permute-start | bytes 196616 | tf_op jit(solution)/shard_map/ppermute | solution.py:104
  187.5 1.9 collective-permute-start.10
  189.4 1.9 collective-permute-start.11
  191.5 4.3 %collective-permute-done.10 = f32[2,64,128]{2,1,0:T(8,128)S(1)} collective-permute-done((f32[2,64,128]{2,1,0:T(8,128)S(1)}, f32[2,64,128]{2,1,0:T(8,128)S(1)}, u32[]{:S(2)}, u32[]{:S(2)}) %collective-permute-start.10) | collective-permute-done | bytes 65568 | tf_op jit(solution)/shard_map/ppermute | solution.py:104
  (66 shorter events, 30.1 us)
Async XLA Ops:
  6.5 1.6 copy-start
  18.2 30.1 %all-to-all-start = ((bf16[8,2,32768]{2,1,0:T(2,128)(2,1)}), bf16[8,2,32768]{2,1,0:T(2,128)(2,1)S(1)}, u32[]{:S(2)}, u32[]{:S(2)}) async-start(bf16[8,2,32768]{2,1,0:T(2,128)(2,1)} %reshape.81), calls=%async_computation | async-start | bytes 2097152 | tf_op jit(solution)/shard_map/all_to_all | solution.py:45
  23.8 92.9 %all-gather.2.cloned.1.call-start = ((), (), s32[]{:S(2)}) async-start(), calls=%async_computation.1 | async-start | bytes 10485760 | tf_op jit(solution)/shard_map/all_gather | solution.py:49
  53.1 5.4 %copy-start.3 = (bf16[16,64,128]{2,1,0:T(8,128)(2,1)S(1)}, bf16[16,64,128]{2,1,0:T(8,128)(2,1)}, u32[]{:S(2)}) copy-start(bf16[16,64,128]{2,1,0:T(8,128)(2,1)} %param.6) | copy-start | bytes 786436
  58.5 14.7 %collective-permute-start = (bf16[16,64,128]{2,1,0:T(8,128)(2,1)S(1)}, bf16[16,64,128]{2,1,0:T(8,128)(2,1)S(1)}, u32[]{:S(2)}, u32[]{:S(2)}) collective-permute-start(bf16[16,64,128]{2,1,0:T(8,128)(2,1)S(1)} %copy-done.3), channel_id=1, source_target_pairs={{0,16},{4,20},{8,24},{12,28},{16,0},{20,4},{24,8},{28,12},{1,17},{... | collective-permute-start | bytes 786440 | tf_op jit(solution)/shard_map/ppermute | solution.py:30
  73.3 21.5 %collective-permute-start.3 = (bf16[2,16,64,128]{3,2,1,0:T(8,128)(2,1)S(1)}, bf16[2,16,64,128]{3,2,1,0:T(8,128)(2,1)}, u32[]{:S(2)}, u32[]{:S(2)}) collective-permute-start(bf16[2,16,64,128]{3,2,1,0:T(8,128)(2,1)S(1)} %get-tuple-element.21), channel_id=1, source_target_pairs={{0,12},{4,0},{8,4},{12,8},{16,28},{20,16},{24,20},{28,24},{1,13},{... | collective-permute-start | bytes 1572872 | tf_op jit(solution)/shard_map/ppermute | solution.py:33
  73.3 25.8 %collective-permute-start.2 = (bf16[2,16,64,128]{3,2,1,0:T(8,128)(2,1)S(1)}, bf16[2,16,64,128]{3,2,1,0:T(8,128)(2,1)}, u32[]{:S(2)}, u32[]{:S(2)}) collective-permute-start(bf16[2,16,64,128]{3,2,1,0:T(8,128)(2,1)S(1)} %get-tuple-element.21), channel_id=1, source_target_pairs={{0,8},{4,12},{8,0},{12,4},{16,24},{20,28},{24,16},{28,20},{1,9},{5... | collective-permute-start | bytes 1572872 | tf_op jit(solution)/shard_map/ppermute | solution.py:33
  76.2 22.9 %collective-permute-start.1 = (bf16[2,16,64,128]{3,2,1,0:T(8,128)(2,1)S(1)}, bf16[2,16,64,128]{3,2,1,0:T(8,128)(2,1)}, u32[]{:S(2)}, u32[]{:S(2)}) collective-permute-start(bf16[2,16,64,128]{3,2,1,0:T(8,128)(2,1)S(1)} %get-tuple-element.21), channel_id=1, source_target_pairs={{0,4},{4,8},{8,12},{12,0},{16,20},{20,24},{24,28},{28,16},{1,5},{5... | collective-permute-start | bytes 1572872 | tf_op jit(solution)/shard_map/ppermute | solution.py:33
  87.4 45.1 %collective-permute-start.6 = (bf16[64,128,64]{1,0,2:T(8,128)(2,1)}, bf16[64,128,64]{1,0,2:T(8,128)(2,1)}, u32[]{:S(2)}, u32[]{:S(2)}) collective-permute-start(bf16[64,128,64]{1,0,2:T(8,128)(2,1)} %bitcast.70), channel_id=1, source_target_pairs={{0,12},{4,0},{8,4},{12,8},{16,28},{20,16},{24,20},{28,24},{1,13},{... | collective-permute-start | bytes 3145736 | tf_op jit(solution)/shard_map/ppermute | solution.py:63
  91.4 52.7 %collective-permute-start.5 = (bf16[64,128,64]{1,0,2:T(8,128)(2,1)}, bf16[64,128,64]{1,0,2:T(8,128)(2,1)}, u32[]{:S(2)}, u32[]{:S(2)}) collective-permute-start(bf16[64,128,64]{1,0,2:T(8,128)(2,1)} %bitcast.71), channel_id=1, source_target_pairs={{0,8},{4,12},{8,0},{12,4},{16,24},{20,28},{24,16},{28,20},{1,9},{5... | collective-permute-start | bytes 3145736 | tf_op jit(solution)/shard_map/ppermute | solution.py:63
  94.8 49.3 %collective-permute-start.4 = (bf16[64,128,64]{1,0,2:T(8,128)(2,1)}, bf16[64,128,64]{1,0,2:T(8,128)(2,1)}, u32[]{:S(2)}, u32[]{:S(2)}) collective-permute-start(bf16[64,128,64]{1,0,2:T(8,128)(2,1)} %bitcast.91), channel_id=1, source_target_pairs={{0,4},{4,8},{8,12},{12,0},{16,20},{20,24},{24,28},{28,16},{1,5},{5... | collective-permute-start | bytes 3145736 | tf_op jit(solution)/shard_map/ppermute | solution.py:63
  144.1 15.4 %copy-start.4 = (s32[2,2]{1,0:T(2,128)S(1)}, s32[2,2]{1,0:T(2,128)}, u32[]{:S(2)}) copy-start(s32[2,2]{1,0:T(2,128)} %param.9) | copy-start | bytes 52
  144.1 15.6 %copy-start.5 = (f32[128]{0:T(128)S(1)}, f32[128]{0:T(128)}, u32[]{:S(2)}) copy-start(f32[128]{0:T(128)} %param.10) | copy-start | bytes 1540
  155.5 10.9 %copy-start.2 = (f32[16,64,256,1]{2,1,0,3:T(8,128)}, f32[16,64,256,1]{2,1,0,3:T(8,128)S(1)}, u32[]{:S(2)}) copy-start(f32[16,64,256,1]{2,1,0,3:T(8,128)S(1)} %fusion.1) | copy-start | bytes 3145732
  155.6 42.3 %copy-start.1 = (bf16[64,64,256]{2,1,0:T(8,128)(2,1)S(1)}, bf16[64,64,256]{2,1,0:T(8,128)(2,1)}, u32[]{:S(2)}) copy-start(bf16[64,64,256]{2,1,0:T(8,128)(2,1)} %param.7) | copy-start | bytes 6291460
  156.4 34.9 %slice-start = ((f32[512]{0:T(512)}), f32[64]{0:T(128)S(1)}, s32[]{:S(2)}) async-start(f32[512]{0:T(512)} %param.11), calls=%async_computation.2 | async-start | bytes 1024 | tf_op jit(solution)/shard_map/slice | solution.py:116
  156.5 34.9 %copy-start.6 = (f32[512]{0:T(512)S(1)}, f32[512]{0:T(512)}, u32[]{:S(2)}) copy-start(f32[512]{0:T(512)} %param.11) | copy-start | bytes 6148
  156.5 8.2 %collective-permute-start.9 = (f32[4,64,256]{2,1,0:T(8,128)}, f32[4,64,256]{2,1,0:T(8,128)}, u32[]{:S(2)}, u32[]{:S(2)}) collective-permute-start(f32[4,64,256]{2,1,0:T(8,128)} %get-tuple-element.14), channel_id=1, source_target_pairs={{0,3},{1,0},{2,1},{3,2},{4,7},{5,4},{6,5},{7,6},{8,11},{9,8},{10,9... | collective-permute-start | bytes 786440 | tf_op jit(solution)/shard_map/ppermute | solution.py:80
  157.8 8.6 %collective-permute-start.8 = (f32[4,64,256]{2,1,0:T(8,128)}, f32[4,64,256]{2,1,0:T(8,128)}, u32[]{:S(2)}, u32[]{:S(2)}) collective-permute-start(f32[4,64,256]{2,1,0:T(8,128)} %get-tuple-element.15), channel_id=1, source_target_pairs={{0,2},{1,3},{2,0},{3,1},{4,6},{5,7},{6,4},{7,5},{8,10},{9,11},{10,... | collective-permute-start | bytes 786440 | tf_op jit(solution)/shard_map/ppermute | solution.py:80
  158.1 12.0 %collective-permute-start.7 = (f32[4,64,256]{2,1,0:T(8,128)S(1)}, f32[4,64,256]{2,1,0:T(8,128)}, u32[]{:S(2)}, u32[]{:S(2)}) collective-permute-start(f32[4,64,256]{2,1,0:T(8,128)S(1)} %get-tuple-element.13), channel_id=1, source_target_pairs={{0,1},{1,2},{2,3},{3,0},{4,5},{5,6},{6,7},{7,4},{8,9},{9,10},{10,1... | collective-permute-start | bytes 786440 | tf_op jit(solution)/shard_map/ppermute | solution.py:80
  177.9 13.6 %collective-permute-start.13 = (f32[2,64,128]{2,1,0:T(8,128)S(1)}, f32[2,64,128]{2,1,0:T(8,128)S(1)}, u32[]{:S(2)}, u32[]{:S(2)}) collective-permute-start(f32[2,64,128]{2,1,0:T(8,128)S(1)} %bitcast.97), channel_id=1, source_target_pairs={{0,5},{1,13},{2,21},{3,29},{4,0},{5,8},{6,16},{7,24},{8,1},{9,9},{... | collective-permute-start | bytes 196616 | tf_op jit(solution)/shard_map/ppermute | solution.py:104
  182.6 8.9 %collective-permute-start.12 = (f32[2,64,128]{2,1,0:T(8,128)S(1)}, f32[2,64,128]{2,1,0:T(8,128)S(1)}, u32[]{:S(2)}, u32[]{:S(2)}) collective-permute-start(f32[2,64,128]{2,1,0:T(8,128)S(1)} %bitcast.96), channel_id=1, source_target_pairs={{0,4},{1,12},{2,20},{3,28},{4,5},{5,13},{6,21},{7,29},{8,0},{9,8},... | collective-permute-start | bytes 196616 | tf_op jit(solution)/shard_map/ppermute | solution.py:104
  187.5 8.3 %collective-permute-start.10 = (f32[2,64,128]{2,1,0:T(8,128)S(1)}, f32[2,64,128]{2,1,0:T(8,128)S(1)}, u32[]{:S(2)}, u32[]{:S(2)}) collective-permute-start(f32[2,64,128]{2,1,0:T(8,128)S(1)} %bitcast.95), channel_id=1, source_target_pairs={{0,0},{1,8},{2,16},{3,24},{4,1},{5,9},{6,17},{7,25},{8,4},{9,12},{... | collective-permute-start | bytes 196616 | tf_op jit(solution)/shard_map/ppermute | solution.py:104
  189.4 7.8 %collective-permute-start.11 = (f32[2,64,128]{2,1,0:T(8,128)S(1)}, f32[2,64,128]{2,1,0:T(8,128)S(1)}, u32[]{:S(2)}, u32[]{:S(2)}) collective-permute-start(f32[2,64,128]{2,1,0:T(8,128)S(1)} %bitcast.94), channel_id=1, source_target_pairs={{0,1},{1,9},{2,17},{3,25},{4,4},{5,12},{6,20},{7,28},{8,5},{9,13},... | collective-permute-start | bytes 196616 | tf_op jit(solution)/shard_map/ppermute | solution.py:104
Sparse Core Ops, SparseCore 0:
  58.6 57.9 all-gather.1

commit v15 on v14

--- a/solution.py
+++ b/solution.py
@@ -53,7 +53,7 @@
         chunks = []
         for shift in range(span):
             dest = (r + shift) % span
-            piece = lax.dynamic_index_in_dim(right_split, dest, 2, keepdims=False)
+            piece = lax.select_n(dest, *[right_split[:, :, j] for j in range(span)])
             if shift:
                 perm = [
                     (gg * span + i, gg * span + (i + shift) % span)

time: 207 us -> 208 us (level)
  local copies, waits for them, and re-layouts: 42.1 us -> 33.9 us
  other arithmetic: 7.53 us -> 14.7 us
    dynamic_slice x5 -> x0, local copies, waits for them, and re-layouts: 9.86 us -> none  [body(): piece = lax.dynamic_index_in_dim(right_split, dest, 2, keepdims=False)]
    select_n x0 -> x2, other arithmetic: none -> 7.47 us  [body(): piece = lax.select_n(dest, *[right_split[:, :, j] for j in range(span)])]
    ppermute x3, waiting for transfers between devices: 4.05 us -> 10.9 us  [body(): lax.ppermute(group_set, 'narrow', perm_of(shift, 0))]
    ppermute x1, waiting for transfers between devices: 14.6 us -> 8.01 us  [body(): lax.ppermute(amps, 'narrow', perm_of(0, step))]
    unnamed x24 -> x28, local copies, waits for them, and re-layouts: 14.2 us -> 15.4 us
  transfers between devices with their start and end apart: 16 -> 16, of which waited for: 10 -> 11; matrix products, arithmetic and copies ran while one was open for 17% -> 16% of each run, Pallas kernels for 0% -> 0%
where the time goes in v15:
time: 208 us; the launch traced here: 206 us
  waiting for transfers between devices  85.8 us (41%)
  local copies, waits for them, and re-layouts  33.9 us (16%)
  starting transfers between devices  29.5 us (14%)
  matrix products  28 us (13%)
  other arithmetic  14.7 us (7%)
  between operations  13.7 us (7%)
    all_to_all x1, waiting for transfers between devices, body(): left_recv = lax.all_to_all(left_send, 'narrow', 0, 0, tiled=True)  24.5 us
    dot_general x1, matrix products, body(): jnp.einsum('wkqia,kpwid->padq', left_all, amps_all, preferred_element_typ...  15.9 us
    unnamed x28, local copies, waits for them, and re-layouts  15.4 us
    all_gather x1, waiting for transfers between devices, body(): left_all = lax.all_gather(left_recv, 'wide', axis=0, tiled=False)  15 us
    ppermute x4, starting transfers between devices, body(): piece = lax.ppermute(piece, ('narrow', 'wide'), perm)  13.3 us
    dot_general x1, matrix products, body(): jnp.einsum('padq,bdq->pab', inter, right_group, preferred_element_type=jn...  12.1 us
    ppermute x3, waiting for transfers between devices, body(): piece = lax.ppermute(piece, 'narrow', perm)  11.6 us
    ppermute x3, waiting for transfers between devices, body(): lax.ppermute(group_set, 'narrow', perm_of(shift, 0))  10.9 us
  transfers between devices with their start and end apart: 16, of which 11 were waited for; matrix products, arithmetic and copies ran while one was open for 16% of the time, Pallas kernels for 0%

profile of v15, /device:TPU:5, one launch (start us, length us, event | category | flops | bytes accessed | tf_op | source)
XLA Modules:
  0.0 205.6 jit_solution(16913919971426467445)
XLA Ops:
  9.0 2.0 reshape.92
  13.9 4.3 %reshape.105 = bf16[8,2,32768]{2,1,0:T(2,128)(2,1)} reshape(bf16[8,64,16,64]{3,2,1,0:T(8,128)(2,1)} %bitcast.82) | data formatting | bytes 2097152
  18.2 5.5 %all-to-all-start = ((bf16[8,2,32768]{2,1,0:T(2,128)(2,1)}), bf16[8,2,32768]{2,1,0:T(2,128)(2,1)S(1)}, u32[]{:S(2)}, u32[]{:S(2)}) async-start(bf16[8,2,32768]{2,1,0:T(2,128)(2,1)} %reshape.105), calls=%async_computation | async-start | bytes 2097152 | tf_op jit(solution)/shard_map/all_to_all | solution.py:45
  23.8 24.5 %all-to-all-done = bf16[8,2,32768]{2,1,0:T(2,128)(2,1)S(1)} async-done(((bf16[8,2,32768]{2,1,0:T(2,128)(2,1)}), bf16[8,2,32768]{2,1,0:T(2,128)(2,1)S(1)}, u32[]{:S(2)}, u32[]{:S(2)}) %all-to-all-start) | async-done | bytes 1048608 | tf_op jit(solution)/shard_map/all_to_all | solution.py:45
  50.8 2.4 %fusion.11 = bf16[2,4,64,16,64]{2,3,4,1,0:T(8,128)(2,1)} fusion(s32[]{:T(128)S(6)} %select_n.282, bf16[2,4,64,16,64]{2,3,4,1,0:T(8,128)(2,1)S(1)} %constant_dynamic-slice_fusion.5), kind=kLoop, calls=%fused_computation.14 | loop fusion | flops 524288 | bytes 2097156 | tf_op jit(solution)/shard_map/concatenate | solution.py:39
  53.1 5.3 %copy.31 = bf16[2,4,64,16,64]{4,3,2,1,0:T(8,128)(2,1)} copy(bf16[2,4,64,16,64]{2,3,4,1,0:T(8,128)(2,1)} %fusion.11) | data formatting | bytes 2097152 | tf_op jit(solution)/shard_map/dynamic_slice | solution.py:39
  58.6 6.6 %copy.33 = bf16[64,128,256]{1,0,2:T(8,128)(2,1)} copy(bf16[64,128,256]{2,1,0:T(8,128)(2,1)} %param.8) | data formatting | bytes 8388608 | tf_op args[2]
  65.2 8.0 %collective-permute-done = bf16[16,64,128]{2,1,0:T(8,128)(2,1)S(1)} collective-permute-done((bf16[16,64,128]{2,1,0:T(8,128)(2,1)S(1)}, bf16[16,64,128]{2,1,0:T(8,128)(2,1)S(1)}, u32[]{:S(2)}, u32[]{:S(2)}) %collective-permute-start) | collective-permute-done | bytes 262176 | tf_op jit(solution)/shard_map/ppermute | solution.py:30
  73.3 2.9 %collective-permute-start.2 = (bf16[2,16,64,128]{3,2,1,0:T(8,128)(2,1)S(1)}, bf16[2,16,64,128]{3,2,1,0:T(8,128)(2,1)S(1)}, u32[]{:S(2)}, u32[]{:S(2)}) collective-permute-start(bf16[2,16,64,128]{3,2,1,0:T(8,128)(2,1)S(1)} %get-tuple-element.21), channel_id=1, source_target_pairs={{0,8},{4,12},{8,0},{12,4},{16,24},{20,28},{24,16},{28,20},{1,9},{5... | collective-permute-start | bytes 1572872 | tf_op jit(solution)/shard_map/ppermute | solution.py:33
  76.2 3.7 %select_bitcast_fusion.1 = (bf16[64,128,64]{1,0,2:T(8,128)(2,1)}, bf16[64,128,64]{1,0,2:T(8,128)(2,1)}) fusion(pred[]{:T(512)S(6)} %select_n.311, pred[]{:T(512)S(6)} %select_n.308, pred[]{:T(512)S(6)} %select_n.306, bf16[64,128,4,64]{1,0,3,2:T(8,128)(2,1)} %bitcast.71, pred[]{:T(512)S(6)} %select_n.322, pred[]{:T(512)S(6)} %select_n.319, pred[]{:T(512)S(6)} %select_n.317), kind=kLoop, calls=%fused_computation.18 | loop fusion | flops 3145728 | bytes 6291462 | tf_op jit(solution)/shard_map/select_n | solution.py:56
  79.9 2.4 %collective-permute-start.6 = (bf16[64,128,64]{1,0,2:T(8,128)(2,1)}, bf16[64,128,64]{1,0,2:T(8,128)(2,1)}, u32[]{:S(2)}, u32[]{:S(2)}) collective-permute-start(bf16[64,128,64]{1,0,2:T(8,128)(2,1)} %get-tuple-element.12), channel_id=1, source_target_pairs={{0,12},{4,0},{8,4},{12,8},{16,28},{20,16},{24,20},{28,24},{1,13},{... | collective-permute-start | bytes 3145736 | tf_op jit(solution)/shard_map/ppermute | solution.py:63
  82.3 3.7 %select_bitcast_fusion.3 = (bf16[64,128,64]{1,0,2:T(8,128)(2,1)}, bf16[64,128,64]{1,0,2:T(8,128)(2,1)}) fusion(pred[]{:T(512)S(6)} %select_n.289, pred[]{:T(512)S(6)} %select_n.286, pred[]{:T(512)S(6)} %select_n.284, bf16[64,128,4,64]{1,0,3,2:T(8,128)(2,1)} %bitcast.72, pred[]{:T(512)S(6)} %select_n.300, pred[]{:T(512)S(6)} %select_n.297, pred[]{:T(512)S(6)} %select_n.295), kind=kLoop, calls=%fused_computation.20 | loop fusion | flops 3145728 | bytes 6291462 | tf_op jit(solution)/shard_map/select_n | solution.py:56
  86.8 2.2 %collective-permute-start.4 = (bf16[64,128,64]{1,0,2:T(8,128)(2,1)}, bf16[64,128,64]{1,0,2:T(8,128)(2,1)}, u32[]{:S(2)}, u32[]{:S(2)}) collective-permute-start(bf16[64,128,64]{1,0,2:T(8,128)(2,1)} %get-tuple-element.10), channel_id=1, source_target_pairs={{0,4},{4,8},{8,12},{12,0},{16,20},{20,24},{24,28},{28,16},{1,5},{5... | collective-permute-start | bytes 3145736 | tf_op jit(solution)/shard_map/ppermute | solution.py:63
  88.9 10.2 %collective-permute-done.2 = bf16[2,16,64,128]{3,2,1,0:T(8,128)(2,1)S(1)} collective-permute-done((bf16[2,16,64,128]{3,2,1,0:T(8,128)(2,1)S(1)}, bf16[2,16,64,128]{3,2,1,0:T(8,128)(2,1)S(1)}, u32[]{:S(2)}, u32[]{:S(2)}) %collective-permute-start.2) | collective-permute-done | bytes 524320 | tf_op jit(solution)/shard_map/ppermute | solution.py:33
  101.6 15.0 %all-gather.2.cloned.1.call-done = bf16[4,8,64,16,64]{4,3,2,1,0:T(8,128)(2,1)} async-done(((bf16[1,8,64,16,64]{4,3,2,1,0:T(8,128)(2,1)}), bf16[4,8,64,16,64]{4,3,2,1,0:T(8,128)(2,1)}) %all-gather.2.cloned.1.call-update) | async-done | bytes 4194320 | tf_op jit(solution)/shard_map/all_gather | solution.py:49
  116.6 15.9 %fusion.3 = bf16[16,128,64,64,1,1]{1,3,5,2,0,4:T(8,128)(2,1)} fusion(bf16[8,16,4,16,128,1]{4,3,2,5,1,0:T(8,128)(2,1)S(1)} %bitcast.84, bf16[4,8,64,16,64]{4,3,2,1,0:T(8,128)(2,1)} %all-gather.2.cloned.1.call-done), kind=kOutput, calls=%fused_computation.3 | convolution fusion | flops 8589934592 | bytes 23068672 | tf_op jit(solution)/shard_map/wkqia,kpwid->padq/dot_general | solution.py:66
  132.5 11.6 %collective-permute-done.5 = bf16[64,128,64]{1,0,2:T(8,128)(2,1)} collective-permute-done((bf16[64,128,64]{1,0,2:T(8,128)(2,1)}, bf16[64,128,64]{1,0,2:T(8,128)(2,1)}, u32[]{:S(2)}, u32[]{:S(2)}) %collective-permute-start.5) | collective-permute-done | bytes 1048608 | tf_op jit(solution)/shard_map/ppermute | solution.py:63
  144.1 12.1 %fusion.1 = f32[16,64,256,1]{2,1,0,3:T(8,128)} fusion(bf16[16,128,64,64,1,1]{1,3,5,2,0,4:T(8,128)(2,1)} %fusion.3, bf16[64,128,64]{1,0,2:T(8,128)(2,1)} %collective-permute-done.6, bf16[64,128,64]{1,0,2:T(8,128)(2,1)} %collective-permute-done.5, bf16[64,128,64]{1,0,2:T(8,128)(2,1)} %collective-permute-done.4, bf16[64,128,64]{1,0,2:T(8,128)(2,1)S(1)} %copy-done.2), kind=kOutput, calls=%fused_computation.2 | convolution fusion | flops 4311744512 | bytes 22020096 | tf_op jit(solution)/shard_map/padq,bdq->pab/dot_general | solution.py:71
  161.1 4.3 %collective-permute-done.9 = f32[4,64,256]{2,1,0:T(8,128)S(1)} collective-permute-done((f32[4,64,256]{2,1,0:T(8,128)S(1)}, f32[4,64,256]{2,1,0:T(8,128)S(1)}, u32[]{:S(2)}, u32[]{:S(2)}) %collective-permute-start.9) | collective-permute-done | bytes 262176 | tf_op jit(solution)/shard_map/ppermute | solution.py:80
  167.3 3.7 %collective-permute-done.7 = f32[4,64,256]{2,1,0:T(8,128)} collective-permute-done((f32[4,64,256]{2,1,0:T(8,128)S(1)}, f32[4,64,256]{2,1,0:T(8,128)}, u32[]{:S(2)}, u32[]{:S(2)}) %collective-permute-start.7) | collective-permute-done | bytes 262176 | tf_op jit(solution)/shard_map/ppermute | solution.py:80
  173.2 2.8 %concatenate.20 = f32[4,64,8,64]{3,2,1,0:T(8,128)S(1)} concatenate(f32[4,64,1,64]{3,2,1,0:T(1,128)} %get-tuple-element.19, f32[4,64,1,64]{3,2,1,0:T(1,128)S(1)} %get-tuple-element.18, f32[4,64,1,64]{3,2,1,0:T(1,128)S(1)} %get-tuple-element.17, f32[4,64,1,64]{3,2,1,0:T(1,128)S(1)} %get-tuple-element.16, f32[4,64,1,64]{3,2,1,0:T(1,128)} %get-tuple-element.19, ...), dimensions={2} | concatenate | bytes 1048576 | tf_op jit(solution)/shard_map/concatenate | solution.py:83
  178.7 4.7 %collective-permute-start.13 = (f32[2,64,128]{2,1,0:T(8,128)S(1)}, f32[2,64,128]{2,1,0:T(8,128)S(1)}, u32[]{:S(2)}, u32[]{:S(2)}) collective-permute-start(f32[2,64,128]{2,1,0:T(8,128)S(1)} %bitcast.95), channel_id=1, source_target_pairs={{0,5},{1,13},{2,21},{3,29},{4,0},{5,8},{6,16},{7,24},{8,1},{9,9},{... | collective-permute-start | bytes 196616 | tf_op jit(solution)/shard_map/ppermute | solution.py:104
  183.4 4.8 %collective-permute-start.12 = (f32[2,64,128]{2,1,0:T(8,128)S(1)}, f32[2,64,128]{2,1,0:T(8,128)S(1)}, u32[]{:S(2)}, u32[]{:S(2)}) collective-permute-start(f32[2,64,128]{2,1,0:T(8,128)S(1)} %bitcast.94), channel_id=1, source_target_pairs={{0,4},{1,12},{2,20},{3,28},{4,5},{5,13},{6,21},{7,29},{8,0},{9,8},... | collective-permute-start | bytes 196616 | tf_op jit(solution)/shard_map/ppermute | solution.py:104
  192.2 4.3 %collective-permute-done.10 = f32[2,64,128]{2,1,0:T(8,128)S(1)} collective-permute-done((f32[2,64,128]{2,1,0:T(8,128)S(1)}, f32[2,64,128]{2,1,0:T(8,128)S(1)}, u32[]{:S(2)}, u32[]{:S(2)}) %collective-permute-start.10) | collective-permute-done | bytes 65568 | tf_op jit(solution)/shard_map/ppermute | solution.py:104
  (67 shorter events, 29.0 us)
Async XLA Ops:
  6.5 1.6 copy-start
  18.2 30.1 %all-to-all-start = ((bf16[8,2,32768]{2,1,0:T(2,128)(2,1)}), bf16[8,2,32768]{2,1,0:T(2,128)(2,1)S(1)}, u32[]{:S(2)}, u32[]{:S(2)}) async-start(bf16[8,2,32768]{2,1,0:T(2,128)(2,1)} %reshape.105), calls=%async_computation | async-start | bytes 2097152 | tf_op jit(solution)/shard_map/all_to_all | solution.py:45
  23.8 92.9 %all-gather.2.cloned.1.call-start = ((), (), s32[]{:S(2)}) async-start(), calls=%async_computation.1 | async-start | bytes 10485760 | tf_op jit(solution)/shard_map/all_gather | solution.py:49
  53.1 5.4 %copy-start.5 = (bf16[16,64,128]{2,1,0:T(8,128)(2,1)S(1)}, bf16[16,64,128]{2,1,0:T(8,128)(2,1)}, u32[]{:S(2)}) copy-start(bf16[16,64,128]{2,1,0:T(8,128)(2,1)} %param.6) | copy-start | bytes 786436
  58.5 14.7 %collective-permute-start = (bf16[16,64,128]{2,1,0:T(8,128)(2,1)S(1)}, bf16[16,64,128]{2,1,0:T(8,128)(2,1)S(1)}, u32[]{:S(2)}, u32[]{:S(2)}) collective-permute-start(bf16[16,64,128]{2,1,0:T(8,128)(2,1)S(1)} %copy-done.5), channel_id=1, source_target_pairs={{0,16},{4,20},{8,24},{12,28},{16,0},{20,4},{24,8},{28,12},{1,17},{... | collective-permute-start | bytes 786440 | tf_op jit(solution)/shard_map/ppermute | solution.py:30
  73.2 13.5 %collective-permute-start.3 = (bf16[2,16,64,128]{3,2,1,0:T(8,128)(2,1)S(1)}, bf16[2,16,64,128]{3,2,1,0:T(8,128)(2,1)S(1)}, u32[]{:S(2)}, u32[]{:S(2)}) collective-permute-start(bf16[2,16,64,128]{3,2,1,0:T(8,128)(2,1)S(1)} %get-tuple-element.21), channel_id=1, source_target_pairs={{0,12},{4,0},{8,4},{12,8},{16,28},{20,16},{24,20},{28,24},{1,13},{... | collective-permute-start | bytes 1572872 | tf_op jit(solution)/shard_map/ppermute | solution.py:33
  73.3 25.8 %collective-permute-start.2 = (bf16[2,16,64,128]{3,2,1,0:T(8,128)(2,1)S(1)}, bf16[2,16,64,128]{3,2,1,0:T(8,128)(2,1)S(1)}, u32[]{:S(2)}, u32[]{:S(2)}) collective-permute-start(bf16[2,16,64,128]{3,2,1,0:T(8,128)(2,1)S(1)} %get-tuple-element.21), channel_id=1, source_target_pairs={{0,8},{4,12},{8,0},{12,4},{16,24},{20,28},{24,16},{28,20},{1,9},{5... | collective-permute-start | bytes 1572872 | tf_op jit(solution)/shard_map/ppermute | solution.py:33
  76.2 22.9 %collective-permute-start.1 = (bf16[2,16,64,128]{3,2,1,0:T(8,128)(2,1)S(1)}, bf16[2,16,64,128]{3,2,1,0:T(8,128)(2,1)S(1)}, u32[]{:S(2)}, u32[]{:S(2)}) collective-permute-start(bf16[2,16,64,128]{3,2,1,0:T(8,128)(2,1)S(1)} %get-tuple-element.21), channel_id=1, source_target_pairs={{0,4},{4,8},{8,12},{12,0},{16,20},{20,24},{24,28},{28,16},{1,5},{5... | collective-permute-start | bytes 1572872 | tf_op jit(solution)/shard_map/ppermute | solution.py:33
  79.9 52.6 %collective-permute-start.6 = (bf16[64,128,64]{1,0,2:T(8,128)(2,1)}, bf16[64,128,64]{1,0,2:T(8,128)(2,1)}, u32[]{:S(2)}, u32[]{:S(2)}) collective-permute-start(bf16[64,128,64]{1,0,2:T(8,128)(2,1)} %get-tuple-element.12), channel_id=1, source_target_pairs={{0,12},{4,0},{8,4},{12,8},{16,28},{20,16},{24,20},{28,24},{1,13},{... | collective-permute-start | bytes 3145736 | tf_op jit(solution)/shard_map/ppermute | solution.py:63
  82.3 61.8 %collective-permute-start.5 = (bf16[64,128,64]{1,0,2:T(8,128)(2,1)}, bf16[64,128,64]{1,0,2:T(8,128)(2,1)}, u32[]{:S(2)}, u32[]{:S(2)}) collective-permute-start(bf16[64,128,64]{1,0,2:T(8,128)(2,1)} %get-tuple-element.11), channel_id=1, source_target_pairs={{0,8},{4,12},{8,0},{12,4},{16,24},{20,28},{24,16},{28,20},{1,9},{5... | collective-permute-start | bytes 3145736 | tf_op jit(solution)/shard_map/ppermute | solution.py:63
  86.8 57.3 %collective-permute-start.4 = (bf16[64,128,64]{1,0,2:T(8,128)(2,1)}, bf16[64,128,64]{1,0,2:T(8,128)(2,1)}, u32[]{:S(2)}, u32[]{:S(2)}) collective-permute-start(bf16[64,128,64]{1,0,2:T(8,128)(2,1)} %get-tuple-element.10), channel_id=1, source_target_pairs={{0,4},{4,8},{8,12},{12,0},{16,20},{20,24},{24,28},{28,16},{1,5},{5... | collective-permute-start | bytes 3145736 | tf_op jit(solution)/shard_map/ppermute | solution.py:63
  116.6 27.5 %copy-start.2 = (bf16[64,128,64]{1,0,2:T(8,128)(2,1)S(1)}, bf16[64,128,64]{1,0,2:T(8,128)(2,1)}, u32[]{:S(2)}) copy-start(bf16[64,128,64]{1,0,2:T(8,128)(2,1)} %get-tuple-element.9) | copy-start | bytes 3145732
  144.1 16.6 %copy-start.6 = (s32[2,2]{1,0:T(2,128)S(1)}, s32[2,2]{1,0:T(2,128)}, u32[]{:S(2)}) copy-start(s32[2,2]{1,0:T(2,128)} %param.9) | copy-start | bytes 52
  144.1 16.8 %copy-start.7 = (f32[128]{0:T(128)S(1)}, f32[128]{0:T(128)}, u32[]{:S(2)}) copy-start(f32[128]{0:T(128)} %param.10) | copy-start | bytes 1540
  156.2 42.5 %copy-start.1 = (bf16[64,64,256]{2,1,0:T(8,128)(2,1)S(1)}, bf16[64,64,256]{2,1,0:T(8,128)(2,1)}, u32[]{:S(2)}) copy-start(bf16[64,64,256]{2,1,0:T(8,128)(2,1)} %param.7) | copy-start | bytes 6291460
  157.6 34.5 %slice-start = ((f32[512]{0:T(512)}), f32[64]{0:T(128)S(1)}, s32[]{:S(2)}) async-start(f32[512]{0:T(512)} %param.11), calls=%async_computation.2 | async-start | bytes 1024 | tf_op jit(solution)/shard_map/slice | solution.py:116
  157.6 34.5 %copy-start.8 = (f32[512]{0:T(512)S(1)}, f32[512]{0:T(512)}, u32[]{:S(2)}) copy-start(f32[512]{0:T(512)} %param.11) | copy-start | bytes 6148
  157.6 7.9 %collective-permute-start.9 = (f32[4,64,256]{2,1,0:T(8,128)S(1)}, f32[4,64,256]{2,1,0:T(8,128)S(1)}, u32[]{:S(2)}, u32[]{:S(2)}) collective-permute-start(f32[4,64,256]{2,1,0:T(8,128)S(1)} %get-tuple-element.14), channel_id=1, source_target_pairs={{0,3},{1,0},{2,1},{3,2},{4,7},{5,4},{6,5},{7,6},{8,11},{9,8},{10,9... | collective-permute-start | bytes 786440 | tf_op jit(solution)/shard_map/ppermute | solution.py:80
  159.0 8.3 %collective-permute-start.8 = (f32[4,64,256]{2,1,0:T(8,128)S(1)}, f32[4,64,256]{2,1,0:T(8,128)S(1)}, u32[]{:S(2)}, u32[]{:S(2)}) collective-permute-start(f32[4,64,256]{2,1,0:T(8,128)S(1)} %get-tuple-element.15), channel_id=1, source_target_pairs={{0,2},{1,3},{2,0},{3,1},{4,6},{5,7},{6,4},{7,5},{8,10},{9,11},{10,... | collective-permute-start | bytes 786440 | tf_op jit(solution)/shard_map/ppermute | solution.py:80
  159.2 11.7 %collective-permute-start.7 = (f32[4,64,256]{2,1,0:T(8,128)S(1)}, f32[4,64,256]{2,1,0:T(8,128)}, u32[]{:S(2)}, u32[]{:S(2)}) collective-permute-start(f32[4,64,256]{2,1,0:T(8,128)S(1)} %get-tuple-element.13), channel_id=1, source_target_pairs={{0,1},{1,2},{2,3},{3,0},{4,5},{5,6},{6,7},{7,4},{8,9},{9,10},{10,1... | collective-permute-start | bytes 786440 | tf_op jit(solution)/shard_map/ppermute | solution.py:80
  178.7 13.5 %collective-permute-start.13 = (f32[2,64,128]{2,1,0:T(8,128)S(1)}, f32[2,64,128]{2,1,0:T(8,128)S(1)}, u32[]{:S(2)}, u32[]{:S(2)}) collective-permute-start(f32[2,64,128]{2,1,0:T(8,128)S(1)} %bitcast.95), channel_id=1, source_target_pairs={{0,5},{1,13},{2,21},{3,29},{4,0},{5,8},{6,16},{7,24},{8,1},{9,9},{... | collective-permute-start | bytes 196616 | tf_op jit(solution)/shard_map/ppermute | solution.py:104
  183.4 8.8 %collective-permute-start.12 = (f32[2,64,128]{2,1,0:T(8,128)S(1)}, f32[2,64,128]{2,1,0:T(8,128)S(1)}, u32[]{:S(2)}, u32[]{:S(2)}) collective-permute-start(f32[2,64,128]{2,1,0:T(8,128)S(1)} %bitcast.94), channel_id=1, source_target_pairs={{0,4},{1,12},{2,20},{3,28},{4,5},{5,13},{6,21},{7,29},{8,0},{9,8},... | collective-permute-start | bytes 196616 | tf_op jit(solution)/shard_map/ppermute | solution.py:104
  188.2 8.3 %collective-permute-start.10 = (f32[2,64,128]{2,1,0:T(8,128)S(1)}, f32[2,64,128]{2,1,0:T(8,128)S(1)}, u32[]{:S(2)}, u32[]{:S(2)}) collective-permute-start(f32[2,64,128]{2,1,0:T(8,128)S(1)} %bitcast.93), channel_id=1, source_target_pairs={{0,0},{1,8},{2,16},{3,24},{4,1},{5,9},{6,17},{7,25},{8,4},{9,12},{... | collective-permute-start | bytes 196616 | tf_op jit(solution)/shard_map/ppermute | solution.py:104
  190.1 7.9 %collective-permute-start.11 = (f32[2,64,128]{2,1,0:T(8,128)S(1)}, f32[2,64,128]{2,1,0:T(8,128)S(1)}, u32[]{:S(2)}, u32[]{:S(2)}) collective-permute-start(f32[2,64,128]{2,1,0:T(8,128)S(1)} %bitcast.92), channel_id=1, source_target_pairs={{0,1},{1,9},{2,17},{3,25},{4,4},{5,12},{6,20},{7,28},{8,5},{9,13},... | collective-permute-start | bytes 196616 | tf_op jit(solution)/shard_map/ppermute | solution.py:104
  (2 other events, 1.8 us)
Sparse Core Ops, SparseCore 0:
  58.6 57.9 all-gather.1

commit v16 on v15

--- a/solution.py
+++ b/solution.py
@@ -29,9 +29,16 @@
 
         own_set = [amps] + [lax.ppermute(amps, "narrow", perm_of(0, step)) for step in range(1, GROUPS)]
         group_set = jnp.stack(own_set, axis=0)
-        shifted_sets = [group_set] + [
-            lax.ppermute(group_set, "narrow", perm_of(shift, 0)) for shift in range(1, span)
-        ]
+        right_split = right_fit.reshape(b_blk, d_blk, span, q_blk)
+        set_size = group_set.size
+        shifted_sets = [group_set]
+        chunks = [lax.dynamic_index_in_dim(right_split, r, 2, keepdims=False)]
+        for shift in range(1, span):
+            piece = lax.dynamic_index_in_dim(right_split, (r + shift) % span, 2, keepdims=False)
+            both = jnp.concatenate([group_set.reshape(-1), piece.reshape(-1)])
+            both = lax.ppermute(both, "narrow", perm_of(shift, 0))
+            shifted_sets.append(both[:set_size].reshape(group_set.shape))
+            chunks.append(both[set_size:].reshape(piece.shape))
         amps_all = jnp.stack(shifted_sets, axis=1)
 
         def rotate_back(x, by, size, axis):
@@ -48,20 +55,6 @@
         left_recv = left_recv.reshape((n_narrow,) + left_recv.shape[2:])
         left_all = lax.all_gather(left_recv, "wide", axis=0, tiled=False)
         amps_all = amps_all.reshape(n_narrow, pairs, n_wide, c_sub, amps.shape[2])
-
-        right_split = right_fit.reshape(b_blk, d_blk, span, q_blk)
-        chunks = []
-        for shift in range(span):
-            dest = (r + shift) % span
-            piece = lax.select_n(dest, *[right_split[:, :, j] for j in range(span)])
-            if shift:
-                perm = [
-                    (gg * span + i, gg * span + (i + shift) % span)
-                    for gg in range(GROUPS)
-                    for i in range(span)
-                ]
-                piece = lax.ppermute(piece, "narrow", perm)
-            chunks.append(piece)
 
         inter = jnp.einsum(
             "wkqia,kpwid->padq", left_all, amps_all, preferred_element_type=jnp.float32

time: 208 us -> 238 us (1.14)
  local copies, waits for them, and re-layouts: 33.9 us -> 67.7 us
  other arithmetic: 14.7 us -> 11.8 us
    ppermute x6 -> x3, waiting for transfers between devices: 22.5 us -> 57.7 us  [body(): both = lax.ppermute(both, 'narrow', perm_of(shift, 0))]
    all_to_all x1, waiting for transfers between devices: 24.5 us -> 0.01 us  [body(): left_recv = lax.all_to_all(left_send, 'narrow', 0, 0, tiled=True)]
    slice x0 -> x12, local copies, waits for them, and re-layouts: none -> 16.9 us  [the longest x9 13.6 us: body(): chunks.append(both[set_size:].reshape(piece.shape))]
    all_gather x1, waiting for transfers between devices: 15 us -> 0.02 us  [body(): left_all = lax.all_gather(left_recv, 'wide', axis=0, tiled=False)]
    dynamic_slice x0 -> x5, local copies, waits for them, and re-layouts: none -> 11.2 us  [the longest x2 6.07 us: body(): chunks = [lax.dynamic_index_in_dim(right_split, r, 2, keepdims=False)]]
    select_n x2 -> x0, other arithmetic: 7.47 us -> none  [body(): piece = lax.select_n(dest, *[right_split[:, :, j] for j in range(span)])]
    reshape x0 -> x3, local copies, waits for them, and re-layouts: none -> 6.41 us  [body(): both = jnp.concatenate([group_set.reshape(-1), piece.reshape(-1)])]
    ppermute x6 -> x3, starting transfers between devices: 7.46 us -> 2.69 us  [body(): both = lax.ppermute(both, 'narrow', perm_of(shift, 0))]
  transfers between devices with their start and end apart: 16 -> 13, of which waited for: 11 -> 7; matrix products, arithmetic and copies ran while one was open for 16% -> 20% of each run, Pallas kernels for 0% -> 0%
where the time goes in v16:
time: 238 us; the launch traced here: 237 us
  waiting for transfers between devices  86.6 us (36%)
  local copies, waits for them, and re-layouts  67.7 us (28%)
  starting transfers between devices  30 us (13%)
  matrix products  27 us (11%)
  between operations  13.8 us (6%)
  other arithmetic  11.8 us (5%)
    ppermute x3, waiting for transfers between devices, body(): both = lax.ppermute(both, 'narrow', perm_of(shift, 0))  57.7 us
    ppermute x4, starting transfers between devices, body(): piece = lax.ppermute(piece, ('narrow', 'wide'), perm)  17.5 us
    unnamed x34, local copies, waits for them, and re-layouts  15.9 us
    dot_general x1, matrix products, body(): jnp.einsum('wkqia,kpwid->padq', left_all, amps_all, preferred_element_typ...  15.9 us
    slice x9, local copies, waits for them, and re-layouts, body(): chunks.append(both[set_size:].reshape(piece.shape))  13.6 us
    ppermute x1, waiting for transfers between devices, body(): lax.ppermute(amps, 'narrow', perm_of(0, step))  11.6 us
    ppermute x3, waiting for transfers between devices, body(): summed = summed + lax.ppermute(piece, 'wide', perm)  11.3 us
    dot_general x1, matrix products, body(): jnp.einsum('padq,bdq->pab', inter, right_group, preferred_element_type=jn...  11.1 us
  transfers between devices with their start and end apart: 13, of which 7 were waited for; matrix products, arithmetic and copies ran while one was open for 20% of the time, Pallas kernels for 0%

profile of v16, /device:TPU:5, one launch (start us, length us, event | category | flops | bytes accessed | tf_op | source)
XLA Modules:
  0.0 237.0 jit_solution(3105892169102579923)
XLA Ops:
  13.9 4.4 %reshape.153 = bf16[8,2,32768]{2,1,0:T(2,128)(2,1)} reshape(bf16[8,64,16,64]{3,2,1,0:T(8,128)(2,1)} %bitcast.83) | data formatting | bytes 2097152
  18.3 5.5 %all-to-all-start = ((bf16[8,2,32768]{2,1,0:T(2,128)(2,1)}), bf16[8,2,32768]{2,1,0:T(2,128)(2,1)}, u32[]{:S(2)}, u32[]{:S(2)}) async-start(bf16[8,2,32768]{2,1,0:T(2,128)(2,1)} %reshape.153), calls=%async_computation | async-start | bytes 2097152 | tf_op jit(solution)/shard_map/all_to_all | solution.py:52
  23.9 2.4 %collective-permute-start = (bf16[16,64,128]{2,1,0:T(8,128)(2,1)S(1)}, bf16[16,64,128]{2,1,0:T(8,128)(2,1)}, u32[]{:S(2)}, u32[]{:S(2)}) collective-permute-start(bf16[16,64,128]{2,1,0:T(8,128)(2,1)S(1)} %copy-done.8), channel_id=1, source_target_pairs={{0,16},{4,20},{8,24},{12,28},{16,0},{20,4},{24,8},{28,12},{1,17},{... | collective-permute-start | bytes 786440 | tf_op jit(solution)/shard_map/ppermute | solution.py:30
  26.3 6.3 %copy.39 = bf16[64,128,256]{1,2,0:T(8,128)(2,1)} copy(bf16[64,128,256]{2,1,0:T(8,128)(2,1)} %param.8) | data formatting | bytes 8388608 | tf_op args[2]
  32.6 4.3 %constant_dynamic-slice_fusion.5 = (bf16[64,128,1,64]{1,3,2,0:T(8,128)(2,1)}, bf16[64,128,1,64]{1,3,2,0:T(8,128)(2,1)}, bf16[64,128,1,64]{1,3,2,0:T(8,128)(2,1)}, bf16[64,128,1,64]{1,3,2,0:T(8,128)(2,1)S(1)}) fusion(bf16[64,128,4,64]{1,3,2,0:T(8,128)(2,1)} %bitcast.81, s32[]{:T(128)S(6)} %select_n.172, s32[]{:T(128)S(6)} %select_n.167, s32[]{:T(128)S(6)} %select_n.165, ...), kind=kLoop, calls=%fused_computation.42 | loop fusion | bytes 8388624 | tf_op jit(solution)/shard_map/jit(dynamic_index_in_dim)/dynamic_slice | solution.py:35
  48.5 11.6 %collective-permute-done = bf16[16,64,128]{2,1,0:T(8,128)(2,1)} collective-permute-done((bf16[16,64,128]{2,1,0:T(8,128)(2,1)S(1)}, bf16[16,64,128]{2,1,0:T(8,128)(2,1)}, u32[]{:S(2)}, u32[]{:S(2)}) %collective-permute-start) | collective-permute-done | bytes 262176 | tf_op jit(solution)/shard_map/ppermute | solution.py:30
  62.1 3.1 %reshape.154 = bf16[8,64,16,64]{3,2,1,0:T(8,128)(2,1)S(1)} reshape(bf16[8,2,32768]{2,1,0:T(2,128)(2,1)} %all-to-all-done) | data formatting | bytes 2097152
  68.5 5.4 %copy.44 = bf16[2,4,64,16,64]{4,3,2,1,0:T(8,128)(2,1)} copy(bf16[2,4,64,16,64]{2,3,4,1,0:T(8,128)(2,1)} %fusion.11) | data formatting | bytes 2097152 | tf_op jit(solution)/shard_map/dynamic_slice | solution.py:46
  74.0 3.8 %pad_maximum_fusion.2 = (bf16[786432]{0:T(1024)(128)(2,1)}, bf16[786432]{0:T(1024)(128)(2,1)}, bf16[786432]{0:T(1024)(128)(2,1)}) fusion(bf16[262144]{0:T(1024)(128)(2,1)} %bitcast.85, bf16[524288]{0:T(1024)(128)(2,1)} %reshape.137, bf16[524288]{0:T(1024)(128)(2,1)S(1)} %copy-done.4, bf16[524288]{0:T(1024)(128)(2,1)S(1)} %copy-done.3), kind=kLoop, calls=%fused_computation.16 | loop fusion | flops 7864320 | bytes 8388608 | tf_op jit(solution)/shard_map/concatenate | solution.py:38
  82.2 30.9 %collective-permute-done.1 = bf16[786432]{0:T(1024)(128)(2,1)} collective-permute-done((bf16[786432]{0:T(1024)(128)(2,1)}, bf16[786432]{0:T(1024)(128)(2,1)}, u32[]{:S(2)}, u32[]{:S(2)}) %collective-permute-start.1) | collective-permute-done | bytes 1572896 | tf_op jit(solution)/shard_map/ppermute | solution.py:39
  115.3 2.4 %copy.47 = bf16[64,128,64]{1,0,2:T(8,128)(2,1)} copy(bf16[64,128,64]{2,1,0:T(8,128)(2,1)S(1)} %slice.126) | data formatting | bytes 2097152 | tf_op jit(solution)/shard_map/slice | solution.py:41
  119.9 2.4 %copy.48 = bf16[64,128,64]{1,0,2:T(8,128)(2,1)} copy(bf16[64,128,64]{2,1,0:T(8,128)(2,1)S(1)} %slice.128) | data formatting | bytes 2097152 | tf_op jit(solution)/shard_map/slice | solution.py:41
  122.3 26.8 %collective-permute-done.3 = bf16[786432]{0:T(1024)(128)(2,1)} collective-permute-done((bf16[786432]{0:T(1024)(128)(2,1)}, bf16[786432]{0:T(1024)(128)(2,1)}, u32[]{:S(2)}, u32[]{:S(2)}) %collective-permute-start.3) | collective-permute-done | bytes 1572896 | tf_op jit(solution)/shard_map/ppermute | solution.py:39
  151.2 2.4 %copy.49 = bf16[64,128,64]{1,0,2:T(8,128)(2,1)} copy(bf16[64,128,64]{2,1,0:T(8,128)(2,1)S(1)} %slice.130) | data formatting | bytes 2097152 | tf_op jit(solution)/shard_map/slice | solution.py:41
  157.1 15.9 %fusion.3 = bf16[16,128,64,64,1,1]{1,3,5,2,0,4:T(8,128)(2,1)} fusion(bf16[8,16,4,16,128,1]{4,3,2,5,1,0:T(8,128)(2,1)S(1)} %bitcast.86, bf16[4,8,64,16,64]{4,3,2,1,0:T(8,128)(2,1)} %all-gather.2.cloned.1.call-done), kind=kOutput, calls=%fused_computation.3 | convolution fusion | flops 8589934592 | bytes 23068672 | tf_op jit(solution)/shard_map/wkqia,kpwid->padq/dot_general | solution.py:59
  173.1 11.1 %fusion.1 = f32[16,64,256,1]{2,1,0,3:T(8,128)S(1)} fusion(bf16[16,128,64,64,1,1]{1,3,5,2,0,4:T(8,128)(2,1)} %fusion.3, bf16[64,128,64]{1,0,2:T(8,128)(2,1)} %copy.49, bf16[64,128,64]{1,0,2:T(8,128)(2,1)} %copy.48, bf16[64,128,64]{1,0,2:T(8,128)(2,1)S(1)} %copy-done.6, bf16[64,128,64]{1,0,2:T(8,128)(2,1)} %bitcast.92), kind=kOutput, calls=%fused_computation.2 | convolution fusion | flops 4311744512 | bytes 22020096 | tf_op jit(solution)/shard_map/padq,bdq->pab/dot_general | solution.py:64
  186.6 2.5 %collective-permute-done.4 = f32[4,64,256]{2,1,0:T(8,128)S(1)} collective-permute-done((f32[4,64,256]{2,1,0:T(8,128)S(1)}, f32[4,64,256]{2,1,0:T(8,128)S(1)}, u32[]{:S(2)}, u32[]{:S(2)}) %collective-permute-start.4) | collective-permute-done | bytes 262176 | tf_op jit(solution)/shard_map/ppermute | solution.py:73
  189.1 4.3 %collective-permute-done.6 = f32[4,64,256]{2,1,0:T(8,128)S(1)} collective-permute-done((f32[4,64,256]{2,1,0:T(8,128)S(1)}, f32[4,64,256]{2,1,0:T(8,128)S(1)}, u32[]{:S(2)}, u32[]{:S(2)}) %collective-permute-start.6) | collective-permute-done | bytes 262176 | tf_op jit(solution)/shard_map/ppermute | solution.py:73
  193.5 4.4 %collective-permute-done.5 = f32[4,64,256]{2,1,0:T(8,128)S(1)} collective-permute-done((f32[4,64,256]{2,1,0:T(8,128)S(1)}, f32[4,64,256]{2,1,0:T(8,128)S(1)}, u32[]{:S(2)}, u32[]{:S(2)}) %collective-permute-start.5) | collective-permute-done | bytes 262176 | tf_op jit(solution)/shard_map/ppermute | solution.py:73
  200.3 2.8 %concatenate.32 = f32[4,64,8,64]{3,2,1,0:T(8,128)S(1)} concatenate(f32[4,64,1,64]{3,2,1,0:T(1,128)} %get-tuple-element.19, f32[4,64,1,64]{3,2,1,0:T(1,128)S(1)} %get-tuple-element.18, f32[4,64,1,64]{3,2,1,0:T(1,128)S(1)} %get-tuple-element.17, f32[4,64,1,64]{3,2,1,0:T(1,128)S(1)} %get-tuple-element.16, f32[4,64,1,64]{3,2,1,0:T(1,128)} %get-tuple-element.19, ...), dimensions={2} | concatenate | bytes 1048576 | tf_op jit(solution)/shard_map/concatenate | solution.py:76
  205.7 7.7 %collective-permute-start.10 = (f32[2,64,128]{2,1,0:T(8,128)S(1)}, f32[2,64,128]{2,1,0:T(8,128)S(1)}, u32[]{:S(2)}, u32[]{:S(2)}) collective-permute-start(f32[2,64,128]{2,1,0:T(8,128)S(1)} %bitcast.97), channel_id=1, source_target_pairs={{0,5},{1,13},{2,21},{3,29},{4,0},{5,8},{6,16},{7,24},{8,1},{9,9},{... | collective-permute-start | bytes 196616 | tf_op jit(solution)/shard_map/ppermute | solution.py:97
  215.3 4.8 %collective-permute-start.9 = (f32[2,64,128]{2,1,0:T(8,128)S(1)}, f32[2,64,128]{2,1,0:T(8,128)S(1)}, u32[]{:S(2)}, u32[]{:S(2)}) collective-permute-start(f32[2,64,128]{2,1,0:T(8,128)S(1)} %bitcast.95), channel_id=1, source_target_pairs={{0,4},{1,12},{2,20},{3,28},{4,5},{5,13},{6,21},{7,29},{8,0},{9,8},... | collective-permute-start | bytes 196616 | tf_op jit(solution)/shard_map/ppermute | solution.py:97
  220.1 3.1 %collective-permute-start.7 = (f32[2,64,128]{2,1,0:T(8,128)S(1)}, f32[2,64,128]{2,1,0:T(8,128)S(1)}, u32[]{:S(2)}, u32[]{:S(2)}) collective-permute-start(f32[2,64,128]{2,1,0:T(8,128)S(1)} %bitcast.94), channel_id=1, source_target_pairs={{0,0},{1,8},{2,16},{3,24},{4,1},{5,9},{6,17},{7,25},{8,4},{9,12},{... | collective-permute-start | bytes 196616 | tf_op jit(solution)/shard_map/ppermute | solution.py:97
  223.4 6.0 %collective-permute-done.7 = f32[2,64,128]{2,1,0:T(8,128)S(1)} collective-permute-done((f32[2,64,128]{2,1,0:T(8,128)S(1)}, f32[2,64,128]{2,1,0:T(8,128)S(1)}, u32[]{:S(2)}, u32[]{:S(2)}) %collective-permute-start.7) | collective-permute-done | bytes 65568 | tf_op jit(solution)/shard_map/ppermute | solution.py:97
  (86 shorter events, 48.8 us)
Async XLA Ops:
  13.9 10.0 %copy-start.8 = (bf16[16,64,128]{2,1,0:T(8,128)(2,1)S(1)}, bf16[16,64,128]{2,1,0:T(8,128)(2,1)}, u32[]{:S(2)}) copy-start(bf16[16,64,128]{2,1,0:T(8,128)(2,1)} %param.6) | copy-start | bytes 786436
  18.3 43.8 %all-to-all-start = ((bf16[8,2,32768]{2,1,0:T(2,128)(2,1)}), bf16[8,2,32768]{2,1,0:T(2,128)(2,1)}, u32[]{:S(2)}, u32[]{:S(2)}) async-start(bf16[8,2,32768]{2,1,0:T(2,128)(2,1)} %reshape.153), calls=%async_computation | async-start | bytes 2097152 | tf_op jit(solution)/shard_map/all_to_all | solution.py:52
  23.8 133.3 %all-gather.2.cloned.1.call-start = ((), (), s32[]{:S(2)}) async-start(), calls=%async_computation.1 | async-start | bytes 10485760 | tf_op jit(solution)/shard_map/all_gather | solution.py:56
  23.9 36.2 %collective-permute-start = (bf16[16,64,128]{2,1,0:T(8,128)(2,1)S(1)}, bf16[16,64,128]{2,1,0:T(8,128)(2,1)}, u32[]{:S(2)}, u32[]{:S(2)}) collective-permute-start(bf16[16,64,128]{2,1,0:T(8,128)(2,1)S(1)} %copy-done.8), channel_id=1, source_target_pairs={{0,16},{4,20},{8,24},{12,28},{16,0},{20,4},{24,8},{28,12},{1,17},{... | collective-permute-start | bytes 786440 | tf_op jit(solution)/shard_map/ppermute | solution.py:30
  68.5 5.5 %copy-start.4 = (bf16[524288]{0:T(1024)(128)(2,1)S(1)}, bf16[524288]{0:T(1024)(128)(2,1)}, u32[]{:S(2)}) copy-start(bf16[524288]{0:T(1024)(128)(2,1)} %reshape.138) | copy-start | bytes 3145732
  74.0 6.5 %copy-start.2 = (bf16[64,128,1,64]{1,3,2,0:T(8,128)(2,1)S(1)}, bf16[64,128,1,64]{1,3,2,0:T(8,128)(2,1)}, u32[]{:S(2)}) copy-start(bf16[64,128,1,64]{1,3,2,0:T(8,128)(2,1)} %get-tuple-element.9) | copy-start | bytes 3145732
  77.8 35.3 %collective-permute-start.1 = (bf16[786432]{0:T(1024)(128)(2,1)}, bf16[786432]{0:T(1024)(128)(2,1)}, u32[]{:S(2)}, u32[]{:S(2)}) collective-permute-start(bf16[786432]{0:T(1024)(128)(2,1)} %get-tuple-element.22), channel_id=1, source_target_pairs={{0,4},{4,8},{8,12},{12,0},{16,20},{20,24},{24,28},{28,16},{1,5},{5... | collective-permute-start | bytes 4718600 | tf_op jit(solution)/shard_map/ppermute | solution.py:39
  79.3 38.4 %collective-permute-start.2 = (bf16[786432]{0:T(1024)(128)(2,1)}, bf16[786432]{0:T(1024)(128)(2,1)}, u32[]{:S(2)}, u32[]{:S(2)}) collective-permute-start(bf16[786432]{0:T(1024)(128)(2,1)} %get-tuple-element.23), channel_id=1, source_target_pairs={{0,8},{4,12},{8,0},{12,4},{16,24},{20,28},{24,16},{28,20},{1,9},{5... | collective-permute-start | bytes 4718600 | tf_op jit(solution)/shard_map/ppermute | solution.py:39
  79.3 69.7 %collective-permute-start.3 = (bf16[786432]{0:T(1024)(128)(2,1)}, bf16[786432]{0:T(1024)(128)(2,1)}, u32[]{:S(2)}, u32[]{:S(2)}) collective-permute-start(bf16[786432]{0:T(1024)(128)(2,1)} %get-tuple-element.24), channel_id=1, source_target_pairs={{0,12},{4,0},{8,4},{12,8},{16,28},{20,16},{24,20},{28,24},{1,13},{... | collective-permute-start | bytes 4718600 | tf_op jit(solution)/shard_map/ppermute | solution.py:39
  151.2 5.6 %copy-start.5 = (bf16[2,1,16,64,128]{4,3,2,1,0:T(8,128)(2,1)S(1)}, bf16[2,1,16,64,128]{4,3,2,1,0:T(8,128)(2,1)}, u32[]{:S(2)}) copy-start(bf16[2,1,16,64,128]{4,3,2,1,0:T(8,128)(2,1)} %get-tuple-element.20) | copy-start | bytes 1572868
  157.1 15.9 %copy-start.6 = (bf16[64,128,64]{1,0,2:T(8,128)(2,1)S(1)}, bf16[64,128,64]{1,0,2:T(8,128)(2,1)}, u32[]{:S(2)}) copy-start(bf16[64,128,64]{1,0,2:T(8,128)(2,1)} %copy.47) | copy-start | bytes 3145732
  173.1 13.2 %copy-start.9 = (s32[2,2]{1,0:T(2,128)S(1)}, s32[2,2]{1,0:T(2,128)}, u32[]{:S(2)}) copy-start(s32[2,2]{1,0:T(2,128)} %param.9) | copy-start | bytes 52
  173.1 13.3 %copy-start.10 = (f32[128]{0:T(128)S(1)}, f32[128]{0:T(128)}, u32[]{:S(2)}) copy-start(f32[128]{0:T(128)} %param.10) | copy-start | bytes 1540
  184.2 9.3 %copy-start.7 = (f32[16,64,256,1]{2,1,0,3:T(8,128)}, f32[16,64,256,1]{2,1,0,3:T(8,128)S(1)}, u32[]{:S(2)}) copy-start(f32[16,64,256,1]{2,1,0,3:T(8,128)S(1)} %fusion.1) | copy-start | bytes 3145732
  184.3 4.9 %collective-permute-start.4 = (f32[4,64,256]{2,1,0:T(8,128)S(1)}, f32[4,64,256]{2,1,0:T(8,128)S(1)}, u32[]{:S(2)}, u32[]{:S(2)}) collective-permute-start(f32[4,64,256]{2,1,0:T(8,128)S(1)} %get-tuple-element.13), channel_id=1, source_target_pairs={{0,1},{1,2},{2,3},{3,0},{4,5},{5,6},{6,7},{7,4},{8,9},{9,10},{10,1... | collective-permute-start | bytes 786440 | tf_op jit(solution)/shard_map/ppermute | solution.py:73
  184.9 8.6 %collective-permute-start.6 = (f32[4,64,256]{2,1,0:T(8,128)S(1)}, f32[4,64,256]{2,1,0:T(8,128)S(1)}, u32[]{:S(2)}, u32[]{:S(2)}) collective-permute-start(f32[4,64,256]{2,1,0:T(8,128)S(1)} %get-tuple-element.14), channel_id=1, source_target_pairs={{0,3},{1,0},{2,1},{3,2},{4,7},{5,4},{6,5},{7,6},{8,11},{9,8},{10,9... | collective-permute-start | bytes 786440 | tf_op jit(solution)/shard_map/ppermute | solution.py:73
  185.1 12.8 %collective-permute-start.5 = (f32[4,64,256]{2,1,0:T(8,128)S(1)}, f32[4,64,256]{2,1,0:T(8,128)S(1)}, u32[]{:S(2)}, u32[]{:S(2)}) collective-permute-start(f32[4,64,256]{2,1,0:T(8,128)S(1)} %get-tuple-element.15), channel_id=1, source_target_pairs={{0,2},{1,3},{2,0},{3,1},{4,6},{5,7},{6,4},{7,5},{8,10},{9,11},{10,... | collective-permute-start | bytes 786440 | tf_op jit(solution)/shard_map/ppermute | solution.py:73
  197.9 32.2 %copy-start.1 = (bf16[64,64,256]{2,1,0:T(8,128)(2,1)S(1)}, bf16[64,64,256]{2,1,0:T(8,128)(2,1)}, u32[]{:S(2)}) copy-start(bf16[64,64,256]{2,1,0:T(8,128)(2,1)} %param.7) | copy-start | bytes 6291460
  199.1 24.2 %slice-start = ((f32[512]{0:T(512)}), f32[64]{0:T(128)S(1)}, s32[]{:S(2)}) async-start(f32[512]{0:T(512)} %param.11), calls=%async_computation.2 | async-start | bytes 1024 | tf_op jit(solution)/shard_map/slice | solution.py:109
  199.1 24.2 %copy-start.11 = (f32[512]{0:T(512)S(1)}, f32[512]{0:T(512)}, u32[]{:S(2)}) copy-start(f32[512]{0:T(512)} %param.11) | copy-start | bytes 6148
  205.7 17.7 %collective-permute-start.10 = (f32[2,64,128]{2,1,0:T(8,128)S(1)}, f32[2,64,128]{2,1,0:T(8,128)S(1)}, u32[]{:S(2)}, u32[]{:S(2)}) collective-permute-start(f32[2,64,128]{2,1,0:T(8,128)S(1)} %bitcast.97), channel_id=1, source_target_pairs={{0,5},{1,13},{2,21},{3,29},{4,0},{5,8},{6,16},{7,24},{8,1},{9,9},{... | collective-permute-start | bytes 196616 | tf_op jit(solution)/shard_map/ppermute | solution.py:97
  213.4 10.0 %collective-permute-start.8 = (f32[2,64,128]{2,1,0:T(8,128)S(1)}, f32[2,64,128]{2,1,0:T(8,128)S(1)}, u32[]{:S(2)}, u32[]{:S(2)}) collective-permute-start(f32[2,64,128]{2,1,0:T(8,128)S(1)} %bitcast.96), channel_id=1, source_target_pairs={{0,1},{1,9},{2,17},{3,25},{4,4},{5,12},{6,20},{7,28},{8,5},{9,13},... | collective-permute-start | bytes 196616 | tf_op jit(solution)/shard_map/ppermute | solution.py:97
  215.3 8.1 %collective-permute-start.9 = (f32[2,64,128]{2,1,0:T(8,128)S(1)}, f32[2,64,128]{2,1,0:T(8,128)S(1)}, u32[]{:S(2)}, u32[]{:S(2)}) collective-permute-start(f32[2,64,128]{2,1,0:T(8,128)S(1)} %bitcast.95), channel_id=1, source_target_pairs={{0,4},{1,12},{2,20},{3,28},{4,5},{5,13},{6,21},{7,29},{8,0},{9,8},... | collective-permute-start | bytes 196616 | tf_op jit(solution)/shard_map/ppermute | solution.py:97
  220.1 9.3 %collective-permute-start.7 = (f32[2,64,128]{2,1,0:T(8,128)S(1)}, f32[2,64,128]{2,1,0:T(8,128)S(1)}, u32[]{:S(2)}, u32[]{:S(2)}) collective-permute-start(f32[2,64,128]{2,1,0:T(8,128)S(1)} %bitcast.94), channel_id=1, source_target_pairs={{0,0},{1,8},{2,16},{3,24},{4,1},{5,9},{6,17},{7,25},{8,4},{9,12},{... | collective-permute-start | bytes 196616 | tf_op jit(solution)/shard_map/ppermute | solution.py:97
  (2 other events, 7.0 us)
Sparse Core Ops, SparseCore 0:
  74.1 57.6 all-gather.1

commit v17 on v14

--- a/solution.py
+++ b/solution.py
@@ -68,16 +68,18 @@
         ).astype(jnp.bfloat16)
 
         right_group = jnp.concatenate(chunks, axis=0)
-        part = jnp.einsum(
-            "padq,bdq->pab", inter, right_group, preferred_element_type=jnp.float32
-        )
         pairs_w = pairs // n_wide
-        part = part.reshape(n_wide, pairs_w, rows, span * b_blk)
-        summed = lax.dynamic_index_in_dim(part, w, 0, keepdims=False)
-        for shift in range(1, n_wide):
-            perm = [(i, (i + shift) % n_wide) for i in range(n_wide)]
-            piece = lax.dynamic_index_in_dim(part, (w + shift) % n_wide, 0, keepdims=False)
-            summed = summed + lax.ppermute(piece, "wide", perm)
+        summed = None
+        for shift in list(range(1, n_wide)) + [0]:
+            blk = (w + shift) % n_wide
+            inter_blk = lax.dynamic_slice_in_dim(inter, blk * pairs_w, pairs_w, 0)
+            piece = jnp.einsum(
+                "padq,bdq->pab", inter_blk, right_group, preferred_element_type=jnp.float32
+            )
+            if shift:
+                perm = [(i, (i + shift) % n_wide) for i in range(n_wide)]
+                piece = lax.ppermute(piece, "wide", perm)
+            summed = piece if summed is None else summed + piece
         part = summed
         part = part.reshape(pairs_w, rows, span, b_blk)
         flipped = jnp.concatenate(

time: 207 us -> 221 us (1.068)
  local copies, waits for them, and re-layouts: 42.1 us -> 55.6 us
  matrix products: 27.2 us -> 36 us
  waiting for transfers between devices: 86.6 us -> 80.6 us
    unnamed x24 -> x34, local copies, waits for them, and re-layouts: 14.2 us -> 28.1 us
    dot_general x1 -> x4, matrix products: 11.4 us -> 19.8 us  [body(): jnp.einsum('padq,bdq->pab', inter_blk, right_group, preferred_element_typ...]
    ppermute x3, waiting for transfers between devices: 10.1 us -> 5.05 us  [body(): piece = lax.ppermute(piece, 'wide', perm)]
    dynamic_slice x2 -> x1, local copies, waits for them, and re-layouts: 5.71 us -> 2.36 us  [rotate_back(): lax.dynamic_slice_in_dim(jnp.concatenate(rev * 2, axis=axis), size - by,...]
  transfers between devices with their start and end apart: 16 -> 16, of which waited for: 10 -> 8; matrix products, arithmetic and copies ran while one was open for 17% -> 21% of each run, Pallas kernels for 0% -> 0%
where the time goes in v17:
time: 221 us; the launch traced here: 220 us
  waiting for transfers between devices  80.6 us (36%)
  local copies, waits for them, and re-layouts  55.6 us (25%)
  matrix products  36 us (16%)
  starting transfers between devices  27.3 us (12%)
  between operations  13.7 us (6%)
  other arithmetic  6.31 us (3%)
    unnamed x34, local copies, waits for them, and re-layouts  28.1 us
    all_to_all x1, waiting for transfers between devices, body(): left_recv = lax.all_to_all(left_send, 'narrow', 0, 0, tiled=True)  24.5 us
    dot_general x4, matrix products, body(): jnp.einsum('padq,bdq->pab', inter_blk, right_group, preferred_element_typ...  19.8 us
    dot_general x1, matrix products, body(): jnp.einsum('wkqia,kpwid->padq', left_all, amps_all, preferred_element_typ...  16.2 us
    all_gather x1, waiting for transfers between devices, body(): left_all = lax.all_gather(left_recv, 'wide', axis=0, tiled=False)  15.4 us
    ppermute x1, waiting for transfers between devices, body(): lax.ppermute(amps, 'narrow', perm_of(0, step))  14.6 us
    ppermute x4, starting transfers between devices, body(): piece = lax.ppermute(piece, ('narrow', 'wide'), perm)  11.7 us
    ppermute x3, waiting for transfers between devices, body(): piece = lax.ppermute(piece, 'narrow', perm)  10.1 us
  transfers between devices with their start and end apart: 16, of which 8 were waited for; matrix products, arithmetic and copies ran while one was open for 21% of the time, Pallas kernels for 0%

profile of v17, /device:TPU:5, one launch (start us, length us, event | category | flops | bytes accessed | tf_op | source)
XLA Modules:
  0.0 219.6 jit_solution(13199706973671701358)
XLA Ops:
  13.9 4.3 %reshape.80 = bf16[8,2,32768]{2,1,0:T(2,128)(2,1)} reshape(bf16[8,64,16,64]{3,2,1,0:T(8,128)(2,1)} %bitcast.89) | data formatting | bytes 2097152
  18.2 5.5 %all-to-all-start = ((bf16[8,2,32768]{2,1,0:T(2,128)(2,1)}), bf16[8,2,32768]{2,1,0:T(2,128)(2,1)S(1)}, u32[]{:S(2)}, u32[]{:S(2)}) async-start(bf16[8,2,32768]{2,1,0:T(2,128)(2,1)} %reshape.80), calls=%async_computation | async-start | bytes 2097152 | tf_op jit(solution)/shard_map/all_to_all | solution.py:45
  23.8 24.5 %all-to-all-done = bf16[8,2,32768]{2,1,0:T(2,128)(2,1)S(1)} async-done(((bf16[8,2,32768]{2,1,0:T(2,128)(2,1)}), bf16[8,2,32768]{2,1,0:T(2,128)(2,1)S(1)}, u32[]{:S(2)}, u32[]{:S(2)}) %all-to-all-start) | async-done | bytes 1048608 | tf_op jit(solution)/shard_map/all_to_all | solution.py:45
  64.6 2.4 %constant_dynamic-slice_fusion.9 = bf16[2,4,64,16,64]{4,3,1,0,2:T(8,128)(2,1)S(1)} fusion(bf16[2,8,64,16,64]{4,3,1,0,2:T(8,128)(2,1)} %constant_dynamic-update-slice_fusion, s32[]{:T(128)S(6)} %select_n.168), kind=kLoop, calls=%fused_computation.52 | loop fusion | bytes 2097156 | tf_op jit(solution)/shard_map/dynamic_slice | solution.py:39
  67.0 2.4 %fusion.13 = bf16[2,4,64,16,64]{4,3,1,0,2:T(8,128)(2,1)} fusion(s32[]{:T(128)S(6)} %select_n.170, bf16[2,4,64,16,64]{4,3,1,0,2:T(8,128)(2,1)S(1)} %constant_dynamic-slice_fusion.9), kind=kLoop, calls=%fused_computation.17 | loop fusion | flops 524288 | bytes 2097156 | tf_op jit(solution)/shard_map/concatenate | solution.py:39
  69.5 14.6 %collective-permute-done = bf16[16,64,128]{2,1,0:T(8,128)(2,1)S(1)} collective-permute-done((bf16[16,64,128]{2,1,0:T(8,128)(2,1)S(1)}, bf16[16,64,128]{2,1,0:T(8,128)(2,1)S(1)}, u32[]{:S(2)}, u32[]{:S(2)}) %collective-permute-start) | collective-permute-done | bytes 262176 | tf_op jit(solution)/shard_map/ppermute | solution.py:30
  84.2 2.9 %collective-permute-start.2 = (bf16[2,16,64,128]{3,2,1,0:T(8,128)(2,1)S(1)}, bf16[2,16,64,128]{3,2,1,0:T(8,128)(2,1)}, u32[]{:S(2)}, u32[]{:S(2)}) collective-permute-start(bf16[2,16,64,128]{3,2,1,0:T(8,128)(2,1)S(1)} %get-tuple-element.22), channel_id=1, source_target_pairs={{0,8},{4,12},{8,0},{12,4},{16,24},{20,28},{24,16},{28,20},{1,9},{5... | collective-permute-start | bytes 1572872 | tf_op jit(solution)/shard_map/ppermute | solution.py:33
  87.1 6.4 %copy.39 = bf16[64,128,256]{1,2,0:T(8,128)(2,1)} copy(bf16[64,128,256]{2,1,0:T(8,128)(2,1)} %param.8) | data formatting | bytes 8388608 | tf_op args[2]
  93.5 3.2 %constant_dynamic-slice_fusion.8 = (bf16[64,128,1,64]{1,3,2,0:T(8,128)(2,1)S(1)}, bf16[64,128,1,64]{1,3,2,0:T(8,128)(2,1)S(1)}, bf16[64,128,1,64]{1,3,2,0:T(8,128)(2,1)S(1)}, bf16[64,128,1,64]{1,3,2,0:T(8,128)(2,1)S(1)}) fusion(bf16[64,128,4,64]{1,3,2,0:T(8,128)(2,1)} %bitcast.86, s32[]{:T(128)S(6)} %select_n.174, s32[]{:T(128)S(6)} %select_n.180, ...), kind=kLoop, calls=%fused_computation.50 | loop fusion | bytes 8388624 | tf_op jit(solution)/shard_map/jit(dynamic_index_in_dim)/dynamic_slice | solution.py:56
  98.3 2.4 %collective-permute-start.6 = (bf16[64,128,64]{1,0,2:T(8,128)(2,1)}, bf16[64,128,64]{1,0,2:T(8,128)(2,1)}, u32[]{:S(2)}, u32[]{:S(2)}) collective-permute-start(bf16[64,128,64]{1,0,2:T(8,128)(2,1)} %bitcast.81), channel_id=1, source_target_pairs={{0,12},{4,0},{8,4},{12,8},{16,28},{20,16},{24,20},{28,24},{1,13},{... | collective-permute-start | bytes 3145736 | tf_op jit(solution)/shard_map/ppermute | solution.py:63
  106.0 4.0 %collective-permute-done.2 = bf16[2,16,64,128]{3,2,1,0:T(8,128)(2,1)} collective-permute-done((bf16[2,16,64,128]{3,2,1,0:T(8,128)(2,1)S(1)}, bf16[2,16,64,128]{3,2,1,0:T(8,128)(2,1)}, u32[]{:S(2)}, u32[]{:S(2)}) %collective-permute-start.2) | collective-permute-done | bytes 524320 | tf_op jit(solution)/shard_map/ppermute | solution.py:33
  113.3 15.4 %all-gather.2.cloned.1.call-done = bf16[4,8,64,16,64]{4,3,0,1,2:T(8,128)(2,1)} async-done(((bf16[1,8,64,16,64]{4,3,0,1,2:T(8,128)(2,1)}), bf16[4,8,64,16,64]{4,3,0,1,2:T(8,128)(2,1)}) %all-gather.2.cloned.1.call-update) | async-done | bytes 4194320 | tf_op jit(solution)/shard_map/all_gather | solution.py:49
  128.7 16.2 %bitcast_convert_fusion = bf16[16,128,64,64]{1,3,2,0:T(8,128)(2,1)} fusion(bf16[8,16,4,16,128,1]{4,3,2,0,5,1:T(8,128)(2,1)} %bitcast.91, bf16[4,8,64,16,64]{4,3,0,1,2:T(8,128)(2,1)} %all-gather.2.cloned.1.call-done), kind=kOutput, calls=%fused_computation | convolution fusion | flops 8598323200 | bytes 23068672 | tf_op jit(solution)/shard_map/wkqia,kpwid->padq/dot_general | solution.py:66
  144.9 10.1 %collective-permute-done.5 = bf16[64,128,64]{1,0,2:T(8,128)(2,1)} collective-permute-done((bf16[64,128,64]{1,0,2:T(8,128)(2,1)}, bf16[64,128,64]{1,0,2:T(8,128)(2,1)}, u32[]{:S(2)}, u32[]{:S(2)}) %collective-permute-start.5) | collective-permute-done | bytes 1048608 | tf_op jit(solution)/shard_map/ppermute | solution.py:63
  155.0 5.8 %fusion.20 = f32[4,64,256]{2,1,0:T(8,128)S(1)} fusion(bf16[16,128,64,64]{1,3,2,0:T(8,128)(2,1)} %bitcast_convert_fusion, s32[]{:T(128)S(6)} %select_n.184, bf16[64,128,64]{1,0,2:T(8,128)(2,1)} %collective-permute-done.6, bf16[64,128,64]{1,0,2:T(8,128)(2,1)} %collective-permute-done.5, bf16[64,128,64]{1,0,2:T(8,128)(2,1)} %collective-permute-done.4, ...), kind=kOutput, calls=%fused_computation.22 | convolution fusion | flops 1090519040 | bytes 8650756 | tf_op jit(solution)/shard_map/padq,bdq->pab/dot_general | solution.py:76
  162.9 4.6 %fusion.14 = f32[4,64,256]{2,1,0:T(8,128)S(1)} fusion(bf16[16,128,64,64]{1,3,2,0:T(8,128)(2,1)S(1)} %copy-done.9, s32[]{:T(128)S(6)} %select_n.172, bf16[64,128,64]{1,0,2:T(8,128)(2,1)} %collective-permute-done.6, bf16[64,128,64]{1,0,2:T(8,128)(2,1)} %collective-permute-done.5, bf16[64,128,64]{1,0,2:T(8,128)(2,1)} %collective-permute-done.4, ...), kind=kOutput, calls=%fused_computation.20 | convolution fusion | flops 1090519040 | bytes 8650756 | tf_op jit(solution)/shard_map/padq,bdq->pab/dot_general | solution.py:76
  169.1 4.6 %fusion.17 = f32[4,64,256]{2,1,0:T(8,128)S(1)} fusion(bf16[16,128,64,64]{1,3,2,0:T(8,128)(2,1)S(1)} %copy-done.9, s32[]{:T(128)S(6)} %select_n.182, bf16[64,128,64]{1,0,2:T(8,128)(2,1)} %collective-permute-done.6, bf16[64,128,64]{1,0,2:T(8,128)(2,1)} %collective-permute-done.5, bf16[64,128,64]{1,0,2:T(8,128)(2,1)} %collective-permute-done.4, ...), kind=kOutput, calls=%fused_computation.21 | convolution fusion | flops 1090519040 | bytes 8650756 | tf_op jit(solution)/shard_map/padq,bdq->pab/dot_general | solution.py:76
  176.9 5.0 %collective-permute-done.8 = f32[4,64,256]{2,1,0:T(8,128)} collective-permute-done((f32[4,64,256]{2,1,0:T(8,128)S(1)}, f32[4,64,256]{2,1,0:T(8,128)}, u32[]{:S(2)}, u32[]{:S(2)}) %collective-permute-start.8) | collective-permute-done | bytes 262176 | tf_op jit(solution)/shard_map/ppermute | solution.py:81
  181.9 4.7 %add_add_fusion = f32[4,64,256]{2,1,0:T(8,128)S(1)} fusion(f32[4,64,256]{2,1,0:T(8,128)} %copy-done.7, f32[4,64,256]{2,1,0:T(8,128)} %copy-done.8, f32[4,64,256]{2,1,0:T(8,128)} %collective-permute-done.8, bf16[16,128,64,64]{1,3,2,0:T(8,128)(2,1)} %bitcast_convert_fusion, s32[]{:T(128)S(6)} %select_n.186, bf16[64,128,64]{1,0,2:T(8,128)(2,1)} %collective-permute-done.6, ...), kind=kOutput, calls=%fused_computation.29 | convolution fusion | flops 1090715648 | bytes 9437188 | tf_op jit(solution)/shard_map/padq,bdq->pab/dot_general | solution.py:76
  187.8 2.8 %concatenate.20 = f32[4,64,8,64]{3,2,1,0:T(8,128)S(1)} concatenate(f32[4,64,1,64]{3,2,1,0:T(1,128)} %get-tuple-element.20, f32[4,64,1,64]{3,2,1,0:T(1,128)S(1)} %get-tuple-element.19, f32[4,64,1,64]{3,2,1,0:T(1,128)S(1)} %get-tuple-element.18, f32[4,64,1,64]{3,2,1,0:T(1,128)S(1)} %get-tuple-element.17, f32[4,64,1,64]{3,2,1,0:T(1,128)} %get-tuple-element.20, ...), dimensions={2} | concatenate | bytes 1048576 | tf_op jit(solution)/shard_map/concatenate | solution.py:85
  193.3 4.2 %collective-permute-start.13 = (f32[2,64,128]{2,1,0:T(8,128)S(1)}, f32[2,64,128]{2,1,0:T(8,128)S(1)}, u32[]{:S(2)}, u32[]{:S(2)}) collective-permute-start(f32[2,64,128]{2,1,0:T(8,128)S(1)} %bitcast.102), channel_id=1, source_target_pairs={{0,5},{1,13},{2,21},{3,29},{4,0},{5,8},{6,16},{7,24},{8,1},{9,9},{... | collective-permute-start | bytes 196616 | tf_op jit(solution)/shard_map/ppermute | solution.py:106
  197.5 3.6 %collective-permute-start.12 = (f32[2,64,128]{2,1,0:T(8,128)S(1)}, f32[2,64,128]{2,1,0:T(8,128)S(1)}, u32[]{:S(2)}, u32[]{:S(2)}) collective-permute-start(f32[2,64,128]{2,1,0:T(8,128)S(1)} %bitcast.101), channel_id=1, source_target_pairs={{0,4},{1,12},{2,20},{3,28},{4,5},{5,13},{6,21},{7,29},{8,0},{9,8},... | collective-permute-start | bytes 196616 | tf_op jit(solution)/shard_map/ppermute | solution.py:106
  205.1 4.2 %collective-permute-done.10 = f32[2,64,128]{2,1,0:T(8,128)S(1)} collective-permute-done((f32[2,64,128]{2,1,0:T(8,128)S(1)}, f32[2,64,128]{2,1,0:T(8,128)S(1)}, u32[]{:S(2)}, u32[]{:S(2)}) %collective-permute-start.10) | collective-permute-done | bytes 65568 | tf_op jit(solution)/shard_map/ppermute | solution.py:106
  209.3 2.7 %collective-permute-done.11 = f32[2,64,128]{2,1,0:T(8,128)S(1)} collective-permute-done((f32[2,64,128]{2,1,0:T(8,128)S(1)}, f32[2,64,128]{2,1,0:T(8,128)S(1)}, u32[]{:S(2)}, u32[]{:S(2)}) %collective-permute-start.11) | collective-permute-done | bytes 65568 | tf_op jit(solution)/shard_map/ppermute | solution.py:106
  (78 shorter events, 49.3 us)
Async XLA Ops:
  18.2 30.1 %all-to-all-start = ((bf16[8,2,32768]{2,1,0:T(2,128)(2,1)}), bf16[8,2,32768]{2,1,0:T(2,128)(2,1)S(1)}, u32[]{:S(2)}, u32[]{:S(2)}) async-start(bf16[8,2,32768]{2,1,0:T(2,128)(2,1)} %reshape.80), calls=%async_computation | async-start | bytes 2097152 | tf_op jit(solution)/shard_map/all_to_all | solution.py:45
  23.8 104.9 %all-gather.2.cloned.1.call-start = ((), (), s32[]{:S(2)}) async-start(), calls=%async_computation.1 | async-start | bytes 10485760 | tf_op jit(solution)/shard_map/all_gather | solution.py:49
  67.0 2.4 %copy-start.3 = (bf16[16,64,128]{2,1,0:T(8,128)(2,1)S(1)}, bf16[16,64,128]{2,1,0:T(8,128)(2,1)}, u32[]{:S(2)}) copy-start(bf16[16,64,128]{2,1,0:T(8,128)(2,1)} %param.6) | copy-start | bytes 786436
  69.4 14.7 %collective-permute-start = (bf16[16,64,128]{2,1,0:T(8,128)(2,1)S(1)}, bf16[16,64,128]{2,1,0:T(8,128)(2,1)S(1)}, u32[]{:S(2)}, u32[]{:S(2)}) collective-permute-start(bf16[16,64,128]{2,1,0:T(8,128)(2,1)S(1)} %copy-done.3), channel_id=1, source_target_pairs={{0,16},{4,20},{8,24},{12,28},{16,0},{20,4},{24,8},{28,12},{1,17},{... | collective-permute-start | bytes 786440 | tf_op jit(solution)/shard_map/ppermute | solution.py:30
  84.2 21.6 %collective-permute-start.3 = (bf16[2,16,64,128]{3,2,1,0:T(8,128)(2,1)S(1)}, bf16[2,16,64,128]{3,2,1,0:T(8,128)(2,1)}, u32[]{:S(2)}, u32[]{:S(2)}) collective-permute-start(bf16[2,16,64,128]{3,2,1,0:T(8,128)(2,1)S(1)} %get-tuple-element.22), channel_id=1, source_target_pairs={{0,12},{4,0},{8,4},{12,8},{16,28},{20,16},{24,20},{28,24},{1,13},{... | collective-permute-start | bytes 1572872 | tf_op jit(solution)/shard_map/ppermute | solution.py:33
  84.2 25.8 %collective-permute-start.2 = (bf16[2,16,64,128]{3,2,1,0:T(8,128)(2,1)S(1)}, bf16[2,16,64,128]{3,2,1,0:T(8,128)(2,1)}, u32[]{:S(2)}, u32[]{:S(2)}) collective-permute-start(bf16[2,16,64,128]{3,2,1,0:T(8,128)(2,1)S(1)} %get-tuple-element.22), channel_id=1, source_target_pairs={{0,8},{4,12},{8,0},{12,4},{16,24},{20,28},{24,16},{28,20},{1,9},{5... | collective-permute-start | bytes 1572872 | tf_op jit(solution)/shard_map/ppermute | solution.py:33
  87.1 22.9 %collective-permute-start.1 = (bf16[2,16,64,128]{3,2,1,0:T(8,128)(2,1)S(1)}, bf16[2,16,64,128]{3,2,1,0:T(8,128)(2,1)}, u32[]{:S(2)}, u32[]{:S(2)}) collective-permute-start(bf16[2,16,64,128]{3,2,1,0:T(8,128)(2,1)S(1)} %get-tuple-element.22), channel_id=1, source_target_pairs={{0,4},{4,8},{8,12},{12,0},{16,20},{20,24},{24,28},{28,16},{1,5},{5... | collective-permute-start | bytes 1572872 | tf_op jit(solution)/shard_map/ppermute | solution.py:33
  98.3 46.6 %collective-permute-start.6 = (bf16[64,128,64]{1,0,2:T(8,128)(2,1)}, bf16[64,128,64]{1,0,2:T(8,128)(2,1)}, u32[]{:S(2)}, u32[]{:S(2)}) collective-permute-start(bf16[64,128,64]{1,0,2:T(8,128)(2,1)} %bitcast.81), channel_id=1, source_target_pairs={{0,12},{4,0},{8,4},{12,8},{16,28},{20,16},{24,20},{28,24},{1,13},{... | collective-permute-start | bytes 3145736 | tf_op jit(solution)/shard_map/ppermute | solution.py:63
  102.3 52.7 %collective-permute-start.5 = (bf16[64,128,64]{1,0,2:T(8,128)(2,1)}, bf16[64,128,64]{1,0,2:T(8,128)(2,1)}, u32[]{:S(2)}, u32[]{:S(2)}) collective-permute-start(bf16[64,128,64]{1,0,2:T(8,128)(2,1)} %bitcast.82), channel_id=1, source_target_pairs={{0,8},{4,12},{8,0},{12,4},{16,24},{20,28},{24,16},{28,20},{1,9},{5... | collective-permute-start | bytes 3145736 | tf_op jit(solution)/shard_map/ppermute | solution.py:63
  105.7 49.3 %collective-permute-start.4 = (bf16[64,128,64]{1,0,2:T(8,128)(2,1)}, bf16[64,128,64]{1,0,2:T(8,128)(2,1)}, u32[]{:S(2)}, u32[]{:S(2)}) collective-permute-start(bf16[64,128,64]{1,0,2:T(8,128)(2,1)} %bitcast.96), channel_id=1, source_target_pairs={{0,4},{4,8},{8,12},{12,0},{16,20},{20,24},{24,28},{28,16},{1,5},{5... | collective-permute-start | bytes 3145736 | tf_op jit(solution)/shard_map/ppermute | solution.py:63
  128.6 26.4 %copy-start.2 = (bf16[64,128,1,64]{1,0,3,2:T(8,128)(2,1)S(1)}, bf16[64,128,1,64]{1,0,3,2:T(8,128)(2,1)}, u32[]{:S(2)}) copy-start(bf16[64,128,1,64]{1,0,3,2:T(8,128)(2,1)} %copy.62) | copy-start | bytes 3145732
  155.0 7.9 %copy-start.9 = (bf16[16,128,64,64]{1,3,2,0:T(8,128)(2,1)S(1)}, bf16[16,128,64,64]{1,3,2,0:T(8,128)(2,1)}, u32[]{:S(2)}) copy-start(bf16[16,128,64,64]{1,3,2,0:T(8,128)(2,1)} %bitcast_convert_fusion) | copy-start | bytes 50331652
  160.9 14.6 %collective-permute-start.9 = (f32[4,64,256]{2,1,0:T(8,128)S(1)}, f32[4,64,256]{2,1,0:T(8,128)S(1)}, u32[]{:S(2)}, u32[]{:S(2)}) collective-permute-start(f32[4,64,256]{2,1,0:T(8,128)S(1)} %fusion.20), channel_id=1, source_target_pairs={{0,3},{1,0},{2,1},{3,2},{4,7},{5,4},{6,5},{7,6},{8,11},{9,8},{10,9... | collective-permute-start | bytes 786440 | tf_op jit(solution)/shard_map/ppermute | solution.py:81
  167.6 7.5 %copy-start.4 = (s32[2,2]{1,0:T(2,128)S(1)}, s32[2,2]{1,0:T(2,128)}, u32[]{:S(2)}) copy-start(s32[2,2]{1,0:T(2,128)} %param.9) | copy-start | bytes 52
  167.6 7.7 %copy-start.5 = (f32[128]{0:T(128)S(1)}, f32[128]{0:T(128)}, u32[]{:S(2)}) copy-start(f32[128]{0:T(128)} %param.10) | copy-start | bytes 1540
  167.6 7.9 %collective-permute-start.7 = (f32[4,64,256]{2,1,0:T(8,128)S(1)}, f32[4,64,256]{2,1,0:T(8,128)S(1)}, u32[]{:S(2)}, u32[]{:S(2)}) collective-permute-start(f32[4,64,256]{2,1,0:T(8,128)S(1)} %fusion.14), channel_id=1, source_target_pairs={{0,1},{1,2},{2,3},{3,0},{4,5},{5,6},{6,7},{7,4},{8,9},{9,10},{10,1... | collective-permute-start | bytes 786440 | tf_op jit(solution)/shard_map/ppermute | solution.py:81
  173.7 8.2 %collective-permute-start.8 = (f32[4,64,256]{2,1,0:T(8,128)S(1)}, f32[4,64,256]{2,1,0:T(8,128)}, u32[]{:S(2)}, u32[]{:S(2)}) collective-permute-start(f32[4,64,256]{2,1,0:T(8,128)S(1)} %fusion.17), channel_id=1, source_target_pairs={{0,2},{1,3},{2,0},{3,1},{4,6},{5,7},{6,4},{7,5},{8,10},{9,11},{10,... | collective-permute-start | bytes 786440 | tf_op jit(solution)/shard_map/ppermute | solution.py:81
  181.9 30.8 %copy-start.1 = (bf16[64,64,256]{2,1,0:T(8,128)(2,1)S(1)}, bf16[64,64,256]{2,1,0:T(8,128)(2,1)}, u32[]{:S(2)}) copy-start(bf16[64,64,256]{2,1,0:T(8,128)(2,1)} %param.7) | copy-start | bytes 6291460
  186.6 18.3 %slice-start = ((f32[512]{0:T(512)}), f32[64]{0:T(128)S(1)}, s32[]{:S(2)}) async-start(f32[512]{0:T(512)} %param.11), calls=%async_computation.2 | async-start | bytes 1024 | tf_op jit(solution)/shard_map/slice | solution.py:118
  186.6 18.4 %copy-start.6 = (f32[512]{0:T(512)S(1)}, f32[512]{0:T(512)}, u32[]{:S(2)}) copy-start(f32[512]{0:T(512)} %param.11) | copy-start | bytes 6148
  193.3 11.8 %collective-permute-start.13 = (f32[2,64,128]{2,1,0:T(8,128)S(1)}, f32[2,64,128]{2,1,0:T(8,128)S(1)}, u32[]{:S(2)}, u32[]{:S(2)}) collective-permute-start(f32[2,64,128]{2,1,0:T(8,128)S(1)} %bitcast.102), channel_id=1, source_target_pairs={{0,5},{1,13},{2,21},{3,29},{4,0},{5,8},{6,16},{7,24},{8,1},{9,9},{... | collective-permute-start | bytes 196616 | tf_op jit(solution)/shard_map/ppermute | solution.py:106
  197.5 7.6 %collective-permute-start.12 = (f32[2,64,128]{2,1,0:T(8,128)S(1)}, f32[2,64,128]{2,1,0:T(8,128)S(1)}, u32[]{:S(2)}, u32[]{:S(2)}) collective-permute-start(f32[2,64,128]{2,1,0:T(8,128)S(1)} %bitcast.101), channel_id=1, source_target_pairs={{0,4},{1,12},{2,20},{3,28},{4,5},{5,13},{6,21},{7,29},{8,0},{9,8},... | collective-permute-start | bytes 196616 | tf_op jit(solution)/shard_map/ppermute | solution.py:106
  201.1 8.3 %collective-permute-start.10 = (f32[2,64,128]{2,1,0:T(8,128)S(1)}, f32[2,64,128]{2,1,0:T(8,128)S(1)}, u32[]{:S(2)}, u32[]{:S(2)}) collective-permute-start(f32[2,64,128]{2,1,0:T(8,128)S(1)} %bitcast.100), channel_id=1, source_target_pairs={{0,0},{1,8},{2,16},{3,24},{4,1},{5,9},{6,17},{7,25},{8,4},{9,12},{... | collective-permute-start | bytes 196616 | tf_op jit(solution)/shard_map/ppermute | solution.py:106
  203.0 9.0 %collective-permute-start.11 = (f32[2,64,128]{2,1,0:T(8,128)S(1)}, f32[2,64,128]{2,1,0:T(8,128)S(1)}, u32[]{:S(2)}, u32[]{:S(2)}) collective-permute-start(f32[2,64,128]{2,1,0:T(8,128)S(1)} %bitcast.99), channel_id=1, source_target_pairs={{0,1},{1,9},{2,17},{3,25},{4,4},{5,12},{6,20},{7,28},{8,5},{9,13},... | collective-permute-start | bytes 196616 | tf_op jit(solution)/shard_map/ppermute | solution.py:106
  (3 other events, 3.0 us)
Sparse Core Ops, SparseCore 0:
  69.5 59.0 all-gather.1

commit v18 on v14

--- a/solution.py
+++ b/solution.py
@@ -38,16 +38,20 @@
             rev = [lax.slice_in_dim(x, (size - j) % size, (size - j) % size + 1, axis=axis) for j in range(size)]
             return lax.dynamic_slice_in_dim(jnp.concatenate(rev * 2, axis=axis), size - by, size, axis)
 
-        c_sub = c_blk // n_wide
-        left_part = lax.dynamic_slice_in_dim(left_fit, w * c_sub, c_sub, 1)
-        left_part = left_part.reshape(rows, c_sub, span, q_blk).transpose(2, 3, 1, 0)
+        c_half = c_blk // 2
+        core = w % 2
+        left_part = lax.dynamic_slice_in_dim(left_fit, core * c_half, c_half, 1)
+        left_part = left_part.reshape(rows, c_half, span, q_blk).transpose(2, 3, 1, 0)
         left_send = jnp.concatenate([left_part] * GROUPS, axis=0)
         left_recv = lax.all_to_all(left_send, "narrow", 0, 0, tiled=True)
         left_recv = left_recv.reshape((GROUPS, span) + left_recv.shape[1:])
         left_recv = rotate_back(rotate_back(left_recv, r, span, 1), g, GROUPS, 0)
         left_recv = left_recv.reshape((n_narrow,) + left_recv.shape[2:])
-        left_all = lax.all_gather(left_recv, "wide", axis=0, tiled=False)
-        amps_all = amps_all.reshape(n_narrow, pairs, n_wide, c_sub, amps.shape[2])
+        partner = lax.ppermute(left_recv, "wide", [(i, i ^ 1) for i in range(n_wide)])
+        left_all = jnp.stack(
+            [jnp.where(core == 0, left_recv, partner), jnp.where(core == 0, partner, left_recv)], axis=0
+        )
+        amps_all = amps_all.reshape(n_narrow, pairs, 2, c_half, amps.shape[2])
 
         right_split = right_fit.reshape(b_blk, d_blk, span, q_blk)
         chunks = []
@@ -64,7 +68,7 @@
             chunks.append(piece)
 
         inter = jnp.einsum(
-            "wkqia,kpwid->padq", left_all, amps_all, preferred_element_type=jnp.float32
+            "hkqia,kphid->padq", left_all, amps_all, preferred_element_type=jnp.float32
         ).astype(jnp.bfloat16)
 
         right_group = jnp.concatenate(chunks, axis=0)

time: 207 us -> 250 us (1.21)
  local copies, waits for them, and re-layouts: 42.1 us -> 71.7 us
  waiting for transfers between devices: 86.6 us -> 105 us
  between operations: 13.7 us -> 0.22 us
  other arithmetic: 7.53 us -> 16.6 us
    unnamed x24 -> x32, local copies, waits for them, and re-layouts: 14.2 us -> 41.4 us
    all_to_all x1, waiting for transfers between devices: 24.5 us -> 47.4 us  [body(): left_recv = lax.all_to_all(left_send, 'narrow', 0, 0, tiled=True)]
    all_gather x1 -> x0, waiting for transfers between devices: 15.9 us -> none  [body(): left_all = lax.all_gather(left_recv, 'wide', axis=0, tiled=False)]
    ppermute x3, waiting for transfers between devices: 11.7 us -> 21.2 us  [body(): piece = lax.ppermute(piece, 'narrow', perm)]
    another operation x0 -> x1, other arithmetic: none -> 5.77 us  [body(): jnp.stack([jnp.where(core == 0, left_recv, partner), jnp.where(core == 0,...]
    slice x0 -> x1, local copies, waits for them, and re-layouts: none -> 4.46 us  [rotate_back(): lax.slice_in_dim(x, (size - j) % size, (size - j) % size + 1, axis=axis)]
    dynamic_slice x2 -> x1, local copies, waits for them, and re-layouts: 5.71 us -> 3.01 us  [rotate_back(): lax.dynamic_slice_in_dim(jnp.concatenate(rev * 2, axis=axis), size - by,...]
  transfers between devices with their start and end apart: 16 -> 16, of which waited for: 10 -> 11; matrix products, arithmetic and copies ran while one was open for 17% -> 17% of each run, Pallas kernels for 0% -> 0%
where the time goes in v18:
time: 250 us; the launch traced here: 248 us
  waiting for transfers between devices  105 us (42%)
  local copies, waits for them, and re-layouts  71.7 us (29%)
  matrix products  27.7 us (11%)
  starting transfers between devices  27 us (11%)
  other arithmetic  16.6 us (7%)
    all_to_all x1, waiting for transfers between devices, body(): left_recv = lax.all_to_all(left_send, 'narrow', 0, 0, tiled=True)  47.4 us
    unnamed x32, local copies, waits for them, and re-layouts  41.4 us
    ppermute x3, waiting for transfers between devices, body(): piece = lax.ppermute(piece, 'narrow', perm)  21.2 us
    dot_general x1, matrix products, body(): jnp.einsum('hkqia,kphid->padq', left_all, amps_all, preferred_element_typ...  16.3 us
    ppermute x1, waiting for transfers between devices, body(): lax.ppermute(amps, 'narrow', perm_of(0, step))  14.4 us
    ppermute x4, starting transfers between devices, body(): piece = lax.ppermute(piece, ('narrow', 'wide'), perm)  12.4 us
    dot_general x1, matrix products, body(): jnp.einsum('padq,bdq->pab', inter, right_group, preferred_element_type=jn...  11.4 us
    dynamic_slice x5, local copies, waits for them, and re-layouts, body(): piece = lax.dynamic_index_in_dim(right_split, dest, 2, keepdims=False)  10.2 us
  transfers between devices with their start and end apart: 16, of which 11 were waited for; matrix products, arithmetic and copies ran while one was open for 17% of the time, Pallas kernels for 0%

profile of v18, /device:TPU:5, one launch (start us, length us, event | category | flops | bytes accessed | tf_op | source)
XLA Modules:
  0.0 247.8 jit_solution(3699256633532896031)
XLA Ops:
  7.7 7.6 %reshape.85 = bf16[8,2,65536]{2,1,0:T(2,128)(2,1)} reshape(bf16[8,64,32,64]{3,2,1,0:T(8,128)(2,1)} %bitcast.86) | data formatting | bytes 4194304
  15.3 5.5 %all-to-all-start = ((bf16[8,2,65536]{2,1,0:T(2,128)(2,1)}), bf16[8,2,65536]{2,1,0:T(2,128)(2,1)S(1)}, u32[]{:S(2)}, u32[]{:S(2)}) async-start(bf16[8,2,65536]{2,1,0:T(2,128)(2,1)} %reshape.85), calls=%async_computation | async-start | bytes 4194304 | tf_op jit(solution)/shard_map/all_to_all | solution.py:46
  20.8 47.4 %all-to-all-done = bf16[8,2,65536]{2,1,0:T(2,128)(2,1)S(1)} async-done(((bf16[8,2,65536]{2,1,0:T(2,128)(2,1)}), bf16[8,2,65536]{2,1,0:T(2,128)(2,1)S(1)}, u32[]{:S(2)}, u32[]{:S(2)}) %all-to-all-start) | async-done | bytes 2097184 | tf_op jit(solution)/shard_map/all_to_all | solution.py:46
  68.2 5.0 %reshape.86 = bf16[8,64,32,64]{3,2,1,0:T(8,128)(2,1)} reshape(bf16[8,2,65536]{2,1,0:T(2,128)(2,1)S(1)} %all-to-all-done) | data formatting | bytes 4194304
  73.2 4.5 %fusion.20 = (bf16[2,1,64,32,64]{2,3,4,1,0:T(8,128)(2,1)}, bf16[2,1,64,32,64]{2,3,4,1,0:T(8,128)(2,1)S(1)}, bf16[2,1,64,32,64]{2,3,4,1,0:T(8,128)(2,1)S(1)}, bf16[2,1,64,32,64]{2,3,4,1,0:T(8,128)(2,1)}) fusion(bf16[2,4,64,32,64]{2,3,4,1,0:T(8,128)(2,1)} %bitcast.85), kind=kLoop, calls=%fused_computation.62 | loop fusion | bytes 4194304 | tf_op jit(solution)/shard_map/slice | solution.py:38
  77.6 3.3 %copy.68 = bf16[2,1,64,32,64]{4,3,2,1,0:T(8,128)(2,1)S(1)} copy(bf16[2,1,64,32,64]{2,3,4,1,0:T(8,128)(2,1)} %get-tuple-element.18) | data formatting | bytes 1048576
  82.0 2.9 %copy.69 = bf16[2,1,64,32,64]{4,3,2,1,0:T(8,128)(2,1)} copy(bf16[2,1,64,32,64]{2,3,4,1,0:T(8,128)(2,1)S(1)} %get-tuple-element.17) | data formatting | bytes 1048576
  87.0 3.3 %copy.71 = bf16[2,1,64,32,64]{4,3,2,1,0:T(8,128)(2,1)S(1)} copy(bf16[2,1,64,32,64]{2,3,4,1,0:T(8,128)(2,1)} %get-tuple-element.15) | data formatting | bytes 1048576
  99.7 3.0 %constant_dynamic-slice_fusion.9 = bf16[2,4,64,32,64]{4,3,2,1,0:T(8,128)(2,1)S(1)} fusion(bf16[2,8,64,32,64]{4,3,2,1,0:T(8,128)(2,1)} %constant_dynamic-update-slice_fusion, s32[]{:T(128)S(6)} %select_n.183), kind=kLoop, calls=%fused_computation.50 | loop fusion | bytes 4194308 | tf_op jit(solution)/shard_map/dynamic_slice | solution.py:39
  102.8 3.4 %fusion.6 = bf16[2,4,64,32,64]{4,3,2,1,0:T(8,128)(2,1)} fusion(s32[]{:T(128)S(6)} %select_n.185, bf16[2,4,64,32,64]{4,3,2,1,0:T(8,128)(2,1)S(1)} %constant_dynamic-slice_fusion.9), kind=kLoop, calls=%fused_computation.9 | loop fusion | flops 1048576 | bytes 4194308 | tf_op jit(solution)/shard_map/concatenate | solution.py:39
  108.0 14.4 %collective-permute-done = bf16[16,64,128]{2,1,0:T(8,128)(2,1)S(1)} collective-permute-done((bf16[16,64,128]{2,1,0:T(8,128)(2,1)S(1)}, bf16[16,64,128]{2,1,0:T(8,128)(2,1)S(1)}, u32[]{:S(2)}, u32[]{:S(2)}) %collective-permute-start) | collective-permute-done | bytes 262176 | tf_op jit(solution)/shard_map/ppermute | solution.py:30
  125.1 6.4 %copy.57 = bf16[64,128,256]{1,2,0:T(8,128)(2,1)} copy(bf16[64,128,256]{2,1,0:T(8,128)(2,1)} %param.8) | data formatting | bytes 8388608 | tf_op args[2]
  131.5 3.5 %constant_dynamic-slice_fusion.8 = (bf16[64,128,1,64]{1,3,2,0:T(8,128)(2,1)S(1)}, bf16[64,128,1,64]{1,3,2,0:T(8,128)(2,1)S(1)}, bf16[64,128,1,64]{1,3,2,0:T(8,128)(2,1)S(1)}, bf16[64,128,1,64]{1,3,2,0:T(8,128)(2,1)S(1)}) fusion(bf16[64,128,4,64]{1,3,2,0:T(8,128)(2,1)} %bitcast.84, s32[]{:T(128)S(6)} %select_n.189, s32[]{:T(128)S(6)} %select_n.195, ...), kind=kLoop, calls=%fused_computation.49 | loop fusion | bytes 8388624 | tf_op jit(solution)/shard_map/jit(dynamic_index_in_dim)/dynamic_slice | solution.py:60
  144.1 4.2 %collective-permute-done.2 = bf16[2,16,64,128]{3,2,1,0:T(8,128)(2,1)} collective-permute-done((bf16[2,16,64,128]{3,2,1,0:T(8,128)(2,1)}, bf16[2,16,64,128]{3,2,1,0:T(8,128)(2,1)}, u32[]{:S(2)}, u32[]{:S(2)}) %collective-permute-start.2) | collective-permute-done | bytes 524320 | tf_op jit(solution)/shard_map/ppermute | solution.py:33
  150.7 5.8 %select_bitcast_fusion.1 = (bf16[1,8,64,32,64]{4,3,0,2,1:T(8,128)(2,1)}, bf16[1,8,64,32,64]{4,3,0,2,1:T(8,128)(2,1)}) fusion(bf16[8,64,32,64]{3,2,1,0:T(8,128)(2,1)} %collective-permute-done.4, pred[]{:T(512)S(6)} %eq.52, bf16[2,4,64,32,64]{4,3,2,1,0:T(8,128)(2,1)} %fusion.6), kind=kLoop, calls=%fused_computation.19 | loop fusion | flops 2097152 | bytes 8388609 | tf_op jit(solution)/shard_map/stack | solution.py:51
  156.4 16.3 %fusion.3 = bf16[16,128,64,64,1,1]{1,3,4,2,0,5:T(8,128)(2,1)} fusion(bf16[8,16,2,32,128,1]{4,3,2,5,1,0:T(8,128)(2,1)S(1)} %bitcast.88, bf16[1,8,64,32,64]{4,3,0,2,1:T(8,128)(2,1)} %get-tuple-element.10, bf16[1,8,64,32,64]{4,3,0,2,1:T(8,128)(2,1)} %get-tuple-element.9), kind=kOutput, calls=%fused_computation.6 | convolution fusion | flops 8598323200 | bytes 23068672 | tf_op jit(solution)/shard_map/hkqia,kphid->padq/dot_general | solution.py:70
  172.7 20.5 %collective-permute-done.6 = bf16[64,128,64]{1,0,2:T(8,128)(2,1)} collective-permute-done((bf16[64,128,64]{1,0,2:T(8,128)(2,1)}, bf16[64,128,64]{1,0,2:T(8,128)(2,1)}, u32[]{:S(2)}, u32[]{:S(2)}) %collective-permute-start.6) | collective-permute-done | bytes 1048608 | tf_op jit(solution)/shard_map/ppermute | solution.py:67
  194.0 11.4 %fusion.1 = f32[16,64,256,1]{2,1,0,3:T(8,128)S(1)} fusion(bf16[16,128,64,64,1,1]{1,3,4,2,0,5:T(8,128)(2,1)} %fusion.3, bf16[64,128,64]{1,0,2:T(8,128)(2,1)} %collective-permute-done.7, bf16[64,128,64]{1,0,2:T(8,128)(2,1)} %collective-permute-done.6, bf16[64,128,64]{1,0,2:T(8,128)(2,1)} %collective-permute-done.5, bf16[64,128,64]{1,0,2:T(8,128)(2,1)} %bitcast.91), kind=kOutput, calls=%fused_computation.2 | convolution fusion | flops 4311744512 | bytes 22020096 | tf_op jit(solution)/shard_map/padq,bdq->pab/dot_general | solution.py:75
  210.0 4.2 %collective-permute-done.10 = f32[4,64,256]{2,1,0:T(8,128)} collective-permute-done((f32[4,64,256]{2,1,0:T(8,128)}, f32[4,64,256]{2,1,0:T(8,128)}, u32[]{:S(2)}, u32[]{:S(2)}) %collective-permute-start.10) | collective-permute-done | bytes 262176 | tf_op jit(solution)/shard_map/ppermute | solution.py:84
  216.5 3.5 %collective-permute-done.8 = f32[4,64,256]{2,1,0:T(8,128)} collective-permute-done((f32[4,64,256]{2,1,0:T(8,128)S(1)}, f32[4,64,256]{2,1,0:T(8,128)}, u32[]{:S(2)}, u32[]{:S(2)}) %collective-permute-start.8) | collective-permute-done | bytes 262176 | tf_op jit(solution)/shard_map/ppermute | solution.py:84
  222.5 2.8 %concatenate.20 = f32[4,64,8,64]{3,2,1,0:T(8,128)S(1)} concatenate(f32[4,64,1,64]{3,2,1,0:T(1,128)} %get-tuple-element.25, f32[4,64,1,64]{3,2,1,0:T(1,128)S(1)} %get-tuple-element.24, f32[4,64,1,64]{3,2,1,0:T(1,128)S(1)} %get-tuple-element.23, f32[4,64,1,64]{3,2,1,0:T(1,128)S(1)} %get-tuple-element.22, f32[4,64,1,64]{3,2,1,0:T(1,128)} %get-tuple-element.25, ...), dimensions={2} | concatenate | bytes 1048576 | tf_op jit(solution)/shard_map/concatenate | solution.py:87
  228.0 4.7 %collective-permute-start.14 = (f32[2,64,128]{2,1,0:T(8,128)S(1)}, f32[2,64,128]{2,1,0:T(8,128)S(1)}, u32[]{:S(2)}, u32[]{:S(2)}) collective-permute-start(f32[2,64,128]{2,1,0:T(8,128)S(1)} %bitcast.99), channel_id=1, source_target_pairs={{0,5},{1,13},{2,21},{3,29},{4,0},{5,8},{6,16},{7,24},{8,1},{9,9},{... | collective-permute-start | bytes 196616 | tf_op jit(solution)/shard_map/ppermute | solution.py:108
  232.6 3.9 %collective-permute-start.13 = (f32[2,64,128]{2,1,0:T(8,128)S(1)}, f32[2,64,128]{2,1,0:T(8,128)S(1)}, u32[]{:S(2)}, u32[]{:S(2)}) collective-permute-start(f32[2,64,128]{2,1,0:T(8,128)S(1)} %bitcast.98), channel_id=1, source_target_pairs={{0,4},{1,12},{2,20},{3,28},{4,5},{5,13},{6,21},{7,29},{8,0},{9,8},... | collective-permute-start | bytes 196616 | tf_op jit(solution)/shard_map/ppermute | solution.py:108
  240.6 4.7 %collective-permute-done.11 = f32[2,64,128]{2,1,0:T(8,128)S(1)} collective-permute-done((f32[2,64,128]{2,1,0:T(8,128)S(1)}, f32[2,64,128]{2,1,0:T(8,128)S(1)}, u32[]{:S(2)}, u32[]{:S(2)}) %collective-permute-start.11) | collective-permute-done | bytes 65568 | tf_op jit(solution)/shard_map/ppermute | solution.py:108
  (74 shorter events, 55.6 us)
Async XLA Ops:
  15.3 52.9 %all-to-all-start = ((bf16[8,2,65536]{2,1,0:T(2,128)(2,1)}), bf16[8,2,65536]{2,1,0:T(2,128)(2,1)S(1)}, u32[]{:S(2)}, u32[]{:S(2)}) async-start(bf16[8,2,65536]{2,1,0:T(2,128)(2,1)} %reshape.85), calls=%async_computation | async-start | bytes 4194304 | tf_op jit(solution)/shard_map/all_to_all | solution.py:46
  90.3 5.9 %copy-start.2 = (bf16[2,1,64,32,64]{4,3,2,1,0:T(8,128)(2,1)S(1)}, bf16[2,1,64,32,64]{4,3,2,1,0:T(8,128)(2,1)}, u32[]{:S(2)}) copy-start(bf16[2,1,64,32,64]{4,3,2,1,0:T(8,128)(2,1)} %copy.69) | copy-start | bytes 1572868
  106.1 44.5 %collective-permute-start.4 = (bf16[8,64,32,64]{3,2,1,0:T(8,128)(2,1)}, bf16[8,64,32,64]{3,2,1,0:T(8,128)(2,1)}, u32[]{:S(2)}, u32[]{:S(2)}) collective-permute-start(bf16[8,64,32,64]{3,2,1,0:T(8,128)(2,1)} %bitcast.14), channel_id=1, source_target_pairs={{0,1},{1,0},{2,3},{3,2},{4,5},{5,4},{6,7},{7,6},{8,9},{9,8},{10,11... | collective-permute-start | bytes 6291464 | tf_op jit(solution)/shard_map/ppermute | solution.py:50
  108.0 14.4 %collective-permute-start = (bf16[16,64,128]{2,1,0:T(8,128)(2,1)S(1)}, bf16[16,64,128]{2,1,0:T(8,128)(2,1)S(1)}, u32[]{:S(2)}, u32[]{:S(2)}) collective-permute-start(bf16[16,64,128]{2,1,0:T(8,128)(2,1)S(1)} %copy-done.5), channel_id=1, source_target_pairs={{0,16},{4,20},{8,24},{12,28},{16,0},{20,4},{24,8},{28,12},{1,17},{... | collective-permute-start | bytes 786440 | tf_op jit(solution)/shard_map/ppermute | solution.py:30
  123.5 20.6 %collective-permute-start.3 = (bf16[2,16,64,128]{3,2,1,0:T(8,128)(2,1)}, bf16[2,16,64,128]{3,2,1,0:T(8,128)(2,1)}, u32[]{:S(2)}, u32[]{:S(2)}) collective-permute-start(bf16[2,16,64,128]{3,2,1,0:T(8,128)(2,1)} %get-tuple-element.27), channel_id=1, source_target_pairs={{0,12},{4,0},{8,4},{12,8},{16,28},{20,16},{24,20},{28,24},{1,13},{... | collective-permute-start | bytes 1572872 | tf_op jit(solution)/shard_map/ppermute | solution.py:33
  123.5 24.7 %collective-permute-start.2 = (bf16[2,16,64,128]{3,2,1,0:T(8,128)(2,1)}, bf16[2,16,64,128]{3,2,1,0:T(8,128)(2,1)}, u32[]{:S(2)}, u32[]{:S(2)}) collective-permute-start(bf16[2,16,64,128]{3,2,1,0:T(8,128)(2,1)} %get-tuple-element.27), channel_id=1, source_target_pairs={{0,8},{4,12},{8,0},{12,4},{16,24},{20,28},{24,16},{28,20},{1,9},{5... | collective-permute-start | bytes 1572872 | tf_op jit(solution)/shard_map/ppermute | solution.py:33
  125.1 24.0 %collective-permute-start.1 = (bf16[2,16,64,128]{3,2,1,0:T(8,128)(2,1)}, bf16[2,16,64,128]{3,2,1,0:T(8,128)(2,1)}, u32[]{:S(2)}, u32[]{:S(2)}) collective-permute-start(bf16[2,16,64,128]{3,2,1,0:T(8,128)(2,1)} %get-tuple-element.27), channel_id=1, source_target_pairs={{0,4},{4,8},{8,12},{12,0},{16,20},{20,24},{24,28},{28,16},{1,5},{5... | collective-permute-start | bytes 1572872 | tf_op jit(solution)/shard_map/ppermute | solution.py:33
  136.6 36.1 %collective-permute-start.7 = (bf16[64,128,64]{1,0,2:T(8,128)(2,1)}, bf16[64,128,64]{1,0,2:T(8,128)(2,1)}, u32[]{:S(2)}, u32[]{:S(2)}) collective-permute-start(bf16[64,128,64]{1,0,2:T(8,128)(2,1)} %bitcast.79), channel_id=1, source_target_pairs={{0,12},{4,0},{8,4},{12,8},{16,28},{20,16},{24,20},{28,24},{1,13},{... | collective-permute-start | bytes 3145736 | tf_op jit(solution)/shard_map/ppermute | solution.py:67
  140.7 8.4 %copy-start.3 = (bf16[2,1,16,64,128]{4,3,2,1,0:T(8,128)(2,1)S(1)}, bf16[2,1,16,64,128]{4,3,2,1,0:T(8,128)(2,1)}, u32[]{:S(2)}) copy-start(bf16[2,1,16,64,128]{4,3,2,1,0:T(8,128)(2,1)} %get-tuple-element.26) | copy-start | bytes 1572868
  144.1 49.2 %collective-permute-start.6 = (bf16[64,128,64]{1,0,2:T(8,128)(2,1)}, bf16[64,128,64]{1,0,2:T(8,128)(2,1)}, u32[]{:S(2)}, u32[]{:S(2)}) collective-permute-start(bf16[64,128,64]{1,0,2:T(8,128)(2,1)} %bitcast.93), channel_id=1, source_target_pairs={{0,8},{4,12},{8,0},{12,4},{16,24},{20,28},{24,16},{28,20},{1,9},{5... | collective-permute-start | bytes 3145736 | tf_op jit(solution)/shard_map/ppermute | solution.py:67
  148.2 45.7 %collective-permute-start.5 = (bf16[64,128,64]{1,0,2:T(8,128)(2,1)}, bf16[64,128,64]{1,0,2:T(8,128)(2,1)}, u32[]{:S(2)}, u32[]{:S(2)}) collective-permute-start(bf16[64,128,64]{1,0,2:T(8,128)(2,1)} %bitcast.92), channel_id=1, source_target_pairs={{0,4},{4,8},{8,12},{12,0},{16,20},{20,24},{24,28},{28,16},{1,5},{5... | collective-permute-start | bytes 3145736 | tf_op jit(solution)/shard_map/ppermute | solution.py:67
  194.0 15.6 %copy-start.6 = (s32[2,2]{1,0:T(2,128)S(1)}, s32[2,2]{1,0:T(2,128)}, u32[]{:S(2)}) copy-start(s32[2,2]{1,0:T(2,128)} %param.9) | copy-start | bytes 52
  194.0 15.8 %copy-start.7 = (f32[128]{0:T(128)S(1)}, f32[128]{0:T(128)}, u32[]{:S(2)}) copy-start(f32[128]{0:T(128)} %param.10) | copy-start | bytes 1540
  205.4 11.1 %copy-start.4 = (f32[16,64,256,1]{2,1,0,3:T(8,128)}, f32[16,64,256,1]{2,1,0,3:T(8,128)S(1)}, u32[]{:S(2)}) copy-start(f32[16,64,256,1]{2,1,0,3:T(8,128)S(1)} %fusion.1) | copy-start | bytes 3145732
  205.4 42.4 %copy-start.1 = (bf16[64,64,256]{2,1,0:T(8,128)(2,1)S(1)}, bf16[64,64,256]{2,1,0:T(8,128)(2,1)}, u32[]{:S(2)}) copy-start(bf16[64,64,256]{2,1,0:T(8,128)(2,1)} %param.7) | copy-start | bytes 6291460
  206.3 34.1 %slice-start = ((f32[512]{0:T(512)}), f32[64]{0:T(128)S(1)}, s32[]{:S(2)}) async-start(f32[512]{0:T(512)} %param.11), calls=%async_computation.1 | async-start | bytes 1024 | tf_op jit(solution)/shard_map/slice | solution.py:120
  206.3 34.2 %copy-start.8 = (f32[512]{0:T(512)S(1)}, f32[512]{0:T(512)}, u32[]{:S(2)}) copy-start(f32[512]{0:T(512)} %param.11) | copy-start | bytes 6148
  206.3 7.9 %collective-permute-start.10 = (f32[4,64,256]{2,1,0:T(8,128)}, f32[4,64,256]{2,1,0:T(8,128)}, u32[]{:S(2)}, u32[]{:S(2)}) collective-permute-start(f32[4,64,256]{2,1,0:T(8,128)} %get-tuple-element.20), channel_id=1, source_target_pairs={{0,3},{1,0},{2,1},{3,2},{4,7},{5,4},{6,5},{7,6},{8,11},{9,8},{10,9... | collective-permute-start | bytes 786440 | tf_op jit(solution)/shard_map/ppermute | solution.py:84
  207.9 8.6 %collective-permute-start.9 = (f32[4,64,256]{2,1,0:T(8,128)}, f32[4,64,256]{2,1,0:T(8,128)}, u32[]{:S(2)}, u32[]{:S(2)}) collective-permute-start(f32[4,64,256]{2,1,0:T(8,128)} %get-tuple-element.21), channel_id=1, source_target_pairs={{0,2},{1,3},{2,0},{3,1},{4,6},{5,7},{6,4},{7,5},{8,10},{9,11},{10,... | collective-permute-start | bytes 786440 | tf_op jit(solution)/shard_map/ppermute | solution.py:84
  208.1 12.0 %collective-permute-start.8 = (f32[4,64,256]{2,1,0:T(8,128)S(1)}, f32[4,64,256]{2,1,0:T(8,128)}, u32[]{:S(2)}, u32[]{:S(2)}) collective-permute-start(f32[4,64,256]{2,1,0:T(8,128)S(1)} %get-tuple-element.19), channel_id=1, source_target_pairs={{0,1},{1,2},{2,3},{3,0},{4,5},{5,6},{6,7},{7,4},{8,9},{9,10},{10,1... | collective-permute-start | bytes 786440 | tf_op jit(solution)/shard_map/ppermute | solution.py:84
  228.0 12.6 %collective-permute-start.14 = (f32[2,64,128]{2,1,0:T(8,128)S(1)}, f32[2,64,128]{2,1,0:T(8,128)S(1)}, u32[]{:S(2)}, u32[]{:S(2)}) collective-permute-start(f32[2,64,128]{2,1,0:T(8,128)S(1)} %bitcast.99), channel_id=1, source_target_pairs={{0,5},{1,13},{2,21},{3,29},{4,0},{5,8},{6,16},{7,24},{8,1},{9,9},{... | collective-permute-start | bytes 196616 | tf_op jit(solution)/shard_map/ppermute | solution.py:108
  232.6 7.9 %collective-permute-start.13 = (f32[2,64,128]{2,1,0:T(8,128)S(1)}, f32[2,64,128]{2,1,0:T(8,128)S(1)}, u32[]{:S(2)}, u32[]{:S(2)}) collective-permute-start(f32[2,64,128]{2,1,0:T(8,128)S(1)} %bitcast.98), channel_id=1, source_target_pairs={{0,4},{1,12},{2,20},{3,28},{4,5},{5,13},{6,21},{7,29},{8,0},{9,8},... | collective-permute-start | bytes 196616 | tf_op jit(solution)/shard_map/ppermute | solution.py:108
  236.5 8.7 %collective-permute-start.11 = (f32[2,64,128]{2,1,0:T(8,128)S(1)}, f32[2,64,128]{2,1,0:T(8,128)S(1)}, u32[]{:S(2)}, u32[]{:S(2)}) collective-permute-start(f32[2,64,128]{2,1,0:T(8,128)S(1)} %bitcast.97), channel_id=1, source_target_pairs={{0,0},{1,8},{2,16},{3,24},{4,1},{5,9},{6,17},{7,25},{8,4},{9,12},{... | collective-permute-start | bytes 196616 | tf_op jit(solution)/shard_map/ppermute | solution.py:108
  238.5 8.6 %collective-permute-start.12 = (f32[2,64,128]{2,1,0:T(8,128)S(1)}, f32[2,64,128]{2,1,0:T(8,128)S(1)}, u32[]{:S(2)}, u32[]{:S(2)}) collective-permute-start(f32[2,64,128]{2,1,0:T(8,128)S(1)} %bitcast.96), channel_id=1, source_target_pairs={{0,1},{1,9},{2,17},{3,25},{4,4},{5,12},{6,20},{7,28},{8,5},{9,13},... | collective-permute-start | bytes 196616 | tf_op jit(solution)/shard_map/ppermute | solution.py:108
  (2 other events, 6.8 us)

commit v19 on v14

--- a/solution.py
+++ b/solution.py
@@ -46,8 +46,8 @@
         left_recv = left_recv.reshape((GROUPS, span) + left_recv.shape[1:])
         left_recv = rotate_back(rotate_back(left_recv, r, span, 1), g, GROUPS, 0)
         left_recv = left_recv.reshape((n_narrow,) + left_recv.shape[2:])
-        left_all = lax.all_gather(left_recv, "wide", axis=0, tiled=False)
-        amps_all = amps_all.reshape(n_narrow, pairs, n_wide, c_sub, amps.shape[2])
+        left_all = lax.all_gather(left_recv, "wide", axis=2, tiled=True)
+        amps_all = amps_all.reshape(n_narrow, pairs, c_blk, amps.shape[2])
 
         right_split = right_fit.reshape(b_blk, d_blk, span, q_blk)
         chunks = []
@@ -64,7 +64,7 @@
             chunks.append(piece)
 
         inter = jnp.einsum(
-            "wkqia,kpwid->padq", left_all, amps_all, preferred_element_type=jnp.float32
+            "kqca,kpcd->padq", left_all, amps_all, preferred_element_type=jnp.float32
         ).astype(jnp.bfloat16)
 
         right_group = jnp.concatenate(chunks, axis=0)

time: 207 us -> 248 us (1.20)
  waiting for transfers between devices: 86.6 us -> 108 us
  local copies, waits for them, and re-layouts: 42.1 us -> 59.6 us
  starting transfers between devices: 27.7 us -> 30.6 us
  matrix products: 27.2 us -> 24.3 us
    ppermute x3, waiting for transfers between devices: 4.05 us -> 60.4 us  [body(): lax.ppermute(group_set, 'narrow', perm_of(shift, 0))]
    unnamed x24 -> x28, local copies, waits for them, and re-layouts: 14.2 us -> 31.6 us
    all_gather x1, waiting for transfers between devices: 15.9 us -> 0.02 us  [body(): left_all = lax.all_gather(left_recv, 'wide', axis=2, tiled=True)]
    dot_general x1 -> x0, matrix products: 15.8 us -> none  [body(): jnp.einsum('wkqia,kpwid->padq', left_all, amps_all, preferred_element_typ...]
    dot_general x1, matrix products: 11.4 us -> 24.3 us  [body(): jnp.einsum('padq,bdq->pab', inter, right_group, preferred_element_type=jn...]
    ppermute x3, waiting for transfers between devices: 11.7 us -> 0.01 us  [body(): piece = lax.ppermute(piece, 'narrow', perm)]
    ppermute x1, waiting for transfers between devices: 14.6 us -> 8.14 us  [body(): lax.ppermute(amps, 'narrow', perm_of(0, step))]
    dynamic_slice x2 -> x1, local copies, waits for them, and re-layouts: 5.71 us -> 2.06 us  [rotate_back(): lax.dynamic_slice_in_dim(jnp.concatenate(rev * 2, axis=axis), size - by,...]
  transfers between devices with their start and end apart: 16 -> 16, of which waited for: 10 -> 10; matrix products, arithmetic and copies ran while one was open for 17% -> 9% of each run, Pallas kernels for 0% -> 0%
where the time goes in v19:
time: 248 us; the launch traced here: 246 us
  waiting for transfers between devices  108 us (44%)
  local copies, waits for them, and re-layouts  59.6 us (24%)
  starting transfers between devices  30.6 us (12%)
  matrix products  24.3 us (10%)
  between operations  13.7 us (6%)
  other arithmetic  9.95 us (4%)
    ppermute x3, waiting for transfers between devices, body(): lax.ppermute(group_set, 'narrow', perm_of(shift, 0))  60.4 us
    unnamed x28, local copies, waits for them, and re-layouts  31.6 us
    all_to_all x1, waiting for transfers between devices, body(): left_recv = lax.all_to_all(left_send, 'narrow', 0, 0, tiled=True)  24.5 us
    dot_general x1, matrix products, body(): jnp.einsum('padq,bdq->pab', inter, right_group, preferred_element_type=jn...  24.3 us
    ppermute x4, starting transfers between devices, body(): piece = lax.ppermute(piece, ('narrow', 'wide'), perm)  16 us
    ppermute x3, waiting for transfers between devices, body(): summed = summed + lax.ppermute(piece, 'wide', perm)  12.1 us
    dynamic_slice x5, local copies, waits for them, and re-layouts, body(): piece = lax.dynamic_index_in_dim(right_split, dest, 2, keepdims=False)  9.89 us
    ppermute x1, waiting for transfers between devices, body(): lax.ppermute(amps, 'narrow', perm_of(0, step))  8.14 us
  transfers between devices with their start and end apart: 16, of which 10 were waited for; matrix products, arithmetic and copies ran while one was open for 9% of the time, Pallas kernels for 0%

profile of v19, /device:TPU:5, one launch (start us, length us, event | category | flops | bytes accessed | tf_op | source)
XLA Modules:
  0.0 246.0 jit_solution(14489230140862297583)
XLA Ops:
  13.9 4.3 %reshape.85 = bf16[8,2,32768]{2,1,0:T(2,128)(2,1)} reshape(bf16[8,64,16,64]{3,2,1,0:T(8,128)(2,1)} %bitcast.79) | data formatting | bytes 2097152
  18.3 5.5 %all-to-all-start = ((bf16[8,2,32768]{2,1,0:T(2,128)(2,1)}), bf16[8,2,32768]{2,1,0:T(2,128)(2,1)S(1)}, u32[]{:S(2)}, u32[]{:S(2)}) async-start(bf16[8,2,32768]{2,1,0:T(2,128)(2,1)} %reshape.85), calls=%async_computation | async-start | bytes 2097152 | tf_op jit(solution)/shard_map/all_to_all | solution.py:45
  23.9 24.5 %all-to-all-done = bf16[8,2,32768]{2,1,0:T(2,128)(2,1)S(1)} async-done(((bf16[8,2,32768]{2,1,0:T(2,128)(2,1)}), bf16[8,2,32768]{2,1,0:T(2,128)(2,1)S(1)}, u32[]{:S(2)}, u32[]{:S(2)}) %all-to-all-start) | async-done | bytes 1048608 | tf_op jit(solution)/shard_map/all_to_all | solution.py:45
  48.4 2.7 %reshape.86 = bf16[8,64,16,64]{3,2,1,0:T(8,128)(2,1)} reshape(bf16[8,2,32768]{2,1,0:T(2,128)(2,1)S(1)} %all-to-all-done) | data formatting | bytes 2097152
  51.1 2.8 %fusion.24 = (bf16[2,1,64,16,64]{2,3,4,1,0:T(8,128)(2,1)}, bf16[2,1,64,16,64]{2,3,4,1,0:T(8,128)(2,1)S(1)}, bf16[2,1,64,16,64]{2,3,4,1,0:T(8,128)(2,1)}, bf16[2,1,64,16,64]{2,3,4,1,0:T(8,128)(2,1)}) fusion(bf16[2,4,64,16,64]{2,3,4,1,0:T(8,128)(2,1)} %bitcast.78), kind=kLoop, calls=%fused_computation.58 | loop fusion | bytes 2097152 | tf_op jit(solution)/shard_map/slice | solution.py:38
  56.9 2.8 %copy.66 = bf16[2,1,64,16,64]{4,3,1,0,2:T(8,128)(2,1)} copy(bf16[2,1,64,16,64]{2,3,4,1,0:T(8,128)(2,1)} %get-tuple-element.15) | data formatting | bytes 524288
  71.4 2.1 constant_dynamic-slice_fusion.9
  73.5 2.4 fusion.15
  76.1 6.4 %copy.55 = bf16[64,128,256]{1,2,0:T(8,128)(2,1)} copy(bf16[64,128,256]{2,1,0:T(8,128)(2,1)} %param.8) | data formatting | bytes 8388608 | tf_op args[2]
  82.5 8.1 %collective-permute-done = bf16[16,64,128]{2,1,0:T(8,128)(2,1)S(1)} collective-permute-done((bf16[16,64,128]{2,1,0:T(8,128)(2,1)S(1)}, bf16[16,64,128]{2,1,0:T(8,128)(2,1)S(1)}, u32[]{:S(2)}, u32[]{:S(2)}) %collective-permute-start) | collective-permute-done | bytes 262176 | tf_op jit(solution)/shard_map/ppermute | solution.py:30
  93.4 3.2 %constant_dynamic-slice_fusion.8 = (bf16[64,128,1,64]{1,3,2,0:T(8,128)(2,1)S(1)}, bf16[64,128,1,64]{1,3,2,0:T(8,128)(2,1)S(1)}, bf16[64,128,1,64]{1,3,2,0:T(8,128)(2,1)S(1)}, bf16[64,128,1,64]{1,3,2,0:T(8,128)(2,1)S(1)}) fusion(bf16[64,128,4,64]{1,3,2,0:T(8,128)(2,1)} %bitcast.75, s32[]{:T(128)S(6)} %select_n.169, s32[]{:T(128)S(6)} %select_n.175, ...), kind=kLoop, calls=%fused_computation.46 | loop fusion | bytes 8388624 | tf_op jit(solution)/shard_map/jit(dynamic_index_in_dim)/dynamic_slice | solution.py:56
  107.4 50.5 %collective-permute-done.2 = bf16[2,16,64,128]{3,2,1,0:T(8,128)(2,1)} collective-permute-done((bf16[2,16,64,128]{3,2,1,0:T(8,128)(2,1)}, bf16[2,16,64,128]{3,2,1,0:T(8,128)(2,1)}, u32[]{:S(2)}, u32[]{:S(2)}) %collective-permute-start.2) | collective-permute-done | bytes 524320 | tf_op jit(solution)/shard_map/ppermute | solution.py:33
  157.9 9.5 %collective-permute-done.3 = bf16[2,16,64,128]{3,2,1,0:T(8,128)(2,1)} collective-permute-done((bf16[2,16,64,128]{3,2,1,0:T(8,128)(2,1)}, bf16[2,16,64,128]{3,2,1,0:T(8,128)(2,1)}, u32[]{:S(2)}, u32[]{:S(2)}) %collective-permute-start.3) | collective-permute-done | bytes 524320 | tf_op jit(solution)/shard_map/ppermute | solution.py:33
  167.5 3.1 %pad_maximum_fusion = bf16[2,4,16,64,128]{4,3,2,1,0:T(8,128)(2,1)} fusion(bf16[2,1,16,64,128]{4,3,2,1,0:T(8,128)(2,1)} %bitcast.8, bf16[2,1,16,64,128]{4,3,2,1,0:T(8,128)(2,1)} %bitcast.7, bf16[2,1,16,64,128]{4,3,2,1,0:T(8,128)(2,1)} %bitcast.5, bf16[2,1,16,64,128]{4,3,2,1,0:T(8,128)(2,1)} %get-tuple-element.24), kind=kLoop, calls=%fused_computation.15 | loop fusion | flops 3145728 | bytes 4194304 | tf_op jit(solution)/shard_map/stack | solution.py:35
  170.6 24.3 %fusion.1 = f32[16,64,256,1]{2,1,3,0:T(8,128)S(1)} fusion(bf16[8,64,64,64]{3,2,0,1:T(8,128)(2,1)} %all-gather.2.cloned.1.call-done, bf16[64,128,64]{1,0,2:T(8,128)(2,1)} %collective-permute-done.6, bf16[64,128,64]{1,0,2:T(8,128)(2,1)} %collective-permute-done.5, bf16[64,128,64]{1,0,2:T(8,128)(2,1)} %collective-permute-done.4, ...), kind=kOutput, calls=%fused_computation.2 | convolution fusion | flops 12910067712 | bytes 11534336 | tf_op jit(solution)/shard_map/padq,bdq->pab/dot_general | solution.py:71
  195.8 2.2 collective-permute-start.7
  199.7 4.2 %collective-permute-done.7 = f32[4,64,256]{2,1,0:T(8,128)} collective-permute-done((f32[4,64,256]{2,1,0:T(8,128)}, f32[4,64,256]{2,1,0:T(8,128)}, u32[]{:S(2)}, u32[]{:S(2)}) %collective-permute-start.7) | collective-permute-done | bytes 262176 | tf_op jit(solution)/shard_map/ppermute | solution.py:80
  203.9 7.3 %collective-permute-done.8 = f32[4,64,256]{2,1,0:T(8,128)} collective-permute-done((f32[4,64,256]{2,1,0:T(8,128)}, f32[4,64,256]{2,1,0:T(8,128)}, u32[]{:S(2)}, u32[]{:S(2)}) %collective-permute-start.8) | collective-permute-done | bytes 262176 | tf_op jit(solution)/shard_map/ppermute | solution.py:80
  214.1 2.8 %concatenate.20 = f32[4,64,8,64]{3,2,1,0:T(8,128)S(1)} concatenate(f32[4,64,1,64]{3,2,1,0:T(1,128)} %get-tuple-element.23, f32[4,64,1,64]{3,2,1,0:T(1,128)S(1)} %get-tuple-element.22, f32[4,64,1,64]{3,2,1,0:T(1,128)S(1)} %get-tuple-element.21, f32[4,64,1,64]{3,2,1,0:T(1,128)S(1)} %get-tuple-element.20, f32[4,64,1,64]{3,2,1,0:T(1,128)} %get-tuple-element.23, ...), dimensions={2} | concatenate | bytes 1048576 | tf_op jit(solution)/shard_map/concatenate | solution.py:83
  219.6 2.4 collective-permute-start.10
  222.0 6.0 %collective-permute-start.11 = (f32[2,64,128]{2,1,0:T(8,128)S(1)}, f32[2,64,128]{2,1,0:T(8,128)S(1)}, u32[]{:S(2)}, u32[]{:S(2)}) collective-permute-start(f32[2,64,128]{2,1,0:T(8,128)S(1)} %bitcast.88), channel_id=1, source_target_pairs={{0,1},{1,9},{2,17},{3,25},{4,4},{5,12},{6,20},{7,28},{8,5},{9,13},... | collective-permute-start | bytes 196616 | tf_op jit(solution)/shard_map/ppermute | solution.py:104
  228.0 2.1 collective-permute-start.12
  230.1 5.5 %collective-permute-start.13 = (f32[2,64,128]{2,1,0:T(8,128)S(1)}, f32[2,64,128]{2,1,0:T(8,128)S(1)}, u32[]{:S(2)}, u32[]{:S(2)}) collective-permute-start(f32[2,64,128]{2,1,0:T(8,128)S(1)} %bitcast.86), channel_id=1, source_target_pairs={{0,5},{1,13},{2,21},{3,29},{4,0},{5,8},{6,16},{7,24},{8,1},{9,9},{... | collective-permute-start | bytes 196616 | tf_op jit(solution)/shard_map/ppermute | solution.py:104
  236.1 2.4 collective-permute-done.13
  (69 shorter events, 45.0 us)
Async XLA Ops:
  6.5 1.6 copy-start
  18.3 30.1 %all-to-all-start = ((bf16[8,2,32768]{2,1,0:T(2,128)(2,1)}), bf16[8,2,32768]{2,1,0:T(2,128)(2,1)S(1)}, u32[]{:S(2)}, u32[]{:S(2)}) async-start(bf16[8,2,32768]{2,1,0:T(2,128)(2,1)} %reshape.85), calls=%async_computation | async-start | bytes 2097152 | tf_op jit(solution)/shard_map/all_to_all | solution.py:45
  23.8 146.8 %all-gather.2.cloned.1.call-start = ((), (), s32[]{:S(2)}) async-start(), calls=%async_computation.1 | async-start | bytes 10485760 | tf_op jit(solution)/shard_map/all_gather | solution.py:49
  55.9 3.8 %copy-start.1 = (bf16[2,1,64,16,64]{4,3,1,0,2:T(8,128)(2,1)}, bf16[2,1,64,16,64]{4,3,1,0,2:T(8,128)(2,1)S(1)}, u32[]{:S(2)}) copy-start(bf16[2,1,64,16,64]{4,3,1,0,2:T(8,128)(2,1)S(1)} %copy.65) | copy-start | bytes 786436
  62.8 5.9 %copy-start.2 = (bf16[2,1,64,16,64]{4,3,1,0,2:T(8,128)(2,1)S(1)}, bf16[2,1,64,16,64]{4,3,1,0,2:T(8,128)(2,1)}, u32[]{:S(2)}) copy-start(bf16[2,1,64,16,64]{4,3,1,0,2:T(8,128)(2,1)} %copy.66) | copy-start | bytes 786436
  73.5 2.5 %copy-start.3 = (bf16[16,64,128]{2,1,0:T(8,128)(2,1)S(1)}, bf16[16,64,128]{2,1,0:T(8,128)(2,1)}, u32[]{:S(2)}) copy-start(bf16[16,64,128]{2,1,0:T(8,128)(2,1)} %param.6) | copy-start | bytes 786436
  75.9 14.7 %collective-permute-start = (bf16[16,64,128]{2,1,0:T(8,128)(2,1)S(1)}, bf16[16,64,128]{2,1,0:T(8,128)(2,1)S(1)}, u32[]{:S(2)}, u32[]{:S(2)}) collective-permute-start(bf16[16,64,128]{2,1,0:T(8,128)(2,1)S(1)} %copy-done.3), channel_id=1, source_target_pairs={{0,16},{4,20},{8,24},{12,28},{16,0},{20,4},{24,8},{28,12},{1,17},{... | collective-permute-start | bytes 786440 | tf_op jit(solution)/shard_map/ppermute | solution.py:30
  91.7 14.1 %collective-permute-start.1 = (bf16[2,16,64,128]{3,2,1,0:T(8,128)(2,1)}, bf16[2,16,64,128]{3,2,1,0:T(8,128)(2,1)}, u32[]{:S(2)}, u32[]{:S(2)}) collective-permute-start(bf16[2,16,64,128]{3,2,1,0:T(8,128)(2,1)} %get-tuple-element.25), channel_id=1, source_target_pairs={{0,4},{4,8},{8,12},{12,0},{16,20},{20,24},{24,28},{28,16},{1,5},{5... | collective-permute-start | bytes 1572872 | tf_op jit(solution)/shard_map/ppermute | solution.py:33
  98.3 72.3 %collective-permute-start.4 = (bf16[64,128,64]{1,0,2:T(8,128)(2,1)}, bf16[64,128,64]{1,0,2:T(8,128)(2,1)}, u32[]{:S(2)}, u32[]{:S(2)}) collective-permute-start(bf16[64,128,64]{1,0,2:T(8,128)(2,1)} %bitcast.72), channel_id=1, source_target_pairs={{0,4},{4,8},{8,12},{12,0},{16,20},{20,24},{24,28},{28,16},{1,5},{5... | collective-permute-start | bytes 3145736 | tf_op jit(solution)/shard_map/ppermute | solution.py:63
  99.9 70.6 %collective-permute-start.5 = (bf16[64,128,64]{1,0,2:T(8,128)(2,1)}, bf16[64,128,64]{1,0,2:T(8,128)(2,1)}, u32[]{:S(2)}, u32[]{:S(2)}) collective-permute-start(bf16[64,128,64]{1,0,2:T(8,128)(2,1)} %bitcast.71), channel_id=1, source_target_pairs={{0,8},{4,12},{8,0},{12,4},{16,24},{20,28},{24,16},{28,20},{1,9},{5... | collective-permute-start | bytes 3145736 | tf_op jit(solution)/shard_map/ppermute | solution.py:63
  102.5 68.0 %collective-permute-start.6 = (bf16[64,128,64]{1,0,2:T(8,128)(2,1)}, bf16[64,128,64]{1,0,2:T(8,128)(2,1)}, u32[]{:S(2)}, u32[]{:S(2)}) collective-permute-start(bf16[64,128,64]{1,0,2:T(8,128)(2,1)} %bitcast.70), channel_id=1, source_target_pairs={{0,12},{4,0},{8,4},{12,8},{16,28},{20,16},{24,20},{28,24},{1,13},{... | collective-permute-start | bytes 3145736 | tf_op jit(solution)/shard_map/ppermute | solution.py:63
  104.0 54.0 %collective-permute-start.2 = (bf16[2,16,64,128]{3,2,1,0:T(8,128)(2,1)}, bf16[2,16,64,128]{3,2,1,0:T(8,128)(2,1)}, u32[]{:S(2)}, u32[]{:S(2)}) collective-permute-start(bf16[2,16,64,128]{3,2,1,0:T(8,128)(2,1)} %get-tuple-element.25), channel_id=1, source_target_pairs={{0,8},{4,12},{8,0},{12,4},{16,24},{20,28},{24,16},{28,20},{1,9},{5... | collective-permute-start | bytes 1572872 | tf_op jit(solution)/shard_map/ppermute | solution.py:33
  105.8 61.7 %collective-permute-start.3 = (bf16[2,16,64,128]{3,2,1,0:T(8,128)(2,1)}, bf16[2,16,64,128]{3,2,1,0:T(8,128)(2,1)}, u32[]{:S(2)}, u32[]{:S(2)}) collective-permute-start(bf16[2,16,64,128]{3,2,1,0:T(8,128)(2,1)} %get-tuple-element.25), channel_id=1, source_target_pairs={{0,12},{4,0},{8,4},{12,8},{16,28},{20,16},{24,20},{28,24},{1,13},{... | collective-permute-start | bytes 1572872 | tf_op jit(solution)/shard_map/ppermute | solution.py:33
  170.6 28.7 %copy-start.4 = (s32[2,2]{1,0:T(2,128)S(1)}, s32[2,2]{1,0:T(2,128)}, u32[]{:S(2)}) copy-start(s32[2,2]{1,0:T(2,128)} %param.9) | copy-start | bytes 52
  170.6 28.9 %copy-start.5 = (f32[128]{0:T(128)S(1)}, f32[128]{0:T(128)}, u32[]{:S(2)}) copy-start(f32[128]{0:T(128)} %param.10) | copy-start | bytes 1540
  195.8 39.8 %slice-start = ((f32[512]{0:T(512)}), f32[64]{0:T(128)S(1)}, s32[]{:S(2)}) async-start(f32[512]{0:T(512)} %param.11), calls=%async_computation.2 | async-start | bytes 1024 | tf_op jit(solution)/shard_map/slice | solution.py:116
  195.8 39.9 %copy-start.6 = (f32[512]{0:T(512)S(1)}, f32[512]{0:T(512)}, u32[]{:S(2)}) copy-start(f32[512]{0:T(512)} %param.11) | copy-start | bytes 6148
  195.8 8.1 %collective-permute-start.7 = (f32[4,64,256]{2,1,0:T(8,128)}, f32[4,64,256]{2,1,0:T(8,128)}, u32[]{:S(2)}, u32[]{:S(2)}) collective-permute-start(f32[4,64,256]{2,1,0:T(8,128)} %get-tuple-element.17), channel_id=1, source_target_pairs={{0,1},{1,2},{2,3},{3,0},{4,5},{5,6},{6,7},{7,4},{8,9},{9,10},{10,1... | collective-permute-start | bytes 786440 | tf_op jit(solution)/shard_map/ppermute | solution.py:80
  198.1 13.2 %collective-permute-start.8 = (f32[4,64,256]{2,1,0:T(8,128)}, f32[4,64,256]{2,1,0:T(8,128)}, u32[]{:S(2)}, u32[]{:S(2)}) collective-permute-start(f32[4,64,256]{2,1,0:T(8,128)} %get-tuple-element.19), channel_id=1, source_target_pairs={{0,2},{1,3},{2,0},{3,1},{4,6},{5,7},{6,4},{7,5},{8,10},{9,11},{10,... | collective-permute-start | bytes 786440 | tf_op jit(solution)/shard_map/ppermute | solution.py:80
  199.3 12.5 %collective-permute-start.9 = (f32[4,64,256]{2,1,0:T(8,128)S(1)}, f32[4,64,256]{2,1,0:T(8,128)}, u32[]{:S(2)}, u32[]{:S(2)}) collective-permute-start(f32[4,64,256]{2,1,0:T(8,128)S(1)} %get-tuple-element.18), channel_id=1, source_target_pairs={{0,3},{1,0},{2,1},{3,2},{4,7},{5,4},{6,5},{7,6},{8,11},{9,8},{10,9... | collective-permute-start | bytes 786440 | tf_op jit(solution)/shard_map/ppermute | solution.py:80
  219.6 16.2 %collective-permute-start.10 = (f32[2,64,128]{2,1,0:T(8,128)S(1)}, f32[2,64,128]{2,1,0:T(8,128)S(1)}, u32[]{:S(2)}, u32[]{:S(2)}) collective-permute-start(f32[2,64,128]{2,1,0:T(8,128)S(1)} %bitcast.89), channel_id=1, source_target_pairs={{0,0},{1,8},{2,16},{3,24},{4,1},{5,9},{6,17},{7,25},{8,4},{9,12},{... | collective-permute-start | bytes 196616 | tf_op jit(solution)/shard_map/ppermute | solution.py:104
  222.0 13.8 %collective-permute-start.11 = (f32[2,64,128]{2,1,0:T(8,128)S(1)}, f32[2,64,128]{2,1,0:T(8,128)S(1)}, u32[]{:S(2)}, u32[]{:S(2)}) collective-permute-start(f32[2,64,128]{2,1,0:T(8,128)S(1)} %bitcast.88), channel_id=1, source_target_pairs={{0,1},{1,9},{2,17},{3,25},{4,4},{5,12},{6,20},{7,28},{8,5},{9,13},... | collective-permute-start | bytes 196616 | tf_op jit(solution)/shard_map/ppermute | solution.py:104
  228.0 8.1 %collective-permute-start.12 = (f32[2,64,128]{2,1,0:T(8,128)S(1)}, f32[2,64,128]{2,1,0:T(8,128)S(1)}, u32[]{:S(2)}, u32[]{:S(2)}) collective-permute-start(f32[2,64,128]{2,1,0:T(8,128)S(1)} %bitcast.87), channel_id=1, source_target_pairs={{0,4},{1,12},{2,20},{3,28},{4,5},{5,13},{6,21},{7,29},{8,0},{9,8},... | collective-permute-start | bytes 196616 | tf_op jit(solution)/shard_map/ppermute | solution.py:104
  230.1 8.4 %collective-permute-start.13 = (f32[2,64,128]{2,1,0:T(8,128)S(1)}, f32[2,64,128]{2,1,0:T(8,128)S(1)}, u32[]{:S(2)}, u32[]{:S(2)}) collective-permute-start(f32[2,64,128]{2,1,0:T(8,128)S(1)} %bitcast.86), channel_id=1, source_target_pairs={{0,5},{1,13},{2,21},{3,29},{4,0},{5,8},{6,16},{7,24},{8,1},{9,9},{... | collective-permute-start | bytes 196616 | tf_op jit(solution)/shard_map/ppermute | solution.py:104
Sparse Core Ops, SparseCore 0:
  76.1 59.0 all-gather.1

commit v20 on v14

--- a/solution.py
+++ b/solution.py
@@ -79,20 +79,22 @@
             piece = lax.dynamic_index_in_dim(part, (w + shift) % n_wide, 0, keepdims=False)
             summed = summed + lax.ppermute(piece, "wide", perm)
         part = summed
-        part = part.reshape(pairs_w, rows, span, b_blk)
-        flipped = jnp.concatenate(
-            [part[:, :, (span - k) % span : (span - k) % span + 1] for k in range(span)] * 2, axis=2
-        )
-        ordered = lax.dynamic_slice_in_dim(flipped, span - r, span, 2)
         n_per_w = n_narrow // n_wide
         w_per_g = n_wide // GROUPS
-        cols = span * b_blk // w_per_g
-        ordered = ordered.reshape(n_per_w, pairs_w // n_per_w, rows, w_per_g, cols)
+        blocks_per_col = span // w_per_g
+        part = part.reshape(n_per_w, pairs_w // n_per_w, rows, span, b_blk)
         ladder = None
         for t in range(span):
             k = (t + r) % span
-            piece = lax.dynamic_index_in_dim(ordered, k // w_per_g, 0, keepdims=False)
-            piece = lax.dynamic_index_in_dim(piece, k % w_per_g, 2, keepdims=False)
+            sub = lax.dynamic_index_in_dim(part, k // w_per_g, 0, keepdims=False)
+            col = k % w_per_g
+            piece = jnp.concatenate(
+                [
+                    lax.dynamic_index_in_dim(sub, (r - col * blocks_per_col - m) % span, 2, keepdims=False)
+                    for m in range(blocks_per_col)
+                ],
+                axis=2,
+            )
             perm = []
             for gg in range(GROUPS):
                 for rr in range(span):

time: 207 us -> 201 us (0.971)
  local copies, waits for them, and re-layouts: 42.1 us -> 36.4 us
    concatenate x1 -> x0, local copies, waits for them, and re-layouts: 2.83 us -> none  [body(): jnp.concatenate([part[:, :, (span - k) % span:(span - k) % span + 1] for...]
where the time goes in v20:
time: 201 us; the launch traced here: 200 us
  waiting for transfers between devices  86.6 us (43%)
  local copies, waits for them, and re-layouts  36.4 us (18%)
  starting transfers between devices  27.6 us (14%)
  matrix products  27.3 us (14%)
  between operations  13.7 us (7%)
  other arithmetic  7.86 us (4%)
    all_to_all x1, waiting for transfers between devices, body(): left_recv = lax.all_to_all(left_send, 'narrow', 0, 0, tiled=True)  24.5 us
    all_gather x1, waiting for transfers between devices, body(): left_all = lax.all_gather(left_recv, 'wide', axis=0, tiled=False)  15.9 us
    dot_general x1, matrix products, body(): jnp.einsum('wkqia,kpwid->padq', left_all, amps_all, preferred_element_typ...  15.8 us
    ppermute x1, waiting for transfers between devices, body(): lax.ppermute(amps, 'narrow', perm_of(0, step))  14.6 us
    unnamed x24, local copies, waits for them, and re-layouts  14.2 us
    ppermute x4, starting transfers between devices, body(): piece = lax.ppermute(piece, ('narrow', 'wide'), perm)  13.4 us
    ppermute x3, waiting for transfers between devices, body(): piece = lax.ppermute(piece, 'narrow', perm)  11.7 us
    dot_general x1, matrix products, body(): jnp.einsum('padq,bdq->pab', inter, right_group, preferred_element_type=jn...  11.6 us
  transfers between devices with their start and end apart: 16, of which 10 were waited for; matrix products, arithmetic and copies ran while one was open for 17% of the time, Pallas kernels for 0%

profile of v20, /device:TPU:5, one launch (start us, length us, event | category | flops | bytes accessed | tf_op | source)
XLA Modules:
  0.0 199.6 jit_solution(3463408708246832558)
XLA Ops:
  9.0 2.0 %reshape.73 = bf16[64,16,4,64]{3,2,1,0:T(4,128)(2,1)S(1)} reshape(bf16[64,16,256]{2,1,0:T(8,128)(2,1)} %constant_dynamic-slice_fusion.13) | data formatting | bytes 1048576 | tf_op jit(solution)/shard_map/reshape | solution.py:43
  13.9 4.3 %reshape.85 = bf16[8,2,32768]{2,1,0:T(2,128)(2,1)} reshape(bf16[8,64,16,64]{3,2,1,0:T(8,128)(2,1)} %bitcast.89) | data formatting | bytes 2097152
  18.2 5.5 %all-to-all-start = ((bf16[8,2,32768]{2,1,0:T(2,128)(2,1)}), bf16[8,2,32768]{2,1,0:T(2,128)(2,1)S(1)}, u32[]{:S(2)}, u32[]{:S(2)}) async-start(bf16[8,2,32768]{2,1,0:T(2,128)(2,1)} %reshape.85), calls=%async_computation | async-start | bytes 2097152 | tf_op jit(solution)/shard_map/all_to_all | solution.py:45
  23.8 24.5 %all-to-all-done = bf16[8,2,32768]{2,1,0:T(2,128)(2,1)S(1)} async-done(((bf16[8,2,32768]{2,1,0:T(2,128)(2,1)}), bf16[8,2,32768]{2,1,0:T(2,128)(2,1)S(1)}, u32[]{:S(2)}, u32[]{:S(2)}) %all-to-all-start) | async-done | bytes 1048608 | tf_op jit(solution)/shard_map/all_to_all | solution.py:45
  50.8 2.4 %fusion.11 = bf16[2,4,64,16,64]{2,3,4,1,0:T(8,128)(2,1)} fusion(s32[]{:T(128)S(6)} %select_n.218, bf16[2,4,64,16,64]{2,3,4,1,0:T(8,128)(2,1)S(1)} %constant_dynamic-slice_fusion.12), kind=kLoop, calls=%fused_computation.14 | loop fusion | flops 524288 | bytes 2097156 | tf_op jit(solution)/shard_map/concatenate | solution.py:39
  53.1 5.3 %copy.46 = bf16[2,4,64,16,64]{4,3,2,1,0:T(8,128)(2,1)} copy(bf16[2,4,64,16,64]{2,3,4,1,0:T(8,128)(2,1)} %fusion.11) | data formatting | bytes 2097152 | tf_op jit(solution)/shard_map/dynamic_slice | solution.py:39
  58.6 14.6 %collective-permute-done = bf16[16,64,128]{2,1,0:T(8,128)(2,1)S(1)} collective-permute-done((bf16[16,64,128]{2,1,0:T(8,128)(2,1)S(1)}, bf16[16,64,128]{2,1,0:T(8,128)(2,1)S(1)}, u32[]{:S(2)}, u32[]{:S(2)}) %collective-permute-start) | collective-permute-done | bytes 262176 | tf_op jit(solution)/shard_map/ppermute | solution.py:30
  73.3 2.9 %collective-permute-start.2 = (bf16[2,16,64,128]{3,2,1,0:T(8,128)(2,1)S(1)}, bf16[2,16,64,128]{3,2,1,0:T(8,128)(2,1)}, u32[]{:S(2)}, u32[]{:S(2)}) collective-permute-start(bf16[2,16,64,128]{3,2,1,0:T(8,128)(2,1)S(1)} %get-tuple-element.25), channel_id=1, source_target_pairs={{0,8},{4,12},{8,0},{12,4},{16,24},{20,28},{24,16},{28,20},{1,9},{5... | collective-permute-start | bytes 1572872 | tf_op jit(solution)/shard_map/ppermute | solution.py:33
  76.2 6.4 %copy.48 = bf16[64,128,256]{1,2,0:T(8,128)(2,1)} copy(bf16[64,128,256]{2,1,0:T(8,128)(2,1)} %param.8) | data formatting | bytes 8388608 | tf_op args[2]
  82.6 3.2 %constant_dynamic-slice_fusion.11 = (bf16[64,128,1,64]{1,3,2,0:T(8,128)(2,1)S(1)}, bf16[64,128,1,64]{1,3,2,0:T(8,128)(2,1)S(1)}, bf16[64,128,1,64]{1,3,2,0:T(8,128)(2,1)S(1)}, bf16[64,128,1,64]{1,3,2,0:T(8,128)(2,1)S(1)}) fusion(bf16[64,128,4,64]{1,3,2,0:T(8,128)(2,1)} %bitcast.87, s32[]{:T(128)S(6)} %select_n.220, s32[]{:T(128)S(6)} %select_n.226, ...), kind=kLoop, calls=%fused_computation.52 | loop fusion | bytes 8388624 | tf_op jit(solution)/shard_map/jit(dynamic_index_in_dim)/dynamic_slice | solution.py:56
  87.4 2.4 %collective-permute-start.6 = (bf16[64,128,64]{1,0,2:T(8,128)(2,1)}, bf16[64,128,64]{1,0,2:T(8,128)(2,1)}, u32[]{:S(2)}, u32[]{:S(2)}) collective-permute-start(bf16[64,128,64]{1,0,2:T(8,128)(2,1)} %bitcast.74), channel_id=1, source_target_pairs={{0,12},{4,0},{8,4},{12,8},{16,28},{20,16},{24,20},{28,24},{1,13},{... | collective-permute-start | bytes 3145736 | tf_op jit(solution)/shard_map/ppermute | solution.py:63
  95.1 4.1 %collective-permute-done.2 = bf16[2,16,64,128]{3,2,1,0:T(8,128)(2,1)} collective-permute-done((bf16[2,16,64,128]{3,2,1,0:T(8,128)(2,1)S(1)}, bf16[2,16,64,128]{3,2,1,0:T(8,128)(2,1)}, u32[]{:S(2)}, u32[]{:S(2)}) %collective-permute-start.2) | collective-permute-done | bytes 524320 | tf_op jit(solution)/shard_map/ppermute | solution.py:33
  100.7 15.9 %all-gather.2.cloned.1.call-done = bf16[4,8,64,16,64]{4,3,2,1,0:T(8,128)(2,1)} async-done(((bf16[1,8,64,16,64]{4,3,2,1,0:T(8,128)(2,1)}), bf16[4,8,64,16,64]{4,3,2,1,0:T(8,128)(2,1)}) %all-gather.2.cloned.1.call-update) | async-done | bytes 4194320 | tf_op jit(solution)/shard_map/all_gather | solution.py:49
  116.6 15.8 %fusion.3 = bf16[16,128,64,64,1,1]{1,3,5,2,0,4:T(8,128)(2,1)} fusion(bf16[8,16,4,16,128,1]{4,3,2,5,1,0:T(8,128)(2,1)S(1)} %bitcast.91, bf16[4,8,64,16,64]{4,3,2,1,0:T(8,128)(2,1)} %all-gather.2.cloned.1.call-done), kind=kOutput, calls=%fused_computation.3 | convolution fusion | flops 8589934592 | bytes 23068672 | tf_op jit(solution)/shard_map/wkqia,kpwid->padq/dot_general | solution.py:66
  132.4 11.7 %collective-permute-done.5 = bf16[64,128,64]{1,0,2:T(8,128)(2,1)} collective-permute-done((bf16[64,128,64]{1,0,2:T(8,128)(2,1)}, bf16[64,128,64]{1,0,2:T(8,128)(2,1)}, u32[]{:S(2)}, u32[]{:S(2)}) %collective-permute-start.5) | collective-permute-done | bytes 1048608 | tf_op jit(solution)/shard_map/ppermute | solution.py:63
  144.1 11.6 %fusion.1 = f32[16,64,256,1]{2,1,0,3:T(8,128)S(1)} fusion(bf16[16,128,64,64,1,1]{1,3,5,2,0,4:T(8,128)(2,1)} %fusion.3, bf16[64,128,64]{1,0,2:T(8,128)(2,1)} %collective-permute-done.6, bf16[64,128,64]{1,0,2:T(8,128)(2,1)} %collective-permute-done.5, bf16[64,128,64]{1,0,2:T(8,128)(2,1)} %collective-permute-done.4, bf16[64,128,64]{1,0,2:T(8,128)(2,1)} %bitcast.94), kind=kOutput, calls=%fused_computation.2 | convolution fusion | flops 4311744512 | bytes 22020096 | tf_op jit(solution)/shard_map/padq,bdq->pab/dot_general | solution.py:71
  160.1 4.7 %collective-permute-done.9 = f32[4,64,256]{2,1,0:T(8,128)} collective-permute-done((f32[4,64,256]{2,1,0:T(8,128)}, f32[4,64,256]{2,1,0:T(8,128)}, u32[]{:S(2)}, u32[]{:S(2)}) %collective-permute-start.9) | collective-permute-done | bytes 262176 | tf_op jit(solution)/shard_map/ppermute | solution.py:80
  164.9 1.8 collective-permute-done.8
  166.7 3.6 %collective-permute-done.7 = f32[4,64,256]{2,1,0:T(8,128)} collective-permute-done((f32[4,64,256]{2,1,0:T(8,128)S(1)}, f32[4,64,256]{2,1,0:T(8,128)}, u32[]{:S(2)}, u32[]{:S(2)}) %collective-permute-start.7) | collective-permute-done | bytes 262176 | tf_op jit(solution)/shard_map/ppermute | solution.py:80
  172.4 4.7 %collective-permute-start.13 = (f32[2,64,128]{2,1,0:T(8,128)S(1)}, f32[2,64,128]{2,1,0:T(8,128)S(1)}, u32[]{:S(2)}, u32[]{:S(2)}) collective-permute-start(f32[2,64,128]{2,1,0:T(8,128)S(1)} %pad_maximum_fusion.6), channel_id=1, source_target_pairs={{0,5},{1,13},{2,21},{3,29},{4,0},{5,8},{6,16},{7,24},{8,1},{9,9},{... | collective-permute-start | bytes 196616 | tf_op jit(solution)/shard_map/ppermute | solution.py:106
  177.2 4.9 %collective-permute-start.12 = (f32[2,64,128]{2,1,0:T(8,128)S(1)}, f32[2,64,128]{2,1,0:T(8,128)S(1)}, u32[]{:S(2)}, u32[]{:S(2)}) collective-permute-start(f32[2,64,128]{2,1,0:T(8,128)S(1)} %pad_maximum_fusion.5), channel_id=1, source_target_pairs={{0,4},{1,12},{2,20},{3,28},{4,5},{5,13},{6,21},{7,29},{8,0},{9,8},... | collective-permute-start | bytes 196616 | tf_op jit(solution)/shard_map/ppermute | solution.py:106
  182.2 1.9 collective-permute-start.10
  184.2 1.9 collective-permute-start.11
  186.3 4.2 %collective-permute-done.10 = f32[2,64,128]{2,1,0:T(8,128)S(1)} collective-permute-done((f32[2,64,128]{2,1,0:T(8,128)S(1)}, f32[2,64,128]{2,1,0:T(8,128)S(1)}, u32[]{:S(2)}, u32[]{:S(2)}) %collective-permute-start.10) | collective-permute-done | bytes 65568 | tf_op jit(solution)/shard_map/ppermute | solution.py:106
  (66 shorter events, 25.8 us)
Async XLA Ops:
  6.5 1.6 copy-start
  18.2 30.1 %all-to-all-start = ((bf16[8,2,32768]{2,1,0:T(2,128)(2,1)}), bf16[8,2,32768]{2,1,0:T(2,128)(2,1)S(1)}, u32[]{:S(2)}, u32[]{:S(2)}) async-start(bf16[8,2,32768]{2,1,0:T(2,128)(2,1)} %reshape.85), calls=%async_computation | async-start | bytes 2097152 | tf_op jit(solution)/shard_map/all_to_all | solution.py:45
  23.8 92.9 %all-gather.2.cloned.1.call-start = ((), (), s32[]{:S(2)}) async-start(), calls=%async_computation.1 | async-start | bytes 10485760 | tf_op jit(solution)/shard_map/all_gather | solution.py:49
  53.1 5.4 %copy-start.3 = (bf16[16,64,128]{2,1,0:T(8,128)(2,1)S(1)}, bf16[16,64,128]{2,1,0:T(8,128)(2,1)}, u32[]{:S(2)}) copy-start(bf16[16,64,128]{2,1,0:T(8,128)(2,1)} %param.6) | copy-start | bytes 786436
  58.5 14.7 %collective-permute-start = (bf16[16,64,128]{2,1,0:T(8,128)(2,1)S(1)}, bf16[16,64,128]{2,1,0:T(8,128)(2,1)S(1)}, u32[]{:S(2)}, u32[]{:S(2)}) collective-permute-start(bf16[16,64,128]{2,1,0:T(8,128)(2,1)S(1)} %copy-done.3), channel_id=1, source_target_pairs={{0,16},{4,20},{8,24},{12,28},{16,0},{20,4},{24,8},{28,12},{1,17},{... | collective-permute-start | bytes 786440 | tf_op jit(solution)/shard_map/ppermute | solution.py:30
  73.3 21.5 %collective-permute-start.3 = (bf16[2,16,64,128]{3,2,1,0:T(8,128)(2,1)S(1)}, bf16[2,16,64,128]{3,2,1,0:T(8,128)(2,1)}, u32[]{:S(2)}, u32[]{:S(2)}) collective-permute-start(bf16[2,16,64,128]{3,2,1,0:T(8,128)(2,1)S(1)} %get-tuple-element.25), channel_id=1, source_target_pairs={{0,12},{4,0},{8,4},{12,8},{16,28},{20,16},{24,20},{28,24},{1,13},{... | collective-permute-start | bytes 1572872 | tf_op jit(solution)/shard_map/ppermute | solution.py:33
  73.3 25.8 %collective-permute-start.2 = (bf16[2,16,64,128]{3,2,1,0:T(8,128)(2,1)S(1)}, bf16[2,16,64,128]{3,2,1,0:T(8,128)(2,1)}, u32[]{:S(2)}, u32[]{:S(2)}) collective-permute-start(bf16[2,16,64,128]{3,2,1,0:T(8,128)(2,1)S(1)} %get-tuple-element.25), channel_id=1, source_target_pairs={{0,8},{4,12},{8,0},{12,4},{16,24},{20,28},{24,16},{28,20},{1,9},{5... | collective-permute-start | bytes 1572872 | tf_op jit(solution)/shard_map/ppermute | solution.py:33
  76.2 22.9 %collective-permute-start.1 = (bf16[2,16,64,128]{3,2,1,0:T(8,128)(2,1)S(1)}, bf16[2,16,64,128]{3,2,1,0:T(8,128)(2,1)}, u32[]{:S(2)}, u32[]{:S(2)}) collective-permute-start(bf16[2,16,64,128]{3,2,1,0:T(8,128)(2,1)S(1)} %get-tuple-element.25), channel_id=1, source_target_pairs={{0,4},{4,8},{8,12},{12,0},{16,20},{20,24},{24,28},{28,16},{1,5},{5... | collective-permute-start | bytes 1572872 | tf_op jit(solution)/shard_map/ppermute | solution.py:33
  87.4 45.1 %collective-permute-start.6 = (bf16[64,128,64]{1,0,2:T(8,128)(2,1)}, bf16[64,128,64]{1,0,2:T(8,128)(2,1)}, u32[]{:S(2)}, u32[]{:S(2)}) collective-permute-start(bf16[64,128,64]{1,0,2:T(8,128)(2,1)} %bitcast.74), channel_id=1, source_target_pairs={{0,12},{4,0},{8,4},{12,8},{16,28},{20,16},{24,20},{28,24},{1,13},{... | collective-permute-start | bytes 3145736 | tf_op jit(solution)/shard_map/ppermute | solution.py:63
  91.4 52.7 %collective-permute-start.5 = (bf16[64,128,64]{1,0,2:T(8,128)(2,1)}, bf16[64,128,64]{1,0,2:T(8,128)(2,1)}, u32[]{:S(2)}, u32[]{:S(2)}) collective-permute-start(bf16[64,128,64]{1,0,2:T(8,128)(2,1)} %bitcast.75), channel_id=1, source_target_pairs={{0,8},{4,12},{8,0},{12,4},{16,24},{20,28},{24,16},{28,20},{1,9},{5... | collective-permute-start | bytes 3145736 | tf_op jit(solution)/shard_map/ppermute | solution.py:63
  94.8 49.3 %collective-permute-start.4 = (bf16[64,128,64]{1,0,2:T(8,128)(2,1)}, bf16[64,128,64]{1,0,2:T(8,128)(2,1)}, u32[]{:S(2)}, u32[]{:S(2)}) collective-permute-start(bf16[64,128,64]{1,0,2:T(8,128)(2,1)} %bitcast.95), channel_id=1, source_target_pairs={{0,4},{4,8},{8,12},{12,0},{16,20},{20,24},{24,28},{28,16},{1,5},{5... | collective-permute-start | bytes 3145736 | tf_op jit(solution)/shard_map/ppermute | solution.py:63
  144.1 15.6 %copy-start.4 = (s32[2,2]{1,0:T(2,128)S(1)}, s32[2,2]{1,0:T(2,128)}, u32[]{:S(2)}) copy-start(s32[2,2]{1,0:T(2,128)} %param.9) | copy-start | bytes 52
  144.1 15.8 %copy-start.5 = (f32[128]{0:T(128)S(1)}, f32[128]{0:T(128)}, u32[]{:S(2)}) copy-start(f32[128]{0:T(128)} %param.10) | copy-start | bytes 1540
  144.1 48.6 %copy-start.1 = (bf16[64,64,256]{2,1,0:T(8,128)(2,1)S(1)}, bf16[64,64,256]{2,1,0:T(8,128)(2,1)}, u32[]{:S(2)}) copy-start(bf16[64,64,256]{2,1,0:T(8,128)(2,1)} %param.7) | copy-start | bytes 6291460
  155.7 11.0 %copy-start.2 = (f32[16,64,256,1]{2,1,0,3:T(8,128)}, f32[16,64,256,1]{2,1,0,3:T(8,128)S(1)}, u32[]{:S(2)}) copy-start(f32[16,64,256,1]{2,1,0,3:T(8,128)S(1)} %fusion.1) | copy-start | bytes 3145732
  155.7 30.5 %slice-start = ((f32[512]{0:T(512)}), f32[64]{0:T(128)S(1)}, s32[]{:S(2)}) async-start(f32[512]{0:T(512)} %param.11), calls=%async_computation.2 | async-start | bytes 1024 | tf_op jit(solution)/shard_map/slice | solution.py:118
  155.7 30.5 %copy-start.6 = (f32[512]{0:T(512)S(1)}, f32[512]{0:T(512)}, u32[]{:S(2)}) copy-start(f32[512]{0:T(512)} %param.11) | copy-start | bytes 6148
  156.7 8.2 %collective-permute-start.9 = (f32[4,64,256]{2,1,0:T(8,128)}, f32[4,64,256]{2,1,0:T(8,128)}, u32[]{:S(2)}, u32[]{:S(2)}) collective-permute-start(f32[4,64,256]{2,1,0:T(8,128)} %get-tuple-element.14), channel_id=1, source_target_pairs={{0,3},{1,0},{2,1},{3,2},{4,7},{5,4},{6,5},{7,6},{8,11},{9,8},{10,9... | collective-permute-start | bytes 786440 | tf_op jit(solution)/shard_map/ppermute | solution.py:80
  158.1 8.6 %collective-permute-start.8 = (f32[4,64,256]{2,1,0:T(8,128)}, f32[4,64,256]{2,1,0:T(8,128)}, u32[]{:S(2)}, u32[]{:S(2)}) collective-permute-start(f32[4,64,256]{2,1,0:T(8,128)} %get-tuple-element.15), channel_id=1, source_target_pairs={{0,2},{1,3},{2,0},{3,1},{4,6},{5,7},{6,4},{7,5},{8,10},{9,11},{10,... | collective-permute-start | bytes 786440 | tf_op jit(solution)/shard_map/ppermute | solution.py:80
  158.3 12.0 %collective-permute-start.7 = (f32[4,64,256]{2,1,0:T(8,128)S(1)}, f32[4,64,256]{2,1,0:T(8,128)}, u32[]{:S(2)}, u32[]{:S(2)}) collective-permute-start(f32[4,64,256]{2,1,0:T(8,128)S(1)} %get-tuple-element.13), channel_id=1, source_target_pairs={{0,1},{1,2},{2,3},{3,0},{4,5},{5,6},{6,7},{7,4},{8,9},{9,10},{10,1... | collective-permute-start | bytes 786440 | tf_op jit(solution)/shard_map/ppermute | solution.py:80
  172.4 13.9 %collective-permute-start.13 = (f32[2,64,128]{2,1,0:T(8,128)S(1)}, f32[2,64,128]{2,1,0:T(8,128)S(1)}, u32[]{:S(2)}, u32[]{:S(2)}) collective-permute-start(f32[2,64,128]{2,1,0:T(8,128)S(1)} %pad_maximum_fusion.6), channel_id=1, source_target_pairs={{0,5},{1,13},{2,21},{3,29},{4,0},{5,8},{6,16},{7,24},{8,1},{9,9},{... | collective-permute-start | bytes 196616 | tf_op jit(solution)/shard_map/ppermute | solution.py:106
  177.2 9.1 %collective-permute-start.12 = (f32[2,64,128]{2,1,0:T(8,128)S(1)}, f32[2,64,128]{2,1,0:T(8,128)S(1)}, u32[]{:S(2)}, u32[]{:S(2)}) collective-permute-start(f32[2,64,128]{2,1,0:T(8,128)S(1)} %pad_maximum_fusion.5), channel_id=1, source_target_pairs={{0,4},{1,12},{2,20},{3,28},{4,5},{5,13},{6,21},{7,29},{8,0},{9,8},... | collective-permute-start | bytes 196616 | tf_op jit(solution)/shard_map/ppermute | solution.py:106
  182.2 8.3 %collective-permute-start.10 = (f32[2,64,128]{2,1,0:T(8,128)S(1)}, f32[2,64,128]{2,1,0:T(8,128)S(1)}, u32[]{:S(2)}, u32[]{:S(2)}) collective-permute-start(f32[2,64,128]{2,1,0:T(8,128)S(1)} %pad_maximum_fusion.3), channel_id=1, source_target_pairs={{0,0},{1,8},{2,16},{3,24},{4,1},{5,9},{6,17},{7,25},{8,4},{9,12},{... | collective-permute-start | bytes 196616 | tf_op jit(solution)/shard_map/ppermute | solution.py:106
  184.2 7.8 %collective-permute-start.11 = (f32[2,64,128]{2,1,0:T(8,128)S(1)}, f32[2,64,128]{2,1,0:T(8,128)S(1)}, u32[]{:S(2)}, u32[]{:S(2)}) collective-permute-start(f32[2,64,128]{2,1,0:T(8,128)S(1)} %pad_maximum_fusion.4), channel_id=1, source_target_pairs={{0,1},{1,9},{2,17},{3,25},{4,4},{5,12},{6,20},{7,28},{8,5},{9,13},... | collective-permute-start | bytes 196616 | tf_op jit(solution)/shard_map/ppermute | solution.py:106
Sparse Core Ops, SparseCore 0:
  58.6 57.9 all-gather.1
